TPU v7x, 32 devices: a whole 2x2x4 slice. The times are simulated.
32 devices in a mesh: groups: 2 (over y), ctx: 4 (over z), fsdp: 2 (over x), sub: 2 (over core).
Axes of the slice: x: 2, y: 2, z: 4, core: 2. Of those that a mesh axis runs over, the one named last changes fastest.
Arguments:
- layer_input: bfloat16 [4, 2048, 2304], P(('groups', 'fsdp'), ('ctx', 'sub')), parts along dimension 0, may hold values from -6 to 6
- query_heads: bfloat16 [4, 2048, 1024], P(('groups', 'fsdp'), ('ctx', 'sub')), parts along dimension 0, may hold values from -11 to 11
- key_heads: bfloat16 [4, 2048, 512], P(('groups', 'fsdp'), ('ctx', 'sub')), parts along dimension 0, may hold values from -11 to 11
- value_heads: bfloat16 [4, 2048, 512], P(('groups', 'fsdp'), ('ctx', 'sub')), parts along dimension 0, may hold values from -6 to 6
- grad_out: bfloat16 [4, 2048, 1024], P(('groups', 'fsdp'), ('ctx', 'sub')), parts along dimension 0, may hold values from -96 to 96
- doc_starts: int32 [4, 12], P(('groups', 'fsdp')), parts along dimension 0, may hold values from 0 to 2047, as said below
Outputs:
- grad_query: bfloat16 [4, 2048, 1024], P(('groups', 'fsdp'), ('ctx', 'sub')), parts along dimension 0
- grad_key: bfloat16 [4, 2048, 512], P(('groups', 'fsdp'), ('ctx', 'sub')), parts along dimension 0
- grad_value: bfloat16 [4, 2048, 512], P(('groups', 'fsdp'), ('ctx', 'sub')), parts along dimension 0
- grad_value_proj: float32 [4608, 512], P(('groups', 'fsdp')), parts along dimension 0
There are 2 independent parts, one for each index of `groups`. A program takes and returns all parts, laid end to end along the dimension named above; each array names one. Nothing has to cross between parts.
Inputs may be any that keep to these rules, and one draw needn't show every extreme that they name: `doc_starts`: each row holds the first positions of the 12 documents of one sequence in increasing order; the first is 0, every document has at least one token, and the longest has exactly 1024 tokens.
All inputs are finite; a program needn't handle non-finite values.
Results may differ from a plain program's by a relative error of at most 0.015.
Values may be sent and summed in bfloat16 or wider, within the bound.
No kernel may reach another device: no remote copies, remote signals or barrier semaphores. Data moves between devices by JAX's collectives and lax.ppermute only.
A program may use at most 64 MiB of HBM per device.

v0:
```python
import jax
import jax.numpy as jnp
from jax import lax
from jax.sharding import PartitionSpec as P

HEAD_DIM = 256
SPAN = 768


def passed_along(value, axis, steps):
    count = lax.axis_size(axis)
    first, last = (max(0, -steps), min(count, count - steps))
    return lax.ppermute(value, axis, [(source, source + steps) for source in range(first, last)])


def doc_start_of(starts, positions):
    covered = starts[None, :] <= positions[:, None]
    return jnp.max(jnp.where(covered, starts[None, :], 0), axis=1)


def attend_block(queries, key_block, value_block, grads, query_pos, key_pos, lowest):
    row_count = queries.shape[0]
    key_count = key_block.shape[0]
    groups = key_block.shape[1] // HEAD_DIM
    per_group = queries.shape[1] // key_block.shape[1]
    inv_root = HEAD_DIM ** (-0.5)
    query_four = queries.reshape(row_count, groups, per_group, HEAD_DIM)
    grad_four = grads.reshape(row_count, groups, per_group, HEAD_DIM)
    key_three = key_block.reshape(key_count, groups, HEAD_DIM)
    value_three = value_block.reshape(key_count, groups, HEAD_DIM)
    allowed = (key_pos[None, :] >= lowest[:, None]) & (key_pos[None, :] <= query_pos[:, None])

    def one_group(group):
        query_g = lax.dynamic_index_in_dim(query_four, group, 1, keepdims=False)
        grad_g = lax.dynamic_index_in_dim(grad_four, group, 1, keepdims=False)
        key_g = lax.dynamic_index_in_dim(key_three, group, 1, keepdims=False)
        value_g = lax.dynamic_index_in_dim(value_three, group, 1, keepdims=False)
        scores = (
            jnp.einsum("thd,kd->htk", query_g, key_g, preferred_element_type=jnp.float32) * inv_root
        )
        scores = jnp.where(allowed[None], scores, -1e30)
        largest = jnp.max(scores, axis=2, keepdims=True)
        raised = jnp.where(allowed[None], jnp.exp(scores - largest), 0.0)
        attn_probs = raised / jnp.sum(raised, axis=2, keepdims=True)
        grad_probs = jnp.einsum("thd,kd->htk", grad_g, value_g, preferred_element_type=jnp.float32)
        row_dot = jnp.sum(attn_probs * grad_probs, axis=2, keepdims=True)
        grad_scores = (attn_probs * (grad_probs - row_dot) * inv_root).astype(jnp.bfloat16)
        probs_low = attn_probs.astype(jnp.bfloat16)
        grad_q = jnp.einsum("htk,kd->thd", grad_scores, key_g, preferred_element_type=jnp.float32)
        grad_k = jnp.einsum("htk,thd->kd", grad_scores, query_g, preferred_element_type=jnp.float32)
        grad_v = jnp.einsum("htk,thd->kd", probs_low, grad_g, preferred_element_type=jnp.float32)
        return (grad_q, grad_k, grad_v)

    grad_q, grad_k, grad_v = lax.map(one_group, jnp.arange(groups, dtype=jnp.int32))
    grad_q = jnp.moveaxis(grad_q, 0, 1).reshape(row_count, -1)
    grad_k = jnp.moveaxis(grad_k, 0, 1).reshape(key_count, -1)
    grad_v = jnp.moveaxis(grad_v, 0, 1).reshape(key_count, -1)
    return (grad_q, grad_k, grad_v)


def body(layer_input, query_heads, key_heads, value_heads, grad_out, doc_starts):
    block_rows = query_heads.shape[1]
    window = min(SPAN, lax.axis_size(("ctx", "sub")) * block_rows // 2)
    reach_blocks = (window + block_rows - 2) // block_rows
    margin_rows = reach_blocks * block_rows
    key_count = margin_rows + block_rows
    first_row = lax.axis_index(("ctx", "sub")) * block_rows
    own_keys = key_heads[0]
    own_values = value_heads[0]
    arrived = []
    moving_k = own_keys
    moving_v = own_values
    for distance in range(reach_blocks):
        moving_k, moving_v = passed_along((moving_k, moving_v), ("ctx", "sub"), 1)
        arrived.append((moving_k, moving_v))
    arrived = arrived[::-1]
    key_span = jnp.concatenate([pair[0] for pair in arrived] + [own_keys], axis=0)
    value_span = jnp.concatenate([pair[1] for pair in arrived] + [own_values], axis=0)
    query_pos = first_row + jnp.arange(block_rows, dtype=jnp.int32)
    key_pos = first_row - margin_rows + jnp.arange(key_count, dtype=jnp.int32)
    lowest = jnp.maximum(doc_start_of(doc_starts[0], query_pos), query_pos - window + 1)
    grad_q, grad_k_span, grad_v_span = attend_block(
        query_heads[0], key_span, value_span, grad_out[0], query_pos, key_pos, lowest
    )

    def own_piece(distance):
        begin = (reach_blocks - distance) * block_rows
        return (grad_k_span[begin : begin + block_rows], grad_v_span[begin : begin + block_rows])

    total_k, total_v = own_piece(reach_blocks)
    for distance in range(reach_blocks - 1, -1, -1):
        moved_k, moved_v = (
            passed_along(total_k.astype(jnp.bfloat16), ("ctx", "sub"), -1).astype(total_k.dtype),
            passed_along(total_v.astype(jnp.bfloat16), ("ctx", "sub"), -1).astype(total_v.dtype),
        )
        piece_k, piece_v = own_piece(distance)
        total_k = moved_k + piece_k
        total_v = moved_v + piece_v
    grad_key = total_k.astype(jnp.bfloat16)
    grad_value = total_v.astype(jnp.bfloat16)
    contract = (((0,), (0,)), ((), ()))
    term_v = lax.dot_general(
        layer_input[0], grad_value, contract, preferred_element_type=jnp.float32
    )
    shard_v = lax.psum_scatter(term_v.astype(jnp.bfloat16), "fsdp", scatter_dimension=0, tiled=True)
    weight_v = lax.psum(shard_v, ("ctx", "sub")).astype(jnp.float32)
    token_scale = float(lax.axis_size("fsdp") * lax.axis_size(("ctx", "sub")) * block_rows) ** (
        -0.5
    )
    return (
        grad_q.astype(jnp.bfloat16)[None],
        grad_key[None],
        grad_value[None],
        weight_v * token_scale,
    )


def solution(mesh):
    placed = (
        P(("groups", "fsdp"), ("ctx", "sub"), None),
        P(("groups", "fsdp"), ("ctx", "sub"), None),
        P(("groups", "fsdp"), ("ctx", "sub"), None),
        P(("groups", "fsdp"), ("ctx", "sub"), None),
        P(("groups", "fsdp"), ("ctx", "sub"), None),
        P(("groups", "fsdp"), None),
    )
    return jax.shard_map(
        body,
        mesh=mesh,
        in_specs=placed,
        out_specs=(
            P(("groups", "fsdp"), ("ctx", "sub"), None),
            P(("groups", "fsdp"), ("ctx", "sub"), None),
            P(("groups", "fsdp"), ("ctx", "sub"), None),
            P(("groups", "fsdp"), None),
        ),
        check_vma=False,
    )
```

profile of v0, /device:TPU:0, one launch (start us, length us, event | category | flops | bytes accessed | tf_op | source)
XLA Modules:
  0.0 211.9 jit_solution(1971740638180802092)
XLA Ops:
  7.2 1.2 copy.68
  8.4 2.4 %collective-permute-start = (bf16[256,512]{0,1:T(8,128)(2,1)S(1)}, bf16[256,512]{0,1:T(8,128)(2,1)S(1)}, u32[]{:S(2)}, u32[]{:S(2)}) collective-permute-start(bf16[256,512]{0,1:T(8,128)(2,1)S(1)} %bitcast.186), channel_id=1, source_target_pairs={{0,1},{1,4},{4,5},{5,8},{8,9},{9,12},{12,13},{2,3},{3,6},{6,7},{7,... | collective-permute-start | bytes 786440 | tf_op jit(solution)/shard_map/ppermute | solution.py:13
  10.8 1.1 copy.71
  11.9 4.6 %collective-permute-start.3 = (bf16[256,512]{0,1:T(8,128)(2,1)S(1)}, bf16[256,512]{0,1:T(8,128)(2,1)S(1)}, u32[]{:S(2)}, u32[]{:S(2)}) collective-permute-start(bf16[256,512]{0,1:T(8,128)(2,1)S(1)} %bitcast.184), channel_id=1, source_target_pairs={{0,1},{1,4},{4,5},{5,8},{8,9},{9,12},{12,13},{2,3},{3,6},{6,7},{7,... | collective-permute-start | bytes 786440 | tf_op jit(solution)/shard_map/ppermute | solution.py:13
  16.5 2.2 %collective-permute-start.1 = (bf16[256,512]{0,1:T(8,128)(2,1)S(1)}, bf16[256,512]{0,1:T(8,128)(2,1)S(1)}, u32[]{:S(2)}, u32[]{:S(2)}) collective-permute-start(bf16[256,512]{0,1:T(8,128)(2,1)S(1)} %collective-permute-done), channel_id=1, source_target_pairs={{0,1},{1,4},{4,5},{5,8},{8,9},{9,12},{12,13},{2,3},{3,6},{6,7},{7,... | collective-permute-start | bytes 786440 | tf_op jit(solution)/shard_map/ppermute | solution.py:13
  18.7 4.4 %collective-permute-start.4 = (bf16[256,512]{0,1:T(8,128)(2,1)S(1)}, bf16[256,512]{0,1:T(8,128)(2,1)S(1)}, u32[]{:S(2)}, u32[]{:S(2)}) collective-permute-start(bf16[256,512]{0,1:T(8,128)(2,1)S(1)} %collective-permute-done.3), channel_id=1, source_target_pairs={{0,1},{1,4},{4,5},{5,8},{8,9},{9,12},{12,13},{2,3},{3,6},{6,7},{7,... | collective-permute-start | bytes 786440 | tf_op jit(solution)/shard_map/ppermute | solution.py:13
  23.1 0.7 select_reduce_fusion
  23.9 3.7 %collective-permute-start.2 = (bf16[256,512]{0,1:T(8,128)(2,1)S(1)}, bf16[256,512]{0,1:T(8,128)(2,1)}, u32[]{:S(2)}, u32[]{:S(2)}) collective-permute-start(bf16[256,512]{0,1:T(8,128)(2,1)S(1)} %collective-permute-done.1), channel_id=1, source_target_pairs={{0,1},{1,4},{4,5},{5,8},{8,9},{9,12},{12,13},{2,3},{3,6},{6,7},{7,... | collective-permute-start | bytes 786440 | tf_op jit(solution)/shard_map/ppermute | solution.py:13
  27.6 3.2 %collective-permute-start.5 = (bf16[256,512]{0,1:T(8,128)(2,1)S(1)}, bf16[256,512]{0,1:T(8,128)(2,1)S(1)}, u32[]{:S(2)}, u32[]{:S(2)}) collective-permute-start(bf16[256,512]{0,1:T(8,128)(2,1)S(1)} %collective-permute-done.4), channel_id=1, source_target_pairs={{0,1},{1,4},{4,5},{5,8},{8,9},{9,12},{12,13},{2,3},{3,6},{6,7},{7,... | collective-permute-start | bytes 786440 | tf_op jit(solution)/shard_map/ppermute | solution.py:13
  30.8 2.1 copy.73
  32.9 1.0 copy.70
  33.9 2.1 pad_maximum_fusion
  36.0 1.2 pad_maximum_fusion.1
  37.1 37.4 %while.15 = (s32[]{:T(128)}, bf16[2,256,2,256]{1,3,2,0:T(8,128)(2,1)}, f32[2,1024,256]{2,1,0:T(8,128)}, f32[2,1024,256]{2,1,0:T(8,128)}, s32[2]{0:T(128)S(1)}, /...) while((s32[]{:T(128)}, ...), condition=%wide.region_5.6_spmd.clone, body=%wide.region_1.5_spmd.clone.sunk | while | flops 1353977856 | bytes 29120200 | solution.py:54
  37.1 0.6 dynamic_slice.82
  39.7 0.3 compare_and_fusion.2
  39.9 3.5 %fusion.90 = (f32[2,256]{1,0:T(2,128)S(1)}, f32[2,256,1024]{1,2,0:T(8,128)}) fusion(pred[256,1024]{0,1:T(8,128)(4,1)S(1)} %compare_and_fusion.2, bf16[256,2,2,256]{0,3,2,1:T(8,128)(2,1)} %get-tuple-element.287, s32[]{:T(128)S(6)} %select_n.34, bf16[1024,2,256]{0,2,1:T(8,128)(2,1)} %get-tuple-element.286), kind=kOutput, calls=%fused_computation.80.clone.1 | convolution fusion | flops 271057920 | bytes 3410944 | tf_op jit(solution)/shard_map/while/body/eval_jaxpr/sub | solution.py:43
  43.4 1.6 fusion.89
  45.0 3.9 %fusion.92 = f32[2,1024,256]{2,1,0:T(8,128)} fusion(f32[2,1024,256]{2,1,0:T(8,128)} %get-tuple-element.268, s32[]{:T(128)} %get-tuple-element.266, f32[1024,256,2]{1,0,2:T(8,128)S(1)} %fusion.89, bf16[256,2,2,256]{0,3,2,1:T(8,128)(2,1)} %get-tuple-element.287, s32[]{:T(128)S(6)} %select_n.34, f32[2,256,1024]{1,2,0:T(8,128)} %get-tuple-element.249, ...), kind=kOutput, calls=%fused_computation.14.clone.1 | convolution fusion | flops 272107008 | bytes 9703940 | tf_op jit(solution)/shard_map/while/body/eval_jaxpr/htk,thd->kd/dot_general | solution.py:50
  48.9 3.0 %fusion.93 = f32[2,1024,256]{2,1,0:T(8,128)} fusion(f32[2,1024,256]{2,1,0:T(8,128)} %get-tuple-element.269, s32[]{:T(128)} %get-tuple-element.266, bf16[256,2,2,256]{0,3,2,1:T(8,128)(2,1)} %get-tuple-element.289, s32[]{:T(128)S(6)} %select_n.34, f32[2,256,1024]{1,2,0:T(8,128)} %get-tuple-element.249, f32[2,256]{1,0:T(2,128)S(1)} %get-tuple-element.250), kind=kOutput, calls=%fused_computation.12.clone.1 | convolution fusion | flops 269484032 | bytes 3410436 | tf_op jit(solution)/shard_map/while/body/eval_jaxpr/htk,thd->kd/dot_general | solution.py:51
  51.9 3.9 %fusion.91 = bf16[2,256,2,256]{1,3,2,0:T(8,128)(2,1)} fusion(bf16[2,256,2,256]{1,3,2,0:T(8,128)(2,1)} %get-tuple-element.267, s32[]{:T(128)} %get-tuple-element.266, f32[1024,256,2]{1,0,2:T(8,128)S(1)} %fusion.89, bf16[1024,2,256]{0,2,1:T(8,128)(2,1)} %get-tuple-element.286, s32[]{:T(128)S(6)} %select_n.34, f32[2,256,1024]{1,2,0:T(8,128)} %get-tuple-element.249, ...), kind=kOutput, calls=%fused_computation.16.clone.1 | convolution fusion | flops 272107008 | bytes 9441796 | tf_op jit(solution)/shard_map/while/body/eval_jaxpr/htk,kd->thd/dot_general | solution.py:49
  55.8 0.6 dynamic_slice.82
  58.3 0.3 compare_and_fusion.2
  58.6 3.5 %fusion.90 = (f32[2,256]{1,0:T(2,128)S(1)}, f32[2,256,1024]{1,2,0:T(8,128)}) fusion(pred[256,1024]{0,1:T(8,128)(4,1)S(1)} %compare_and_fusion.2, bf16[256,2,2,256]{0,3,2,1:T(8,128)(2,1)} %get-tuple-element.287, s32[]{:T(128)S(6)} %select_n.34, bf16[1024,2,256]{0,2,1:T(8,128)(2,1)} %get-tuple-element.286), kind=kOutput, calls=%fused_computation.80.clone.1 | convolution fusion | flops 271057920 | bytes 3410944 | tf_op jit(solution)/shard_map/while/body/eval_jaxpr/sub | solution.py:43
  62.1 1.6 fusion.89
  63.6 4.0 %fusion.92 = f32[2,1024,256]{2,1,0:T(8,128)} fusion(f32[2,1024,256]{2,1,0:T(8,128)} %get-tuple-element.268, s32[]{:T(128)} %get-tuple-element.266, f32[1024,256,2]{1,0,2:T(8,128)S(1)} %fusion.89, bf16[256,2,2,256]{0,3,2,1:T(8,128)(2,1)} %get-tuple-element.287, s32[]{:T(128)S(6)} %select_n.34, f32[2,256,1024]{1,2,0:T(8,128)} %get-tuple-element.249, ...), kind=kOutput, calls=%fused_computation.14.clone.1 | convolution fusion | flops 272107008 | bytes 9703940 | tf_op jit(solution)/shard_map/while/body/eval_jaxpr/htk,thd->kd/dot_general | solution.py:50
  67.6 3.0 %fusion.93 = f32[2,1024,256]{2,1,0:T(8,128)} fusion(f32[2,1024,256]{2,1,0:T(8,128)} %get-tuple-element.269, s32[]{:T(128)} %get-tuple-element.266, bf16[256,2,2,256]{0,3,2,1:T(8,128)(2,1)} %get-tuple-element.289, s32[]{:T(128)S(6)} %select_n.34, f32[2,256,1024]{1,2,0:T(8,128)} %get-tuple-element.249, f32[2,256]{1,0:T(2,128)S(1)} %get-tuple-element.250), kind=kOutput, calls=%fused_computation.12.clone.1 | convolution fusion | flops 269484032 | bytes 3410436 | tf_op jit(solution)/shard_map/while/body/eval_jaxpr/htk,thd->kd/dot_general | solution.py:51
  70.7 3.9 %fusion.91 = bf16[2,256,2,256]{1,3,2,0:T(8,128)(2,1)} fusion(bf16[2,256,2,256]{1,3,2,0:T(8,128)(2,1)} %get-tuple-element.267, s32[]{:T(128)} %get-tuple-element.266, f32[1024,256,2]{1,0,2:T(8,128)S(1)} %fusion.89, bf16[1024,2,256]{0,2,1:T(8,128)(2,1)} %get-tuple-element.286, s32[]{:T(128)S(6)} %select_n.34, f32[2,256,1024]{1,2,0:T(8,128)} %get-tuple-element.249, ...), kind=kOutput, calls=%fused_computation.16.clone.1 | convolution fusion | flops 272107008 | bytes 9441796 | tf_op jit(solution)/shard_map/while/body/eval_jaxpr/htk,kd->thd/dot_general | solution.py:49
  74.5 1.1 fusion.61
  75.6 1.3 collective-permute-start.9
  76.9 1.5 slice_bitcast_fusion.2
  78.4 0.1 copy.103
  78.5 1.2 collective-permute-done.9
  79.6 0.1 add_convert_fusion.2
  79.7 1.3 collective-permute-start.10
  81.0 0.1 copy.104
  81.1 6.3 %collective-permute-done.10 = bf16[256,512]{1,0:T(8,128)(2,1)S(1)} collective-permute-done((bf16[256,512]{1,0:T(8,128)(2,1)S(1)}, bf16[256,512]{1,0:T(8,128)(2,1)S(1)}, u32[]{:S(2)}, u32[]{:S(2)}) %collective-permute-start.10) | collective-permute-done | bytes 262176 | tf_op jit(solution)/shard_map/ppermute | solution.py:13
  87.4 0.1 add_convert_fusion.1
  87.5 1.3 collective-permute-start.11
  88.8 0.1 copy.105
  88.9 6.3 %collective-permute-done.11 = bf16[256,512]{1,0:T(8,128)(2,1)S(1)} collective-permute-done((bf16[256,512]{1,0:T(8,128)(2,1)S(1)}, bf16[256,512]{1,0:T(8,128)(2,1)S(1)}, u32[]{:S(2)}, u32[]{:S(2)}) %collective-permute-start.11) | collective-permute-done | bytes 262176 | tf_op jit(solution)/shard_map/ppermute | solution.py:13
  95.2 0.7 copy-done.3
  95.9 0.8 fusion.57
  96.7 2.4 %copy.92 = bf16[2304,512]{1,0:T(8,128)(2,1)} copy(bf16[2304,512]{0,1:T(8,128)(2,1)S(1)} %fusion.57) | data formatting | bytes 4718592
  99.2 1.1 fusion.60
  100.4 1.3 collective-permute-start.6
  101.7 1.5 slice_bitcast_fusion.5
  103.1 0.1 copy.99
  103.2 4.9 %collective-permute-done.6 = bf16[256,512]{1,0:T(8,128)(2,1)S(1)} collective-permute-done((bf16[256,512]{1,0:T(8,128)(2,1)S(1)}, bf16[256,512]{1,0:T(8,128)(2,1)S(1)}, u32[]{:S(2)}, u32[]{:S(2)}) %collective-permute-start.6) | collective-permute-done | bytes 262176 | tf_op jit(solution)/shard_map/ppermute | solution.py:13
  108.0 0.8 add_convert_fusion.5
  108.8 1.3 collective-permute-start.7
  110.1 0.1 copy.100
  110.2 28.5 %reduce-scatter.4.cloned.1.call-done = bf16[1152,512]{1,0:T(8,128)(2,1)} async-done(((bf16[2304,512]{1,0:T(8,128)(2,1)}), bf16[1152,512]{1,0:T(8,128)(2,1)}) %reduce-scatter.4.cloned.1.call-update) | async-done | bytes 1179664
  138.7 2.4 %copy.93 = bf16[1152,512]{0,1:T(8,128)(2,1)} copy(bf16[1152,512]{1,0:T(8,128)(2,1)} %reduce-scatter.4.cloned.1.call-done) | data formatting | bytes 2359296
  141.1 1.8 add_convert_fusion.4
  142.9 1.3 collective-permute-start.8
  144.2 0.1 copy.101
  144.3 1.0 copy.90
  145.3 0.8 fusion.62
  146.1 0.6 collective-permute-done.8
  146.7 1.7 fusion.59
  148.4 53.2 %all-reduce.2.cloned.1.call-done = bf16[1152,512]{0,1:T(8,128)(2,1)} async-done(((bf16[1152,512]{0,1:T(8,128)(2,1)}), bf16[1152,512]{0,1:T(8,128)(2,1)}) %all-reduce.2.cloned.1.call-update) | async-done | bytes 1179664 | tf_op jit(solution)/shard_map/psum | solution.py:106
  201.6 1.4 convert_multiply_fusion
  203.1 2.0 copy.87
  (33 shorter events, 0.2 us)
Async XLA Ops:
  7.2 88.7 %copy-start = (bf16[1,256,2304]{2,1,0:T(8,128)(2,1)S(1)}, bf16[1,256,2304]{2,1,0:T(8,128)(2,1)}, u32[]{:S(2)}) copy-start(bf16[1,256,2304]{2,1,0:T(8,128)(2,1)} %param.8) | copy-start | bytes 3538948
  7.2 25.7 %copy-start.5 = (bf16[1,256,1024]{2,1,0:T(8,128)(2,1)S(1)}, bf16[1,256,1024]{2,1,0:T(8,128)(2,1)}, u32[]{:S(2)}) copy-start(bf16[1,256,1024]{2,1,0:T(8,128)(2,1)} %param.9) | copy-start | bytes 1572868
  7.2 131.5 %reduce-scatter.4.cloned.1.call-start = ((), (), s32[]{:S(2)}) async-start(), calls=%async_computation.2 | async-start | bytes 3538944
  8.4 8.1 %collective-permute-start = (bf16[256,512]{0,1:T(8,128)(2,1)S(1)}, bf16[256,512]{0,1:T(8,128)(2,1)S(1)}, u32[]{:S(2)}, u32[]{:S(2)}) collective-permute-start(bf16[256,512]{0,1:T(8,128)(2,1)S(1)} %bitcast.186), channel_id=1, source_target_pairs={{0,1},{1,4},{4,5},{5,8},{8,9},{9,12},{12,13},{2,3},{3,6},{6,7},{7,... | collective-permute-start | bytes 786440 | tf_op jit(solution)/shard_map/ppermute | solution.py:13
  11.9 6.8 %collective-permute-start.3 = (bf16[256,512]{0,1:T(8,128)(2,1)S(1)}, bf16[256,512]{0,1:T(8,128)(2,1)S(1)}, u32[]{:S(2)}, u32[]{:S(2)}) collective-permute-start(bf16[256,512]{0,1:T(8,128)(2,1)S(1)} %bitcast.184), channel_id=1, source_target_pairs={{0,1},{1,4},{4,5},{5,8},{8,9},{9,12},{12,13},{2,3},{3,6},{6,7},{7,... | collective-permute-start | bytes 786440 | tf_op jit(solution)/shard_map/ppermute | solution.py:13
  16.5 7.4 %collective-permute-start.1 = (bf16[256,512]{0,1:T(8,128)(2,1)S(1)}, bf16[256,512]{0,1:T(8,128)(2,1)S(1)}, u32[]{:S(2)}, u32[]{:S(2)}) collective-permute-start(bf16[256,512]{0,1:T(8,128)(2,1)S(1)} %collective-permute-done), channel_id=1, source_target_pairs={{0,1},{1,4},{4,5},{5,8},{8,9},{9,12},{12,13},{2,3},{3,6},{6,7},{7,... | collective-permute-start | bytes 786440 | tf_op jit(solution)/shard_map/ppermute | solution.py:13
  18.7 8.9 %collective-permute-start.4 = (bf16[256,512]{0,1:T(8,128)(2,1)S(1)}, bf16[256,512]{0,1:T(8,128)(2,1)S(1)}, u32[]{:S(2)}, u32[]{:S(2)}) collective-permute-start(bf16[256,512]{0,1:T(8,128)(2,1)S(1)} %collective-permute-done.3), channel_id=1, source_target_pairs={{0,1},{1,4},{4,5},{5,8},{8,9},{9,12},{12,13},{2,3},{3,6},{6,7},{7,... | collective-permute-start | bytes 786440 | tf_op jit(solution)/shard_map/ppermute | solution.py:13
  23.9 10.0 %collective-permute-start.2 = (bf16[256,512]{0,1:T(8,128)(2,1)S(1)}, bf16[256,512]{0,1:T(8,128)(2,1)}, u32[]{:S(2)}, u32[]{:S(2)}) collective-permute-start(bf16[256,512]{0,1:T(8,128)(2,1)S(1)} %collective-permute-done.1), channel_id=1, source_target_pairs={{0,1},{1,4},{4,5},{5,8},{8,9},{9,12},{12,13},{2,3},{3,6},{6,7},{7,... | collective-permute-start | bytes 786440 | tf_op jit(solution)/shard_map/ppermute | solution.py:13
  27.6 8.4 %collective-permute-start.5 = (bf16[256,512]{0,1:T(8,128)(2,1)S(1)}, bf16[256,512]{0,1:T(8,128)(2,1)S(1)}, u32[]{:S(2)}, u32[]{:S(2)}) collective-permute-start(bf16[256,512]{0,1:T(8,128)(2,1)S(1)} %collective-permute-done.4), channel_id=1, source_target_pairs={{0,1},{1,4},{4,5},{5,8},{8,9},{9,12},{12,13},{2,3},{3,6},{6,7},{7,... | collective-permute-start | bytes 786440 | tf_op jit(solution)/shard_map/ppermute | solution.py:13
  75.6 4.0 %collective-permute-start.9 = (bf16[256,512]{1,0:T(8,128)(2,1)S(1)}, bf16[256,512]{1,0:T(8,128)(2,1)S(1)}, u32[]{:S(2)}, u32[]{:S(2)}) collective-permute-start(bf16[256,512]{1,0:T(8,128)(2,1)S(1)} %bitcast.189), channel_id=1, source_target_pairs={{1,0},{4,1},{5,4},{8,5},{9,8},{12,9},{13,12},{3,2},{6,3},{7,6},{10... | collective-permute-start | bytes 786440 | tf_op jit(solution)/shard_map/ppermute | solution.py:13
  79.7 7.7 %collective-permute-start.10 = (bf16[256,512]{1,0:T(8,128)(2,1)S(1)}, bf16[256,512]{1,0:T(8,128)(2,1)S(1)}, u32[]{:S(2)}, u32[]{:S(2)}) collective-permute-start(bf16[256,512]{1,0:T(8,128)(2,1)S(1)} %add_convert_fusion.2), channel_id=1, source_target_pairs={{1,0},{4,1},{5,4},{8,5},{9,8},{12,9},{13,12},{3,2},{6,3},{7,6},{10... | collective-permute-start | bytes 786440 | tf_op jit(solution)/shard_map/ppermute | solution.py:13
  87.5 7.7 %collective-permute-start.11 = (bf16[256,512]{1,0:T(8,128)(2,1)S(1)}, bf16[256,512]{1,0:T(8,128)(2,1)S(1)}, u32[]{:S(2)}, u32[]{:S(2)}) collective-permute-start(bf16[256,512]{1,0:T(8,128)(2,1)S(1)} %add_convert_fusion.1), channel_id=1, source_target_pairs={{1,0},{4,1},{5,4},{8,5},{9,8},{12,9},{13,12},{3,2},{6,3},{7,6},{10... | collective-permute-start | bytes 786440 | tf_op jit(solution)/shard_map/ppermute | solution.py:13
  88.9 6.3 %copy-start.1 = (f32[2,32,8,256]{3,2,0,1:T(8,128)}, f32[2,32,8,256]{3,2,0,1:T(8,128)S(1)}, u32[]{:S(2)}) copy-start(f32[2,32,8,256]{3,2,0,1:T(8,128)S(1)} %copy.105) | copy-start | bytes 1572868
  95.2 0.7 copy-start.3
  99.2 102.4 %all-reduce.2.cloned.1.call-start = ((), (), s32[]{:S(2)}) async-start(), calls=%async_computation.1 | async-start | bytes 2359296 | tf_op jit(solution)/shard_map/psum | solution.py:106
  100.4 7.7 %collective-permute-start.6 = (bf16[256,512]{1,0:T(8,128)(2,1)S(1)}, bf16[256,512]{1,0:T(8,128)(2,1)S(1)}, u32[]{:S(2)}, u32[]{:S(2)}) collective-permute-start(bf16[256,512]{1,0:T(8,128)(2,1)S(1)} %bitcast.190), channel_id=1, source_target_pairs={{1,0},{4,1},{5,4},{8,5},{9,8},{12,9},{13,12},{3,2},{6,3},{7,6},{10... | collective-permute-start | bytes 786440 | tf_op jit(solution)/shard_map/ppermute | solution.py:13
  108.8 32.3 %collective-permute-start.7 = (bf16[256,512]{1,0:T(8,128)(2,1)}, bf16[256,512]{1,0:T(8,128)(2,1)}, u32[]{:S(2)}, u32[]{:S(2)}) collective-permute-start(bf16[256,512]{1,0:T(8,128)(2,1)} %add_convert_fusion.5), channel_id=1, source_target_pairs={{1,0},{4,1},{5,4},{8,5},{9,8},{12,9},{13,12},{3,2},{6,3},{7,6},{10... | collective-permute-start | bytes 786440 | tf_op jit(solution)/shard_map/ppermute | solution.py:13
  141.1 3.2 %copy-start.6 = (bf16[2,256,2,256]{1,3,2,0:T(8,128)(2,1)S(1)}, bf16[2,256,2,256]{1,3,2,0:T(8,128)(2,1)}, u32[]{:S(2)}) copy-start(bf16[2,256,2,256]{1,3,2,0:T(8,128)(2,1)} %get-tuple-element.58) | copy-start | bytes 1572868
  141.1 4.2 %copy-start.2 = (f32[2,32,8,256]{3,2,0,1:T(8,128)S(1)}, f32[2,32,8,256]{3,2,0,1:T(8,128)}, u32[]{:S(2)}) copy-start(f32[2,32,8,256]{3,2,0,1:T(8,128)} %copy-done.1) | copy-start | bytes 1572868
  141.1 4.2 %copy-start.4 = (bf16[256,512]{1,0:T(8,128)(2,1)S(1)}, bf16[256,512]{1,0:T(8,128)(2,1)}, u32[]{:S(2)}) copy-start(bf16[256,512]{1,0:T(8,128)(2,1)} %copy-done.3) | copy-start | bytes 786436
  142.9 3.8 %collective-permute-start.8 = (bf16[256,512]{1,0:T(8,128)(2,1)}, bf16[256,512]{1,0:T(8,128)(2,1)}, u32[]{:S(2)}, u32[]{:S(2)}) collective-permute-start(bf16[256,512]{1,0:T(8,128)(2,1)} %add_convert_fusion.4), channel_id=1, source_target_pairs={{1,0},{4,1},{5,4},{8,5},{9,8},{12,9},{13,12},{3,2},{6,3},{7,6},{10... | collective-permute-start | bytes 786440 | tf_op jit(solution)/shard_map/ppermute | solution.py:13
Sparse Core Ops, SparseCore 0:
  99.3 39.3 reduce-scatter.3
  141.7 59.8 all-reduce.1
where the time goes:
time: 213 us; the launch traced here: 212 us
  waiting for transfers between devices  101 us (47%)
  matrix products  32.6 us (15%)
  starting transfers between devices  28.2 us (13%)
  local copies, waits for them, and re-layouts  20.5 us (10%)
  between operations  14.4 us (7%)
  other arithmetic  11.2 us (5%)
  loops' own time  3.92 us (2%)
    psum x1, waiting for transfers between devices, body(): weight_v = lax.psum(shard_v, ('ctx', 'sub')).astype(jnp.float32)  53.2 us
    unnamed x3, waiting for transfers between devices  28.5 us
    ppermute x12, starting transfers between devices, passed_along(): lax.ppermute(value, axis, [(source, source + steps) for source in range(f...  28.2 us
    ppermute x12, waiting for transfers between devices, passed_along(): lax.ppermute(value, axis, [(source, source + steps) for source in range(f...  19.3 us
    unnamed x25, local copies, waits for them, and re-layouts  17.9 us
    dot_general x2, matrix products, one_group(): jnp.einsum('htk,thd->kd', grad_scores, query_g, preferred_element_type=jn...  7.91 us
    dot_general x2, matrix products, one_group(): jnp.einsum('htk,kd->thd', grad_scores, key_g, preferred_element_type=jnp....  7.74 us
    sub x2, matrix products, one_group(): raised = jnp.where(allowed[None], jnp.exp(scores - largest), 0.0)  6.91 us
  transfers between devices with their start and end apart: 14, of which 7 were waited for; matrix products, arithmetic and copies ran while one was open for 9% of the time, Pallas kernels for 0%

commit v1 on v0

v1 whole, which is shorter than its diff:
```python
import functools

import jax
import jax.numpy as jnp
from jax import lax
from jax.experimental import pallas as pl
from jax.experimental.pallas import tpu as pltpu
from jax.sharding import PartitionSpec as P

HEAD_DIM = 256
SPAN = 768
RING = ("ctx", "sub")
NT = (((1,), (1,)), ((), ()))
TN = (((0,), (0,)), ((), ()))


def passed_along(value, axis, steps):
    count = lax.axis_size(axis)
    first, last = (max(0, -steps), min(count, count - steps))
    return lax.ppermute(value, axis, [(source, source + steps) for source in range(first, last)])


def rotated(value, axis, steps):
    count = lax.axis_size(axis)
    return lax.ppermute(value, axis, [(source, (source + steps) % count) for source in range(count)])


def doc_start_of(starts, positions):
    covered = starts[None, :] <= positions[:, None]
    return jnp.max(jnp.where(covered, starts[None, :], 0), axis=1)


def attention_kernel(lo_ref, q_ref, do_ref, kv_ref, dq_ref, dkv_ref, *, heads, kv_heads, margin):
    rows = q_ref.shape[0]
    keys = kv_ref.shape[0]
    scale = HEAD_DIM ** (-0.5)
    kv_width = kv_heads * HEAD_DIM
    per_group = heads // kv_heads
    col = lax.broadcasted_iota(jnp.int32, (rows, keys), 1)
    row = lax.broadcasted_iota(jnp.int32, (rows, keys), 0)
    allowed = (col >= lo_ref[...]) & (col <= row + margin)
    for group in range(kv_heads):
        k_cols = pl.ds(group * HEAD_DIM, HEAD_DIM)
        v_cols = pl.ds(kv_width + group * HEAD_DIM, HEAD_DIM)
        key_g = kv_ref[:, k_cols]
        value_g = kv_ref[:, v_cols]
        grad_k = None
        grad_v = None
        for member in range(per_group):
            q_cols = pl.ds((group * per_group + member) * HEAD_DIM, HEAD_DIM)
            query_h = q_ref[:, q_cols]
            grad_h = do_ref[:, q_cols]
            scores = lax.dot_general(query_h, key_g, NT, preferred_element_type=jnp.float32) * scale
            scores = jnp.where(allowed, scores, -1e30)
            largest = jnp.max(scores, axis=1, keepdims=True)
            raised = jnp.where(allowed, jnp.exp(scores - largest), 0.0)
            probs = raised / jnp.sum(raised, axis=1, keepdims=True)
            grad_probs = lax.dot_general(grad_h, value_g, NT, preferred_element_type=jnp.float32)
            row_dot = jnp.sum(probs * grad_probs, axis=1, keepdims=True)
            grad_scores = (probs * (grad_probs - row_dot) * scale).astype(jnp.bfloat16)
            probs_low = probs.astype(jnp.bfloat16)
            dq_ref[:, q_cols] = jnp.dot(
                grad_scores, key_g, preferred_element_type=jnp.float32
            ).astype(dq_ref.dtype)
            term_k = lax.dot_general(grad_scores, query_h, TN, preferred_element_type=jnp.float32)
            term_v = lax.dot_general(probs_low, grad_h, TN, preferred_element_type=jnp.float32)
            grad_k = term_k if grad_k is None else grad_k + term_k
            grad_v = term_v if grad_v is None else grad_v + term_v
        dkv_ref[:, k_cols] = grad_k
        dkv_ref[:, v_cols] = grad_v


def attention(lo_rel, queries, grads, kv_span, heads, kv_heads, margin):
    rows, width = queries.shape
    keys, kv_cols = kv_span.shape
    kernel = functools.partial(
        attention_kernel, heads=heads, kv_heads=kv_heads, margin=margin
    )
    vmem = pl.BlockSpec(memory_space=pltpu.VMEM)
    flops = 2 * 5 * heads * rows * keys * HEAD_DIM
    moved = 2 * (2 * rows * width + keys * kv_cols + rows * width) + 4 * keys * kv_cols
    return pl.pallas_call(
        kernel,
        out_shape=(
            jax.ShapeDtypeStruct((rows, width), jnp.bfloat16),
            jax.ShapeDtypeStruct((keys, kv_cols), jnp.float32),
        ),
        in_specs=[vmem] * 4,
        out_specs=(vmem, vmem),
        cost_estimate=pl.CostEstimate(
            flops=flops, transcendentals=heads * rows * keys, bytes_accessed=moved
        ),
    )(lo_rel, queries, grads, kv_span)


def body(layer_input, query_heads, key_heads, value_heads, grad_out, doc_starts):
    block_rows = query_heads.shape[1]
    window = min(SPAN, lax.axis_size(RING) * block_rows // 2)
    reach = (window + block_rows - 2) // block_rows
    margin = reach * block_rows
    kv_width = key_heads.shape[2]
    heads = query_heads.shape[2] // HEAD_DIM
    kv_heads = kv_width // HEAD_DIM
    first_row = lax.axis_index(RING) * block_rows

    own_kv = jnp.concatenate([key_heads[0], value_heads[0]], axis=1)
    arrived = []
    moving = own_kv
    for _ in range(reach):
        moving = passed_along(moving, RING, 1)
        arrived.append(moving)
    kv_span = jnp.concatenate(arrived[::-1] + [own_kv], axis=0)
    query_pos = first_row + jnp.arange(block_rows, dtype=jnp.int32)
    lowest = jnp.maximum(doc_start_of(doc_starts[0], query_pos), query_pos - window + 1)
    lo_rel = (lowest - first_row + margin).astype(jnp.int32)[:, None]
    grad_q, grad_kv_span = attention(
        lo_rel, query_heads[0], grad_out[0], kv_span, heads, kv_heads, margin
    )

    def own_piece(distance):
        begin = (reach - distance) * block_rows
        return grad_kv_span[begin : begin + block_rows]

    total = own_piece(reach)
    for distance in range(reach - 1, -1, -1):
        moved = passed_along(total.astype(jnp.bfloat16), RING, -1).astype(jnp.float32)
        total = moved + own_piece(distance)
    grad_kv = total.astype(jnp.bfloat16)
    grad_key = grad_kv[:, :kv_width]
    grad_value = grad_kv[:, kv_width:]

    fsdp_count = lax.axis_size("fsdp")
    fsdp_at = lax.axis_index("fsdp")
    model_width = layer_input.shape[2]
    shard_rows = model_width // fsdp_count
    own_input = layer_input[0]
    inputs = [lax.dynamic_slice_in_dim(own_input, fsdp_at * shard_rows, shard_rows, axis=1)]
    values = [grad_value]
    for steps in range(1, fsdp_count):
        target = (fsdp_at + steps) % fsdp_count
        outgoing = lax.dynamic_slice_in_dim(own_input, target * shard_rows, shard_rows, axis=1)
        inputs.append(rotated(outgoing, "fsdp", steps))
        values.append(rotated(grad_value, "fsdp", steps))
    stacked_inputs = jnp.concatenate(inputs, axis=0)
    stacked_values = jnp.concatenate(values, axis=0)
    shard = lax.dot_general(stacked_inputs, stacked_values, TN, preferred_element_type=jnp.float32)

    sub_count = lax.axis_size("sub")
    sub_at = lax.axis_index("sub")
    piece_rows = shard_rows // sub_count
    mine = lax.dynamic_slice_in_dim(shard, sub_at * piece_rows, piece_rows, axis=0)
    for steps in range(1, sub_count):
        target = (sub_at + steps) % sub_count
        outgoing = lax.dynamic_slice_in_dim(shard, target * piece_rows, piece_rows, axis=0)
        mine = mine + rotated(outgoing.astype(jnp.bfloat16), "sub", steps).astype(jnp.float32)
    reduced = lax.psum(mine.astype(jnp.bfloat16), "ctx").astype(jnp.float32)
    if sub_count == 2:
        other = rotated(reduced.astype(jnp.bfloat16), "sub", 1).astype(jnp.float32)
        first = jnp.where(sub_at == 0, reduced, other)
        second = jnp.where(sub_at == 0, other, reduced)
        weight_v = jnp.concatenate([first, second], axis=0)
    else:
        weight_v = lax.all_gather(reduced, "sub", axis=0, tiled=True)
    token_scale = float(fsdp_count * lax.axis_size(RING) * block_rows) ** (-0.5)
    return (
        grad_q[None],
        grad_key[None],
        grad_value[None],
        weight_v * token_scale,
    )


def solution(mesh):
    placed = (
        P(("groups", "fsdp"), ("ctx", "sub"), None),
        P(("groups", "fsdp"), ("ctx", "sub"), None),
        P(("groups", "fsdp"), ("ctx", "sub"), None),
        P(("groups", "fsdp"), ("ctx", "sub"), None),
        P(("groups", "fsdp"), ("ctx", "sub"), None),
        P(("groups", "fsdp"), None),
    )
    return jax.shard_map(
        body,
        mesh=mesh,
        in_specs=placed,
        out_specs=(
            P(("groups", "fsdp"), ("ctx", "sub"), None),
            P(("groups", "fsdp"), ("ctx", "sub"), None),
            P(("groups", "fsdp"), ("ctx", "sub"), None),
            P(("groups", "fsdp"), None),
        ),
        check_vma=False,
    )
```

time: 213 us -> 160 us (0.75)
  matrix products: 32.6 us -> 1.87 us
  local copies, waits for them, and re-layouts: 20.5 us -> 2.54 us
  waiting for transfers between devices: 101 us -> 84.9 us
  Pallas kernels: 0 us -> 8.91 us
  other arithmetic: 11.2 us -> 15.2 us
  loops' own time: 3.92 us -> 0 us
  starting transfers between devices: 28.2 us -> 32 us
    unnamed x3 -> x1, waiting for transfers between devices: 28.5 us -> 0.02 us
    dot_general x9 -> x1, matrix products: 25.7 us -> 1.87 us  [body(): lax.dot_general(stacked_inputs, stacked_values, TN, preferred_element_typ...]
    unnamed x25 -> x2, local copies, waits for them, and re-layouts: 17.9 us -> 0.01 us
    ppermute x0 -> x4, waiting for transfers between devices: none -> 10.7 us  [rotated(): lax.ppermute(value, axis, [(source, (source + steps) % count) for source...]
    ppermute x12 -> x6, waiting for transfers between devices: 19.3 us -> 29.8 us  [passed_along(): lax.ppermute(value, axis, [(source, source + steps) for source in range(f...]
    pallas_call x0 -> x1, Pallas kernels: none -> 8.91 us  [attention(): pl.pallas_call(kernel, out_shape=(jax.ShapeDtypeStruct((rows, width), jnp...]
    psum x1, waiting for transfers between devices: 53.2 us -> 44.4 us  [body(): reduced = lax.psum(mine.astype(jnp.bfloat16), 'ctx').astype(jnp.float32)]
    ppermute x0 -> x4, starting transfers between devices: none -> 7.4 us  [rotated(): lax.ppermute(value, axis, [(source, (source + steps) % count) for source...]
  transfers between devices with their start and end apart: 14 -> 11, of which waited for: 7 -> 9; matrix products, arithmetic and copies ran while one was open for 9% -> 2% of each run, Pallas kernels for 0% -> 0%
where the time goes in v1:
time: 160 us
  waiting for transfers between devices  84.9 us (53%)
  starting transfers between devices  32 us (20%)
  other arithmetic  15.2 us (10%)
  between operations  14.2 us (9%)
  Pallas kernels  8.91 us (6%)
  local copies, waits for them, and re-layouts  2.54 us (2%)
  matrix products  1.87 us (1%)
    psum x1, waiting for transfers between devices, body(): reduced = lax.psum(mine.astype(jnp.bfloat16), 'ctx').astype(jnp.float32)  44.4 us
    ppermute x6, waiting for transfers between devices, passed_along(): lax.ppermute(value, axis, [(source, source + steps) for source in range(f...  29.8 us
    ppermute x6, starting transfers between devices, passed_along(): lax.ppermute(value, axis, [(source, source + steps) for source in range(f...  24.6 us
    ppermute x4, waiting for transfers between devices, rotated(): lax.ppermute(value, axis, [(source, (source + steps) % count) for source...  10.7 us
    pallas_call x1, Pallas kernels, attention(): pl.pallas_call(kernel, out_shape=(jax.ShapeDtypeStruct((rows, width), jnp...  8.91 us
    ppermute x4, starting transfers between devices, rotated(): lax.ppermute(value, axis, [(source, (source + steps) % count) for source...  7.4 us
    concatenate x1, other arithmetic, body(): kv_span = jnp.concatenate(arrived[::-1] + [own_kv], axis=0)  4.52 us
  transfers between devices with their start and end apart: 11, of which 9 were waited for; matrix products, arithmetic and copies ran while one was open for 2% of the time, Pallas kernels for 0%

profile of v1, /device:TPU:0, one launch (start us, length us, event | category | flops | bytes accessed | tf_op | source)
XLA Modules:
  0.0 159.6 jit_solution(17922892962649845548)
XLA Ops:
  7.2 0.0 all-reduce.2.cloned.1.call-start
  7.2 1.1 pad_maximum_fusion
  8.3 2.4 %collective-permute-start = (bf16[256,1024]{1,0:T(8,128)(2,1)S(1)}, bf16[256,1024]{1,0:T(8,128)(2,1)S(1)}, u32[]{:S(2)}, u32[]{:S(2)}) collective-permute-start(bf16[256,1024]{1,0:T(8,128)(2,1)S(1)} %pad_maximum_fusion), channel_id=1, source_target_pairs={{0,1},{1,4},{4,5},{5,8},{8,9},{9,12},{12,13},{2,3},{3,6},{6,7},{7,... | collective-permute-start | bytes 1572872 | tf_op jit(solution)/shard_map/ppermute | solution.py:20
  10.7 1.5 collective-permute-done
  12.2 9.2 %collective-permute-start.1 = (bf16[256,1024]{1,0:T(8,128)(2,1)S(1)}, bf16[256,1024]{1,0:T(8,128)(2,1)S(1)}, u32[]{:S(2)}, u32[]{:S(2)}) collective-permute-start(bf16[256,1024]{1,0:T(8,128)(2,1)S(1)} %collective-permute-done), channel_id=1, source_target_pairs={{0,1},{1,4},{4,5},{5,8},{8,9},{9,12},{12,13},{2,3},{3,6},{6,7},{7,... | collective-permute-start | bytes 1572872 | tf_op jit(solution)/shard_map/ppermute | solution.py:20
  21.4 1.5 collective-permute-done.1
  22.9 9.0 %collective-permute-start.2 = (bf16[256,1024]{1,0:T(8,128)(2,1)S(1)}, bf16[256,1024]{1,0:T(8,128)(2,1)S(1)}, u32[]{:S(2)}, u32[]{:S(2)}) collective-permute-start(bf16[256,1024]{1,0:T(8,128)(2,1)S(1)} %collective-permute-done.1), channel_id=1, source_target_pairs={{0,1},{1,4},{4,5},{5,8},{8,9},{9,12},{12,13},{2,3},{3,6},{6,7},{7,... | collective-permute-start | bytes 1572872 | tf_op jit(solution)/shard_map/ppermute | solution.py:20
  31.9 0.7 select_reduce_fusion
  32.6 0.1 copy.13
  32.8 0.7 subtract_add_fusion.lo_ref
  33.5 0.0 collective-permute-done.2
  33.5 4.5 %maximum_maximum_fusion.kv_ref = bf16[1024,1024]{1,0:T(8,128)(2,1)} fusion(bf16[256,512]{1,0:T(8,128)(2,1)} %bitcast.16, bf16[256,512]{1,0:T(8,128)(2,1)} %bitcast.18, bf16[256,1024]{1,0:T(8,128)(2,1)S(1)} %collective-permute-done, bf16[256,1024]{1,0:T(8,128)(2,1)S(1)} %collective-permute-done.1, bf16[256,1024]{1,0:T(8,128)(2,1)S(1)} %collective-permute-done.2), kind=kLoop, calls=%fused_computation.1 | loop fusion | flops 10485760 | bytes 4194304 | tf_op jit(solution)/shard_map/concatenate | solution.py:112
  38.0 8.9 %shard_map.93 = (bf16[256,1024]{1,0:T(8,128)(2,1)}, f32[1024,1024]{1,0:T(8,128)}) custom-call(s32[256,1]{1,0:T(8,128)} %subtract_add_fusion.lo_ref, bf16[256,1024]{1,0:T(8,128)(2,1)} %bitcast.21, bf16[256,1024]{1,0:T(8,128)(2,1)} %bitcast.22, bf16[1024,1024]{1,0:T(8,128)(2,1)} %maximum_maximum_fusion.kv_ref), custom_call_target="tpu_custom_call" | custom-call | flops 2684354560 | bytes 7864320 | tf_op jit(solution)/shard_map/pallas_call | solution.py:82
  46.9 1.3 slice.34
  48.2 0.0 copy-start
  48.2 1.4 collective-permute-start.3
  49.7 8.9 %collective-permute-done.3 = bf16[256,1024]{1,0:T(8,128)(2,1)S(1)} collective-permute-done((bf16[256,1024]{1,0:T(8,128)(2,1)S(1)}, bf16[256,1024]{1,0:T(8,128)(2,1)S(1)}, u32[]{:S(2)}, u32[]{:S(2)}) %collective-permute-start.3) | collective-permute-done | bytes 524320 | tf_op jit(solution)/shard_map/ppermute | solution.py:20
  58.6 1.4 add_convert_fusion.3
  60.0 1.3 collective-permute-start.4
  61.3 9.9 %collective-permute-done.4 = bf16[256,1024]{1,0:T(8,128)(2,1)S(1)} collective-permute-done((bf16[256,1024]{1,0:T(8,128)(2,1)S(1)}, bf16[256,1024]{1,0:T(8,128)(2,1)S(1)}, u32[]{:S(2)}, u32[]{:S(2)}) %collective-permute-start.4) | collective-permute-done | bytes 524320 | tf_op jit(solution)/shard_map/ppermute | solution.py:20
  71.2 1.4 add_convert_fusion.2
  72.6 1.3 collective-permute-start.5
  73.9 0.0 copy-done
  73.9 0.2 dynamic-slice_bitcast_fusion.1
  74.1 1.5 collective-permute-start.6
  75.6 7.9 %collective-permute-done.5 = bf16[256,1024]{1,0:T(8,128)(2,1)S(1)} collective-permute-done((bf16[256,1024]{1,0:T(8,128)(2,1)S(1)}, bf16[256,1024]{1,0:T(8,128)(2,1)S(1)}, u32[]{:S(2)}, u32[]{:S(2)}) %collective-permute-start.5) | collective-permute-done | bytes 524320 | tf_op jit(solution)/shard_map/ppermute | solution.py:20
  83.5 1.4 add_convert_fusion.1
  84.9 0.9 fusion.8
  85.7 1.5 collective-permute-start.7
  87.2 0.0 collective-permute-done.6
  87.2 6.9 %collective-permute-done.7 = bf16[256,512]{1,0:T(8,128)(2,1)S(1)} collective-permute-done((bf16[256,512]{1,0:T(8,128)(2,1)S(1)}, bf16[256,512]{1,0:T(8,128)(2,1)S(1)}, u32[]{:S(2)}, u32[]{:S(2)}) %collective-permute-start.7) | collective-permute-done | bytes 262176 | tf_op jit(solution)/shard_map/ppermute | solution.py:25
  94.1 1.9 %fusion = f32[1152,512]{1,0:T(8,128)S(1)} fusion(bf16[256,1152]{1,0:T(8,128)(2,1)} %collective-permute-done.6, bf16[256,1152]{1,0:T(8,128)(2,1)S(1)} %get-tuple-element.10, bf16[256,512]{1,0:T(8,128)(2,1)S(1)} %collective-permute-done.7, bf16[256,512]{1,0:T(8,128)(2,1)S(1)} %get-tuple-element.12), kind=kOutput, calls=%fused_computation.4 | convolution fusion | flops 607387648 | bytes 4063232 | tf_op jit(solution)/shard_map/dot_general | solution.py:146
  96.0 0.1 dynamic-slice_convert_fusion
  96.0 4.4 %collective-permute-start.8 = (bf16[576,512]{1,0:T(8,128)(2,1)S(1)}, bf16[576,512]{1,0:T(8,128)(2,1)S(1)}, u32[]{:S(2)}, u32[]{:S(2)}) collective-permute-start(bf16[576,512]{1,0:T(8,128)(2,1)S(1)} %dynamic-slice_convert_fusion), channel_id=1, source_target_pairs={{0,1},{1,0},{2,3},{3,2},{4,5},{5,4},{6,7},{7,6},{8,9},{9,8},{10,11... | collective-permute-start | bytes 1769480 | tf_op jit(solution)/shard_map/ppermute | solution.py:25
  100.5 1.6 %collective-permute-done.8 = bf16[576,512]{1,0:T(8,128)(2,1)S(1)} collective-permute-done((bf16[576,512]{1,0:T(8,128)(2,1)S(1)}, bf16[576,512]{1,0:T(8,128)(2,1)S(1)}, u32[]{:S(2)}, u32[]{:S(2)}) %collective-permute-start.8) | collective-permute-done | bytes 589856 | tf_op jit(solution)/shard_map/ppermute | solution.py:25
  102.1 1.0 add_convert_fusion
  103.1 0.0 all-reduce.2.cloned.1.call-update
  103.1 44.4 %all-reduce.2.cloned.1.call-done = bf16[576,512]{1,0:T(8,128)(2,1)} async-done(((bf16[576,512]{1,0:T(8,128)(2,1)}), bf16[576,512]{1,0:T(8,128)(2,1)}) %all-reduce.2.cloned.1.call-update) | async-done | bytes 589840 | tf_op jit(solution)/shard_map/psum | solution.py:156
  147.5 0.0 collective-permute-start.9
  147.5 2.2 %collective-permute-done.9 = bf16[576,512]{1,0:T(8,128)(2,1)S(1)} collective-permute-done((bf16[576,512]{1,0:T(8,128)(2,1)}, bf16[576,512]{1,0:T(8,128)(2,1)S(1)}, u32[]{:S(2)}, u32[]{:S(2)}) %collective-permute-start.9) | collective-permute-done | bytes 589856 | tf_op jit(solution)/shard_map/ppermute | solution.py:25
  149.7 1.4 convert_select_fusion.1
  151.1 1.7 %maximum_multiply_fusion = f32[1152,512]{1,0:T(8,128)} fusion(f32[576,512]{1,0:T(8,128)S(1)} %get-tuple-element.9, f32[576,512]{1,0:T(8,128)S(1)} %get-tuple-element.8), kind=kLoop, calls=%fused_computation | loop fusion | flops 1179648 | bytes 4718592 | tf_op jit(solution)/shard_map/mul | solution.py:169
  (1 shorter events, 0.0 us)
Async XLA Ops:
  7.2 140.3 %all-reduce.2.cloned.1.call-start = ((), (), s32[]{:S(2)}) async-start(), calls=%async_computation | async-start | bytes 1179648 | tf_op jit(solution)/shard_map/psum | solution.py:156
  8.3 3.9 %collective-permute-start = (bf16[256,1024]{1,0:T(8,128)(2,1)S(1)}, bf16[256,1024]{1,0:T(8,128)(2,1)S(1)}, u32[]{:S(2)}, u32[]{:S(2)}) collective-permute-start(bf16[256,1024]{1,0:T(8,128)(2,1)S(1)} %pad_maximum_fusion), channel_id=1, source_target_pairs={{0,1},{1,4},{4,5},{5,8},{8,9},{9,12},{12,13},{2,3},{3,6},{6,7},{7,... | collective-permute-start | bytes 1572872 | tf_op jit(solution)/shard_map/ppermute | solution.py:20
  12.2 10.7 %collective-permute-start.1 = (bf16[256,1024]{1,0:T(8,128)(2,1)S(1)}, bf16[256,1024]{1,0:T(8,128)(2,1)S(1)}, u32[]{:S(2)}, u32[]{:S(2)}) collective-permute-start(bf16[256,1024]{1,0:T(8,128)(2,1)S(1)} %collective-permute-done), channel_id=1, source_target_pairs={{0,1},{1,4},{4,5},{5,8},{8,9},{9,12},{12,13},{2,3},{3,6},{6,7},{7,... | collective-permute-start | bytes 1572872 | tf_op jit(solution)/shard_map/ppermute | solution.py:20
  22.9 10.6 %collective-permute-start.2 = (bf16[256,1024]{1,0:T(8,128)(2,1)S(1)}, bf16[256,1024]{1,0:T(8,128)(2,1)S(1)}, u32[]{:S(2)}, u32[]{:S(2)}) collective-permute-start(bf16[256,1024]{1,0:T(8,128)(2,1)S(1)} %collective-permute-done.1), channel_id=1, source_target_pairs={{0,1},{1,4},{4,5},{5,8},{8,9},{9,12},{12,13},{2,3},{3,6},{6,7},{7,... | collective-permute-start | bytes 1572872 | tf_op jit(solution)/shard_map/ppermute | solution.py:20
  48.2 25.7 %copy-start = (bf16[1,256,2304]{2,1,0:T(8,128)(2,1)S(1)}, bf16[1,256,2304]{2,1,0:T(8,128)(2,1)}, u32[]{:S(2)}) copy-start(bf16[1,256,2304]{2,1,0:T(8,128)(2,1)} %param.6) | copy-start | bytes 3538948
  48.2 10.4 %collective-permute-start.3 = (bf16[256,1024]{1,0:T(8,128)(2,1)S(1)}, bf16[256,1024]{1,0:T(8,128)(2,1)S(1)}, u32[]{:S(2)}, u32[]{:S(2)}) collective-permute-start(bf16[256,1024]{1,0:T(8,128)(2,1)S(1)} %slice.34), channel_id=1, source_target_pairs={{1,0},{4,1},{5,4},{8,5},{9,8},{12,9},{13,12},{3,2},{6,3},{7,6},{10... | collective-permute-start | bytes 1572872 | tf_op jit(solution)/shard_map/ppermute | solution.py:20
  60.0 11.2 %collective-permute-start.4 = (bf16[256,1024]{1,0:T(8,128)(2,1)S(1)}, bf16[256,1024]{1,0:T(8,128)(2,1)S(1)}, u32[]{:S(2)}, u32[]{:S(2)}) collective-permute-start(bf16[256,1024]{1,0:T(8,128)(2,1)S(1)} %add_convert_fusion.3), channel_id=1, source_target_pairs={{1,0},{4,1},{5,4},{8,5},{9,8},{12,9},{13,12},{3,2},{6,3},{7,6},{10... | collective-permute-start | bytes 1572872 | tf_op jit(solution)/shard_map/ppermute | solution.py:20
  72.6 10.9 %collective-permute-start.5 = (bf16[256,1024]{1,0:T(8,128)(2,1)S(1)}, bf16[256,1024]{1,0:T(8,128)(2,1)S(1)}, u32[]{:S(2)}, u32[]{:S(2)}) collective-permute-start(bf16[256,1024]{1,0:T(8,128)(2,1)S(1)} %add_convert_fusion.2), channel_id=1, source_target_pairs={{1,0},{4,1},{5,4},{8,5},{9,8},{12,9},{13,12},{3,2},{6,3},{7,6},{10... | collective-permute-start | bytes 1572872 | tf_op jit(solution)/shard_map/ppermute | solution.py:20
  74.1 13.1 %collective-permute-start.6 = (bf16[256,1152]{1,0:T(8,128)(2,1)S(1)}, bf16[256,1152]{1,0:T(8,128)(2,1)}, u32[]{:S(2)}, u32[]{:S(2)}) collective-permute-start(bf16[256,1152]{1,0:T(8,128)(2,1)S(1)} %get-tuple-element.11), channel_id=1, source_target_pairs={{0,2},{2,0},{1,3},{3,1},{4,6},{6,4},{5,7},{7,5},{8,10},{10,8},{9,1... | collective-permute-start | bytes 1769480 | tf_op jit(solution)/shard_map/ppermute | solution.py:25
  85.7 8.4 %collective-permute-start.7 = (bf16[256,512]{1,0:T(8,128)(2,1)S(1)}, bf16[256,512]{1,0:T(8,128)(2,1)S(1)}, u32[]{:S(2)}, u32[]{:S(2)}) collective-permute-start(bf16[256,512]{1,0:T(8,128)(2,1)S(1)} %get-tuple-element.12), channel_id=1, source_target_pairs={{0,2},{2,0},{1,3},{3,1},{4,6},{6,4},{5,7},{7,5},{8,10},{10,8},{9,1... | collective-permute-start | bytes 786440 | tf_op jit(solution)/shard_map/ppermute | solution.py:25
  96.0 6.0 %collective-permute-start.8 = (bf16[576,512]{1,0:T(8,128)(2,1)S(1)}, bf16[576,512]{1,0:T(8,128)(2,1)S(1)}, u32[]{:S(2)}, u32[]{:S(2)}) collective-permute-start(bf16[576,512]{1,0:T(8,128)(2,1)S(1)} %dynamic-slice_convert_fusion), channel_id=1, source_target_pairs={{0,1},{1,0},{2,3},{3,2},{4,5},{5,4},{6,7},{7,6},{8,9},{9,8},{10,11... | collective-permute-start | bytes 1769480 | tf_op jit(solution)/shard_map/ppermute | solution.py:25
  147.5 2.2 %collective-permute-start.9 = (bf16[576,512]{1,0:T(8,128)(2,1)}, bf16[576,512]{1,0:T(8,128)(2,1)S(1)}, u32[]{:S(2)}, u32[]{:S(2)}) collective-permute-start(bf16[576,512]{1,0:T(8,128)(2,1)} %all-reduce.2.cloned.1.call-done), channel_id=1, source_target_pairs={{0,1},{1,0},{2,3},{3,2},{4,5},{5,4},{6,7},{7,6},{8,9},{9,8},{10,11... | collective-permute-start | bytes 1769480 | tf_op jit(solution)/shard_map/ppermute | solution.py:25
Sparse Core Ops, SparseCore 0:
  103.2 44.2 all-reduce.1

commit v2 on v1

--- a/solution.py
+++ b/solution.py
@@ -30,7 +30,16 @@
     return jnp.max(jnp.where(covered, starts[None, :], 0), axis=1)
 
 
-def attention_kernel(lo_ref, q_ref, do_ref, kv_ref, dq_ref, dkv_ref, *, heads, kv_heads, margin):
+def attention_kernel(*refs, heads, kv_heads, margin, blocks):
+    lo_ref, q_ref, do_ref = refs[:3]
+    block_refs = refs[3 : 3 + blocks]
+    dq_ref = refs[3 + blocks]
+    out_refs = refs[4 + blocks : 4 + 2 * blocks]
+    kv_ref = refs[4 + 2 * blocks]
+    dkv_ref = refs[5 + 2 * blocks]
+    block_rows = block_refs[0].shape[0]
+    for index, block_ref in enumerate(block_refs):
+        kv_ref[pl.ds(index * block_rows, block_rows), :] = block_ref[...]
     rows = q_ref.shape[0]
     keys = kv_ref.shape[0]
     scale = HEAD_DIM ** (-0.5)
@@ -68,29 +77,35 @@
             grad_v = term_v if grad_v is None else grad_v + term_v
         dkv_ref[:, k_cols] = grad_k
         dkv_ref[:, v_cols] = grad_v
-
-
-def attention(lo_rel, queries, grads, kv_span, heads, kv_heads, margin):
+    for index, out_ref in enumerate(out_refs):
+        out_ref[...] = dkv_ref[pl.ds(index * block_rows, block_rows), :]
+
+
+def attention(lo_rel, queries, grads, kv_blocks, heads, kv_heads, margin):
     rows, width = queries.shape
-    keys, kv_cols = kv_span.shape
+    blocks = len(kv_blocks)
+    block_rows, kv_cols = kv_blocks[0].shape
+    keys = blocks * block_rows
     kernel = functools.partial(
-        attention_kernel, heads=heads, kv_heads=kv_heads, margin=margin
+        attention_kernel, heads=heads, kv_heads=kv_heads, margin=margin, blocks=blocks
     )
     vmem = pl.BlockSpec(memory_space=pltpu.VMEM)
     flops = 2 * 5 * heads * rows * keys * HEAD_DIM
     moved = 2 * (2 * rows * width + keys * kv_cols + rows * width) + 4 * keys * kv_cols
     return pl.pallas_call(
         kernel,
-        out_shape=(
-            jax.ShapeDtypeStruct((rows, width), jnp.bfloat16),
-            jax.ShapeDtypeStruct((keys, kv_cols), jnp.float32),
-        ),
-        in_specs=[vmem] * 4,
-        out_specs=(vmem, vmem),
+        out_shape=(jax.ShapeDtypeStruct((rows, width), jnp.bfloat16),)
+        + tuple(jax.ShapeDtypeStruct((block_rows, kv_cols), jnp.float32) for _ in kv_blocks),
+        in_specs=[vmem] * (3 + blocks),
+        out_specs=(vmem,) * (1 + blocks),
+        scratch_shapes=[
+            pltpu.VMEM((keys, kv_cols), kv_blocks[0].dtype),
+            pltpu.VMEM((keys, kv_cols), jnp.float32),
+        ],
         cost_estimate=pl.CostEstimate(
             flops=flops, transcendentals=heads * rows * keys, bytes_accessed=moved
         ),
-    )(lo_rel, queries, grads, kv_span)
+    )(lo_rel, queries, grads, *kv_blocks)
 
 
 def body(layer_input, query_heads, key_heads, value_heads, grad_out, doc_starts):
@@ -109,17 +124,15 @@
     for _ in range(reach):
         moving = passed_along(moving, RING, 1)
         arrived.append(moving)
-    kv_span = jnp.concatenate(arrived[::-1] + [own_kv], axis=0)
     query_pos = first_row + jnp.arange(block_rows, dtype=jnp.int32)
     lowest = jnp.maximum(doc_start_of(doc_starts[0], query_pos), query_pos - window + 1)
     lo_rel = (lowest - first_row + margin).astype(jnp.int32)[:, None]
-    grad_q, grad_kv_span = attention(
-        lo_rel, query_heads[0], grad_out[0], kv_span, heads, kv_heads, margin
+    grad_q, *grad_pieces = attention(
+        lo_rel, query_heads[0], grad_out[0], arrived[::-1] + [own_kv], heads, kv_heads, margin
     )
 
     def own_piece(distance):
-        begin = (reach - distance) * block_rows
-        return grad_kv_span[begin : begin + block_rows]
+        return grad_pieces[reach - distance]
 
     total = own_piece(reach)
     for distance in range(reach - 1, -1, -1):
@@ -153,7 +166,8 @@
         target = (sub_at + steps) % sub_count
         outgoing = lax.dynamic_slice_in_dim(shard, target * piece_rows, piece_rows, axis=0)
         mine = mine + rotated(outgoing.astype(jnp.bfloat16), "sub", steps).astype(jnp.float32)
-    reduced = lax.psum(mine.astype(jnp.bfloat16), "ctx").astype(jnp.float32)
+    scattered = lax.psum_scatter(mine.astype(jnp.bfloat16), "ctx", scatter_dimension=0, tiled=True)
+    reduced = lax.all_gather(scattered, "ctx", axis=0, tiled=True).astype(jnp.float32)
     if sub_count == 2:
         other = rotated(reduced.astype(jnp.bfloat16), "sub", 1).astype(jnp.float32)
         first = jnp.where(sub_at == 0, reduced, other)

time: 160 us -> 152 us (0.950)
  blocking collectives: 0 us -> 16.5 us
  waiting for transfers between devices: 84.9 us -> 69.5 us
  other arithmetic: 15.2 us -> 7.32 us
    psum x1 -> x0, waiting for transfers between devices: 44.4 us -> none  [body(): reduced = lax.psum(mine.astype(jnp.bfloat16), 'ctx').astype(jnp.float32)]
    reduce_scatter x0 -> x1, waiting for transfers between devices: none -> 28.4 us  [body(): lax.psum_scatter(mine.astype(jnp.bfloat16), 'ctx', scatter_dimension=0, t...]
    all_gather x0 -> x1, blocking collectives: none -> 16.5 us  [body(): lax.all_gather(scattered, 'ctx', axis=0, tiled=True).astype(jnp.float32)]
    concatenate x1 -> x0, other arithmetic: 4.52 us -> none  [body(): kv_span = jnp.concatenate(arrived[::-1] + [own_kv], axis=0)]
where the time goes in v2:
time: 152 us
  waiting for transfers between devices  69.5 us (46%)
  starting transfers between devices  31.3 us (21%)
  blocking collectives  16.5 us (11%)
  between operations  14.2 us (9%)
  Pallas kernels  8.69 us (6%)
  other arithmetic  7.32 us (5%)
  local copies, waits for them, and re-layouts  2.04 us (1%)
  matrix products  1.87 us (1%)
    ppermute x6, waiting for transfers between devices, passed_along(): lax.ppermute(value, axis, [(source, source + steps) for source in range(f...  29.8 us
    reduce_scatter x1, waiting for transfers between devices, body(): lax.psum_scatter(mine.astype(jnp.bfloat16), 'ctx', scatter_dimension=0, t...  28.4 us
    ppermute x6, starting transfers between devices, passed_along(): lax.ppermute(value, axis, [(source, source + steps) for source in range(f...  24.7 us
    all_gather x1, blocking collectives, body(): lax.all_gather(scattered, 'ctx', axis=0, tiled=True).astype(jnp.float32)  16.5 us
    ppermute x4, waiting for transfers between devices, rotated(): lax.ppermute(value, axis, [(source, (source + steps) % count) for source...  11.4 us
    pallas_call x1, Pallas kernels, attention(): pl.pallas_call(kernel, out_shape=(jax.ShapeDtypeStruct((rows, width), jnp...  8.69 us
    ppermute x4, starting transfers between devices, rotated(): lax.ppermute(value, axis, [(source, (source + steps) % count) for source...  6.52 us
  transfers between devices with their start and end apart: 11, of which 9 were waited for; matrix products, arithmetic and copies ran while one was open for 2% of the time, Pallas kernels for 0%

profile of v2, /device:TPU:0, one launch (start us, length us, event | category | flops | bytes accessed | tf_op | source)
XLA Modules:
  0.0 151.5 jit_solution(1644080902376590444)
XLA Ops:
  7.2 0.0 reduce-scatter.2.cloned.1.call-start
  7.2 1.1 pad_maximum_fusion.refs_6_
  8.3 0.0 copy-start.4
  8.3 2.4 %collective-permute-start = (bf16[256,1024]{1,0:T(8,128)(2,1)S(1)}, bf16[256,1024]{1,0:T(8,128)(2,1)S(1)}, u32[]{:S(2)}, u32[]{:S(2)}) collective-permute-start(bf16[256,1024]{1,0:T(8,128)(2,1)S(1)} %pad_maximum_fusion.refs_6_), channel_id=1, source_target_pairs={{0,1},{1,4},{4,5},{5,8},{8,9},{9,12},{12,13},{2,3},{3,6},{6,7},{7,... | collective-permute-start | bytes 1572872 | tf_op jit(solution)/shard_map/ppermute | solution.py:20
  10.7 1.5 collective-permute-done.refs_5_
  12.2 0.0 copy-start.5
  12.2 9.2 %collective-permute-start.1 = (bf16[256,1024]{1,0:T(8,128)(2,1)S(1)}, bf16[256,1024]{1,0:T(8,128)(2,1)S(1)}, u32[]{:S(2)}, u32[]{:S(2)}) collective-permute-start(bf16[256,1024]{1,0:T(8,128)(2,1)S(1)} %collective-permute-done.refs_5_), channel_id=1, source_target_pairs={{0,1},{1,4},{4,5},{5,8},{8,9},{9,12},{12,13},{2,3},{3,6},{6,7},{7,... | collective-permute-start | bytes 1572872 | tf_op jit(solution)/shard_map/ppermute | solution.py:20
  21.4 1.5 collective-permute-done.1.refs_4_
  22.9 0.0 copy-start.6
  22.9 9.0 %collective-permute-start.2 = (bf16[256,1024]{1,0:T(8,128)(2,1)S(1)}, bf16[256,1024]{1,0:T(8,128)(2,1)S(1)}, u32[]{:S(2)}, u32[]{:S(2)}) collective-permute-start(bf16[256,1024]{1,0:T(8,128)(2,1)S(1)} %collective-permute-done.1.refs_4_), channel_id=1, source_target_pairs={{0,1},{1,4},{4,5},{5,8},{8,9},{9,12},{12,13},{2,3},{3,6},{6,7},{7,... | collective-permute-start | bytes 1572872 | tf_op jit(solution)/shard_map/ppermute | solution.py:20
  31.9 0.7 select_reduce_fusion
  32.7 0.1 copy.13
  32.8 0.7 subtract_add_fusion.refs_0_
  33.5 0.0 collective-permute-done.2.refs_3_
  33.5 0.0 copy-start.7
  33.5 0.0 copy-done.4
  33.5 0.0 copy-done.5
  33.5 0.0 copy-done.6
  33.5 0.8 copy-done.7
  34.3 8.7 %shard_map.93 = (bf16[256,1024]{1,0:T(8,128)(2,1)}, f32[256,1024]{1,0:T(8,128)}, f32[256,1024]{1,0:T(8,128)}, f32[256,1024]{1,0:T(8,128)}, f32[256,1024]{1,0:T(8,128)}) custom-call(s32[256,1]{1,0:T(8,128)} %subtract_add_fusion.refs_0_, bf16[256,1024]{1,0:T(8,128)(2,1)} %bitcast.19, bf16[256,1024]{1,0:T(8,128)(2,1)} %bitcast.20, bf16[256,1024]{1,0:T(8,128)(2,1)} %copy-done.7, ...), custom_call_target="tpu_custom_call" | custom-call | flops 2684354560 | bytes 7864320 | tf_op jit(solution)/shard_map/pallas_call | solution.py:95
  43.0 0.0 copy-start.3
  43.0 1.4 convert_element_type.37
  44.4 0.0 copy-start.2
  44.4 1.4 collective-permute-start.3
  45.8 9.0 %collective-permute-done.3 = bf16[256,1024]{1,0:T(8,128)(2,1)S(1)} collective-permute-done((bf16[256,1024]{1,0:T(8,128)(2,1)S(1)}, bf16[256,1024]{1,0:T(8,128)(2,1)S(1)}, u32[]{:S(2)}, u32[]{:S(2)}) %collective-permute-start.3) | collective-permute-done | bytes 524320 | tf_op jit(solution)/shard_map/ppermute | solution.py:20
  54.8 0.0 copy-done.3
  54.8 0.1 add_convert_fusion.3
  54.9 0.0 copy-start
  54.9 1.4 collective-permute-start.4
  56.4 9.9 %collective-permute-done.4 = bf16[256,1024]{1,0:T(8,128)(2,1)S(1)} collective-permute-done((bf16[256,1024]{1,0:T(8,128)(2,1)S(1)}, bf16[256,1024]{1,0:T(8,128)(2,1)S(1)}, u32[]{:S(2)}, u32[]{:S(2)}) %collective-permute-start.4) | collective-permute-done | bytes 524320 | tf_op jit(solution)/shard_map/ppermute | solution.py:20
  66.3 0.0 copy-done.2
  66.3 0.1 add_convert_fusion.2
  66.5 1.3 collective-permute-start.5
  67.8 0.0 copy-done
  67.8 0.0 copy-start.1
  67.8 0.2 dynamic-slice_bitcast_fusion.1
  68.0 1.5 collective-permute-start.6
  69.5 7.9 %collective-permute-done.5 = bf16[256,1024]{1,0:T(8,128)(2,1)S(1)} collective-permute-done((bf16[256,1024]{1,0:T(8,128)(2,1)S(1)}, bf16[256,1024]{1,0:T(8,128)(2,1)S(1)}, u32[]{:S(2)}, u32[]{:S(2)}) %collective-permute-start.5) | collective-permute-done | bytes 524320 | tf_op jit(solution)/shard_map/ppermute | solution.py:20
  77.4 0.0 copy-done.1
  77.4 0.1 add_convert_fusion.1
  77.5 0.9 fusion.8
  78.4 1.5 collective-permute-start.7
  79.9 0.0 collective-permute-done.6
  79.9 7.7 %collective-permute-done.7 = bf16[256,512]{1,0:T(8,128)(2,1)S(1)} collective-permute-done((bf16[256,512]{1,0:T(8,128)(2,1)S(1)}, bf16[256,512]{1,0:T(8,128)(2,1)S(1)}, u32[]{:S(2)}, u32[]{:S(2)}) %collective-permute-start.7) | collective-permute-done | bytes 262176 | tf_op jit(solution)/shard_map/ppermute | solution.py:25
  87.6 1.9 %fusion = f32[1152,512]{1,0:T(8,128)S(1)} fusion(bf16[256,1152]{1,0:T(8,128)(2,1)} %collective-permute-done.6, bf16[256,1152]{1,0:T(8,128)(2,1)S(1)} %get-tuple-element.16, bf16[256,512]{1,0:T(8,128)(2,1)S(1)} %collective-permute-done.7, bf16[256,512]{1,0:T(8,128)(2,1)S(1)} %get-tuple-element.18), kind=kOutput, calls=%fused_computation.3 | convolution fusion | flops 607387648 | bytes 4063232 | tf_op jit(solution)/shard_map/dot_general | solution.py:159
  89.5 0.1 dynamic-slice_convert_fusion
  89.6 3.5 %collective-permute-start.8 = (bf16[576,512]{1,0:T(8,128)(2,1)S(1)}, bf16[576,512]{1,0:T(8,128)(2,1)S(1)}, u32[]{:S(2)}, u32[]{:S(2)}) collective-permute-start(bf16[576,512]{1,0:T(8,128)(2,1)S(1)} %dynamic-slice_convert_fusion), channel_id=1, source_target_pairs={{0,1},{1,0},{2,3},{3,2},{4,5},{5,4},{6,7},{7,6},{8,9},{9,8},{10,11... | collective-permute-start | bytes 1769480 | tf_op jit(solution)/shard_map/ppermute | solution.py:25
  93.1 1.6 %collective-permute-done.8 = bf16[576,512]{1,0:T(8,128)(2,1)S(1)} collective-permute-done((bf16[576,512]{1,0:T(8,128)(2,1)S(1)}, bf16[576,512]{1,0:T(8,128)(2,1)S(1)}, u32[]{:S(2)}, u32[]{:S(2)}) %collective-permute-start.8) | collective-permute-done | bytes 589856 | tf_op jit(solution)/shard_map/ppermute | solution.py:25
  94.7 1.0 add_convert_fusion
  95.7 0.0 reduce-scatter.2.cloned.1.call-update
  95.8 28.4 %reduce-scatter.2.cloned.1.call-done = bf16[144,512]{1,0:T(8,128)(2,1)} async-done(((bf16[576,512]{1,0:T(8,128)(2,1)}), bf16[144,512]{1,0:T(8,128)(2,1)}) %reduce-scatter.2.cloned.1.call-update) | async-done | bytes 147472 | tf_op jit(solution)/shard_map/reduce_scatter | solution.py:169
  124.1 16.5 %all_gather.3 = bf16[576,512]{1,0:T(8,128)(2,1)S(1)} all-gather(bf16[144,512]{1,0:T(8,128)(2,1)} %reduce-scatter.2.cloned.1.call-done), channel_id=1, replica_groups=mesh['groups'=2,'ctx'=4,'fsdp'=2,'sub'=2] {'ctx'}, dimensions={0}, use_global_device_ids=true | all-gather | bytes 737280 | tf_op jit(solution)/shard_map/all_gather | solution.py:170
  140.7 0.0 collective-permute-start.9
  140.7 2.0 %collective-permute-done.9 = bf16[576,512]{1,0:T(8,128)(2,1)S(1)} collective-permute-done((bf16[576,512]{1,0:T(8,128)(2,1)S(1)}, bf16[576,512]{1,0:T(8,128)(2,1)S(1)}, u32[]{:S(2)}, u32[]{:S(2)}) %collective-permute-start.9) | collective-permute-done | bytes 589856 | tf_op jit(solution)/shard_map/ppermute | solution.py:25
  142.7 0.3 convert_select_fusion.1
  143.0 1.7 %maximum_multiply_fusion = f32[1152,512]{1,0:T(8,128)} fusion(f32[576,512]{1,0:T(8,128)S(1)} %get-tuple-element.15, f32[576,512]{1,0:T(8,128)S(1)} %get-tuple-element.14), kind=kLoop, calls=%fused_computation | loop fusion | flops 1179648 | bytes 4718592 | tf_op jit(solution)/shard_map/mul | solution.py:183
  (1 shorter events, 0.0 us)
Async XLA Ops:
  7.2 117.0 %reduce-scatter.2.cloned.1.call-start = ((), (), s32[]{:S(2)}) async-start(), calls=%async_computation.1 | async-start | bytes 737280 | tf_op jit(solution)/shard_map/reduce_scatter | solution.py:169
  8.3 25.2 %copy-start.4 = (bf16[256,1024]{1,0:T(8,128)(2,1)}, bf16[256,1024]{1,0:T(8,128)(2,1)S(1)}, u32[]{:S(2)}) copy-start(bf16[256,1024]{1,0:T(8,128)(2,1)S(1)} %pad_maximum_fusion.refs_6_) | copy-start | bytes 1572868
  8.3 3.9 %collective-permute-start = (bf16[256,1024]{1,0:T(8,128)(2,1)S(1)}, bf16[256,1024]{1,0:T(8,128)(2,1)S(1)}, u32[]{:S(2)}, u32[]{:S(2)}) collective-permute-start(bf16[256,1024]{1,0:T(8,128)(2,1)S(1)} %pad_maximum_fusion.refs_6_), channel_id=1, source_target_pairs={{0,1},{1,4},{4,5},{5,8},{8,9},{9,12},{12,13},{2,3},{3,6},{6,7},{7,... | collective-permute-start | bytes 1572872 | tf_op jit(solution)/shard_map/ppermute | solution.py:20
  12.2 21.3 %copy-start.5 = (bf16[256,1024]{1,0:T(8,128)(2,1)}, bf16[256,1024]{1,0:T(8,128)(2,1)S(1)}, u32[]{:S(2)}) copy-start(bf16[256,1024]{1,0:T(8,128)(2,1)S(1)} %collective-permute-done.refs_5_) | copy-start | bytes 1572868
  12.2 10.7 %collective-permute-start.1 = (bf16[256,1024]{1,0:T(8,128)(2,1)S(1)}, bf16[256,1024]{1,0:T(8,128)(2,1)S(1)}, u32[]{:S(2)}, u32[]{:S(2)}) collective-permute-start(bf16[256,1024]{1,0:T(8,128)(2,1)S(1)} %collective-permute-done.refs_5_), channel_id=1, source_target_pairs={{0,1},{1,4},{4,5},{5,8},{8,9},{9,12},{12,13},{2,3},{3,6},{6,7},{7,... | collective-permute-start | bytes 1572872 | tf_op jit(solution)/shard_map/ppermute | solution.py:20
  22.9 10.6 %copy-start.6 = (bf16[256,1024]{1,0:T(8,128)(2,1)}, bf16[256,1024]{1,0:T(8,128)(2,1)S(1)}, u32[]{:S(2)}) copy-start(bf16[256,1024]{1,0:T(8,128)(2,1)S(1)} %collective-permute-done.1.refs_4_) | copy-start | bytes 1572868
  22.9 10.6 %collective-permute-start.2 = (bf16[256,1024]{1,0:T(8,128)(2,1)S(1)}, bf16[256,1024]{1,0:T(8,128)(2,1)S(1)}, u32[]{:S(2)}, u32[]{:S(2)}) collective-permute-start(bf16[256,1024]{1,0:T(8,128)(2,1)S(1)} %collective-permute-done.1.refs_4_), channel_id=1, source_target_pairs={{0,1},{1,4},{4,5},{5,8},{8,9},{9,12},{12,13},{2,3},{3,6},{6,7},{7,... | collective-permute-start | bytes 1572872 | tf_op jit(solution)/shard_map/ppermute | solution.py:20
  33.5 0.8 copy-start.7
  43.0 11.8 %copy-start.3 = (f32[256,1024]{1,0:T(8,128)S(1)}, f32[256,1024]{1,0:T(8,128)}, u32[]{:S(2)}) copy-start(f32[256,1024]{1,0:T(8,128)} %get-tuple-element.11) | copy-start | bytes 3145732
  44.4 21.9 %copy-start.2 = (f32[256,1024]{1,0:T(8,128)S(1)}, f32[256,1024]{1,0:T(8,128)}, u32[]{:S(2)}) copy-start(f32[256,1024]{1,0:T(8,128)} %get-tuple-element.12) | copy-start | bytes 3145732
  44.4 10.4 %collective-permute-start.3 = (bf16[256,1024]{1,0:T(8,128)(2,1)S(1)}, bf16[256,1024]{1,0:T(8,128)(2,1)S(1)}, u32[]{:S(2)}, u32[]{:S(2)}) collective-permute-start(bf16[256,1024]{1,0:T(8,128)(2,1)S(1)} %convert_element_type.37), channel_id=1, source_target_pairs={{1,0},{4,1},{5,4},{8,5},{9,8},{12,9},{13,12},{3,2},{6,3},{7,6},{10... | collective-permute-start | bytes 1572872 | tf_op jit(solution)/shard_map/ppermute | solution.py:20
  54.9 12.9 %copy-start = (bf16[1,256,2304]{2,1,0:T(8,128)(2,1)S(1)}, bf16[1,256,2304]{2,1,0:T(8,128)(2,1)}, u32[]{:S(2)}) copy-start(bf16[1,256,2304]{2,1,0:T(8,128)(2,1)} %param.6) | copy-start | bytes 3538948
  54.9 11.4 %collective-permute-start.4 = (bf16[256,1024]{1,0:T(8,128)(2,1)S(1)}, bf16[256,1024]{1,0:T(8,128)(2,1)S(1)}, u32[]{:S(2)}, u32[]{:S(2)}) collective-permute-start(bf16[256,1024]{1,0:T(8,128)(2,1)S(1)} %add_convert_fusion.3), channel_id=1, source_target_pairs={{1,0},{4,1},{5,4},{8,5},{9,8},{12,9},{13,12},{3,2},{6,3},{7,6},{10... | collective-permute-start | bytes 1572872 | tf_op jit(solution)/shard_map/ppermute | solution.py:20
  66.5 10.9 %collective-permute-start.5 = (bf16[256,1024]{1,0:T(8,128)(2,1)S(1)}, bf16[256,1024]{1,0:T(8,128)(2,1)S(1)}, u32[]{:S(2)}, u32[]{:S(2)}) collective-permute-start(bf16[256,1024]{1,0:T(8,128)(2,1)S(1)} %add_convert_fusion.2), channel_id=1, source_target_pairs={{1,0},{4,1},{5,4},{8,5},{9,8},{12,9},{13,12},{3,2},{6,3},{7,6},{10... | collective-permute-start | bytes 1572872 | tf_op jit(solution)/shard_map/ppermute | solution.py:20
  67.8 9.6 %copy-start.1 = (f32[256,1024]{1,0:T(8,128)S(1)}, f32[256,1024]{1,0:T(8,128)}, u32[]{:S(2)}) copy-start(f32[256,1024]{1,0:T(8,128)} %get-tuple-element.13) | copy-start | bytes 3145732
  68.0 11.9 %collective-permute-start.6 = (bf16[256,1152]{1,0:T(8,128)(2,1)S(1)}, bf16[256,1152]{1,0:T(8,128)(2,1)}, u32[]{:S(2)}, u32[]{:S(2)}) collective-permute-start(bf16[256,1152]{1,0:T(8,128)(2,1)S(1)} %get-tuple-element.17), channel_id=1, source_target_pairs={{0,2},{2,0},{1,3},{3,1},{4,6},{6,4},{5,7},{7,5},{8,10},{10,8},{9,1... | collective-permute-start | bytes 1769480 | tf_op jit(solution)/shard_map/ppermute | solution.py:25
  78.4 9.2 %collective-permute-start.7 = (bf16[256,512]{1,0:T(8,128)(2,1)S(1)}, bf16[256,512]{1,0:T(8,128)(2,1)S(1)}, u32[]{:S(2)}, u32[]{:S(2)}) collective-permute-start(bf16[256,512]{1,0:T(8,128)(2,1)S(1)} %get-tuple-element.18), channel_id=1, source_target_pairs={{0,2},{2,0},{1,3},{3,1},{4,6},{6,4},{5,7},{7,5},{8,10},{10,8},{9,1... | collective-permute-start | bytes 786440 | tf_op jit(solution)/shard_map/ppermute | solution.py:25
  89.6 5.2 %collective-permute-start.8 = (bf16[576,512]{1,0:T(8,128)(2,1)S(1)}, bf16[576,512]{1,0:T(8,128)(2,1)S(1)}, u32[]{:S(2)}, u32[]{:S(2)}) collective-permute-start(bf16[576,512]{1,0:T(8,128)(2,1)S(1)} %dynamic-slice_convert_fusion), channel_id=1, source_target_pairs={{0,1},{1,0},{2,3},{3,2},{4,5},{5,4},{6,7},{7,6},{8,9},{9,8},{10,11... | collective-permute-start | bytes 1769480 | tf_op jit(solution)/shard_map/ppermute | solution.py:25
  140.7 2.0 %collective-permute-start.9 = (bf16[576,512]{1,0:T(8,128)(2,1)S(1)}, bf16[576,512]{1,0:T(8,128)(2,1)S(1)}, u32[]{:S(2)}, u32[]{:S(2)}) collective-permute-start(bf16[576,512]{1,0:T(8,128)(2,1)S(1)} %all_gather.3), channel_id=1, source_target_pairs={{0,1},{1,0},{2,3},{3,2},{4,5},{5,4},{6,7},{7,6},{8,9},{9,8},{10,11... | collective-permute-start | bytes 1769480 | tf_op jit(solution)/shard_map/ppermute | solution.py:25
Sparse Core Ops, SparseCore 0:
  95.9 28.1 reduce-scatter.1

commit v3 on v2

--- a/solution.py
+++ b/solution.py
@@ -25,6 +25,25 @@
     return lax.ppermute(value, axis, [(source, (source + steps) % count) for source in range(count)])
 
 
+def ring_sum(piece, axis):
+    count = lax.axis_size(axis)
+    at = lax.axis_index(axis)
+    rows = piece.shape[0] // count
+    total = lax.dynamic_slice_in_dim(piece, at * rows, rows, axis=0)
+    for steps in range(1, count):
+        outgoing = lax.dynamic_slice_in_dim(piece, ((at + steps) % count) * rows, rows, axis=0)
+        total = total + rotated(outgoing.astype(jnp.bfloat16), axis, steps).astype(jnp.float32)
+    low = total.astype(jnp.bfloat16)
+    gathered = jnp.zeros(piece.shape, jnp.float32)
+    gathered = lax.dynamic_update_slice_in_dim(gathered, total, at * rows, axis=0)
+    for steps in range(1, count):
+        arrived = rotated(low, axis, steps).astype(jnp.float32)
+        gathered = lax.dynamic_update_slice_in_dim(
+            gathered, arrived, ((at - steps) % count) * rows, axis=0
+        )
+    return gathered
+
+
 def doc_start_of(starts, positions):
     covered = starts[None, :] <= positions[:, None]
     return jnp.max(jnp.where(covered, starts[None, :], 0), axis=1)
@@ -33,10 +52,10 @@
 def attention_kernel(*refs, heads, kv_heads, margin, blocks):
     lo_ref, q_ref, do_ref = refs[:3]
     block_refs = refs[3 : 3 + blocks]
-    dq_ref = refs[3 + blocks]
-    out_refs = refs[4 + blocks : 4 + 2 * blocks]
-    kv_ref = refs[4 + 2 * blocks]
-    dkv_ref = refs[5 + 2 * blocks]
+    kv_ref, dkv_ref = refs[-2:]
+    outs = refs[-3 - blocks : -2]
+    dq_ref = outs[0]
+    out_refs = outs[1:]
     block_rows = block_refs[0].shape[0]
     for index, block_ref in enumerate(block_refs):
         kv_ref[pl.ds(index * block_rows, block_rows), :] = block_ref[...]
@@ -81,7 +100,7 @@
         out_ref[...] = dkv_ref[pl.ds(index * block_rows, block_rows), :]
 
 
-def attention(lo_rel, queries, grads, kv_blocks, heads, kv_heads, margin):
+def attention(lo_rel, queries, grads, kv_blocks, heads, kv_heads, margin, early):
     rows, width = queries.shape
     blocks = len(kv_blocks)
     block_rows, kv_cols = kv_blocks[0].shape
@@ -96,7 +115,7 @@
         kernel,
         out_shape=(jax.ShapeDtypeStruct((rows, width), jnp.bfloat16),)
         + tuple(jax.ShapeDtypeStruct((block_rows, kv_cols), jnp.float32) for _ in kv_blocks),
-        in_specs=[vmem] * (3 + blocks),
+        in_specs=[vmem] * (3 + blocks) + [pl.BlockSpec(memory_space=pl.ANY)] * len(early),
         out_specs=(vmem,) * (1 + blocks),
         scratch_shapes=[
             pltpu.VMEM((keys, kv_cols), kv_blocks[0].dtype),
@@ -105,7 +124,7 @@
         cost_estimate=pl.CostEstimate(
             flops=flops, transcendentals=heads * rows * keys, bytes_accessed=moved
         ),
-    )(lo_rel, queries, grads, *kv_blocks)
+    )(lo_rel, queries, grads, *kv_blocks, *early)
 
 
 def body(layer_input, query_heads, key_heads, value_heads, grad_out, doc_starts):
@@ -117,6 +136,17 @@
     heads = query_heads.shape[2] // HEAD_DIM
     kv_heads = kv_width // HEAD_DIM
     first_row = lax.axis_index(RING) * block_rows
+
+    fsdp_count = lax.axis_size("fsdp")
+    fsdp_at = lax.axis_index("fsdp")
+    model_width = layer_input.shape[2]
+    shard_rows = model_width // fsdp_count
+    own_input = layer_input[0]
+    inputs = [lax.dynamic_slice_in_dim(own_input, fsdp_at * shard_rows, shard_rows, axis=1)]
+    for steps in range(1, fsdp_count):
+        target = (fsdp_at + steps) % fsdp_count
+        outgoing = lax.dynamic_slice_in_dim(own_input, target * shard_rows, shard_rows, axis=1)
+        inputs.append(rotated(outgoing, "fsdp", steps))
 
     own_kv = jnp.concatenate([key_heads[0], value_heads[0]], axis=1)
     arrived = []
@@ -128,7 +158,8 @@
     lowest = jnp.maximum(doc_start_of(doc_starts[0], query_pos), query_pos - window + 1)
     lo_rel = (lowest - first_row + margin).astype(jnp.int32)[:, None]
     grad_q, *grad_pieces = attention(
-        lo_rel, query_heads[0], grad_out[0], arrived[::-1] + [own_kv], heads, kv_heads, margin
+        lo_rel, query_heads[0], grad_out[0], arrived[::-1] + [own_kv], heads, kv_heads, margin,
+        inputs[1:],
     )
 
     def own_piece(distance):
@@ -142,17 +173,8 @@
     grad_key = grad_kv[:, :kv_width]
     grad_value = grad_kv[:, kv_width:]
 
-    fsdp_count = lax.axis_size("fsdp")
-    fsdp_at = lax.axis_index("fsdp")
-    model_width = layer_input.shape[2]
-    shard_rows = model_width // fsdp_count
-    own_input = layer_input[0]
-    inputs = [lax.dynamic_slice_in_dim(own_input, fsdp_at * shard_rows, shard_rows, axis=1)]
     values = [grad_value]
     for steps in range(1, fsdp_count):
-        target = (fsdp_at + steps) % fsdp_count
-        outgoing = lax.dynamic_slice_in_dim(own_input, target * shard_rows, shard_rows, axis=1)
-        inputs.append(rotated(outgoing, "fsdp", steps))
         values.append(rotated(grad_value, "fsdp", steps))
     stacked_inputs = jnp.concatenate(inputs, axis=0)
     stacked_values = jnp.concatenate(values, axis=0)
@@ -166,8 +188,7 @@
         target = (sub_at + steps) % sub_count
         outgoing = lax.dynamic_slice_in_dim(shard, target * piece_rows, piece_rows, axis=0)
         mine = mine + rotated(outgoing.astype(jnp.bfloat16), "sub", steps).astype(jnp.float32)
-    scattered = lax.psum_scatter(mine.astype(jnp.bfloat16), "ctx", scatter_dimension=0, tiled=True)
-    reduced = lax.all_gather(scattered, "ctx", axis=0, tiled=True).astype(jnp.float32)
+    reduced = ring_sum(mine, "ctx")
     if sub_count == 2:
         other = rotated(reduced.astype(jnp.bfloat16), "sub", 1).astype(jnp.float32)
         first = jnp.where(sub_at == 0, reduced, other)

time: 152 us -> 125 us (0.82)
  blocking collectives: 16.5 us -> 0 us
  between operations: 14.2 us -> 0.95 us
  starting transfers between devices: 31.3 us -> 44.5 us
  waiting for transfers between devices: 69.5 us -> 56.5 us
  local copies, waits for them, and re-layouts: 2.04 us -> 5.02 us
    reduce_scatter x1 -> x0, waiting for transfers between devices: 28.4 us -> none  [body(): lax.psum_scatter(mine.astype(jnp.bfloat16), 'ctx', scatter_dimension=0, t...]
    ppermute x4 -> x10, waiting for transfers between devices: 11.4 us -> 31.1 us  [rotated(): lax.ppermute(value, axis, [(source, (source + steps) % count) for source...]
    all_gather x1 -> x0, blocking collectives: 16.5 us -> none  [body(): lax.all_gather(scattered, 'ctx', axis=0, tiled=True).astype(jnp.float32)]
    ppermute x4 -> x10, starting transfers between devices: 6.52 us -> 21.2 us  [rotated(): lax.ppermute(value, axis, [(source, (source + steps) % count) for source...]
    ppermute x6, waiting for transfers between devices: 29.8 us -> 25.4 us  [passed_along(): lax.ppermute(value, axis, [(source, source + steps) for source in range(f...]
    unnamed x16 -> x22, local copies, waits for them, and re-layouts: 0.8 us -> 2.42 us
  transfers between devices with their start and end apart: 11 -> 16, of which waited for: 9 -> 12; matrix products, arithmetic and copies ran while one was open for 2% -> 2% of each run, Pallas kernels for 0% -> 0%
where the time goes in v3:
time: 125 us; the launch traced here: 124 us
  waiting for transfers between devices  56.5 us (45%)
  starting transfers between devices  44.5 us (36%)
  Pallas kernels  8.69 us (7%)
  other arithmetic  7.32 us (6%)
  local copies, waits for them, and re-layouts  5.02 us (4%)
    ppermute x10, waiting for transfers between devices, rotated(): lax.ppermute(value, axis, [(source, (source + steps) % count) for source...  31.1 us
    ppermute x6, waiting for transfers between devices, passed_along(): lax.ppermute(value, axis, [(source, source + steps) for source in range(f...  25.4 us
    ppermute x6, starting transfers between devices, passed_along(): lax.ppermute(value, axis, [(source, source + steps) for source in range(f...  23.3 us
    ppermute x10, starting transfers between devices, rotated(): lax.ppermute(value, axis, [(source, (source + steps) % count) for source...  21.2 us
    pallas_call x1, Pallas kernels, attention(): pl.pallas_call(kernel, out_shape=(jax.ShapeDtypeStruct((rows, width), jnp...  8.69 us
  transfers between devices with their start and end apart: 16, of which 12 were waited for; matrix products, arithmetic and copies ran while one was open for 2% of the time, Pallas kernels for 0%

profile of v3, /device:TPU:0, one launch (start us, length us, event | category | flops | bytes accessed | tf_op | source)
XLA Modules:
  0.0 123.8 jit_solution(17019492762018346284)
XLA Ops:
  0.6 1.1 pad_maximum_fusion.refs_6_
  1.7 0.0 copy-start.4
  1.7 2.4 %collective-permute-start = (bf16[256,1024]{1,0:T(8,128)(2,1)S(1)}, bf16[256,1024]{1,0:T(8,128)(2,1)S(1)}, u32[]{:S(2)}, u32[]{:S(2)}) collective-permute-start(bf16[256,1024]{1,0:T(8,128)(2,1)S(1)} %pad_maximum_fusion.refs_6_), channel_id=1, source_target_pairs={{0,1},{1,4},{4,5},{5,8},{8,9},{9,12},{12,13},{2,3},{3,6},{6,7},{7,... | collective-permute-start | bytes 1572872 | tf_op jit(solution)/shard_map/ppermute | solution.py:20
  4.1 1.5 %collective-permute-done.refs_5_ = bf16[256,1024]{1,0:T(8,128)(2,1)S(1)} collective-permute-done((bf16[256,1024]{1,0:T(8,128)(2,1)S(1)}, bf16[256,1024]{1,0:T(8,128)(2,1)S(1)}, u32[]{:S(2)}, u32[]{:S(2)}) %collective-permute-start) | collective-permute-done | bytes 524320 | tf_op jit(solution)/shard_map/ppermute | solution.py:20
  5.6 9.2 %collective-permute-start.1 = (bf16[256,1024]{1,0:T(8,128)(2,1)S(1)}, bf16[256,1024]{1,0:T(8,128)(2,1)S(1)}, u32[]{:S(2)}, u32[]{:S(2)}) collective-permute-start(bf16[256,1024]{1,0:T(8,128)(2,1)S(1)} %collective-permute-done.refs_5_), channel_id=1, source_target_pairs={{0,1},{1,4},{4,5},{5,8},{8,9},{9,12},{12,13},{2,3},{3,6},{6,7},{7,... | collective-permute-start | bytes 1572872 | tf_op jit(solution)/shard_map/ppermute | solution.py:20
  14.8 0.0 copy-start.5
  14.9 1.3 %dynamic-slice_bitcast_fusion = (bf16[256,1152]{1,0:T(8,128)(2,1)S(1)}, bf16[256,1152]{1,0:T(8,128)(2,1)S(1)}) fusion(bf16[1,256,2304]{2,1,0:T(8,128)(2,1)} %param.6, s32[]{:T(128)S(6)} %select_n.89, s32[]{:T(128)S(6)} %select_n.87), kind=kLoop, calls=%fused_computation.12 | loop fusion | bytes 2359304 | tf_op jit(solution)/shard_map/dynamic_slice | solution.py:145
  16.2 0.0 copy-done.4
  16.2 0.0 copy-done.8
  16.2 1.6 %collective-permute-start.3 = (bf16[256,1152]{1,0:T(8,128)(2,1)S(1)}, bf16[256,1152]{1,0:T(8,128)(2,1)S(1)}, u32[]{:S(2)}, u32[]{:S(2)}) collective-permute-start(bf16[256,1152]{1,0:T(8,128)(2,1)S(1)} %get-tuple-element.22), channel_id=1, source_target_pairs={{0,2},{2,0},{1,3},{3,1},{4,6},{6,4},{5,7},{7,5},{8,10},{10,8},{9,1... | collective-permute-start | bytes 1769480 | tf_op jit(solution)/shard_map/ppermute | solution.py:25
  17.8 0.0 collective-permute-done.1.refs_4_
  17.8 7.5 %collective-permute-start.2 = (bf16[256,1024]{1,0:T(8,128)(2,1)S(1)}, bf16[256,1024]{1,0:T(8,128)(2,1)S(1)}, u32[]{:S(2)}, u32[]{:S(2)}) collective-permute-start(bf16[256,1024]{1,0:T(8,128)(2,1)S(1)} %collective-permute-done.1.refs_4_), channel_id=1, source_target_pairs={{0,1},{1,4},{4,5},{5,8},{8,9},{9,12},{12,13},{2,3},{3,6},{6,7},{7,... | collective-permute-start | bytes 1572872 | tf_op jit(solution)/shard_map/ppermute | solution.py:20
  25.3 0.0 copy-done.5
  25.3 0.1 select_reduce_fusion
  25.4 0.1 copy.13
  25.6 0.7 subtract_add_fusion.refs_0_
  26.3 4.7 %collective-permute-done.3.refs_7_ = bf16[256,1152]{1,0:T(8,128)(2,1)S(1)} collective-permute-done((bf16[256,1152]{1,0:T(8,128)(2,1)S(1)}, bf16[256,1152]{1,0:T(8,128)(2,1)S(1)}, u32[]{:S(2)}, u32[]{:S(2)}) %collective-permute-start.3) | collective-permute-done | bytes 589856 | tf_op jit(solution)/shard_map/ppermute | solution.py:25
  30.9 0.0 collective-permute-done.2.refs_3_
  30.9 0.0 copy-done.9
  30.9 0.8 copy-done.6
  31.7 0.2 copy-done.10
  31.9 8.7 %shard_map.93 = (bf16[256,1024]{1,0:T(8,128)(2,1)}, f32[256,1024]{1,0:T(8,128)}, f32[256,1024]{1,0:T(8,128)}, f32[256,1024]{1,0:T(8,128)}, f32[256,1024]{1,0:T(8,128)}) custom-call(s32[256,1]{1,0:T(8,128)} %subtract_add_fusion.refs_0_, bf16[256,1024]{1,0:T(8,128)(2,1)} %bitcast.19, bf16[256,1024]{1,0:T(8,128)(2,1)} %bitcast.20, ...), custom_call_target="tpu_custom_call" | custom-call | flops 2684354560 | bytes 7864320 | tf_op jit(solution)/shard_map/pallas_call | solution.py:114
  40.6 1.4 %convert_element_type.63 = bf16[256,1024]{1,0:T(8,128)(2,1)S(1)} convert(f32[256,1024]{1,0:T(8,128)} %get-tuple-element.10) | non-fusion elementwise | flops 262144 | bytes 1572864 | tf_op jit(solution)/shard_map/convert_element_type | solution.py:170
  42.0 0.0 copy-start.2
  42.0 1.4 %collective-permute-start.4 = (bf16[256,1024]{1,0:T(8,128)(2,1)S(1)}, bf16[256,1024]{1,0:T(8,128)(2,1)S(1)}, u32[]{:S(2)}, u32[]{:S(2)}) collective-permute-start(bf16[256,1024]{1,0:T(8,128)(2,1)S(1)} %convert_element_type.63), channel_id=1, source_target_pairs={{1,0},{4,1},{5,4},{8,5},{9,8},{12,9},{13,12},{3,2},{6,3},{7,6},{10... | collective-permute-start | bytes 1572872 | tf_op jit(solution)/shard_map/ppermute | solution.py:20
  43.4 4.7 %collective-permute-done.4 = bf16[256,1024]{1,0:T(8,128)(2,1)S(1)} collective-permute-done((bf16[256,1024]{1,0:T(8,128)(2,1)S(1)}, bf16[256,1024]{1,0:T(8,128)(2,1)S(1)}, u32[]{:S(2)}, u32[]{:S(2)}) %collective-permute-start.4) | collective-permute-done | bytes 524320 | tf_op jit(solution)/shard_map/ppermute | solution.py:20
  48.2 0.0 copy-done.3
  48.2 0.1 add_convert_fusion.2
  48.4 1.4 %collective-permute-start.5 = (bf16[256,1024]{1,0:T(8,128)(2,1)S(1)}, bf16[256,1024]{1,0:T(8,128)(2,1)S(1)}, u32[]{:S(2)}, u32[]{:S(2)}) collective-permute-start(bf16[256,1024]{1,0:T(8,128)(2,1)S(1)} %add_convert_fusion.2), channel_id=1, source_target_pairs={{1,0},{4,1},{5,4},{8,5},{9,8},{12,9},{13,12},{3,2},{6,3},{7,6},{10... | collective-permute-start | bytes 1572872 | tf_op jit(solution)/shard_map/ppermute | solution.py:20
  49.8 9.9 %collective-permute-done.5 = bf16[256,1024]{1,0:T(8,128)(2,1)S(1)} collective-permute-done((bf16[256,1024]{1,0:T(8,128)(2,1)S(1)}, bf16[256,1024]{1,0:T(8,128)(2,1)S(1)}, u32[]{:S(2)}, u32[]{:S(2)}) %collective-permute-start.5) | collective-permute-done | bytes 524320 | tf_op jit(solution)/shard_map/ppermute | solution.py:20
  59.7 0.1 add_convert_fusion.1
  59.9 1.3 %collective-permute-start.6 = (bf16[256,1024]{1,0:T(8,128)(2,1)S(1)}, bf16[256,1024]{1,0:T(8,128)(2,1)S(1)}, u32[]{:S(2)}, u32[]{:S(2)}) collective-permute-start(bf16[256,1024]{1,0:T(8,128)(2,1)S(1)} %add_convert_fusion.1), channel_id=1, source_target_pairs={{1,0},{4,1},{5,4},{8,5},{9,8},{12,9},{13,12},{3,2},{6,3},{7,6},{10... | collective-permute-start | bytes 1572872 | tf_op jit(solution)/shard_map/ppermute | solution.py:20
  61.2 9.2 %collective-permute-done.6 = bf16[256,1024]{1,0:T(8,128)(2,1)S(1)} collective-permute-done((bf16[256,1024]{1,0:T(8,128)(2,1)S(1)}, bf16[256,1024]{1,0:T(8,128)(2,1)S(1)}, u32[]{:S(2)}, u32[]{:S(2)}) %collective-permute-start.6) | collective-permute-done | bytes 524320 | tf_op jit(solution)/shard_map/ppermute | solution.py:20
  70.4 0.1 add_convert_fusion
  70.5 0.9 fusion.10
  71.4 1.5 %collective-permute-start.7 = (bf16[256,512]{1,0:T(8,128)(2,1)S(1)}, bf16[256,512]{1,0:T(8,128)(2,1)S(1)}, u32[]{:S(2)}, u32[]{:S(2)}) collective-permute-start(bf16[256,512]{1,0:T(8,128)(2,1)S(1)} %get-tuple-element.23), channel_id=1, source_target_pairs={{0,2},{2,0},{1,3},{3,1},{4,6},{6,4},{5,7},{7,5},{8,10},{10,8},{9,1... | collective-permute-start | bytes 786440 | tf_op jit(solution)/shard_map/ppermute | solution.py:25
  72.9 4.9 %collective-permute-done.7 = bf16[256,512]{1,0:T(8,128)(2,1)S(1)} collective-permute-done((bf16[256,512]{1,0:T(8,128)(2,1)S(1)}, bf16[256,512]{1,0:T(8,128)(2,1)S(1)}, u32[]{:S(2)}, u32[]{:S(2)}) %collective-permute-start.7) | collective-permute-done | bytes 262176 | tf_op jit(solution)/shard_map/ppermute | solution.py:25
  77.8 0.8 fusion
  78.6 0.0 copy-start
  78.6 1.4 %copy-done = f32[1152,512]{1,0:T(8,128)} copy-done((f32[1152,512]{1,0:T(8,128)}, f32[1152,512]{1,0:T(8,128)S(1)}, u32[]{:S(2)}) %copy-start) | copy-done | bytes 2359320
  80.0 0.1 dynamic-slice_convert_fusion
  80.1 6.4 %collective-permute-start.8 = (bf16[576,512]{1,0:T(8,128)(2,1)S(1)}, bf16[576,512]{1,0:T(8,128)(2,1)S(1)}, u32[]{:S(2)}, u32[]{:S(2)}) collective-permute-start(bf16[576,512]{1,0:T(8,128)(2,1)S(1)} %dynamic-slice_convert_fusion), channel_id=1, source_target_pairs={{0,1},{1,0},{2,3},{3,2},{4,5},{5,4},{6,7},{7,6},{8,9},{9,8},{10,11... | collective-permute-start | bytes 1769480 | tf_op jit(solution)/shard_map/ppermute | solution.py:25
  86.5 1.6 %collective-permute-done.8 = bf16[576,512]{1,0:T(8,128)(2,1)S(1)} collective-permute-done((bf16[576,512]{1,0:T(8,128)(2,1)S(1)}, bf16[576,512]{1,0:T(8,128)(2,1)S(1)}, u32[]{:S(2)}, u32[]{:S(2)}) %collective-permute-start.8) | collective-permute-done | bytes 589856 | tf_op jit(solution)/shard_map/ppermute | solution.py:25
  88.1 1.4 %convert_add_fusion = f32[576,512]{1,0:T(8,128)S(1)} fusion(bf16[576,512]{1,0:T(8,128)(2,1)S(1)} %collective-permute-done.8, f32[1152,512]{1,0:T(8,128)} %copy-done, s32[]{:T(128)S(6)} %select_n.90), kind=kLoop, calls=%fused_computation.7 | loop fusion | flops 589824 | bytes 2949124 | tf_op jit(solution)/shard_map/add | solution.py:190
  89.6 0.1 dynamic-slice_convert_fusion.3
  89.6 4.3 %collective-permute-start.10 = (bf16[144,512]{1,0:T(8,128)(2,1)S(1)}, bf16[144,512]{1,0:T(8,128)(2,1)S(1)}, u32[]{:S(2)}, u32[]{:S(2)}) collective-permute-start(bf16[144,512]{1,0:T(8,128)(2,1)S(1)} %get-tuple-element.20), channel_id=1, source_target_pairs={{0,8},{4,12},{8,0},{12,4},{1,9},{5,13},{9,1},{13,5},{2,10},{6,14},... | collective-permute-start | bytes 442376 | tf_op jit(solution)/shard_map/ppermute | solution.py:25
  93.9 1.3 %collective-permute-start.11 = (bf16[144,512]{1,0:T(8,128)(2,1)S(1)}, bf16[144,512]{1,0:T(8,128)(2,1)S(1)}, u32[]{:S(2)}, u32[]{:S(2)}) collective-permute-start(bf16[144,512]{1,0:T(8,128)(2,1)S(1)} %get-tuple-element.19), channel_id=1, source_target_pairs={{0,12},{4,0},{8,4},{12,8},{1,13},{5,1},{9,5},{13,9},{2,14},{6,2},{... | collective-permute-start | bytes 442376 | tf_op jit(solution)/shard_map/ppermute | solution.py:25
  95.3 0.7 collective-permute-start.9
  96.0 5.9 %collective-permute-done.10 = bf16[144,512]{1,0:T(8,128)(2,1)S(1)} collective-permute-done((bf16[144,512]{1,0:T(8,128)(2,1)S(1)}, bf16[144,512]{1,0:T(8,128)(2,1)S(1)}, u32[]{:S(2)}, u32[]{:S(2)}) %collective-permute-start.10) | collective-permute-done | bytes 147488 | tf_op jit(solution)/shard_map/ppermute | solution.py:25
  101.8 0.0 collective-permute-done.11
  101.8 4.0 %collective-permute-done.9 = bf16[144,512]{1,0:T(8,128)(2,1)S(1)} collective-permute-done((bf16[144,512]{1,0:T(8,128)(2,1)S(1)}, bf16[144,512]{1,0:T(8,128)(2,1)S(1)}, u32[]{:S(2)}, u32[]{:S(2)}) %collective-permute-start.9) | collective-permute-done | bytes 147488 | tf_op jit(solution)/shard_map/ppermute | solution.py:25
  105.8 0.1 broadcast_in_dim.28
  106.0 0.1 fusion.7
  106.1 2.6 %collective-permute-start.12 = (bf16[144,512]{1,0:T(8,128)(2,1)S(1)}, bf16[144,512]{1,0:T(8,128)(2,1)S(1)}, u32[]{:S(2)}, u32[]{:S(2)}) collective-permute-start(bf16[144,512]{1,0:T(8,128)(2,1)S(1)} %get-tuple-element.16), channel_id=1, source_target_pairs={{0,4},{4,8},{8,12},{12,0},{1,5},{5,9},{9,13},{13,1},{2,6},{6,10},{... | collective-permute-start | bytes 442376 | tf_op jit(solution)/shard_map/ppermute | solution.py:25
  108.7 0.0 collective-permute-start.13
  108.7 2.8 %collective-permute-start.14 = (bf16[144,512]{1,0:T(8,128)(2,1)S(1)}, bf16[144,512]{1,0:T(8,128)(2,1)S(1)}, u32[]{:S(2)}, u32[]{:S(2)}) collective-permute-start(bf16[144,512]{1,0:T(8,128)(2,1)S(1)} %get-tuple-element.16), channel_id=1, source_target_pairs={{0,12},{4,0},{8,4},{12,8},{1,13},{5,1},{9,5},{13,9},{2,14},{6,2},{... | collective-permute-start | bytes 442376 | tf_op jit(solution)/shard_map/ppermute | solution.py:25
  111.4 3.4 %collective-permute-done.12 = bf16[144,512]{1,0:T(8,128)(2,1)S(1)} collective-permute-done((bf16[144,512]{1,0:T(8,128)(2,1)S(1)}, bf16[144,512]{1,0:T(8,128)(2,1)S(1)}, u32[]{:S(2)}, u32[]{:S(2)}) %collective-permute-start.12) | collective-permute-done | bytes 147488 | tf_op jit(solution)/shard_map/ppermute | solution.py:25
  114.8 4.7 %collective-permute-done.13 = bf16[144,512]{1,0:T(8,128)(2,1)S(1)} collective-permute-done((bf16[144,512]{1,0:T(8,128)(2,1)S(1)}, bf16[144,512]{1,0:T(8,128)(2,1)S(1)}, u32[]{:S(2)}, u32[]{:S(2)}) %collective-permute-start.13) | collective-permute-done | bytes 147488 | tf_op jit(solution)/shard_map/ppermute | solution.py:25
  119.6 0.0 collective-permute-done.14
  119.7 0.1 convert_element_type.82
  119.7 0.1 collective-permute-start.15
  119.8 2.0 %collective-permute-done.15 = bf16[576,512]{1,0:T(8,128)(2,1)S(1)} collective-permute-done((bf16[576,512]{1,0:T(8,128)(2,1)S(1)}, bf16[576,512]{1,0:T(8,128)(2,1)S(1)}, u32[]{:S(2)}, u32[]{:S(2)}) %collective-permute-start.15) | collective-permute-done | bytes 589856 | tf_op jit(solution)/shard_map/ppermute | solution.py:25
  121.8 0.3 convert_select_fusion.1
  122.1 1.7 %maximum_multiply_fusion = f32[1152,512]{1,0:T(8,128)} fusion(f32[576,512]{1,0:T(8,128)S(1)} %get-tuple-element.15, f32[576,512]{1,0:T(8,128)S(1)} %get-tuple-element.14), kind=kLoop, calls=%fused_computation | loop fusion | flops 1179648 | bytes 4718592 | tf_op jit(solution)/shard_map/mul | solution.py:204
  (14 shorter events, 0.1 us)
Async XLA Ops:
  1.7 14.5 %copy-start.4 = (bf16[256,1024]{1,0:T(8,128)(2,1)}, bf16[256,1024]{1,0:T(8,128)(2,1)S(1)}, u32[]{:S(2)}) copy-start(bf16[256,1024]{1,0:T(8,128)(2,1)S(1)} %pad_maximum_fusion.refs_6_) | copy-start | bytes 1572868
  1.7 3.9 %collective-permute-start = (bf16[256,1024]{1,0:T(8,128)(2,1)S(1)}, bf16[256,1024]{1,0:T(8,128)(2,1)S(1)}, u32[]{:S(2)}, u32[]{:S(2)}) collective-permute-start(bf16[256,1024]{1,0:T(8,128)(2,1)S(1)} %pad_maximum_fusion.refs_6_), channel_id=1, source_target_pairs={{0,1},{1,4},{4,5},{5,8},{8,9},{9,12},{12,13},{2,3},{3,6},{6,7},{7,... | collective-permute-start | bytes 1572872 | tf_op jit(solution)/shard_map/ppermute | solution.py:20
  5.6 10.6 %copy-start.8 = (bf16[256,1024]{1,0:T(8,128)(2,1)}, bf16[256,1024]{1,0:T(8,128)(2,1)S(1)}, u32[]{:S(2)}) copy-start(bf16[256,1024]{1,0:T(8,128)(2,1)S(1)} %collective-permute-done.refs_5_) | copy-start | bytes 1572868
  5.6 12.2 %collective-permute-start.1 = (bf16[256,1024]{1,0:T(8,128)(2,1)S(1)}, bf16[256,1024]{1,0:T(8,128)(2,1)S(1)}, u32[]{:S(2)}, u32[]{:S(2)}) collective-permute-start(bf16[256,1024]{1,0:T(8,128)(2,1)S(1)} %collective-permute-done.refs_5_), channel_id=1, source_target_pairs={{0,1},{1,4},{4,5},{5,8},{8,9},{9,12},{12,13},{2,3},{3,6},{6,7},{7,... | collective-permute-start | bytes 1572872 | tf_op jit(solution)/shard_map/ppermute | solution.py:20
  14.8 10.5 %copy-start.5 = (s32[1,12]{1,0:T(1,128)S(1)}, s32[1,12]{1,0:T(1,128)}, u32[]{:S(2)}) copy-start(s32[1,12]{1,0:T(1,128)} %param.11) | copy-start | bytes 148
  16.2 14.7 %collective-permute-start.3 = (bf16[256,1152]{1,0:T(8,128)(2,1)S(1)}, bf16[256,1152]{1,0:T(8,128)(2,1)S(1)}, u32[]{:S(2)}, u32[]{:S(2)}) collective-permute-start(bf16[256,1152]{1,0:T(8,128)(2,1)S(1)} %get-tuple-element.22), channel_id=1, source_target_pairs={{0,2},{2,0},{1,3},{3,1},{4,6},{6,4},{5,7},{7,5},{8,10},{10,8},{9,1... | collective-permute-start | bytes 1769480 | tf_op jit(solution)/shard_map/ppermute | solution.py:25
  17.8 13.2 %copy-start.9 = (bf16[256,1024]{1,0:T(8,128)(2,1)}, bf16[256,1024]{1,0:T(8,128)(2,1)S(1)}, u32[]{:S(2)}) copy-start(bf16[256,1024]{1,0:T(8,128)(2,1)S(1)} %collective-permute-done.1.refs_4_) | copy-start | bytes 1572868
  17.8 13.2 %collective-permute-start.2 = (bf16[256,1024]{1,0:T(8,128)(2,1)S(1)}, bf16[256,1024]{1,0:T(8,128)(2,1)S(1)}, u32[]{:S(2)}, u32[]{:S(2)}) collective-permute-start(bf16[256,1024]{1,0:T(8,128)(2,1)S(1)} %collective-permute-done.1.refs_4_), channel_id=1, source_target_pairs={{0,1},{1,4},{4,5},{5,8},{8,9},{9,12},{12,13},{2,3},{3,6},{6,7},{7,... | collective-permute-start | bytes 1572872 | tf_op jit(solution)/shard_map/ppermute | solution.py:20
  30.9 0.8 copy-start.6
  30.9 1.0 copy-start.10
  40.6 7.6 %copy-start.3 = (f32[256,1024]{1,0:T(8,128)S(1)}, f32[256,1024]{1,0:T(8,128)}, u32[]{:S(2)}) copy-start(f32[256,1024]{1,0:T(8,128)} %get-tuple-element.11) | copy-start | bytes 3145732
  42.0 17.7 %copy-start.2 = (f32[256,1024]{1,0:T(8,128)S(1)}, f32[256,1024]{1,0:T(8,128)}, u32[]{:S(2)}) copy-start(f32[256,1024]{1,0:T(8,128)} %get-tuple-element.12) | copy-start | bytes 3145732
  42.0 6.2 %collective-permute-start.4 = (bf16[256,1024]{1,0:T(8,128)(2,1)S(1)}, bf16[256,1024]{1,0:T(8,128)(2,1)S(1)}, u32[]{:S(2)}, u32[]{:S(2)}) collective-permute-start(bf16[256,1024]{1,0:T(8,128)(2,1)S(1)} %convert_element_type.63), channel_id=1, source_target_pairs={{1,0},{4,1},{5,4},{8,5},{9,8},{12,9},{13,12},{3,2},{6,3},{7,6},{10... | collective-permute-start | bytes 1572872 | tf_op jit(solution)/shard_map/ppermute | solution.py:20
  48.3 22.0 %copy-start.1 = (f32[256,1024]{1,0:T(8,128)S(1)}, f32[256,1024]{1,0:T(8,128)}, u32[]{:S(2)}) copy-start(f32[256,1024]{1,0:T(8,128)} %get-tuple-element.13) | copy-start | bytes 3145732
  48.4 11.4 %collective-permute-start.5 = (bf16[256,1024]{1,0:T(8,128)(2,1)S(1)}, bf16[256,1024]{1,0:T(8,128)(2,1)S(1)}, u32[]{:S(2)}, u32[]{:S(2)}) collective-permute-start(bf16[256,1024]{1,0:T(8,128)(2,1)S(1)} %add_convert_fusion.2), channel_id=1, source_target_pairs={{1,0},{4,1},{5,4},{8,5},{9,8},{12,9},{13,12},{3,2},{6,3},{7,6},{10... | collective-permute-start | bytes 1572872 | tf_op jit(solution)/shard_map/ppermute | solution.py:20
  59.9 10.5 %collective-permute-start.6 = (bf16[256,1024]{1,0:T(8,128)(2,1)S(1)}, bf16[256,1024]{1,0:T(8,128)(2,1)S(1)}, u32[]{:S(2)}, u32[]{:S(2)}) collective-permute-start(bf16[256,1024]{1,0:T(8,128)(2,1)S(1)} %add_convert_fusion.1), channel_id=1, source_target_pairs={{1,0},{4,1},{5,4},{8,5},{9,8},{12,9},{13,12},{3,2},{6,3},{7,6},{10... | collective-permute-start | bytes 1572872 | tf_op jit(solution)/shard_map/ppermute | solution.py:20
  70.5 7.2 %copy-start.7 = (bf16[256,1152]{1,0:T(8,128)(2,1)S(1)}, bf16[256,1152]{1,0:T(8,128)(2,1)}, u32[]{:S(2)}) copy-start(bf16[256,1152]{1,0:T(8,128)(2,1)} %copy-done.6) | copy-start | bytes 1769476
  71.4 6.4 %collective-permute-start.7 = (bf16[256,512]{1,0:T(8,128)(2,1)S(1)}, bf16[256,512]{1,0:T(8,128)(2,1)S(1)}, u32[]{:S(2)}, u32[]{:S(2)}) collective-permute-start(bf16[256,512]{1,0:T(8,128)(2,1)S(1)} %get-tuple-element.23), channel_id=1, source_target_pairs={{0,2},{2,0},{1,3},{3,1},{4,6},{6,4},{5,7},{7,5},{8,10},{10,8},{9,1... | collective-permute-start | bytes 786440 | tf_op jit(solution)/shard_map/ppermute | solution.py:25
  78.6 1.4 %copy-start = (f32[1152,512]{1,0:T(8,128)}, f32[1152,512]{1,0:T(8,128)S(1)}, u32[]{:S(2)}) copy-start(f32[1152,512]{1,0:T(8,128)S(1)} %fusion) | copy-start | bytes 7077892
  80.1 8.0 %collective-permute-start.8 = (bf16[576,512]{1,0:T(8,128)(2,1)S(1)}, bf16[576,512]{1,0:T(8,128)(2,1)S(1)}, u32[]{:S(2)}, u32[]{:S(2)}) collective-permute-start(bf16[576,512]{1,0:T(8,128)(2,1)S(1)} %dynamic-slice_convert_fusion), channel_id=1, source_target_pairs={{0,1},{1,0},{2,3},{3,2},{4,5},{5,4},{6,7},{7,6},{8,9},{9,8},{10,11... | collective-permute-start | bytes 1769480 | tf_op jit(solution)/shard_map/ppermute | solution.py:25
  89.6 12.2 %collective-permute-start.10 = (bf16[144,512]{1,0:T(8,128)(2,1)S(1)}, bf16[144,512]{1,0:T(8,128)(2,1)S(1)}, u32[]{:S(2)}, u32[]{:S(2)}) collective-permute-start(bf16[144,512]{1,0:T(8,128)(2,1)S(1)} %get-tuple-element.20), channel_id=1, source_target_pairs={{0,8},{4,12},{8,0},{12,4},{1,9},{5,13},{9,1},{13,5},{2,10},{6,14},... | collective-permute-start | bytes 442376 | tf_op jit(solution)/shard_map/ppermute | solution.py:25
  93.9 7.9 %collective-permute-start.11 = (bf16[144,512]{1,0:T(8,128)(2,1)S(1)}, bf16[144,512]{1,0:T(8,128)(2,1)S(1)}, u32[]{:S(2)}, u32[]{:S(2)}) collective-permute-start(bf16[144,512]{1,0:T(8,128)(2,1)S(1)} %get-tuple-element.19), channel_id=1, source_target_pairs={{0,12},{4,0},{8,4},{12,8},{1,13},{5,1},{9,5},{13,9},{2,14},{6,2},{... | collective-permute-start | bytes 442376 | tf_op jit(solution)/shard_map/ppermute | solution.py:25
  95.3 10.6 %collective-permute-start.9 = (bf16[144,512]{1,0:T(8,128)(2,1)S(1)}, bf16[144,512]{1,0:T(8,128)(2,1)S(1)}, u32[]{:S(2)}, u32[]{:S(2)}) collective-permute-start(bf16[144,512]{1,0:T(8,128)(2,1)S(1)} %get-tuple-element.18), channel_id=1, source_target_pairs={{0,4},{4,8},{8,12},{12,0},{1,5},{5,9},{9,13},{13,1},{2,6},{6,10},{... | collective-permute-start | bytes 442376 | tf_op jit(solution)/shard_map/ppermute | solution.py:25
  106.1 8.7 %collective-permute-start.12 = (bf16[144,512]{1,0:T(8,128)(2,1)S(1)}, bf16[144,512]{1,0:T(8,128)(2,1)S(1)}, u32[]{:S(2)}, u32[]{:S(2)}) collective-permute-start(bf16[144,512]{1,0:T(8,128)(2,1)S(1)} %get-tuple-element.16), channel_id=1, source_target_pairs={{0,4},{4,8},{8,12},{12,0},{1,5},{5,9},{9,13},{13,1},{2,6},{6,10},{... | collective-permute-start | bytes 442376 | tf_op jit(solution)/shard_map/ppermute | solution.py:25
  108.7 10.9 %collective-permute-start.13 = (bf16[144,512]{1,0:T(8,128)(2,1)S(1)}, bf16[144,512]{1,0:T(8,128)(2,1)S(1)}, u32[]{:S(2)}, u32[]{:S(2)}) collective-permute-start(bf16[144,512]{1,0:T(8,128)(2,1)S(1)} %get-tuple-element.16), channel_id=1, source_target_pairs={{0,8},{4,12},{8,0},{12,4},{1,9},{5,13},{9,1},{13,5},{2,10},{6,14},... | collective-permute-start | bytes 442376 | tf_op jit(solution)/shard_map/ppermute | solution.py:25
  108.7 10.9 %collective-permute-start.14 = (bf16[144,512]{1,0:T(8,128)(2,1)S(1)}, bf16[144,512]{1,0:T(8,128)(2,1)S(1)}, u32[]{:S(2)}, u32[]{:S(2)}) collective-permute-start(bf16[144,512]{1,0:T(8,128)(2,1)S(1)} %get-tuple-element.16), channel_id=1, source_target_pairs={{0,12},{4,0},{8,4},{12,8},{1,13},{5,1},{9,5},{13,9},{2,14},{6,2},{... | collective-permute-start | bytes 442376 | tf_op jit(solution)/shard_map/ppermute | solution.py:25
  119.7 2.1 %collective-permute-start.15 = (bf16[576,512]{1,0:T(8,128)(2,1)S(1)}, bf16[576,512]{1,0:T(8,128)(2,1)S(1)}, u32[]{:S(2)}, u32[]{:S(2)}) collective-permute-start(bf16[576,512]{1,0:T(8,128)(2,1)S(1)} %convert_element_type.82), channel_id=1, source_target_pairs={{0,1},{1,0},{2,3},{3,2},{4,5},{5,4},{6,7},{7,6},{8,9},{9,8},{10,11... | collective-permute-start | bytes 1769480 | tf_op jit(solution)/shard_map/ppermute | solution.py:25

commit v4 on v3

--- a/solution.py
+++ b/solution.py
@@ -49,16 +49,29 @@
     return jnp.max(jnp.where(covered, starts[None, :], 0), axis=1)
 
 
-def attention_kernel(*refs, heads, kv_heads, margin, blocks):
-    lo_ref, q_ref, do_ref = refs[:3]
-    block_refs = refs[3 : 3 + blocks]
+def attention_kernel(*refs, heads, kv_heads, margin, slots, blocks):
+    flag_ref, lo_ref, q_ref, do_ref = refs[:4]
+    block_refs = refs[4 : 4 + blocks]
     kv_ref, dkv_ref = refs[-2:]
-    outs = refs[-3 - blocks : -2]
+    outs = refs[-3 - len(slots) : -2]
     dq_ref = outs[0]
     out_refs = outs[1:]
     block_rows = block_refs[0].shape[0]
-    for index, block_ref in enumerate(block_refs):
-        kv_ref[pl.ds(index * block_rows, block_rows), :] = block_ref[...]
+    flag = flag_ref[0]
+    for index, (when_low, when_high) in enumerate(slots):
+        target = kv_ref.at[pl.ds(index * block_rows, block_rows), :]
+        if when_low == when_high:
+            target[...] = block_refs[when_low][...]
+        else:
+
+            @pl.when(flag == 0)
+            def _():
+                target[...] = block_refs[when_low][...]
+
+            @pl.when(flag != 0)
+            def _():
+                target[...] = block_refs[when_high][...]
+
     rows = q_ref.shape[0]
     keys = kv_ref.shape[0]
     scale = HEAD_DIM ** (-0.5)
@@ -100,23 +113,29 @@
         out_ref[...] = dkv_ref[pl.ds(index * block_rows, block_rows), :]
 
 
-def attention(lo_rel, queries, grads, kv_blocks, heads, kv_heads, margin, early):
+def attention(flag, lo_rel, queries, grads, kv_blocks, slots, heads, kv_heads, margin, early):
     rows, width = queries.shape
     blocks = len(kv_blocks)
     block_rows, kv_cols = kv_blocks[0].shape
-    keys = blocks * block_rows
+    keys = len(slots) * block_rows
     kernel = functools.partial(
-        attention_kernel, heads=heads, kv_heads=kv_heads, margin=margin, blocks=blocks
+        attention_kernel,
+        heads=heads,
+        kv_heads=kv_heads,
+        margin=margin,
+        slots=tuple(slots),
+        blocks=blocks,
     )
     vmem = pl.BlockSpec(memory_space=pltpu.VMEM)
+    smem = pl.BlockSpec(memory_space=pltpu.SMEM)
     flops = 2 * 5 * heads * rows * keys * HEAD_DIM
     moved = 2 * (2 * rows * width + keys * kv_cols + rows * width) + 4 * keys * kv_cols
     return pl.pallas_call(
         kernel,
         out_shape=(jax.ShapeDtypeStruct((rows, width), jnp.bfloat16),)
-        + tuple(jax.ShapeDtypeStruct((block_rows, kv_cols), jnp.float32) for _ in kv_blocks),
-        in_specs=[vmem] * (3 + blocks) + [pl.BlockSpec(memory_space=pl.ANY)] * len(early),
-        out_specs=(vmem,) * (1 + blocks),
+        + tuple(jax.ShapeDtypeStruct((block_rows, kv_cols), jnp.float32) for _ in slots),
+        in_specs=[smem] + [vmem] * (3 + blocks) + [pl.BlockSpec(memory_space=pl.ANY)] * len(early),
+        out_specs=(vmem,) * (1 + len(slots)),
         scratch_shapes=[
             pltpu.VMEM((keys, kv_cols), kv_blocks[0].dtype),
             pltpu.VMEM((keys, kv_cols), jnp.float32),
@@ -124,7 +143,7 @@
         cost_estimate=pl.CostEstimate(
             flops=flops, transcendentals=heads * rows * keys, bytes_accessed=moved
         ),
-    )(lo_rel, queries, grads, *kv_blocks, *early)
+    )(flag, lo_rel, queries, grads, *kv_blocks, *early)
 
 
 def body(layer_input, query_heads, key_heads, value_heads, grad_out, doc_starts):
@@ -149,26 +168,55 @@
         inputs.append(rotated(outgoing, "fsdp", steps))
 
     own_kv = jnp.concatenate([key_heads[0], value_heads[0]], axis=1)
-    arrived = []
-    moving = own_kv
-    for _ in range(reach):
-        moving = passed_along(moving, RING, 1)
-        arrived.append(moving)
     query_pos = first_row + jnp.arange(block_rows, dtype=jnp.int32)
     lowest = jnp.maximum(doc_start_of(doc_starts[0], query_pos), query_pos - window + 1)
     lo_rel = (lowest - first_row + margin).astype(jnp.int32)[:, None]
+    sub_count = lax.axis_size("sub")
+    sub_at = lax.axis_index("sub")
+    flag = jnp.reshape(sub_at, (1,)).astype(jnp.int32)
+    chip_route = sub_count == 2 and reach == 3
+    if chip_route:
+        ring_count = lax.axis_size(RING)
+        across = [(2 * chip + 1, 2 * chip + 2) for chip in range(ring_count // 2 - 1)]
+        two_back = passed_along(own_kv, "ctx", 1)
+        one_back_high = passed_along(own_kv, "sub", 1)
+        three_back_low = lax.ppermute(two_back, RING, across)
+        swapped = rotated(two_back, "sub", 1)
+        kv_blocks = [two_back, one_back_high, three_back_low, swapped, own_kv]
+        slots = [(2, 3), (0, 0), (3, 1), (4, 4)]
+    else:
+        arrived = []
+        moving = own_kv
+        for _ in range(reach):
+            moving = passed_along(moving, RING, 1)
+            arrived.append(moving)
+        kv_blocks = arrived[::-1] + [own_kv]
+        slots = [(index, index) for index in range(reach + 1)]
     grad_q, *grad_pieces = attention(
-        lo_rel, query_heads[0], grad_out[0], arrived[::-1] + [own_kv], heads, kv_heads, margin,
+        flag, lo_rel, query_heads[0], grad_out[0], kv_blocks, slots, heads, kv_heads, margin,
         inputs[1:],
     )
 
-    def own_piece(distance):
-        return grad_pieces[reach - distance]
-
-    total = own_piece(reach)
-    for distance in range(reach - 1, -1, -1):
-        moved = passed_along(total.astype(jnp.bfloat16), RING, -1).astype(jnp.float32)
-        total = moved + own_piece(distance)
+    def low(value):
+        return value.astype(jnp.bfloat16)
+
+    if chip_route:
+        back = [(target, source) for source, target in across]
+        g3, g2, g1, g0 = grad_pieces
+        from_next_chip = lax.ppermute(low(g3), RING, back).astype(jnp.float32)
+        from_mate = rotated(low(jnp.where(sub_at == 0, g1, g3)), "sub", 1).astype(jnp.float32)
+        from_high = passed_along(low(g1), "sub", -1).astype(jnp.float32)
+        two_back_sum = g2 + from_mate + from_next_chip
+        total = g0 + from_high + passed_along(low(two_back_sum), "ctx", -1).astype(jnp.float32)
+    else:
+
+        def own_piece(distance):
+            return grad_pieces[reach - distance]
+
+        total = own_piece(reach)
+        for distance in range(reach - 1, -1, -1):
+            moved = passed_along(low(total), RING, -1).astype(jnp.float32)
+            total = moved + own_piece(distance)
     grad_kv = total.astype(jnp.bfloat16)
     grad_key = grad_kv[:, :kv_width]
     grad_value = grad_kv[:, kv_width:]

time: 125 us -> 116 us (0.928)
  starting transfers between devices: 44.5 us -> 35.9 us
    ppermute x6 -> x4, starting transfers between devices: 23.3 us -> 8.99 us  [passed_along(): lax.ppermute(value, axis, [(source, source + steps) for source in range(f...]
    ppermute x10 -> x12, starting transfers between devices: 21.2 us -> 24.8 us  [rotated(): lax.ppermute(value, axis, [(source, (source + steps) % count) for source...]
    ppermute x10 -> x12, waiting for transfers between devices: 31.1 us -> 28.8 us  [rotated(): lax.ppermute(value, axis, [(source, (source + steps) % count) for source...]
    ppermute x0 -> x2, starting transfers between devices: none -> 2.16 us  [the longest x1 1.47 us: body(): three_back_low = lax.ppermute(two_back, RING, across)]
    ppermute x6 -> x4, waiting for transfers between devices: 25.4 us -> 27.2 us  [passed_along(): lax.ppermute(value, axis, [(source, source + steps) for source in range(f...]
  transfers between devices with their start and end apart: 16 -> 18, of which waited for: 12 -> 11; matrix products, arithmetic and copies ran while one was open for 2% -> 2% of each run, Pallas kernels for 0% -> 0%
where the time goes in v4:
time: 116 us; the launch traced here: 115 us
  waiting for transfers between devices  55.9 us (48%)
  starting transfers between devices  35.9 us (31%)
  Pallas kernels  8.94 us (8%)
  other arithmetic  7.58 us (7%)
  local copies, waits for them, and re-layouts  4.45 us (4%)
    ppermute x12, waiting for transfers between devices, rotated(): lax.ppermute(value, axis, [(source, (source + steps) % count) for source...  28.8 us
    ppermute x4, waiting for transfers between devices, passed_along(): lax.ppermute(value, axis, [(source, source + steps) for source in range(f...  27.2 us
    ppermute x12, starting transfers between devices, rotated(): lax.ppermute(value, axis, [(source, (source + steps) % count) for source...  24.8 us
    ppermute x4, starting transfers between devices, passed_along(): lax.ppermute(value, axis, [(source, source + steps) for source in range(f...  8.99 us
    pallas_call x1, Pallas kernels, attention(): pl.pallas_call(kernel, out_shape=(jax.ShapeDtypeStruct((rows, width), jnp...  8.94 us
  transfers between devices with their start and end apart: 18, of which 11 were waited for; matrix products, arithmetic and copies ran while one was open for 2% of the time, Pallas kernels for 0%

profile of v4, /device:TPU:0, one launch (start us, length us, event | category | flops | bytes accessed | tf_op | source)
XLA Modules:
  0.0 114.6 jit_solution(10126452843135047760)
XLA Ops:
  0.6 1.1 pad_maximum_fusion.refs_8_
  1.7 5.0 %collective-permute-start = (bf16[256,1024]{1,0:T(8,128)(2,1)S(1)}, bf16[256,1024]{1,0:T(8,128)(2,1)S(1)}, u32[]{:S(2)}, u32[]{:S(2)}) collective-permute-start(bf16[256,1024]{1,0:T(8,128)(2,1)S(1)} %pad_maximum_fusion.refs_8_), channel_id=1, source_target_pairs={{0,4},{4,8},{8,12},{1,5},{5,9},{9,13},{2,6},{6,10},{10,14},{3,7},{... | collective-permute-start | bytes 1572872 | tf_op jit(solution)/shard_map/ppermute | solution.py:20
  6.7 0.0 copy-start.5
  6.7 1.3 %dynamic-slice_bitcast_fusion = (bf16[256,1152]{1,0:T(8,128)(2,1)S(1)}, bf16[256,1152]{1,0:T(8,128)(2,1)S(1)}) fusion(bf16[1,256,2304]{2,1,0:T(8,128)(2,1)} %param.6, s32[]{:T(128)S(6)} %select_n.99, s32[]{:T(128)S(6)} %select_n.95), kind=kLoop, calls=%fused_computation.12 | loop fusion | bytes 2359304 | tf_op jit(solution)/shard_map/dynamic_slice | solution.py:164
  8.1 1.6 %collective-permute-start.4 = (bf16[256,1152]{1,0:T(8,128)(2,1)S(1)}, bf16[256,1152]{1,0:T(8,128)(2,1)S(1)}, u32[]{:S(2)}, u32[]{:S(2)}) collective-permute-start(bf16[256,1152]{1,0:T(8,128)(2,1)S(1)} %get-tuple-element.22), channel_id=1, source_target_pairs={{0,2},{2,0},{1,3},{3,1},{4,6},{6,4},{5,7},{7,5},{8,10},{10,8},{9,1... | collective-permute-start | bytes 1769480 | tf_op jit(solution)/shard_map/ppermute | solution.py:25
  9.6 1.3 %collective-permute-start.1 = (bf16[256,1024]{1,0:T(8,128)(2,1)S(1)}, bf16[256,1024]{1,0:T(8,128)(2,1)S(1)}, u32[]{:S(2)}, u32[]{:S(2)}) collective-permute-start(bf16[256,1024]{1,0:T(8,128)(2,1)S(1)} %pad_maximum_fusion.refs_8_), channel_id=1, source_target_pairs={{0,1},{2,3},{4,5},{6,7},{8,9},{10,11},{12,13},{14,15},{16,17},{18,... | collective-permute-start | bytes 1572872 | tf_op jit(solution)/shard_map/ppermute | solution.py:20
  10.9 6.9 %collective-permute-done.refs_4_ = bf16[256,1024]{1,0:T(8,128)(2,1)S(1)} collective-permute-done((bf16[256,1024]{1,0:T(8,128)(2,1)S(1)}, bf16[256,1024]{1,0:T(8,128)(2,1)S(1)}, u32[]{:S(2)}, u32[]{:S(2)}) %collective-permute-start) | collective-permute-done | bytes 524320 | tf_op jit(solution)/shard_map/ppermute | solution.py:20
  17.8 1.5 %collective-permute-start.2 = (bf16[256,1024]{1,0:T(8,128)(2,1)S(1)}, bf16[256,1024]{1,0:T(8,128)(2,1)}, u32[]{:S(2)}, u32[]{:S(2)}) collective-permute-start(bf16[256,1024]{1,0:T(8,128)(2,1)S(1)} %collective-permute-done.refs_4_), channel_id=1, source_target_pairs={{1,4},{5,8},{9,12},{3,6},{7,10},{11,14},{17,20},{21,24},{25,28},{1... | collective-permute-start | bytes 1572872 | tf_op jit(solution)/shard_map/ppermute | solution.py:183
  19.3 3.8 %collective-permute-start.3 = (bf16[256,1024]{1,0:T(8,128)(2,1)S(1)}, bf16[256,1024]{1,0:T(8,128)(2,1)}, u32[]{:S(2)}, u32[]{:S(2)}) collective-permute-start(bf16[256,1024]{1,0:T(8,128)(2,1)S(1)} %collective-permute-done.refs_4_), channel_id=1, source_target_pairs={{0,1},{1,0},{2,3},{3,2},{4,5},{5,4},{6,7},{7,6},{8,9},{9,8},{10,11... | collective-permute-start | bytes 1572872 | tf_op jit(solution)/shard_map/ppermute | solution.py:25
  23.1 0.0 copy-done.5
  23.2 0.1 select_reduce_fusion
  23.2 0.1 copy.13
  23.4 0.7 subtract_add_fusion.refs_1_
  24.1 0.0 collective-permute-done.1.refs_5_
  24.1 0.0 collective-permute-done.4.refs_9_
  24.1 0.0 collective-permute-done.2.refs_6_
  24.1 0.7 collective-permute-done.3.refs_7_
  24.8 0.1 copy-done.9
  24.9 0.2 copy-done.6
  25.1 8.9 %shard_map.93 = (bf16[256,1024]{1,0:T(8,128)(2,1)}, f32[256,1024]{1,0:T(8,128)}, f32[256,1024]{1,0:T(8,128)}, f32[256,1024]{1,0:T(8,128)}, f32[256,1024]{1,0:T(8,128)}) custom-call(s32[1]{0:T(128)} %bitcast.refs_0_, s32[256,1]{1,0:T(8,128)} %subtract_add_fusion.refs_1_, bf16[256,1024]{1,0:T(8,128)(2,1)} %bitcast.20, bf16[256,1024]{1,0:T(8,128)(2,1)} %bitcast.21, ...), custom_call_target="tpu_custom_call" | custom-call | flops 2684354560 | bytes 7864320 | tf_op jit(solution)/shard_map/pallas_call | solution.py:133
  34.0 1.4 %convert_element_type.73 = bf16[256,1024]{1,0:T(8,128)(2,1)S(1)} convert(f32[256,1024]{1,0:T(8,128)} %get-tuple-element.13) | non-fusion elementwise | flops 262144 | bytes 1572864 | tf_op jit(solution)/shard_map/convert_element_type | solution.py:201
  35.4 0.1 copy-done
  35.6 0.1 select_convert_fusion
  35.7 4.7 %collective-permute-start.6 = (bf16[256,1024]{1,0:T(8,128)(2,1)S(1)}, bf16[256,1024]{1,0:T(8,128)(2,1)S(1)}, u32[]{:S(2)}, u32[]{:S(2)}) collective-permute-start(bf16[256,1024]{1,0:T(8,128)(2,1)S(1)} %select_convert_fusion), channel_id=1, source_target_pairs={{0,1},{1,0},{2,3},{3,2},{4,5},{5,4},{6,7},{7,6},{8,9},{9,8},{10,11... | collective-permute-start | bytes 1572872 | tf_op jit(solution)/shard_map/ppermute | solution.py:25
  40.4 0.7 collective-permute-start.7
  41.1 0.1 convert_element_type.69
  41.1 1.3 %collective-permute-start.5 = (bf16[256,1024]{1,0:T(8,128)(2,1)S(1)}, bf16[256,1024]{1,0:T(8,128)(2,1)S(1)}, u32[]{:S(2)}, u32[]{:S(2)}) collective-permute-start(bf16[256,1024]{1,0:T(8,128)(2,1)S(1)} %convert_element_type.69), channel_id=1, source_target_pairs={{1,0},{3,2},{5,4},{7,6},{9,8},{11,10},{13,12},{15,14},{17,16},{19,... | collective-permute-start | bytes 1572872 | tf_op jit(solution)/shard_map/ppermute | solution.py:20
  42.4 0.0 collective-permute-done.6
  42.4 0.0 collective-permute-done.7
  42.5 0.2 add_convert_fusion.1
  42.7 1.4 %collective-permute-start.8 = (bf16[256,1024]{1,0:T(8,128)(2,1)S(1)}, bf16[256,1024]{1,0:T(8,128)(2,1)S(1)}, u32[]{:S(2)}, u32[]{:S(2)}) collective-permute-start(bf16[256,1024]{1,0:T(8,128)(2,1)S(1)} %add_convert_fusion.1), channel_id=1, source_target_pairs={{4,0},{8,4},{12,8},{5,1},{9,5},{13,9},{6,2},{10,6},{14,10},{7,3},{... | collective-permute-start | bytes 1572872 | tf_op jit(solution)/shard_map/ppermute | solution.py:20
  44.2 0.8 collective-permute-done.5
  44.9 19.5 %collective-permute-done.8 = bf16[256,1024]{1,0:T(8,128)(2,1)S(1)} collective-permute-done((bf16[256,1024]{1,0:T(8,128)(2,1)S(1)}, bf16[256,1024]{1,0:T(8,128)(2,1)S(1)}, u32[]{:S(2)}, u32[]{:S(2)}) %collective-permute-start.8) | collective-permute-done | bytes 524320 | tf_op jit(solution)/shard_map/ppermute | solution.py:20
  64.4 0.2 add_convert_fusion
  64.7 0.9 fusion.10
  65.5 1.5 %collective-permute-start.9 = (bf16[256,512]{1,0:T(8,128)(2,1)S(1)}, bf16[256,512]{1,0:T(8,128)(2,1)S(1)}, u32[]{:S(2)}, u32[]{:S(2)}) collective-permute-start(bf16[256,512]{1,0:T(8,128)(2,1)S(1)} %get-tuple-element.23), channel_id=1, source_target_pairs={{0,2},{2,0},{1,3},{3,1},{4,6},{6,4},{5,7},{7,5},{8,10},{10,8},{9,1... | collective-permute-start | bytes 786440 | tf_op jit(solution)/shard_map/ppermute | solution.py:25
  67.0 7.5 %collective-permute-done.9 = bf16[256,512]{1,0:T(8,128)(2,1)S(1)} collective-permute-done((bf16[256,512]{1,0:T(8,128)(2,1)S(1)}, bf16[256,512]{1,0:T(8,128)(2,1)S(1)}, u32[]{:S(2)}, u32[]{:S(2)}) %collective-permute-start.9) | collective-permute-done | bytes 262176 | tf_op jit(solution)/shard_map/ppermute | solution.py:25
  74.5 0.8 fusion
  75.3 0.0 copy-start.1
  75.3 1.4 %copy-done.1 = f32[1152,512]{1,0:T(8,128)} copy-done((f32[1152,512]{1,0:T(8,128)}, f32[1152,512]{1,0:T(8,128)S(1)}, u32[]{:S(2)}) %copy-start.1) | copy-done | bytes 2359320
  76.7 0.1 dynamic-slice_convert_fusion
  76.8 0.2 collective-permute-start.10
  77.0 1.9 %collective-permute-done.10 = bf16[576,512]{1,0:T(8,128)(2,1)S(1)} collective-permute-done((bf16[576,512]{1,0:T(8,128)(2,1)S(1)}, bf16[576,512]{1,0:T(8,128)(2,1)S(1)}, u32[]{:S(2)}, u32[]{:S(2)}) %collective-permute-start.10) | collective-permute-done | bytes 589856 | tf_op jit(solution)/shard_map/ppermute | solution.py:25
  78.9 1.4 %convert_add_fusion = f32[576,512]{1,0:T(8,128)S(1)} fusion(bf16[576,512]{1,0:T(8,128)(2,1)S(1)} %collective-permute-done.10, f32[1152,512]{1,0:T(8,128)} %copy-done.1, s32[]{:T(128)S(6)} %select_n.100), kind=kLoop, calls=%fused_computation.7 | loop fusion | flops 589824 | bytes 2949124 | tf_op jit(solution)/shard_map/add | solution.py:238
  80.3 0.1 dynamic-slice_convert_fusion.3
  80.4 2.5 %collective-permute-start.11 = (bf16[144,512]{1,0:T(8,128)(2,1)S(1)}, bf16[144,512]{1,0:T(8,128)(2,1)S(1)}, u32[]{:S(2)}, u32[]{:S(2)}) collective-permute-start(bf16[144,512]{1,0:T(8,128)(2,1)S(1)} %get-tuple-element.18), channel_id=1, source_target_pairs={{0,4},{4,8},{8,12},{12,0},{1,5},{5,9},{9,13},{13,1},{2,6},{6,10},{... | collective-permute-start | bytes 442376 | tf_op jit(solution)/shard_map/ppermute | solution.py:25
  82.9 1.2 %collective-permute-start.12 = (bf16[144,512]{1,0:T(8,128)(2,1)S(1)}, bf16[144,512]{1,0:T(8,128)(2,1)S(1)}, u32[]{:S(2)}, u32[]{:S(2)}) collective-permute-start(bf16[144,512]{1,0:T(8,128)(2,1)S(1)} %get-tuple-element.20), channel_id=1, source_target_pairs={{0,8},{4,12},{8,0},{12,4},{1,9},{5,13},{9,1},{13,5},{2,10},{6,14},... | collective-permute-start | bytes 442376 | tf_op jit(solution)/shard_map/ppermute | solution.py:25
  84.2 2.8 %collective-permute-start.13 = (bf16[144,512]{1,0:T(8,128)(2,1)S(1)}, bf16[144,512]{1,0:T(8,128)(2,1)S(1)}, u32[]{:S(2)}, u32[]{:S(2)}) collective-permute-start(bf16[144,512]{1,0:T(8,128)(2,1)S(1)} %get-tuple-element.19), channel_id=1, source_target_pairs={{0,12},{4,0},{8,4},{12,8},{1,13},{5,1},{9,5},{13,9},{2,14},{6,2},{... | collective-permute-start | bytes 442376 | tf_op jit(solution)/shard_map/ppermute | solution.py:25
  87.0 1.9 %collective-permute-done.11 = bf16[144,512]{1,0:T(8,128)(2,1)S(1)} collective-permute-done((bf16[144,512]{1,0:T(8,128)(2,1)S(1)}, bf16[144,512]{1,0:T(8,128)(2,1)S(1)}, u32[]{:S(2)}, u32[]{:S(2)}) %collective-permute-start.11) | collective-permute-done | bytes 147488 | tf_op jit(solution)/shard_map/ppermute | solution.py:25
  88.9 5.7 %collective-permute-done.12 = bf16[144,512]{1,0:T(8,128)(2,1)S(1)} collective-permute-done((bf16[144,512]{1,0:T(8,128)(2,1)S(1)}, bf16[144,512]{1,0:T(8,128)(2,1)S(1)}, u32[]{:S(2)}, u32[]{:S(2)}) %collective-permute-start.12) | collective-permute-done | bytes 147488 | tf_op jit(solution)/shard_map/ppermute | solution.py:25
  94.6 0.0 collective-permute-done.13
  94.6 0.1 broadcast_in_dim.28
  94.7 0.1 fusion.7
  94.8 3.7 %collective-permute-start.14 = (bf16[144,512]{1,0:T(8,128)(2,1)S(1)}, bf16[144,512]{1,0:T(8,128)(2,1)S(1)}, u32[]{:S(2)}, u32[]{:S(2)}) collective-permute-start(bf16[144,512]{1,0:T(8,128)(2,1)S(1)} %get-tuple-element.16), channel_id=1, source_target_pairs={{0,4},{4,8},{8,12},{12,0},{1,5},{5,9},{9,13},{13,1},{2,6},{6,10},{... | collective-permute-start | bytes 442376 | tf_op jit(solution)/shard_map/ppermute | solution.py:25
  98.5 2.7 %collective-permute-start.15 = (bf16[144,512]{1,0:T(8,128)(2,1)S(1)}, bf16[144,512]{1,0:T(8,128)(2,1)S(1)}, u32[]{:S(2)}, u32[]{:S(2)}) collective-permute-start(bf16[144,512]{1,0:T(8,128)(2,1)S(1)} %get-tuple-element.16), channel_id=1, source_target_pairs={{0,8},{4,12},{8,0},{12,4},{1,9},{5,13},{9,1},{13,5},{2,10},{6,14},... | collective-permute-start | bytes 442376 | tf_op jit(solution)/shard_map/ppermute | solution.py:25
  101.2 0.0 collective-permute-start.16
  101.2 4.3 %collective-permute-done.14 = bf16[144,512]{1,0:T(8,128)(2,1)S(1)} collective-permute-done((bf16[144,512]{1,0:T(8,128)(2,1)S(1)}, bf16[144,512]{1,0:T(8,128)(2,1)S(1)}, u32[]{:S(2)}, u32[]{:S(2)}) %collective-permute-start.14) | collective-permute-done | bytes 147488 | tf_op jit(solution)/shard_map/ppermute | solution.py:25
  105.5 4.9 %collective-permute-done.15 = bf16[144,512]{1,0:T(8,128)(2,1)S(1)} collective-permute-done((bf16[144,512]{1,0:T(8,128)(2,1)S(1)}, bf16[144,512]{1,0:T(8,128)(2,1)S(1)}, u32[]{:S(2)}, u32[]{:S(2)}) %collective-permute-start.15) | collective-permute-done | bytes 147488 | tf_op jit(solution)/shard_map/ppermute | solution.py:25
  110.4 0.0 collective-permute-done.16
  110.4 0.1 convert_element_type.90
  110.5 0.1 collective-permute-start.17
  110.6 2.0 %collective-permute-done.17 = bf16[576,512]{1,0:T(8,128)(2,1)S(1)} collective-permute-done((bf16[576,512]{1,0:T(8,128)(2,1)S(1)}, bf16[576,512]{1,0:T(8,128)(2,1)S(1)}, u32[]{:S(2)}, u32[]{:S(2)}) %collective-permute-start.17) | collective-permute-done | bytes 589856 | tf_op jit(solution)/shard_map/ppermute | solution.py:25
  112.6 0.3 convert_select_fusion.1
  112.9 1.7 %maximum_multiply_fusion = f32[1152,512]{1,0:T(8,128)} fusion(f32[576,512]{1,0:T(8,128)S(1)} %get-tuple-element.15, f32[576,512]{1,0:T(8,128)S(1)} %get-tuple-element.14), kind=kLoop, calls=%fused_computation | loop fusion | flops 1179648 | bytes 4718592 | tf_op jit(solution)/shard_map/mul | solution.py:252
  (17 shorter events, 0.1 us)
Async XLA Ops:
  1.7 7.9 %copy-start.4 = (bf16[256,1024]{1,0:T(8,128)(2,1)}, bf16[256,1024]{1,0:T(8,128)(2,1)S(1)}, u32[]{:S(2)}) copy-start(bf16[256,1024]{1,0:T(8,128)(2,1)S(1)} %pad_maximum_fusion.refs_8_) | copy-start | bytes 1572868
  1.7 16.1 %collective-permute-start = (bf16[256,1024]{1,0:T(8,128)(2,1)S(1)}, bf16[256,1024]{1,0:T(8,128)(2,1)S(1)}, u32[]{:S(2)}, u32[]{:S(2)}) collective-permute-start(bf16[256,1024]{1,0:T(8,128)(2,1)S(1)} %pad_maximum_fusion.refs_8_), channel_id=1, source_target_pairs={{0,4},{4,8},{8,12},{1,5},{5,9},{9,13},{2,6},{6,10},{10,14},{3,7},{... | collective-permute-start | bytes 1572872 | tf_op jit(solution)/shard_map/ppermute | solution.py:20
  6.7 16.4 %copy-start.5 = (s32[1,12]{1,0:T(1,128)S(1)}, s32[1,12]{1,0:T(1,128)}, u32[]{:S(2)}) copy-start(s32[1,12]{1,0:T(1,128)} %param.11) | copy-start | bytes 148
  8.1 16.0 %collective-permute-start.4 = (bf16[256,1152]{1,0:T(8,128)(2,1)S(1)}, bf16[256,1152]{1,0:T(8,128)(2,1)S(1)}, u32[]{:S(2)}, u32[]{:S(2)}) collective-permute-start(bf16[256,1152]{1,0:T(8,128)(2,1)S(1)} %get-tuple-element.22), channel_id=1, source_target_pairs={{0,2},{2,0},{1,3},{3,1},{4,6},{6,4},{5,7},{7,5},{8,10},{10,8},{9,1... | collective-permute-start | bytes 1769480 | tf_op jit(solution)/shard_map/ppermute | solution.py:25
  9.6 14.5 %collective-permute-start.1 = (bf16[256,1024]{1,0:T(8,128)(2,1)S(1)}, bf16[256,1024]{1,0:T(8,128)(2,1)S(1)}, u32[]{:S(2)}, u32[]{:S(2)}) collective-permute-start(bf16[256,1024]{1,0:T(8,128)(2,1)S(1)} %pad_maximum_fusion.refs_8_), channel_id=1, source_target_pairs={{0,1},{2,3},{4,5},{6,7},{8,9},{10,11},{12,13},{14,15},{16,17},{18,... | collective-permute-start | bytes 1572872 | tf_op jit(solution)/shard_map/ppermute | solution.py:20
  17.8 7.0 %copy-start.8 = (bf16[256,1024]{1,0:T(8,128)(2,1)}, bf16[256,1024]{1,0:T(8,128)(2,1)S(1)}, u32[]{:S(2)}) copy-start(bf16[256,1024]{1,0:T(8,128)(2,1)S(1)} %collective-permute-done.refs_4_) | copy-start | bytes 1572868
  17.8 6.3 %collective-permute-start.2 = (bf16[256,1024]{1,0:T(8,128)(2,1)S(1)}, bf16[256,1024]{1,0:T(8,128)(2,1)}, u32[]{:S(2)}, u32[]{:S(2)}) collective-permute-start(bf16[256,1024]{1,0:T(8,128)(2,1)S(1)} %collective-permute-done.refs_4_), channel_id=1, source_target_pairs={{1,4},{5,8},{9,12},{3,6},{7,10},{11,14},{17,20},{21,24},{25,28},{1... | collective-permute-start | bytes 1572872 | tf_op jit(solution)/shard_map/ppermute | solution.py:183
  19.3 5.5 %collective-permute-start.3 = (bf16[256,1024]{1,0:T(8,128)(2,1)S(1)}, bf16[256,1024]{1,0:T(8,128)(2,1)}, u32[]{:S(2)}, u32[]{:S(2)}) collective-permute-start(bf16[256,1024]{1,0:T(8,128)(2,1)S(1)} %collective-permute-done.refs_4_), channel_id=1, source_target_pairs={{0,1},{1,0},{2,3},{3,2},{4,5},{5,4},{6,7},{7,6},{8,9},{9,8},{10,11... | collective-permute-start | bytes 1572872 | tf_op jit(solution)/shard_map/ppermute | solution.py:25
  24.1 0.8 copy-start.9
  24.1 1.0 copy-start.6
  34.0 1.5 %copy-start = (f32[256,1024]{1,0:T(8,128)S(1)}, f32[256,1024]{1,0:T(8,128)}, u32[]{:S(2)}) copy-start(f32[256,1024]{1,0:T(8,128)} %get-tuple-element.11) | copy-start | bytes 3145732
  35.7 6.8 %copy-start.3 = (f32[256,1024]{1,0:T(8,128)S(1)}, f32[256,1024]{1,0:T(8,128)}, u32[]{:S(2)}) copy-start(f32[256,1024]{1,0:T(8,128)} %get-tuple-element.12) | copy-start | bytes 3145732
  35.7 6.7 %collective-permute-start.6 = (bf16[256,1024]{1,0:T(8,128)(2,1)S(1)}, bf16[256,1024]{1,0:T(8,128)(2,1)S(1)}, u32[]{:S(2)}, u32[]{:S(2)}) collective-permute-start(bf16[256,1024]{1,0:T(8,128)(2,1)S(1)} %select_convert_fusion), channel_id=1, source_target_pairs={{0,1},{1,0},{2,3},{3,2},{4,5},{5,4},{6,7},{7,6},{8,9},{9,8},{10,11... | collective-permute-start | bytes 1572872 | tf_op jit(solution)/shard_map/ppermute | solution.py:25
  40.4 2.1 %collective-permute-start.7 = (bf16[256,1024]{1,0:T(8,128)(2,1)S(1)}, bf16[256,1024]{1,0:T(8,128)(2,1)S(1)}, u32[]{:S(2)}, u32[]{:S(2)}) collective-permute-start(bf16[256,1024]{1,0:T(8,128)(2,1)S(1)} %convert_element_type.73), channel_id=1, source_target_pairs={{4,1},{8,5},{12,9},{6,3},{10,7},{14,11},{20,17},{24,21},{28,25},{2... | collective-permute-start | bytes 1572872 | tf_op jit(solution)/shard_map/ppermute | solution.py:206
  41.1 3.8 %collective-permute-start.5 = (bf16[256,1024]{1,0:T(8,128)(2,1)S(1)}, bf16[256,1024]{1,0:T(8,128)(2,1)S(1)}, u32[]{:S(2)}, u32[]{:S(2)}) collective-permute-start(bf16[256,1024]{1,0:T(8,128)(2,1)S(1)} %convert_element_type.69), channel_id=1, source_target_pairs={{1,0},{3,2},{5,4},{7,6},{9,8},{11,10},{13,12},{15,14},{17,16},{19,... | collective-permute-start | bytes 1572872 | tf_op jit(solution)/shard_map/ppermute | solution.py:20
  42.5 22.0 %copy-start.2 = (f32[256,1024]{1,0:T(8,128)S(1)}, f32[256,1024]{1,0:T(8,128)}, u32[]{:S(2)}) copy-start(f32[256,1024]{1,0:T(8,128)} %get-tuple-element.10) | copy-start | bytes 3145732
  42.7 21.7 %collective-permute-start.8 = (bf16[256,1024]{1,0:T(8,128)(2,1)S(1)}, bf16[256,1024]{1,0:T(8,128)(2,1)S(1)}, u32[]{:S(2)}, u32[]{:S(2)}) collective-permute-start(bf16[256,1024]{1,0:T(8,128)(2,1)S(1)} %add_convert_fusion.1), channel_id=1, source_target_pairs={{4,0},{8,4},{12,8},{5,1},{9,5},{13,9},{6,2},{10,6},{14,10},{7,3},{... | collective-permute-start | bytes 1572872 | tf_op jit(solution)/shard_map/ppermute | solution.py:20
  64.7 9.8 %copy-start.7 = (bf16[256,1152]{1,0:T(8,128)(2,1)S(1)}, bf16[256,1152]{1,0:T(8,128)(2,1)}, u32[]{:S(2)}) copy-start(bf16[256,1152]{1,0:T(8,128)(2,1)} %copy-done.6) | copy-start | bytes 1769476
  65.5 9.0 %collective-permute-start.9 = (bf16[256,512]{1,0:T(8,128)(2,1)S(1)}, bf16[256,512]{1,0:T(8,128)(2,1)S(1)}, u32[]{:S(2)}, u32[]{:S(2)}) collective-permute-start(bf16[256,512]{1,0:T(8,128)(2,1)S(1)} %get-tuple-element.23), channel_id=1, source_target_pairs={{0,2},{2,0},{1,3},{3,1},{4,6},{6,4},{5,7},{7,5},{8,10},{10,8},{9,1... | collective-permute-start | bytes 786440 | tf_op jit(solution)/shard_map/ppermute | solution.py:25
  75.3 1.4 %copy-start.1 = (f32[1152,512]{1,0:T(8,128)}, f32[1152,512]{1,0:T(8,128)S(1)}, u32[]{:S(2)}) copy-start(f32[1152,512]{1,0:T(8,128)S(1)} %fusion) | copy-start | bytes 7077892
  76.8 2.1 %collective-permute-start.10 = (bf16[576,512]{1,0:T(8,128)(2,1)S(1)}, bf16[576,512]{1,0:T(8,128)(2,1)S(1)}, u32[]{:S(2)}, u32[]{:S(2)}) collective-permute-start(bf16[576,512]{1,0:T(8,128)(2,1)S(1)} %dynamic-slice_convert_fusion), channel_id=1, source_target_pairs={{0,1},{1,0},{2,3},{3,2},{4,5},{5,4},{6,7},{7,6},{8,9},{9,8},{10,11... | collective-permute-start | bytes 1769480 | tf_op jit(solution)/shard_map/ppermute | solution.py:25
  80.4 8.5 %collective-permute-start.11 = (bf16[144,512]{1,0:T(8,128)(2,1)S(1)}, bf16[144,512]{1,0:T(8,128)(2,1)S(1)}, u32[]{:S(2)}, u32[]{:S(2)}) collective-permute-start(bf16[144,512]{1,0:T(8,128)(2,1)S(1)} %get-tuple-element.18), channel_id=1, source_target_pairs={{0,4},{4,8},{8,12},{12,0},{1,5},{5,9},{9,13},{13,1},{2,6},{6,10},{... | collective-permute-start | bytes 442376 | tf_op jit(solution)/shard_map/ppermute | solution.py:25
  82.9 11.7 %collective-permute-start.12 = (bf16[144,512]{1,0:T(8,128)(2,1)S(1)}, bf16[144,512]{1,0:T(8,128)(2,1)S(1)}, u32[]{:S(2)}, u32[]{:S(2)}) collective-permute-start(bf16[144,512]{1,0:T(8,128)(2,1)S(1)} %get-tuple-element.20), channel_id=1, source_target_pairs={{0,8},{4,12},{8,0},{12,4},{1,9},{5,13},{9,1},{13,5},{2,10},{6,14},... | collective-permute-start | bytes 442376 | tf_op jit(solution)/shard_map/ppermute | solution.py:25
  84.2 10.4 %collective-permute-start.13 = (bf16[144,512]{1,0:T(8,128)(2,1)S(1)}, bf16[144,512]{1,0:T(8,128)(2,1)S(1)}, u32[]{:S(2)}, u32[]{:S(2)}) collective-permute-start(bf16[144,512]{1,0:T(8,128)(2,1)S(1)} %get-tuple-element.19), channel_id=1, source_target_pairs={{0,12},{4,0},{8,4},{12,8},{1,13},{5,1},{9,5},{13,9},{2,14},{6,2},{... | collective-permute-start | bytes 442376 | tf_op jit(solution)/shard_map/ppermute | solution.py:25
  94.8 10.7 %collective-permute-start.14 = (bf16[144,512]{1,0:T(8,128)(2,1)S(1)}, bf16[144,512]{1,0:T(8,128)(2,1)S(1)}, u32[]{:S(2)}, u32[]{:S(2)}) collective-permute-start(bf16[144,512]{1,0:T(8,128)(2,1)S(1)} %get-tuple-element.16), channel_id=1, source_target_pairs={{0,4},{4,8},{8,12},{12,0},{1,5},{5,9},{9,13},{13,1},{2,6},{6,10},{... | collective-permute-start | bytes 442376 | tf_op jit(solution)/shard_map/ppermute | solution.py:25
  98.5 11.9 %collective-permute-start.15 = (bf16[144,512]{1,0:T(8,128)(2,1)S(1)}, bf16[144,512]{1,0:T(8,128)(2,1)S(1)}, u32[]{:S(2)}, u32[]{:S(2)}) collective-permute-start(bf16[144,512]{1,0:T(8,128)(2,1)S(1)} %get-tuple-element.16), channel_id=1, source_target_pairs={{0,8},{4,12},{8,0},{12,4},{1,9},{5,13},{9,1},{13,5},{2,10},{6,14},... | collective-permute-start | bytes 442376 | tf_op jit(solution)/shard_map/ppermute | solution.py:25
  101.2 9.2 %collective-permute-start.16 = (bf16[144,512]{1,0:T(8,128)(2,1)S(1)}, bf16[144,512]{1,0:T(8,128)(2,1)S(1)}, u32[]{:S(2)}, u32[]{:S(2)}) collective-permute-start(bf16[144,512]{1,0:T(8,128)(2,1)S(1)} %get-tuple-element.16), channel_id=1, source_target_pairs={{0,12},{4,0},{8,4},{12,8},{1,13},{5,1},{9,5},{13,9},{2,14},{6,2},{... | collective-permute-start | bytes 442376 | tf_op jit(solution)/shard_map/ppermute | solution.py:25
  110.5 2.1 %collective-permute-start.17 = (bf16[576,512]{1,0:T(8,128)(2,1)S(1)}, bf16[576,512]{1,0:T(8,128)(2,1)S(1)}, u32[]{:S(2)}, u32[]{:S(2)}) collective-permute-start(bf16[576,512]{1,0:T(8,128)(2,1)S(1)} %convert_element_type.90), channel_id=1, source_target_pairs={{0,1},{1,0},{2,3},{3,2},{4,5},{5,4},{6,7},{7,6},{8,9},{9,8},{10,11... | collective-permute-start | bytes 1769480 | tf_op jit(solution)/shard_map/ppermute | solution.py:25

commit v5 on v4

--- a/solution.py
+++ b/solution.py
@@ -177,10 +177,10 @@
     chip_route = sub_count == 2 and reach == 3
     if chip_route:
         ring_count = lax.axis_size(RING)
-        across = [(2 * chip + 1, 2 * chip + 2) for chip in range(ring_count // 2 - 1)]
+        across = [(2 * chip - 3, 2 * chip) for chip in range(2, ring_count // 2)]
         two_back = passed_along(own_kv, "ctx", 1)
         one_back_high = passed_along(own_kv, "sub", 1)
-        three_back_low = lax.ppermute(two_back, RING, across)
+        three_back_low = lax.ppermute(own_kv, RING, across)
         swapped = rotated(two_back, "sub", 1)
         kv_blocks = [two_back, one_back_high, three_back_low, swapped, own_kv]
         slots = [(2, 3), (0, 0), (3, 1), (4, 4)]
@@ -203,11 +203,12 @@
     if chip_route:
         back = [(target, source) for source, target in across]
         g3, g2, g1, g0 = grad_pieces
-        from_next_chip = lax.ppermute(low(g3), RING, back).astype(jnp.float32)
+        from_far = lax.ppermute(low(g3), RING, back).astype(jnp.float32)
         from_mate = rotated(low(jnp.where(sub_at == 0, g1, g3)), "sub", 1).astype(jnp.float32)
         from_high = passed_along(low(g1), "sub", -1).astype(jnp.float32)
-        two_back_sum = g2 + from_mate + from_next_chip
-        total = g0 + from_high + passed_along(low(two_back_sum), "ctx", -1).astype(jnp.float32)
+        two_back_sum = g2 + from_mate
+        from_next = passed_along(low(two_back_sum), "ctx", -1).astype(jnp.float32)
+        total = g0 + from_high + from_far + from_next
     else:
 
         def own_piece(distance):

time: 116 us -> 115 us (level)
  starting transfers between devices: 35.9 us -> 29.3 us
  waiting for transfers between devices: 55.9 us -> 60.9 us
    ppermute x12, starting transfers between devices: 24.8 us -> 18.1 us  [rotated(): lax.ppermute(value, axis, [(source, (source + steps) % count) for source...]
    ppermute x4, waiting for transfers between devices: 27.2 us -> 30.3 us  [passed_along(): lax.ppermute(value, axis, [(source, source + steps) for source in range(f...]
    ppermute x12, waiting for transfers between devices: 28.8 us -> 30.6 us  [rotated(): lax.ppermute(value, axis, [(source, (source + steps) % count) for source...]
    unnamed x20 -> x22, local copies, waits for them, and re-layouts: 1.85 us -> 2.63 us
  transfers between devices with their start and end apart: 18 -> 18, of which waited for: 11 -> 12; matrix products, arithmetic and copies ran while one was open for 2% -> 2% of each run, Pallas kernels for 0% -> 0%
where the time goes in v5:
time: 115 us; the launch traced here: 114 us
  waiting for transfers between devices  60.9 us (53%)
  starting transfers between devices  29.3 us (25%)
  Pallas kernels  8.93 us (8%)
  other arithmetic  7.6 us (7%)
  local copies, waits for them, and re-layouts  5.23 us (5%)
    ppermute x12, waiting for transfers between devices, rotated(): lax.ppermute(value, axis, [(source, (source + steps) % count) for source...  30.6 us
    ppermute x4, waiting for transfers between devices, passed_along(): lax.ppermute(value, axis, [(source, source + steps) for source in range(f...  30.3 us
    ppermute x12, starting transfers between devices, rotated(): lax.ppermute(value, axis, [(source, (source + steps) % count) for source...  18.1 us
    ppermute x4, starting transfers between devices, passed_along(): lax.ppermute(value, axis, [(source, source + steps) for source in range(f...  8.99 us
    pallas_call x1, Pallas kernels, attention(): pl.pallas_call(kernel, out_shape=(jax.ShapeDtypeStruct((rows, width), jnp...  8.93 us
    unnamed x22, local copies, waits for them, and re-layouts  2.63 us
  transfers between devices with their start and end apart: 18, of which 12 were waited for; matrix products, arithmetic and copies ran while one was open for 2% of the time, Pallas kernels for 0%

profile of v5, /device:TPU:0, one launch (start us, length us, event | category | flops | bytes accessed | tf_op | source)
XLA Modules:
  0.0 113.7 jit_solution(9900811044487203521)
XLA Ops:
  0.6 1.1 pad_maximum_fusion.refs_8_
  1.7 5.0 %collective-permute-start = (bf16[256,1024]{1,0:T(8,128)(2,1)S(1)}, bf16[256,1024]{1,0:T(8,128)(2,1)S(1)}, u32[]{:S(2)}, u32[]{:S(2)}) collective-permute-start(bf16[256,1024]{1,0:T(8,128)(2,1)S(1)} %pad_maximum_fusion.refs_8_), channel_id=1, source_target_pairs={{0,4},{4,8},{8,12},{1,5},{5,9},{9,13},{2,6},{6,10},{10,14},{3,7},{... | collective-permute-start | bytes 1572872 | tf_op jit(solution)/shard_map/ppermute | solution.py:20
  6.7 0.0 copy-start.6
  6.7 1.3 %dynamic-slice_bitcast_fusion = (bf16[256,1152]{1,0:T(8,128)(2,1)S(1)}, bf16[256,1152]{1,0:T(8,128)(2,1)S(1)}) fusion(bf16[1,256,2304]{2,1,0:T(8,128)(2,1)} %param.6, s32[]{:T(128)S(6)} %select_n.99, s32[]{:T(128)S(6)} %select_n.95), kind=kLoop, calls=%fused_computation.12 | loop fusion | bytes 2359304 | tf_op jit(solution)/shard_map/dynamic_slice | solution.py:164
  8.1 1.6 %collective-permute-start.4 = (bf16[256,1152]{1,0:T(8,128)(2,1)S(1)}, bf16[256,1152]{1,0:T(8,128)(2,1)S(1)}, u32[]{:S(2)}, u32[]{:S(2)}) collective-permute-start(bf16[256,1152]{1,0:T(8,128)(2,1)S(1)} %get-tuple-element.22), channel_id=1, source_target_pairs={{0,2},{2,0},{1,3},{3,1},{4,6},{6,4},{5,7},{7,5},{8,10},{10,8},{9,1... | collective-permute-start | bytes 1769480 | tf_op jit(solution)/shard_map/ppermute | solution.py:25
  9.6 1.3 %collective-permute-start.1 = (bf16[256,1024]{1,0:T(8,128)(2,1)S(1)}, bf16[256,1024]{1,0:T(8,128)(2,1)S(1)}, u32[]{:S(2)}, u32[]{:S(2)}) collective-permute-start(bf16[256,1024]{1,0:T(8,128)(2,1)S(1)} %pad_maximum_fusion.refs_8_), channel_id=1, source_target_pairs={{0,1},{2,3},{4,5},{6,7},{8,9},{10,11},{12,13},{14,15},{16,17},{18,... | collective-permute-start | bytes 1572872 | tf_op jit(solution)/shard_map/ppermute | solution.py:20
  11.0 1.5 %collective-permute-start.2 = (bf16[256,1024]{1,0:T(8,128)(2,1)S(1)}, bf16[256,1024]{1,0:T(8,128)(2,1)}, u32[]{:S(2)}, u32[]{:S(2)}) collective-permute-start(bf16[256,1024]{1,0:T(8,128)(2,1)S(1)} %pad_maximum_fusion.refs_8_), channel_id=1, source_target_pairs={{1,8},{5,12},{3,10},{7,14},{17,24},{21,28},{19,26},{23,30}} | collective-permute-start | bytes 1572872 | tf_op jit(solution)/shard_map/ppermute | solution.py:183
  12.4 6.5 %collective-permute-done.refs_4_ = bf16[256,1024]{1,0:T(8,128)(2,1)S(1)} collective-permute-done((bf16[256,1024]{1,0:T(8,128)(2,1)S(1)}, bf16[256,1024]{1,0:T(8,128)(2,1)S(1)}, u32[]{:S(2)}, u32[]{:S(2)}) %collective-permute-start) | collective-permute-done | bytes 524320 | tf_op jit(solution)/shard_map/ppermute | solution.py:20
  19.0 0.0 collective-permute-start.3
  19.0 0.1 select_reduce_fusion
  19.1 0.1 copy.13
  19.2 0.7 subtract_add_fusion.refs_1_
  19.9 0.0 collective-permute-done.1.refs_5_
  19.9 0.0 collective-permute-done.2.refs_6_
  19.9 3.0 %collective-permute-done.4.refs_9_ = bf16[256,1152]{1,0:T(8,128)(2,1)S(1)} collective-permute-done((bf16[256,1152]{1,0:T(8,128)(2,1)S(1)}, bf16[256,1152]{1,0:T(8,128)(2,1)S(1)}, u32[]{:S(2)}, u32[]{:S(2)}) %collective-permute-start.4) | collective-permute-done | bytes 589856 | tf_op jit(solution)/shard_map/ppermute | solution.py:25
  22.9 0.0 collective-permute-done.3.refs_7_
  22.9 0.0 copy-done.10
  22.9 0.8 copy-done.7
  23.7 8.9 %shard_map.93 = (bf16[256,1024]{1,0:T(8,128)(2,1)}, f32[256,1024]{1,0:T(8,128)}, f32[256,1024]{1,0:T(8,128)}, f32[256,1024]{1,0:T(8,128)}, f32[256,1024]{1,0:T(8,128)}) custom-call(s32[1]{0:T(128)} %bitcast.refs_0_, s32[256,1]{1,0:T(8,128)} %subtract_add_fusion.refs_1_, bf16[256,1024]{1,0:T(8,128)(2,1)} %bitcast.20, bf16[256,1024]{1,0:T(8,128)(2,1)} %bitcast.21, ...), custom_call_target="tpu_custom_call" | custom-call | flops 2684354560 | bytes 7864320 | tf_op jit(solution)/shard_map/pallas_call | solution.py:133
  32.7 1.5 %select_convert_fusion = bf16[256,1024]{1,0:T(8,128)(2,1)S(1)} fusion(f32[256,1024]{1,0:T(8,128)} %get-tuple-element.11, f32[256,1024]{1,0:T(8,128)} %get-tuple-element.12, pred[]{:T(512)S(6)} %eq.14), kind=kLoop, calls=%fused_computation.11 | loop fusion | flops 262144 | bytes 2621441 | tf_op jit(solution)/shard_map/convert_element_type | solution.py:201
  34.1 0.0 copy-start
  34.1 0.8 collective-permute-start.7
  34.9 0.1 convert_element_type.69
  35.0 0.4 copy-done
  35.4 0.1 convert_element_type.71
  35.5 1.4 %collective-permute-start.5 = (bf16[256,1024]{1,0:T(8,128)(2,1)S(1)}, bf16[256,1024]{1,0:T(8,128)(2,1)S(1)}, u32[]{:S(2)}, u32[]{:S(2)}) collective-permute-start(bf16[256,1024]{1,0:T(8,128)(2,1)S(1)} %convert_element_type.69), channel_id=1, source_target_pairs={{1,0},{3,2},{5,4},{7,6},{9,8},{11,10},{13,12},{15,14},{17,16},{19,... | collective-permute-start | bytes 1572872 | tf_op jit(solution)/shard_map/ppermute | solution.py:20
  36.9 0.7 collective-permute-start.6
  37.6 0.0 collective-permute-done.7
  37.6 0.2 add_convert_fusion.1
  37.8 1.3 %collective-permute-start.8 = (bf16[256,1024]{1,0:T(8,128)(2,1)S(1)}, bf16[256,1024]{1,0:T(8,128)(2,1)S(1)}, u32[]{:S(2)}, u32[]{:S(2)}) collective-permute-start(bf16[256,1024]{1,0:T(8,128)(2,1)S(1)} %add_convert_fusion.1), channel_id=1, source_target_pairs={{4,0},{8,4},{12,8},{5,1},{9,5},{13,9},{6,2},{10,6},{14,10},{7,3},{... | collective-permute-start | bytes 1572872 | tf_op jit(solution)/shard_map/ppermute | solution.py:20
  39.1 0.3 collective-permute-done.5
  39.4 0.0 collective-permute-done.6
  39.4 23.5 %collective-permute-done.8 = bf16[256,1024]{1,0:T(8,128)(2,1)S(1)} collective-permute-done((bf16[256,1024]{1,0:T(8,128)(2,1)S(1)}, bf16[256,1024]{1,0:T(8,128)(2,1)S(1)}, u32[]{:S(2)}, u32[]{:S(2)}) %collective-permute-start.8) | collective-permute-done | bytes 524320 | tf_op jit(solution)/shard_map/ppermute | solution.py:20
  62.9 0.3 add_convert_fusion
  63.2 0.9 fusion.10
  64.1 1.5 %collective-permute-start.9 = (bf16[256,512]{1,0:T(8,128)(2,1)S(1)}, bf16[256,512]{1,0:T(8,128)(2,1)S(1)}, u32[]{:S(2)}, u32[]{:S(2)}) collective-permute-start(bf16[256,512]{1,0:T(8,128)(2,1)S(1)} %get-tuple-element.23), channel_id=1, source_target_pairs={{0,2},{2,0},{1,3},{3,1},{4,6},{6,4},{5,7},{7,5},{8,10},{10,8},{9,1... | collective-permute-start | bytes 786440 | tf_op jit(solution)/shard_map/ppermute | solution.py:25
  65.6 6.8 %collective-permute-done.9 = bf16[256,512]{1,0:T(8,128)(2,1)S(1)} collective-permute-done((bf16[256,512]{1,0:T(8,128)(2,1)S(1)}, bf16[256,512]{1,0:T(8,128)(2,1)S(1)}, u32[]{:S(2)}, u32[]{:S(2)}) %collective-permute-start.9) | collective-permute-done | bytes 262176 | tf_op jit(solution)/shard_map/ppermute | solution.py:25
  72.4 0.8 fusion
  73.2 0.0 copy-start.2
  73.2 1.4 %copy-done.2 = f32[1152,512]{1,0:T(8,128)} copy-done((f32[1152,512]{1,0:T(8,128)}, f32[1152,512]{1,0:T(8,128)S(1)}, u32[]{:S(2)}) %copy-start.2) | copy-done | bytes 2359320
  74.6 0.1 dynamic-slice_convert_fusion
  74.7 0.1 collective-permute-start.10
  74.8 1.9 %collective-permute-done.10 = bf16[576,512]{1,0:T(8,128)(2,1)S(1)} collective-permute-done((bf16[576,512]{1,0:T(8,128)(2,1)S(1)}, bf16[576,512]{1,0:T(8,128)(2,1)S(1)}, u32[]{:S(2)}, u32[]{:S(2)}) %collective-permute-start.10) | collective-permute-done | bytes 589856 | tf_op jit(solution)/shard_map/ppermute | solution.py:25
  76.8 1.4 %convert_add_fusion = f32[576,512]{1,0:T(8,128)S(1)} fusion(bf16[576,512]{1,0:T(8,128)(2,1)S(1)} %collective-permute-done.10, f32[1152,512]{1,0:T(8,128)} %copy-done.2, s32[]{:T(128)S(6)} %select_n.100), kind=kLoop, calls=%fused_computation.7 | loop fusion | flops 589824 | bytes 2949124 | tf_op jit(solution)/shard_map/add | solution.py:239
  78.2 0.1 dynamic-slice_convert_fusion.3
  78.3 4.9 %collective-permute-start.11 = (bf16[144,512]{1,0:T(8,128)(2,1)S(1)}, bf16[144,512]{1,0:T(8,128)(2,1)S(1)}, u32[]{:S(2)}, u32[]{:S(2)}) collective-permute-start(bf16[144,512]{1,0:T(8,128)(2,1)S(1)} %get-tuple-element.18), channel_id=1, source_target_pairs={{0,4},{4,8},{8,12},{12,0},{1,5},{5,9},{9,13},{13,1},{2,6},{6,10},{... | collective-permute-start | bytes 442376 | tf_op jit(solution)/shard_map/ppermute | solution.py:25
  83.2 0.0 collective-permute-start.12
  83.2 2.4 %collective-permute-start.13 = (bf16[144,512]{1,0:T(8,128)(2,1)S(1)}, bf16[144,512]{1,0:T(8,128)(2,1)S(1)}, u32[]{:S(2)}, u32[]{:S(2)}) collective-permute-start(bf16[144,512]{1,0:T(8,128)(2,1)S(1)} %get-tuple-element.19), channel_id=1, source_target_pairs={{0,12},{4,0},{8,4},{12,8},{1,13},{5,1},{9,5},{13,9},{2,14},{6,2},{... | collective-permute-start | bytes 442376 | tf_op jit(solution)/shard_map/ppermute | solution.py:25
  85.6 1.8 %collective-permute-done.11 = bf16[144,512]{1,0:T(8,128)(2,1)S(1)} collective-permute-done((bf16[144,512]{1,0:T(8,128)(2,1)S(1)}, bf16[144,512]{1,0:T(8,128)(2,1)S(1)}, u32[]{:S(2)}, u32[]{:S(2)}) %collective-permute-start.11) | collective-permute-done | bytes 147488 | tf_op jit(solution)/shard_map/ppermute | solution.py:25
  87.4 5.3 %collective-permute-done.12 = bf16[144,512]{1,0:T(8,128)(2,1)S(1)} collective-permute-done((bf16[144,512]{1,0:T(8,128)(2,1)S(1)}, bf16[144,512]{1,0:T(8,128)(2,1)S(1)}, u32[]{:S(2)}, u32[]{:S(2)}) %collective-permute-start.12) | collective-permute-done | bytes 147488 | tf_op jit(solution)/shard_map/ppermute | solution.py:25
  92.7 0.2 collective-permute-done.13
  93.0 0.1 broadcast_in_dim.28
  93.1 0.1 fusion.7
  93.2 3.5 %collective-permute-start.14 = (bf16[144,512]{1,0:T(8,128)(2,1)S(1)}, bf16[144,512]{1,0:T(8,128)(2,1)S(1)}, u32[]{:S(2)}, u32[]{:S(2)}) collective-permute-start(bf16[144,512]{1,0:T(8,128)(2,1)S(1)} %get-tuple-element.16), channel_id=1, source_target_pairs={{0,4},{4,8},{8,12},{12,0},{1,5},{5,9},{9,13},{13,1},{2,6},{6,10},{... | collective-permute-start | bytes 442376 | tf_op jit(solution)/shard_map/ppermute | solution.py:25
  96.6 3.4 %collective-permute-start.15 = (bf16[144,512]{1,0:T(8,128)(2,1)S(1)}, bf16[144,512]{1,0:T(8,128)(2,1)S(1)}, u32[]{:S(2)}, u32[]{:S(2)}) collective-permute-start(bf16[144,512]{1,0:T(8,128)(2,1)S(1)} %get-tuple-element.16), channel_id=1, source_target_pairs={{0,8},{4,12},{8,0},{12,4},{1,9},{5,13},{9,1},{13,5},{2,10},{6,14},... | collective-permute-start | bytes 442376 | tf_op jit(solution)/shard_map/ppermute | solution.py:25
  100.0 0.0 collective-permute-start.16
  100.0 4.2 %collective-permute-done.14 = bf16[144,512]{1,0:T(8,128)(2,1)S(1)} collective-permute-done((bf16[144,512]{1,0:T(8,128)(2,1)S(1)}, bf16[144,512]{1,0:T(8,128)(2,1)S(1)}, u32[]{:S(2)}, u32[]{:S(2)}) %collective-permute-start.14) | collective-permute-done | bytes 147488 | tf_op jit(solution)/shard_map/ppermute | solution.py:25
  104.3 5.2 %collective-permute-done.15 = bf16[144,512]{1,0:T(8,128)(2,1)S(1)} collective-permute-done((bf16[144,512]{1,0:T(8,128)(2,1)S(1)}, bf16[144,512]{1,0:T(8,128)(2,1)S(1)}, u32[]{:S(2)}, u32[]{:S(2)}) %collective-permute-start.15) | collective-permute-done | bytes 147488 | tf_op jit(solution)/shard_map/ppermute | solution.py:25
  109.5 0.0 collective-permute-done.16
  109.6 0.1 convert_element_type.90
  109.7 0.1 collective-permute-start.17
  109.7 2.0 %collective-permute-done.17 = bf16[576,512]{1,0:T(8,128)(2,1)S(1)} collective-permute-done((bf16[576,512]{1,0:T(8,128)(2,1)S(1)}, bf16[576,512]{1,0:T(8,128)(2,1)S(1)}, u32[]{:S(2)}, u32[]{:S(2)}) %collective-permute-start.17) | collective-permute-done | bytes 589856 | tf_op jit(solution)/shard_map/ppermute | solution.py:25
  111.7 0.3 convert_select_fusion.1
  112.1 1.7 %maximum_multiply_fusion = f32[1152,512]{1,0:T(8,128)} fusion(f32[576,512]{1,0:T(8,128)S(1)} %get-tuple-element.15, f32[576,512]{1,0:T(8,128)S(1)} %get-tuple-element.14), kind=kLoop, calls=%fused_computation | loop fusion | flops 1179648 | bytes 4718592 | tf_op jit(solution)/shard_map/mul | solution.py:253
  (19 shorter events, 0.1 us)
Async XLA Ops:
  1.7 9.2 %copy-start.5 = (bf16[256,1024]{1,0:T(8,128)(2,1)}, bf16[256,1024]{1,0:T(8,128)(2,1)S(1)}, u32[]{:S(2)}) copy-start(bf16[256,1024]{1,0:T(8,128)(2,1)S(1)} %pad_maximum_fusion.refs_8_) | copy-start | bytes 1572868
  1.7 17.2 %collective-permute-start = (bf16[256,1024]{1,0:T(8,128)(2,1)S(1)}, bf16[256,1024]{1,0:T(8,128)(2,1)S(1)}, u32[]{:S(2)}, u32[]{:S(2)}) collective-permute-start(bf16[256,1024]{1,0:T(8,128)(2,1)S(1)} %pad_maximum_fusion.refs_8_), channel_id=1, source_target_pairs={{0,4},{4,8},{8,12},{1,5},{5,9},{9,13},{2,6},{6,10},{10,14},{3,7},{... | collective-permute-start | bytes 1572872 | tf_op jit(solution)/shard_map/ppermute | solution.py:20
  6.7 12.3 %copy-start.6 = (s32[1,12]{1,0:T(1,128)S(1)}, s32[1,12]{1,0:T(1,128)}, u32[]{:S(2)}) copy-start(s32[1,12]{1,0:T(1,128)} %param.11) | copy-start | bytes 148
  8.1 14.9 %collective-permute-start.4 = (bf16[256,1152]{1,0:T(8,128)(2,1)S(1)}, bf16[256,1152]{1,0:T(8,128)(2,1)S(1)}, u32[]{:S(2)}, u32[]{:S(2)}) collective-permute-start(bf16[256,1152]{1,0:T(8,128)(2,1)S(1)} %get-tuple-element.22), channel_id=1, source_target_pairs={{0,2},{2,0},{1,3},{3,1},{4,6},{6,4},{5,7},{7,5},{8,10},{10,8},{9,1... | collective-permute-start | bytes 1769480 | tf_op jit(solution)/shard_map/ppermute | solution.py:25
  9.6 10.3 %collective-permute-start.1 = (bf16[256,1024]{1,0:T(8,128)(2,1)S(1)}, bf16[256,1024]{1,0:T(8,128)(2,1)S(1)}, u32[]{:S(2)}, u32[]{:S(2)}) collective-permute-start(bf16[256,1024]{1,0:T(8,128)(2,1)S(1)} %pad_maximum_fusion.refs_8_), channel_id=1, source_target_pairs={{0,1},{2,3},{4,5},{6,7},{8,9},{10,11},{12,13},{14,15},{16,17},{18,... | collective-permute-start | bytes 1572872 | tf_op jit(solution)/shard_map/ppermute | solution.py:20
  11.0 9.0 %collective-permute-start.2 = (bf16[256,1024]{1,0:T(8,128)(2,1)S(1)}, bf16[256,1024]{1,0:T(8,128)(2,1)}, u32[]{:S(2)}, u32[]{:S(2)}) collective-permute-start(bf16[256,1024]{1,0:T(8,128)(2,1)S(1)} %pad_maximum_fusion.refs_8_), channel_id=1, source_target_pairs={{1,8},{5,12},{3,10},{7,14},{17,24},{21,28},{19,26},{23,30}} | collective-permute-start | bytes 1572872 | tf_op jit(solution)/shard_map/ppermute | solution.py:183
  19.0 4.0 %copy-start.9 = (bf16[256,1024]{1,0:T(8,128)(2,1)}, bf16[256,1024]{1,0:T(8,128)(2,1)S(1)}, u32[]{:S(2)}) copy-start(bf16[256,1024]{1,0:T(8,128)(2,1)S(1)} %collective-permute-done.refs_4_) | copy-start | bytes 1572868
  19.0 4.0 %collective-permute-start.3 = (bf16[256,1024]{1,0:T(8,128)(2,1)S(1)}, bf16[256,1024]{1,0:T(8,128)(2,1)}, u32[]{:S(2)}, u32[]{:S(2)}) collective-permute-start(bf16[256,1024]{1,0:T(8,128)(2,1)S(1)} %collective-permute-done.refs_4_), channel_id=1, source_target_pairs={{0,1},{1,0},{2,3},{3,2},{4,5},{5,4},{6,7},{7,6},{8,9},{9,8},{10,11... | collective-permute-start | bytes 1572872 | tf_op jit(solution)/shard_map/ppermute | solution.py:25
  19.9 3.0 %copy-start.10 = (bf16[256,1024]{1,0:T(8,128)(2,1)}, bf16[256,1024]{1,0:T(8,128)(2,1)S(1)}, u32[]{:S(2)}) copy-start(bf16[256,1024]{1,0:T(8,128)(2,1)S(1)} %collective-permute-done.1.refs_5_) | copy-start | bytes 1572868
  22.9 0.8 copy-start.7
  32.7 2.2 %copy-start.1 = (f32[256,1024]{1,0:T(8,128)S(1)}, f32[256,1024]{1,0:T(8,128)}, u32[]{:S(2)}) copy-start(f32[256,1024]{1,0:T(8,128)} %get-tuple-element.11) | copy-start | bytes 3145732
  34.1 1.2 %copy-start = (f32[256,1024]{1,0:T(8,128)S(1)}, f32[256,1024]{1,0:T(8,128)}, u32[]{:S(2)}) copy-start(f32[256,1024]{1,0:T(8,128)} %get-tuple-element.12) | copy-start | bytes 3145732
  34.1 3.5 %collective-permute-start.7 = (bf16[256,1024]{1,0:T(8,128)(2,1)S(1)}, bf16[256,1024]{1,0:T(8,128)(2,1)S(1)}, u32[]{:S(2)}, u32[]{:S(2)}) collective-permute-start(bf16[256,1024]{1,0:T(8,128)(2,1)S(1)} %select_convert_fusion), channel_id=1, source_target_pairs={{0,1},{1,0},{2,3},{3,2},{4,5},{5,4},{6,7},{7,6},{8,9},{9,8},{10,11... | collective-permute-start | bytes 1572872 | tf_op jit(solution)/shard_map/ppermute | solution.py:25
  35.4 2.2 %copy-start.4 = (f32[256,1024]{1,0:T(8,128)S(1)}, f32[256,1024]{1,0:T(8,128)}, u32[]{:S(2)}) copy-start(f32[256,1024]{1,0:T(8,128)} %get-tuple-element.13) | copy-start | bytes 3145732
  35.4 27.4 %copy-start.3 = (f32[256,1024]{1,0:T(8,128)S(1)}, f32[256,1024]{1,0:T(8,128)}, u32[]{:S(2)}) copy-start(f32[256,1024]{1,0:T(8,128)} %get-tuple-element.10) | copy-start | bytes 3145732
  35.5 3.9 %collective-permute-start.5 = (bf16[256,1024]{1,0:T(8,128)(2,1)S(1)}, bf16[256,1024]{1,0:T(8,128)(2,1)S(1)}, u32[]{:S(2)}, u32[]{:S(2)}) collective-permute-start(bf16[256,1024]{1,0:T(8,128)(2,1)S(1)} %convert_element_type.69), channel_id=1, source_target_pairs={{1,0},{3,2},{5,4},{7,6},{9,8},{11,10},{13,12},{15,14},{17,16},{19,... | collective-permute-start | bytes 1572872 | tf_op jit(solution)/shard_map/ppermute | solution.py:20
  36.9 2.5 %collective-permute-start.6 = (bf16[256,1024]{1,0:T(8,128)(2,1)S(1)}, bf16[256,1024]{1,0:T(8,128)(2,1)S(1)}, u32[]{:S(2)}, u32[]{:S(2)}) collective-permute-start(bf16[256,1024]{1,0:T(8,128)(2,1)S(1)} %convert_element_type.71), channel_id=1, source_target_pairs={{8,1},{12,5},{10,3},{14,7},{24,17},{28,21},{26,19},{30,23}} | collective-permute-start | bytes 1572872 | tf_op jit(solution)/shard_map/ppermute | solution.py:206
  37.8 25.1 %collective-permute-start.8 = (bf16[256,1024]{1,0:T(8,128)(2,1)S(1)}, bf16[256,1024]{1,0:T(8,128)(2,1)S(1)}, u32[]{:S(2)}, u32[]{:S(2)}) collective-permute-start(bf16[256,1024]{1,0:T(8,128)(2,1)S(1)} %add_convert_fusion.1), channel_id=1, source_target_pairs={{4,0},{8,4},{12,8},{5,1},{9,5},{13,9},{6,2},{10,6},{14,10},{7,3},{... | collective-permute-start | bytes 1572872 | tf_op jit(solution)/shard_map/ppermute | solution.py:20
  63.2 9.2 %copy-start.8 = (bf16[256,1152]{1,0:T(8,128)(2,1)S(1)}, bf16[256,1152]{1,0:T(8,128)(2,1)}, u32[]{:S(2)}) copy-start(bf16[256,1152]{1,0:T(8,128)(2,1)} %copy-done.7) | copy-start | bytes 1769476
  64.1 8.3 %collective-permute-start.9 = (bf16[256,512]{1,0:T(8,128)(2,1)S(1)}, bf16[256,512]{1,0:T(8,128)(2,1)S(1)}, u32[]{:S(2)}, u32[]{:S(2)}) collective-permute-start(bf16[256,512]{1,0:T(8,128)(2,1)S(1)} %get-tuple-element.23), channel_id=1, source_target_pairs={{0,2},{2,0},{1,3},{3,1},{4,6},{6,4},{5,7},{7,5},{8,10},{10,8},{9,1... | collective-permute-start | bytes 786440 | tf_op jit(solution)/shard_map/ppermute | solution.py:25
  73.2 1.4 %copy-start.2 = (f32[1152,512]{1,0:T(8,128)}, f32[1152,512]{1,0:T(8,128)S(1)}, u32[]{:S(2)}) copy-start(f32[1152,512]{1,0:T(8,128)S(1)} %fusion) | copy-start | bytes 7077892
  74.7 2.1 %collective-permute-start.10 = (bf16[576,512]{1,0:T(8,128)(2,1)S(1)}, bf16[576,512]{1,0:T(8,128)(2,1)S(1)}, u32[]{:S(2)}, u32[]{:S(2)}) collective-permute-start(bf16[576,512]{1,0:T(8,128)(2,1)S(1)} %dynamic-slice_convert_fusion), channel_id=1, source_target_pairs={{0,1},{1,0},{2,3},{3,2},{4,5},{5,4},{6,7},{7,6},{8,9},{9,8},{10,11... | collective-permute-start | bytes 1769480 | tf_op jit(solution)/shard_map/ppermute | solution.py:25
  78.3 9.1 %collective-permute-start.11 = (bf16[144,512]{1,0:T(8,128)(2,1)S(1)}, bf16[144,512]{1,0:T(8,128)(2,1)S(1)}, u32[]{:S(2)}, u32[]{:S(2)}) collective-permute-start(bf16[144,512]{1,0:T(8,128)(2,1)S(1)} %get-tuple-element.18), channel_id=1, source_target_pairs={{0,4},{4,8},{8,12},{12,0},{1,5},{5,9},{9,13},{13,1},{2,6},{6,10},{... | collective-permute-start | bytes 442376 | tf_op jit(solution)/shard_map/ppermute | solution.py:25
  83.2 9.6 %collective-permute-start.12 = (bf16[144,512]{1,0:T(8,128)(2,1)S(1)}, bf16[144,512]{1,0:T(8,128)(2,1)S(1)}, u32[]{:S(2)}, u32[]{:S(2)}) collective-permute-start(bf16[144,512]{1,0:T(8,128)(2,1)S(1)} %get-tuple-element.20), channel_id=1, source_target_pairs={{0,8},{4,12},{8,0},{12,4},{1,9},{5,13},{9,1},{13,5},{2,10},{6,14},... | collective-permute-start | bytes 442376 | tf_op jit(solution)/shard_map/ppermute | solution.py:25
  83.2 9.8 %collective-permute-start.13 = (bf16[144,512]{1,0:T(8,128)(2,1)S(1)}, bf16[144,512]{1,0:T(8,128)(2,1)S(1)}, u32[]{:S(2)}, u32[]{:S(2)}) collective-permute-start(bf16[144,512]{1,0:T(8,128)(2,1)S(1)} %get-tuple-element.19), channel_id=1, source_target_pairs={{0,12},{4,0},{8,4},{12,8},{1,13},{5,1},{9,5},{13,9},{2,14},{6,2},{... | collective-permute-start | bytes 442376 | tf_op jit(solution)/shard_map/ppermute | solution.py:25
  93.2 11.1 %collective-permute-start.14 = (bf16[144,512]{1,0:T(8,128)(2,1)S(1)}, bf16[144,512]{1,0:T(8,128)(2,1)S(1)}, u32[]{:S(2)}, u32[]{:S(2)}) collective-permute-start(bf16[144,512]{1,0:T(8,128)(2,1)S(1)} %get-tuple-element.16), channel_id=1, source_target_pairs={{0,4},{4,8},{8,12},{12,0},{1,5},{5,9},{9,13},{13,1},{2,6},{6,10},{... | collective-permute-start | bytes 442376 | tf_op jit(solution)/shard_map/ppermute | solution.py:25
  96.6 12.9 %collective-permute-start.15 = (bf16[144,512]{1,0:T(8,128)(2,1)S(1)}, bf16[144,512]{1,0:T(8,128)(2,1)S(1)}, u32[]{:S(2)}, u32[]{:S(2)}) collective-permute-start(bf16[144,512]{1,0:T(8,128)(2,1)S(1)} %get-tuple-element.16), channel_id=1, source_target_pairs={{0,8},{4,12},{8,0},{12,4},{1,9},{5,13},{9,1},{13,5},{2,10},{6,14},... | collective-permute-start | bytes 442376 | tf_op jit(solution)/shard_map/ppermute | solution.py:25
  100.0 9.5 %collective-permute-start.16 = (bf16[144,512]{1,0:T(8,128)(2,1)S(1)}, bf16[144,512]{1,0:T(8,128)(2,1)S(1)}, u32[]{:S(2)}, u32[]{:S(2)}) collective-permute-start(bf16[144,512]{1,0:T(8,128)(2,1)S(1)} %get-tuple-element.16), channel_id=1, source_target_pairs={{0,12},{4,0},{8,4},{12,8},{1,13},{5,1},{9,5},{13,9},{2,14},{6,2},{... | collective-permute-start | bytes 442376 | tf_op jit(solution)/shard_map/ppermute | solution.py:25
  109.7 2.1 %collective-permute-start.17 = (bf16[576,512]{1,0:T(8,128)(2,1)S(1)}, bf16[576,512]{1,0:T(8,128)(2,1)S(1)}, u32[]{:S(2)}, u32[]{:S(2)}) collective-permute-start(bf16[576,512]{1,0:T(8,128)(2,1)S(1)} %convert_element_type.90), channel_id=1, source_target_pairs={{0,1},{1,0},{2,3},{3,2},{4,5},{5,4},{6,7},{7,6},{8,9},{9,8},{10,11... | collective-permute-start | bytes 1769480 | tf_op jit(solution)/shard_map/ppermute | solution.py:25

commit v6 on v5

--- a/solution.py
+++ b/solution.py
@@ -202,13 +202,21 @@
 
     if chip_route:
         back = [(target, source) for source, target in across]
-        g3, g2, g1, g0 = grad_pieces
-        from_far = lax.ppermute(low(g3), RING, back).astype(jnp.float32)
-        from_mate = rotated(low(jnp.where(sub_at == 0, g1, g3)), "sub", 1).astype(jnp.float32)
-        from_high = passed_along(low(g1), "sub", -1).astype(jnp.float32)
-        two_back_sum = g2 + from_mate
-        from_next = passed_along(low(two_back_sum), "ctx", -1).astype(jnp.float32)
-        total = g0 + from_high + from_far + from_next
+
+        def returned(g3, g2, g1, g0):
+            from_far = lax.ppermute(low(g3), RING, back).astype(jnp.float32)
+            from_mate = rotated(low(jnp.where(sub_at == 0, g1, g3)), "sub", 1).astype(jnp.float32)
+            from_high = passed_along(low(g1), "sub", -1).astype(jnp.float32)
+            two_back_sum = g2 + from_mate
+            from_next = passed_along(low(two_back_sum), "ctx", -1).astype(jnp.float32)
+            return g0 + from_high + from_far + from_next
+
+        total_v = returned(*[piece[:, kv_width:] for piece in grad_pieces])
+        total_v, key_pieces = lax.optimization_barrier(
+            (total_v, [piece[:, :kv_width] for piece in grad_pieces])
+        )
+        total_k = returned(*key_pieces)
+        total = jnp.concatenate([total_k, total_v], axis=1)
     else:
 
         def own_piece(distance):

time: 115 us -> 117 us (1.017)
  starting transfers between devices: 29.3 us -> 34.1 us
  waiting for transfers between devices: 60.9 us -> 58.8 us
    ppermute x4 -> x6, starting transfers between devices: 8.99 us -> 12.2 us  [passed_along(): lax.ppermute(value, axis, [(source, source + steps) for source in range(f...]
    slice x0 -> x2, other arithmetic: none -> 1.86 us  [body(): piece[:, :kv_width]]
    convert_element_type x4 -> x2, other arithmetic: 1.75 us -> 0.1 us  [low(): return value.astype(jnp.bfloat16)]
    ppermute x12 -> x13, waiting for transfers between devices: 30.6 us -> 29.5 us  [rotated(): lax.ppermute(value, axis, [(source, (source + steps) % count) for source...]
    ppermute x4 -> x6, waiting for transfers between devices: 30.3 us -> 29.3 us  [passed_along(): lax.ppermute(value, axis, [(source, source + steps) for source in range(f...]
    ppermute x12 -> x13, starting transfers between devices: 18.1 us -> 19 us  [rotated(): lax.ppermute(value, axis, [(source, (source + steps) % count) for source...]
    unnamed x22 -> x18, local copies, waits for them, and re-layouts: 2.63 us -> 2.23 us
  transfers between devices with their start and end apart: 18 -> 22, of which waited for: 12 -> 12; matrix products, arithmetic and copies ran while one was open for 2% -> 3% of each run, Pallas kernels for 0% -> 0%
where the time goes in v6:
time: 117 us
  waiting for transfers between devices  58.8 us (50%)
  starting transfers between devices  34.1 us (29%)
  Pallas kernels  8.93 us (8%)
  other arithmetic  8.46 us (7%)
  local copies, waits for them, and re-layouts  4.68 us (4%)
    ppermute x13, waiting for transfers between devices, rotated(): lax.ppermute(value, axis, [(source, (source + steps) % count) for source...  29.5 us
    ppermute x6, waiting for transfers between devices, passed_along(): lax.ppermute(value, axis, [(source, source + steps) for source in range(f...  29.3 us
    ppermute x13, starting transfers between devices, rotated(): lax.ppermute(value, axis, [(source, (source + steps) % count) for source...  19 us
    ppermute x6, starting transfers between devices, passed_along(): lax.ppermute(value, axis, [(source, source + steps) for source in range(f...  12.2 us
    pallas_call x1, Pallas kernels, attention(): pl.pallas_call(kernel, out_shape=(jax.ShapeDtypeStruct((rows, width), jnp...  8.93 us
  transfers between devices with their start and end apart: 22, of which 12 were waited for; matrix products, arithmetic and copies ran while one was open for 3% of the time, Pallas kernels for 0%

profile of v6, /device:TPU:0, one launch (start us, length us, event | category | flops | bytes accessed | tf_op | source)
XLA Modules:
  0.0 116.8 jit_solution(12883754379726170265)
XLA Ops:
  0.6 1.1 pad_maximum_fusion.refs_8_
  1.7 5.0 %collective-permute-start = (bf16[256,1024]{1,0:T(8,128)(2,1)S(1)}, bf16[256,1024]{1,0:T(8,128)(2,1)S(1)}, u32[]{:S(2)}, u32[]{:S(2)}) collective-permute-start(bf16[256,1024]{1,0:T(8,128)(2,1)S(1)} %pad_maximum_fusion.refs_8_), channel_id=1, source_target_pairs={{0,4},{4,8},{8,12},{1,5},{5,9},{9,13},{2,6},{6,10},{10,14},{3,7},{... | collective-permute-start | bytes 1572872 | tf_op jit(solution)/shard_map/ppermute | solution.py:20
  6.7 0.0 copy-start.5
  6.7 1.3 %dynamic-slice_bitcast_fusion = (bf16[256,1152]{1,0:T(8,128)(2,1)S(1)}, bf16[256,1152]{1,0:T(8,128)(2,1)S(1)}) fusion(bf16[1,256,2304]{2,1,0:T(8,128)(2,1)} %param.6, s32[]{:T(128)S(6)} %select_n.104, s32[]{:T(128)S(6)} %select_n.99), kind=kLoop, calls=%fused_computation.9 | loop fusion | bytes 2359304 | tf_op jit(solution)/shard_map/dynamic_slice | solution.py:164
  8.1 1.6 %collective-permute-start.4 = (bf16[256,1152]{1,0:T(8,128)(2,1)S(1)}, bf16[256,1152]{1,0:T(8,128)(2,1)S(1)}, u32[]{:S(2)}, u32[]{:S(2)}) collective-permute-start(bf16[256,1152]{1,0:T(8,128)(2,1)S(1)} %get-tuple-element.32), channel_id=1, source_target_pairs={{0,2},{2,0},{1,3},{3,1},{4,6},{6,4},{5,7},{7,5},{8,10},{10,8},{9,1... | collective-permute-start | bytes 1769480 | tf_op jit(solution)/shard_map/ppermute | solution.py:25
  9.6 2.1 %collective-permute-start.1 = (bf16[256,1024]{1,0:T(8,128)(2,1)S(1)}, bf16[256,1024]{1,0:T(8,128)(2,1)}, u32[]{:S(2)}, u32[]{:S(2)}) collective-permute-start(bf16[256,1024]{1,0:T(8,128)(2,1)S(1)} %pad_maximum_fusion.refs_8_), channel_id=1, source_target_pairs={{0,1},{2,3},{4,5},{6,7},{8,9},{10,11},{12,13},{14,15},{16,17},{18,... | collective-permute-start | bytes 1572872 | tf_op jit(solution)/shard_map/ppermute | solution.py:20
  11.7 1.5 %collective-permute-start.2 = (bf16[256,1024]{1,0:T(8,128)(2,1)S(1)}, bf16[256,1024]{1,0:T(8,128)(2,1)}, u32[]{:S(2)}, u32[]{:S(2)}) collective-permute-start(bf16[256,1024]{1,0:T(8,128)(2,1)S(1)} %pad_maximum_fusion.refs_8_), channel_id=1, source_target_pairs={{1,8},{5,12},{3,10},{7,14},{17,24},{21,28},{19,26},{23,30}} | collective-permute-start | bytes 1572872 | tf_op jit(solution)/shard_map/ppermute | solution.py:183
  13.2 5.8 %collective-permute-done.refs_4_ = bf16[256,1024]{1,0:T(8,128)(2,1)S(1)} collective-permute-done((bf16[256,1024]{1,0:T(8,128)(2,1)S(1)}, bf16[256,1024]{1,0:T(8,128)(2,1)S(1)}, u32[]{:S(2)}, u32[]{:S(2)}) %collective-permute-start) | collective-permute-done | bytes 524320 | tf_op jit(solution)/shard_map/ppermute | solution.py:20
  19.0 0.0 collective-permute-start.3
  19.0 0.1 select_reduce_fusion
  19.1 0.1 copy.13
  19.2 0.7 subtract_add_fusion.refs_1_
  19.9 0.0 collective-permute-done.1.refs_5_
  19.9 0.0 collective-permute-done.2.refs_6_
  19.9 3.0 %collective-permute-done.4.refs_9_ = bf16[256,1152]{1,0:T(8,128)(2,1)S(1)} collective-permute-done((bf16[256,1152]{1,0:T(8,128)(2,1)S(1)}, bf16[256,1152]{1,0:T(8,128)(2,1)S(1)}, u32[]{:S(2)}, u32[]{:S(2)}) %collective-permute-start.4) | collective-permute-done | bytes 589856 | tf_op jit(solution)/shard_map/ppermute | solution.py:25
  22.9 0.8 copy-done.6
  23.7 8.9 %shard_map.93 = (bf16[256,1024]{1,0:T(8,128)(2,1)}, f32[256,1024]{1,0:T(8,128)}, f32[256,1024]{1,0:T(8,128)}, f32[256,1024]{1,0:T(8,128)}, f32[256,1024]{1,0:T(8,128)}) custom-call(s32[1]{0:T(128)} %bitcast.refs_0_, s32[256,1]{1,0:T(8,128)} %subtract_add_fusion.refs_1_, bf16[256,1024]{1,0:T(8,128)(2,1)} %bitcast.20, bf16[256,1024]{1,0:T(8,128)(2,1)} %bitcast.21, ...), custom_call_target="tpu_custom_call" | custom-call | flops 2684354560 | bytes 7864320 | tf_op jit(solution)/shard_map/pallas_call | solution.py:133
  32.7 1.7 %fusion.11 = (bf16[256,512]{1,0:T(8,128)(2,1)S(1)}, bf16[256,512]{1,0:T(8,128)(2,1)S(1)}, bf16[256,512]{1,0:T(8,128)(2,1)S(1)}, bf16[256,512]{1,0:T(8,128)(2,1)S(1)}, bf16[256,512]{1,0:T(8,128)(2,1)S(1)}) fusion(f32[256,1024]{1,0:T(8,128)} %get-tuple-element.16, f32[256,1024]{1,0:T(8,128)} %get-tuple-element.17, pred[]{:T(512)S(6)} %eq.15), kind=kLoop, calls=%fused_computation.37 | loop fusion | flops 131072 | bytes 2359297 | tf_op jit(solution)/shard_map/slice | solution.py:216
  34.4 0.8 collective-permute-start.7
  35.1 1.3 %collective-permute-start.5 = (bf16[256,512]{1,0:T(8,128)(2,1)S(1)}, bf16[256,512]{1,0:T(8,128)(2,1)S(1)}, u32[]{:S(2)}, u32[]{:S(2)}) collective-permute-start(bf16[256,512]{1,0:T(8,128)(2,1)S(1)} %get-tuple-element.37), channel_id=1, source_target_pairs={{1,0},{3,2},{5,4},{7,6},{9,8},{11,10},{13,12},{15,14},{17,16},{19,... | collective-permute-start | bytes 786440 | tf_op jit(solution)/shard_map/ppermute | solution.py:20
  36.4 0.7 collective-permute-start.6
  37.1 0.0 collective-permute-done.7
  37.1 0.1 fusion.12
  37.3 1.3 %collective-permute-start.8 = (bf16[256,512]{1,0:T(8,128)(2,1)S(1)}, bf16[256,512]{1,0:T(8,128)(2,1)S(1)}, u32[]{:S(2)}, u32[]{:S(2)}) collective-permute-start(bf16[256,512]{1,0:T(8,128)(2,1)S(1)} %get-tuple-element.39), channel_id=1, source_target_pairs={{4,0},{8,4},{12,8},{5,1},{9,5},{13,9},{6,2},{10,6},{14,10},{7,3},{... | collective-permute-start | bytes 786440 | tf_op jit(solution)/shard_map/ppermute | solution.py:20
  38.6 0.0 collective-permute-done.5
  38.7 0.0 collective-permute-done.6
  38.7 14.3 %collective-permute-done.8 = bf16[256,512]{1,0:T(8,128)(2,1)S(1)} collective-permute-done((bf16[256,512]{1,0:T(8,128)(2,1)S(1)}, bf16[256,512]{1,0:T(8,128)(2,1)S(1)}, u32[]{:S(2)}, u32[]{:S(2)}) %collective-permute-start.8) | collective-permute-done | bytes 262176 | tf_op jit(solution)/shard_map/ppermute | solution.py:20
  52.9 0.1 convert_add_fusion.1
  53.1 0.0 copy-start.4
  53.1 1.5 %collective-permute-start.13 = (bf16[256,512]{1,0:T(8,128)(2,1)S(1)}, bf16[256,512]{1,0:T(8,128)(2,1)S(1)}, u32[]{:S(2)}, u32[]{:S(2)}) collective-permute-start(bf16[256,512]{1,0:T(8,128)(2,1)S(1)} %convert_add_fusion.1), channel_id=1, source_target_pairs={{0,2},{2,0},{1,3},{3,1},{4,6},{6,4},{5,7},{7,5},{8,10},{10,8},{9,1... | collective-permute-start | bytes 786440 | tf_op jit(solution)/shard_map/ppermute | solution.py:25
  54.6 7.4 %collective-permute-done.13 = bf16[256,512]{1,0:T(8,128)(2,1)S(1)} collective-permute-done((bf16[256,512]{1,0:T(8,128)(2,1)S(1)}, bf16[256,512]{1,0:T(8,128)(2,1)S(1)}, u32[]{:S(2)}, u32[]{:S(2)}) %collective-permute-start.13) | collective-permute-done | bytes 262176 | tf_op jit(solution)/shard_map/ppermute | solution.py:25
  62.0 0.8 fusion
  62.8 0.0 copy-start
  62.8 1.4 %copy-done = f32[1152,512]{1,0:T(8,128)} copy-done((f32[1152,512]{1,0:T(8,128)}, f32[1152,512]{1,0:T(8,128)S(1)}, u32[]{:S(2)}) %copy-start) | copy-done | bytes 2359320
  64.2 0.1 dynamic-slice_convert_fusion
  64.3 0.1 collective-permute-start.14
  64.4 1.9 %collective-permute-done.14 = bf16[576,512]{1,0:T(8,128)(2,1)S(1)} collective-permute-done((bf16[576,512]{1,0:T(8,128)(2,1)S(1)}, bf16[576,512]{1,0:T(8,128)(2,1)S(1)}, u32[]{:S(2)}, u32[]{:S(2)}) %collective-permute-start.14) | collective-permute-done | bytes 589856 | tf_op jit(solution)/shard_map/ppermute | solution.py:25
  66.4 1.4 %convert_add_fusion = f32[576,512]{1,0:T(8,128)S(1)} fusion(bf16[576,512]{1,0:T(8,128)(2,1)S(1)} %collective-permute-done.14, f32[1152,512]{1,0:T(8,128)} %copy-done, s32[]{:T(128)S(6)} %select_n.105), kind=kLoop, calls=%fused_computation.7 | loop fusion | flops 589824 | bytes 2949124 | tf_op jit(solution)/shard_map/add | solution.py:247
  67.8 0.7 dynamic-slice_convert_fusion.3
  68.6 4.6 %collective-permute-start.15 = (bf16[144,512]{1,0:T(8,128)(2,1)}, bf16[144,512]{1,0:T(8,128)(2,1)S(1)}, u32[]{:S(2)}, u32[]{:S(2)}) collective-permute-start(bf16[144,512]{1,0:T(8,128)(2,1)} %get-tuple-element.28), channel_id=1, source_target_pairs={{0,4},{4,8},{8,12},{12,0},{1,5},{5,9},{9,13},{13,1},{2,6},{6,10},{... | collective-permute-start | bytes 442376 | tf_op jit(solution)/shard_map/ppermute | solution.py:25
  73.1 0.0 collective-permute-start.16
  73.1 2.4 %collective-permute-start.17 = (bf16[144,512]{1,0:T(8,128)(2,1)S(1)}, bf16[144,512]{1,0:T(8,128)(2,1)S(1)}, u32[]{:S(2)}, u32[]{:S(2)}) collective-permute-start(bf16[144,512]{1,0:T(8,128)(2,1)S(1)} %get-tuple-element.29), channel_id=1, source_target_pairs={{0,12},{4,0},{8,4},{12,8},{1,13},{5,1},{9,5},{13,9},{2,14},{6,2},{... | collective-permute-start | bytes 442376 | tf_op jit(solution)/shard_map/ppermute | solution.py:25
  75.5 0.7 collective-permute-start.10
  76.2 1.3 %collective-permute-start.9 = (bf16[256,512]{1,0:T(8,128)(2,1)S(1)}, bf16[256,512]{1,0:T(8,128)(2,1)S(1)}, u32[]{:S(2)}, u32[]{:S(2)}) collective-permute-start(bf16[256,512]{1,0:T(8,128)(2,1)S(1)} %get-tuple-element.20), channel_id=1, source_target_pairs={{1,0},{3,2},{5,4},{7,6},{9,8},{11,10},{13,12},{15,14},{17,16},{19,... | collective-permute-start | bytes 786440 | tf_op jit(solution)/shard_map/ppermute | solution.py:20
  77.5 0.2 collective-permute-done.15
  77.6 5.2 %collective-permute-done.16 = bf16[144,512]{1,0:T(8,128)(2,1)S(1)} collective-permute-done((bf16[144,512]{1,0:T(8,128)(2,1)S(1)}, bf16[144,512]{1,0:T(8,128)(2,1)S(1)}, u32[]{:S(2)}, u32[]{:S(2)}) %collective-permute-start.16) | collective-permute-done | bytes 147488 | tf_op jit(solution)/shard_map/ppermute | solution.py:25
  82.9 0.2 collective-permute-done.17
  83.1 0.1 broadcast_in_dim.28
  83.2 0.1 fusion.8
  83.3 6.3 %collective-permute-start.18 = (bf16[144,512]{1,0:T(8,128)(2,1)S(1)}, bf16[144,512]{1,0:T(8,128)(2,1)S(1)}, u32[]{:S(2)}, u32[]{:S(2)}) collective-permute-start(bf16[144,512]{1,0:T(8,128)(2,1)S(1)} %get-tuple-element.26), channel_id=1, source_target_pairs={{0,4},{4,8},{8,12},{12,0},{1,5},{5,9},{9,13},{13,1},{2,6},{6,10},{... | collective-permute-start | bytes 442376 | tf_op jit(solution)/shard_map/ppermute | solution.py:25
  89.6 0.1 collective-permute-start.11
  89.7 0.6 collective-permute-start.19
  90.3 3.5 %collective-permute-done.18 = bf16[144,512]{1,0:T(8,128)(2,1)S(1)} collective-permute-done((bf16[144,512]{1,0:T(8,128)(2,1)S(1)}, bf16[144,512]{1,0:T(8,128)(2,1)S(1)}, u32[]{:S(2)}, u32[]{:S(2)}) %collective-permute-start.18) | collective-permute-done | bytes 147488 | tf_op jit(solution)/shard_map/ppermute | solution.py:25
  93.8 1.2 collective-permute-start.20
  95.0 7.4 %collective-permute-done.19 = bf16[144,512]{1,0:T(8,128)(2,1)S(1)} collective-permute-done((bf16[144,512]{1,0:T(8,128)(2,1)S(1)}, bf16[144,512]{1,0:T(8,128)(2,1)S(1)}, u32[]{:S(2)}, u32[]{:S(2)}) %collective-permute-start.19) | collective-permute-done | bytes 147488 | tf_op jit(solution)/shard_map/ppermute | solution.py:25
  102.4 0.7 collective-permute-done.20
  103.1 0.1 convert_element_type.119
  103.2 0.1 collective-permute-start.21
  103.3 0.1 add_convert_fusion.1
  103.4 1.3 %collective-permute-start.12 = (bf16[256,512]{1,0:T(8,128)(2,1)S(1)}, bf16[256,512]{1,0:T(8,128)(2,1)S(1)}, u32[]{:S(2)}, u32[]{:S(2)}) collective-permute-start(bf16[256,512]{1,0:T(8,128)(2,1)S(1)} %add_convert_fusion.1), channel_id=1, source_target_pairs={{4,0},{8,4},{12,8},{5,1},{9,5},{13,9},{6,2},{10,6},{14,10},{7,3},{... | collective-permute-start | bytes 786440 | tf_op jit(solution)/shard_map/ppermute | solution.py:20
  104.7 9.3 %collective-permute-done.12 = bf16[256,512]{1,0:T(8,128)(2,1)S(1)} collective-permute-done((bf16[256,512]{1,0:T(8,128)(2,1)S(1)}, bf16[256,512]{1,0:T(8,128)(2,1)S(1)}, u32[]{:S(2)}, u32[]{:S(2)}) %collective-permute-start.12) | collective-permute-done | bytes 262176 | tf_op jit(solution)/shard_map/ppermute | solution.py:20
  114.0 0.8 fusion.7
  114.8 0.3 convert_select_fusion.1
  115.1 1.7 %maximum_multiply_fusion = f32[1152,512]{1,0:T(8,128)} fusion(f32[576,512]{1,0:T(8,128)S(1)} %get-tuple-element.25, f32[576,512]{1,0:T(8,128)S(1)} %get-tuple-element.24), kind=kLoop, calls=%fused_computation | loop fusion | flops 1179648 | bytes 4718592 | tf_op jit(solution)/shard_map/mul | solution.py:261
  (24 shorter events, 0.2 us)
Async XLA Ops:
  1.7 10.0 %copy-start.3 = (bf16[256,1024]{1,0:T(8,128)(2,1)}, bf16[256,1024]{1,0:T(8,128)(2,1)S(1)}, u32[]{:S(2)}) copy-start(bf16[256,1024]{1,0:T(8,128)(2,1)S(1)} %pad_maximum_fusion.refs_8_) | copy-start | bytes 1572868
  1.7 17.2 %collective-permute-start = (bf16[256,1024]{1,0:T(8,128)(2,1)S(1)}, bf16[256,1024]{1,0:T(8,128)(2,1)S(1)}, u32[]{:S(2)}, u32[]{:S(2)}) collective-permute-start(bf16[256,1024]{1,0:T(8,128)(2,1)S(1)} %pad_maximum_fusion.refs_8_), channel_id=1, source_target_pairs={{0,4},{4,8},{8,12},{1,5},{5,9},{9,13},{2,6},{6,10},{10,14},{3,7},{... | collective-permute-start | bytes 1572872 | tf_op jit(solution)/shard_map/ppermute | solution.py:20
  6.7 12.3 %copy-start.5 = (s32[1,12]{1,0:T(1,128)S(1)}, s32[1,12]{1,0:T(1,128)}, u32[]{:S(2)}) copy-start(s32[1,12]{1,0:T(1,128)} %param.11) | copy-start | bytes 148
  8.1 14.9 %collective-permute-start.4 = (bf16[256,1152]{1,0:T(8,128)(2,1)S(1)}, bf16[256,1152]{1,0:T(8,128)(2,1)S(1)}, u32[]{:S(2)}, u32[]{:S(2)}) collective-permute-start(bf16[256,1152]{1,0:T(8,128)(2,1)S(1)} %get-tuple-element.32), channel_id=1, source_target_pairs={{0,2},{2,0},{1,3},{3,1},{4,6},{6,4},{5,7},{7,5},{8,10},{10,8},{9,1... | collective-permute-start | bytes 1769480 | tf_op jit(solution)/shard_map/ppermute | solution.py:25
  9.6 10.3 %collective-permute-start.1 = (bf16[256,1024]{1,0:T(8,128)(2,1)S(1)}, bf16[256,1024]{1,0:T(8,128)(2,1)}, u32[]{:S(2)}, u32[]{:S(2)}) collective-permute-start(bf16[256,1024]{1,0:T(8,128)(2,1)S(1)} %pad_maximum_fusion.refs_8_), channel_id=1, source_target_pairs={{0,1},{2,3},{4,5},{6,7},{8,9},{10,11},{12,13},{14,15},{16,17},{18,... | collective-permute-start | bytes 1572872 | tf_op jit(solution)/shard_map/ppermute | solution.py:20
  11.7 8.2 %collective-permute-start.2 = (bf16[256,1024]{1,0:T(8,128)(2,1)S(1)}, bf16[256,1024]{1,0:T(8,128)(2,1)}, u32[]{:S(2)}, u32[]{:S(2)}) collective-permute-start(bf16[256,1024]{1,0:T(8,128)(2,1)S(1)} %pad_maximum_fusion.refs_8_), channel_id=1, source_target_pairs={{1,8},{5,12},{3,10},{7,14},{17,24},{21,28},{19,26},{23,30}} | collective-permute-start | bytes 1572872 | tf_op jit(solution)/shard_map/ppermute | solution.py:183
  19.0 4.0 %copy-start.8 = (bf16[256,1024]{1,0:T(8,128)(2,1)}, bf16[256,1024]{1,0:T(8,128)(2,1)S(1)}, u32[]{:S(2)}) copy-start(bf16[256,1024]{1,0:T(8,128)(2,1)S(1)} %collective-permute-done.refs_4_) | copy-start | bytes 1572868
  19.0 4.0 %collective-permute-start.3 = (bf16[256,1024]{1,0:T(8,128)(2,1)S(1)}, bf16[256,1024]{1,0:T(8,128)(2,1)}, u32[]{:S(2)}, u32[]{:S(2)}) collective-permute-start(bf16[256,1024]{1,0:T(8,128)(2,1)S(1)} %collective-permute-done.refs_4_), channel_id=1, source_target_pairs={{0,1},{1,0},{2,3},{3,2},{4,5},{5,4},{6,7},{7,6},{8,9},{9,8},{10,11... | collective-permute-start | bytes 1572872 | tf_op jit(solution)/shard_map/ppermute | solution.py:25
  22.9 0.8 copy-start.6
  32.7 4.5 %copy-start.2 = (f32[256,1024]{1,0:T(8,128)S(1)}, f32[256,1024]{1,0:T(8,128)}, u32[]{:S(2)}) copy-start(f32[256,1024]{1,0:T(8,128)} %get-tuple-element.18) | copy-start | bytes 3145732
  34.4 4.2 %copy-start.1 = (f32[256,1024]{1,0:T(8,128)S(1)}, f32[256,1024]{1,0:T(8,128)}, u32[]{:S(2)}) copy-start(f32[256,1024]{1,0:T(8,128)} %get-tuple-element.15) | copy-start | bytes 3145732
  34.4 2.7 %collective-permute-start.7 = (bf16[256,512]{1,0:T(8,128)(2,1)S(1)}, bf16[256,512]{1,0:T(8,128)(2,1)S(1)}, u32[]{:S(2)}, u32[]{:S(2)}) collective-permute-start(bf16[256,512]{1,0:T(8,128)(2,1)S(1)} %get-tuple-element.34), channel_id=1, source_target_pairs={{0,1},{1,0},{2,3},{3,2},{4,5},{5,4},{6,7},{7,6},{8,9},{9,8},{10,11... | collective-permute-start | bytes 786440 | tf_op jit(solution)/shard_map/ppermute | solution.py:25
  35.1 3.5 %collective-permute-start.5 = (bf16[256,512]{1,0:T(8,128)(2,1)S(1)}, bf16[256,512]{1,0:T(8,128)(2,1)S(1)}, u32[]{:S(2)}, u32[]{:S(2)}) collective-permute-start(bf16[256,512]{1,0:T(8,128)(2,1)S(1)} %get-tuple-element.37), channel_id=1, source_target_pairs={{1,0},{3,2},{5,4},{7,6},{9,8},{11,10},{13,12},{15,14},{17,16},{19,... | collective-permute-start | bytes 786440 | tf_op jit(solution)/shard_map/ppermute | solution.py:20
  36.4 2.2 %collective-permute-start.6 = (bf16[256,512]{1,0:T(8,128)(2,1)S(1)}, bf16[256,512]{1,0:T(8,128)(2,1)S(1)}, u32[]{:S(2)}, u32[]{:S(2)}) collective-permute-start(bf16[256,512]{1,0:T(8,128)(2,1)S(1)} %get-tuple-element.36), channel_id=1, source_target_pairs={{8,1},{12,5},{10,3},{14,7},{24,17},{28,21},{26,19},{30,23}} | collective-permute-start | bytes 786440 | tf_op jit(solution)/shard_map/ppermute | solution.py:207
  37.3 15.7 %collective-permute-start.8 = (bf16[256,512]{1,0:T(8,128)(2,1)S(1)}, bf16[256,512]{1,0:T(8,128)(2,1)S(1)}, u32[]{:S(2)}, u32[]{:S(2)}) collective-permute-start(bf16[256,512]{1,0:T(8,128)(2,1)S(1)} %get-tuple-element.39), channel_id=1, source_target_pairs={{4,0},{8,4},{12,8},{5,1},{9,5},{13,9},{6,2},{10,6},{14,10},{7,3},{... | collective-permute-start | bytes 786440 | tf_op jit(solution)/shard_map/ppermute | solution.py:20
  38.6 23.4 %copy-start.7 = (bf16[256,1152]{1,0:T(8,128)(2,1)S(1)}, bf16[256,1152]{1,0:T(8,128)(2,1)}, u32[]{:S(2)}) copy-start(bf16[256,1152]{1,0:T(8,128)(2,1)} %copy-done.6) | copy-start | bytes 1769476
  53.1 9.7 %copy-start.4 = (bf16[256,512]{1,0:T(8,128)(2,1)}, bf16[256,512]{1,0:T(8,128)(2,1)S(1)}, u32[]{:S(2)}) copy-start(bf16[256,512]{1,0:T(8,128)(2,1)S(1)} %convert_add_fusion.1) | copy-start | bytes 786436
  53.1 8.9 %collective-permute-start.13 = (bf16[256,512]{1,0:T(8,128)(2,1)S(1)}, bf16[256,512]{1,0:T(8,128)(2,1)S(1)}, u32[]{:S(2)}, u32[]{:S(2)}) collective-permute-start(bf16[256,512]{1,0:T(8,128)(2,1)S(1)} %convert_add_fusion.1), channel_id=1, source_target_pairs={{0,2},{2,0},{1,3},{3,1},{4,6},{6,4},{5,7},{7,5},{8,10},{10,8},{9,1... | collective-permute-start | bytes 786440 | tf_op jit(solution)/shard_map/ppermute | solution.py:25
  62.8 1.4 %copy-start = (f32[1152,512]{1,0:T(8,128)}, f32[1152,512]{1,0:T(8,128)S(1)}, u32[]{:S(2)}) copy-start(f32[1152,512]{1,0:T(8,128)S(1)} %fusion) | copy-start | bytes 7077892
  64.3 2.1 %collective-permute-start.14 = (bf16[576,512]{1,0:T(8,128)(2,1)S(1)}, bf16[576,512]{1,0:T(8,128)(2,1)S(1)}, u32[]{:S(2)}, u32[]{:S(2)}) collective-permute-start(bf16[576,512]{1,0:T(8,128)(2,1)S(1)} %dynamic-slice_convert_fusion), channel_id=1, source_target_pairs={{0,1},{1,0},{2,3},{3,2},{4,5},{5,4},{6,7},{7,6},{8,9},{9,8},{10,11... | collective-permute-start | bytes 1769480 | tf_op jit(solution)/shard_map/ppermute | solution.py:25
  68.6 9.1 %collective-permute-start.15 = (bf16[144,512]{1,0:T(8,128)(2,1)}, bf16[144,512]{1,0:T(8,128)(2,1)S(1)}, u32[]{:S(2)}, u32[]{:S(2)}) collective-permute-start(bf16[144,512]{1,0:T(8,128)(2,1)} %get-tuple-element.28), channel_id=1, source_target_pairs={{0,4},{4,8},{8,12},{12,0},{1,5},{5,9},{9,13},{13,1},{2,6},{6,10},{... | collective-permute-start | bytes 442376 | tf_op jit(solution)/shard_map/ppermute | solution.py:25
  73.1 9.8 %collective-permute-start.16 = (bf16[144,512]{1,0:T(8,128)(2,1)S(1)}, bf16[144,512]{1,0:T(8,128)(2,1)S(1)}, u32[]{:S(2)}, u32[]{:S(2)}) collective-permute-start(bf16[144,512]{1,0:T(8,128)(2,1)S(1)} %get-tuple-element.30), channel_id=1, source_target_pairs={{0,8},{4,12},{8,0},{12,4},{1,9},{5,13},{9,1},{13,5},{2,10},{6,14},... | collective-permute-start | bytes 442376 | tf_op jit(solution)/shard_map/ppermute | solution.py:25
  73.1 10.0 %collective-permute-start.17 = (bf16[144,512]{1,0:T(8,128)(2,1)S(1)}, bf16[144,512]{1,0:T(8,128)(2,1)S(1)}, u32[]{:S(2)}, u32[]{:S(2)}) collective-permute-start(bf16[144,512]{1,0:T(8,128)(2,1)S(1)} %get-tuple-element.29), channel_id=1, source_target_pairs={{0,12},{4,0},{8,4},{12,8},{1,13},{5,1},{9,5},{13,9},{2,14},{6,2},{... | collective-permute-start | bytes 442376 | tf_op jit(solution)/shard_map/ppermute | solution.py:25
  75.5 29.2 %collective-permute-start.10 = (bf16[256,512]{1,0:T(8,128)(2,1)S(1)}, bf16[256,512]{1,0:T(8,128)(2,1)S(1)}, u32[]{:S(2)}, u32[]{:S(2)}) collective-permute-start(bf16[256,512]{1,0:T(8,128)(2,1)S(1)} %get-tuple-element.21), channel_id=1, source_target_pairs={{8,1},{12,5},{10,3},{14,7},{24,17},{28,21},{26,19},{30,23}} | collective-permute-start | bytes 786440 | tf_op jit(solution)/shard_map/ppermute | solution.py:207
  76.2 28.5 %collective-permute-start.9 = (bf16[256,512]{1,0:T(8,128)(2,1)S(1)}, bf16[256,512]{1,0:T(8,128)(2,1)S(1)}, u32[]{:S(2)}, u32[]{:S(2)}) collective-permute-start(bf16[256,512]{1,0:T(8,128)(2,1)S(1)} %get-tuple-element.20), channel_id=1, source_target_pairs={{1,0},{3,2},{5,4},{7,6},{9,8},{11,10},{13,12},{15,14},{17,16},{19,... | collective-permute-start | bytes 786440 | tf_op jit(solution)/shard_map/ppermute | solution.py:20
  83.3 10.5 %collective-permute-start.18 = (bf16[144,512]{1,0:T(8,128)(2,1)S(1)}, bf16[144,512]{1,0:T(8,128)(2,1)S(1)}, u32[]{:S(2)}, u32[]{:S(2)}) collective-permute-start(bf16[144,512]{1,0:T(8,128)(2,1)S(1)} %get-tuple-element.26), channel_id=1, source_target_pairs={{0,4},{4,8},{8,12},{12,0},{1,5},{5,9},{9,13},{13,1},{2,6},{6,10},{... | collective-permute-start | bytes 442376 | tf_op jit(solution)/shard_map/ppermute | solution.py:25
  89.6 13.7 %collective-permute-start.11 = (bf16[256,512]{1,0:T(8,128)(2,1)S(1)}, bf16[256,512]{1,0:T(8,128)(2,1)S(1)}, u32[]{:S(2)}, u32[]{:S(2)}) collective-permute-start(bf16[256,512]{1,0:T(8,128)(2,1)S(1)} %select_convert_fusion), channel_id=1, source_target_pairs={{0,1},{1,0},{2,3},{3,2},{4,5},{5,4},{6,7},{7,6},{8,9},{9,8},{10,11... | collective-permute-start | bytes 786440 | tf_op jit(solution)/shard_map/ppermute | solution.py:25
  89.7 12.7 %collective-permute-start.19 = (bf16[144,512]{1,0:T(8,128)(2,1)S(1)}, bf16[144,512]{1,0:T(8,128)(2,1)S(1)}, u32[]{:S(2)}, u32[]{:S(2)}) collective-permute-start(bf16[144,512]{1,0:T(8,128)(2,1)S(1)} %get-tuple-element.26), channel_id=1, source_target_pairs={{0,8},{4,12},{8,0},{12,4},{1,9},{5,13},{9,1},{13,5},{2,10},{6,14},... | collective-permute-start | bytes 442376 | tf_op jit(solution)/shard_map/ppermute | solution.py:25
  93.8 9.3 %collective-permute-start.20 = (bf16[144,512]{1,0:T(8,128)(2,1)S(1)}, bf16[144,512]{1,0:T(8,128)(2,1)S(1)}, u32[]{:S(2)}, u32[]{:S(2)}) collective-permute-start(bf16[144,512]{1,0:T(8,128)(2,1)S(1)} %get-tuple-element.26), channel_id=1, source_target_pairs={{0,12},{4,0},{8,4},{12,8},{1,13},{5,1},{9,5},{13,9},{2,14},{6,2},{... | collective-permute-start | bytes 442376 | tf_op jit(solution)/shard_map/ppermute | solution.py:25
  103.2 11.6 %collective-permute-start.21 = (bf16[576,512]{1,0:T(8,128)(2,1)S(1)}, bf16[576,512]{1,0:T(8,128)(2,1)S(1)}, u32[]{:S(2)}, u32[]{:S(2)}) collective-permute-start(bf16[576,512]{1,0:T(8,128)(2,1)S(1)} %convert_element_type.119), channel_id=1, source_target_pairs={{0,1},{1,0},{2,3},{3,2},{4,5},{5,4},{6,7},{7,6},{8,9},{9,8},{10,11... | collective-permute-start | bytes 1769480 | tf_op jit(solution)/shard_map/ppermute | solution.py:25
  103.4 10.6 %collective-permute-start.12 = (bf16[256,512]{1,0:T(8,128)(2,1)S(1)}, bf16[256,512]{1,0:T(8,128)(2,1)S(1)}, u32[]{:S(2)}, u32[]{:S(2)}) collective-permute-start(bf16[256,512]{1,0:T(8,128)(2,1)S(1)} %add_convert_fusion.1), channel_id=1, source_target_pairs={{4,0},{8,4},{12,8},{5,1},{9,5},{13,9},{6,2},{10,6},{14,10},{7,3},{... | collective-permute-start | bytes 786440 | tf_op jit(solution)/shard_map/ppermute | solution.py:20

commit v7 on v5

--- a/solution.py
+++ b/solution.py
@@ -1,4 +1,5 @@
 import functools
+import math
 
 import jax
 import jax.numpy as jnp
@@ -49,7 +50,7 @@
     return jnp.max(jnp.where(covered, starts[None, :], 0), axis=1)
 
 
-def attention_kernel(*refs, heads, kv_heads, margin, slots, blocks):
+def attention_kernel(*refs, heads, kv_heads, margin, slots, blocks, chip_outputs):
     flag_ref, lo_ref, q_ref, do_ref = refs[:4]
     block_refs = refs[4 : 4 + blocks]
     kv_ref, dkv_ref = refs[-2:]
@@ -94,8 +95,8 @@
             scores = lax.dot_general(query_h, key_g, NT, preferred_element_type=jnp.float32) * scale
             scores = jnp.where(allowed, scores, -1e30)
             largest = jnp.max(scores, axis=1, keepdims=True)
-            raised = jnp.where(allowed, jnp.exp(scores - largest), 0.0)
-            probs = raised / jnp.sum(raised, axis=1, keepdims=True)
+            raised = jnp.exp(scores - largest)
+            probs = raised * (1.0 / jnp.sum(raised, axis=1, keepdims=True))
             grad_probs = lax.dot_general(grad_h, value_g, NT, preferred_element_type=jnp.float32)
             row_dot = jnp.sum(probs * grad_probs, axis=1, keepdims=True)
             grad_scores = (probs * (grad_probs - row_dot) * scale).astype(jnp.bfloat16)
@@ -109,11 +110,32 @@
             grad_v = term_v if grad_v is None else grad_v + term_v
         dkv_ref[:, k_cols] = grad_k
         dkv_ref[:, v_cols] = grad_v
-    for index, out_ref in enumerate(out_refs):
-        out_ref[...] = dkv_ref[pl.ds(index * block_rows, block_rows), :]
-
-
-def attention(flag, lo_rel, queries, grads, kv_blocks, slots, heads, kv_heads, margin, early):
+    def slot_rows(index):
+        return dkv_ref[pl.ds(index * block_rows, block_rows), :]
+
+    if chip_outputs:
+        mate_ref, other_ref, two_ref, own_ref = out_refs
+        two_ref[...] = slot_rows(1)
+        own_ref[...] = slot_rows(3)
+
+        @pl.when(flag == 0)
+        def _():
+            mate_ref[...] = slot_rows(2).astype(mate_ref.dtype)
+            other_ref[...] = slot_rows(0).astype(other_ref.dtype)
+
+        @pl.when(flag != 0)
+        def _():
+            mate_ref[...] = slot_rows(0).astype(mate_ref.dtype)
+            other_ref[...] = slot_rows(2).astype(other_ref.dtype)
+
+    else:
+        for index, out_ref in enumerate(out_refs):
+            out_ref[...] = slot_rows(index)
+
+
+def attention(
+    flag, lo_rel, queries, grads, kv_blocks, slots, heads, kv_heads, margin, early, chip_outputs
+):
     rows, width = queries.shape
     blocks = len(kv_blocks)
     block_rows, kv_cols = kv_blocks[0].shape
@@ -125,7 +147,12 @@
         margin=margin,
         slots=tuple(slots),
         blocks=blocks,
-    )
+        chip_outputs=chip_outputs,
+    )
+    if chip_outputs:
+        piece_types = [jnp.bfloat16, jnp.bfloat16, jnp.float32, jnp.float32]
+    else:
+        piece_types = [jnp.float32] * len(slots)
     vmem = pl.BlockSpec(memory_space=pltpu.VMEM)
     smem = pl.BlockSpec(memory_space=pltpu.SMEM)
     flops = 2 * 5 * heads * rows * keys * HEAD_DIM
@@ -133,7 +160,7 @@
     return pl.pallas_call(
         kernel,
         out_shape=(jax.ShapeDtypeStruct((rows, width), jnp.bfloat16),)
-        + tuple(jax.ShapeDtypeStruct((block_rows, kv_cols), jnp.float32) for _ in slots),
+        + tuple(jax.ShapeDtypeStruct((block_rows, kv_cols), kind) for kind in piece_types),
         in_specs=[smem] + [vmem] * (3 + blocks) + [pl.BlockSpec(memory_space=pl.ANY)] * len(early),
         out_specs=(vmem,) * (1 + len(slots)),
         scratch_shapes=[
@@ -195,6 +222,7 @@
     grad_q, *grad_pieces = attention(
         flag, lo_rel, query_heads[0], grad_out[0], kv_blocks, slots, heads, kv_heads, margin,
         inputs[1:],
+        chip_route,
     )
 
     def low(value):
@@ -202,10 +230,10 @@
 
     if chip_route:
         back = [(target, source) for source, target in across]
-        g3, g2, g1, g0 = grad_pieces
-        from_far = lax.ppermute(low(g3), RING, back).astype(jnp.float32)
-        from_mate = rotated(low(jnp.where(sub_at == 0, g1, g3)), "sub", 1).astype(jnp.float32)
-        from_high = passed_along(low(g1), "sub", -1).astype(jnp.float32)
+        to_mate, to_other, g2, g0 = grad_pieces
+        from_far = lax.ppermute(to_other, RING, back).astype(jnp.float32)
+        from_mate = rotated(to_mate, "sub", 1).astype(jnp.float32)
+        from_high = passed_along(to_other, "sub", -1).astype(jnp.float32)
         two_back_sum = g2 + from_mate
         from_next = passed_along(low(two_back_sum), "ctx", -1).astype(jnp.float32)
         total = g0 + from_high + from_far + from_next
@@ -228,6 +256,10 @@
     stacked_inputs = jnp.concatenate(inputs, axis=0)
     stacked_values = jnp.concatenate(values, axis=0)
     shard = lax.dot_general(stacked_inputs, stacked_values, TN, preferred_element_type=jnp.float32)
+    token_scale = float(fsdp_count * lax.axis_size(RING) * block_rows) ** (-0.5)
+    scale_early = token_scale == 2.0 ** round(math.log2(token_scale))
+    if scale_early:
+        shard = shard * token_scale
 
     sub_count = lax.axis_size("sub")
     sub_at = lax.axis_index("sub")
@@ -245,12 +277,13 @@
         weight_v = jnp.concatenate([first, second], axis=0)
     else:
         weight_v = lax.all_gather(reduced, "sub", axis=0, tiled=True)
-    token_scale = float(fsdp_count * lax.axis_size(RING) * block_rows) ** (-0.5)
+    if not scale_early:
+        weight_v = weight_v * token_scale
     return (
         grad_q[None],
         grad_key[None],
         grad_value[None],
-        weight_v * token_scale,
+        weight_v,
     )
 
 

time: 115 us -> 113 us (0.983)
  waiting for transfers between devices: 60.9 us -> 59.6 us
    mul x1 -> x0, other arithmetic: 1.67 us -> none  [body(): weight_v * token_scale]
    concatenate x0 -> x1, other arithmetic: none -> 1.61 us  [body(): weight_v = jnp.concatenate([first, second], axis=0)]
    ppermute x4, waiting for transfers between devices: 30.3 us -> 29 us  [passed_along(): lax.ppermute(value, axis, [(source, source + steps) for source in range(f...]
    unnamed x22 -> x16, local copies, waits for them, and re-layouts: 2.63 us -> 2.23 us
  transfers between devices with their start and end apart: 18 -> 18, of which waited for: 12 -> 11; matrix products, arithmetic and copies ran while one was open for 2% -> 3% of each run, Pallas kernels for 0% -> 0%
where the time goes in v7:
time: 113 us; the launch traced here: 112 us
  waiting for transfers between devices  59.6 us (53%)
  starting transfers between devices  29.8 us (26%)
  Pallas kernels  8.83 us (8%)
  other arithmetic  7.16 us (6%)
  local copies, waits for them, and re-layouts  4.83 us (4%)
    ppermute x12, waiting for transfers between devices, rotated(): lax.ppermute(value, axis, [(source, (source + steps) % count) for source...  30.5 us
    ppermute x4, waiting for transfers between devices, passed_along(): lax.ppermute(value, axis, [(source, source + steps) for source in range(f...  29 us
    ppermute x12, starting transfers between devices, rotated(): lax.ppermute(value, axis, [(source, (source + steps) % count) for source...  18.8 us
    ppermute x4, starting transfers between devices, passed_along(): lax.ppermute(value, axis, [(source, source + steps) for source in range(f...  8.84 us
    pallas_call x1, Pallas kernels, attention(): pl.pallas_call(kernel, out_shape=(jax.ShapeDtypeStruct((rows, width), jnp...  8.83 us
  transfers between devices with their start and end apart: 18, of which 11 were waited for; matrix products, arithmetic and copies ran while one was open for 3% of the time, Pallas kernels for 0%

profile of v7, /device:TPU:0, one launch (start us, length us, event | category | flops | bytes accessed | tf_op | source)
XLA Modules:
  0.0 112.0 jit_solution(7023423354142190755)
XLA Ops:
  0.6 1.1 pad_maximum_fusion.1.refs_8_
  1.7 0.0 copy-start.2
  1.7 5.0 %collective-permute-start = (bf16[256,1024]{1,0:T(8,128)(2,1)S(1)}, bf16[256,1024]{1,0:T(8,128)(2,1)S(1)}, u32[]{:S(2)}, u32[]{:S(2)}) collective-permute-start(bf16[256,1024]{1,0:T(8,128)(2,1)S(1)} %pad_maximum_fusion.1.refs_8_), channel_id=1, source_target_pairs={{0,4},{4,8},{8,12},{1,5},{5,9},{9,13},{2,6},{6,10},{10,14},{3,7},{... | collective-permute-start | bytes 1572872 | tf_op jit(solution)/shard_map/ppermute | solution.py:21
  6.7 0.0 copy-start.3
  6.7 1.3 %dynamic-slice_bitcast_fusion = (bf16[256,1152]{1,0:T(8,128)(2,1)S(1)}, bf16[256,1152]{1,0:T(8,128)(2,1)S(1)}) fusion(bf16[1,256,2304]{2,1,0:T(8,128)(2,1)} %param.6, s32[]{:T(128)S(6)} %select_n.89, s32[]{:T(128)S(6)} %select_n.87), kind=kLoop, calls=%fused_computation.11 | loop fusion | bytes 2359304 | tf_op jit(solution)/shard_map/dynamic_slice | solution.py:191
  8.1 1.6 %collective-permute-start.4 = (bf16[256,1152]{1,0:T(8,128)(2,1)S(1)}, bf16[256,1152]{1,0:T(8,128)(2,1)S(1)}, u32[]{:S(2)}, u32[]{:S(2)}) collective-permute-start(bf16[256,1152]{1,0:T(8,128)(2,1)S(1)} %get-tuple-element.22), channel_id=1, source_target_pairs={{0,2},{2,0},{1,3},{3,1},{4,6},{6,4},{5,7},{7,5},{8,10},{10,8},{9,1... | collective-permute-start | bytes 1769480 | tf_op jit(solution)/shard_map/ppermute | solution.py:26
  9.6 1.3 %collective-permute-start.1 = (bf16[256,1024]{1,0:T(8,128)(2,1)S(1)}, bf16[256,1024]{1,0:T(8,128)(2,1)S(1)}, u32[]{:S(2)}, u32[]{:S(2)}) collective-permute-start(bf16[256,1024]{1,0:T(8,128)(2,1)S(1)} %pad_maximum_fusion.1.refs_8_), channel_id=1, source_target_pairs={{0,1},{2,3},{4,5},{6,7},{8,9},{10,11},{12,13},{14,15},{16,17},{18,... | collective-permute-start | bytes 1572872 | tf_op jit(solution)/shard_map/ppermute | solution.py:21
  10.9 0.0 copy-done.2
  11.0 1.5 %collective-permute-start.2 = (bf16[256,1024]{1,0:T(8,128)(2,1)S(1)}, bf16[256,1024]{1,0:T(8,128)(2,1)}, u32[]{:S(2)}, u32[]{:S(2)}) collective-permute-start(bf16[256,1024]{1,0:T(8,128)(2,1)S(1)} %pad_maximum_fusion.1.refs_8_), channel_id=1, source_target_pairs={{1,8},{5,12},{3,10},{7,14},{17,24},{21,28},{19,26},{23,30}} | collective-permute-start | bytes 1572872 | tf_op jit(solution)/shard_map/ppermute | solution.py:210
  12.4 6.5 %collective-permute-done.refs_4_ = bf16[256,1024]{1,0:T(8,128)(2,1)S(1)} collective-permute-done((bf16[256,1024]{1,0:T(8,128)(2,1)S(1)}, bf16[256,1024]{1,0:T(8,128)(2,1)S(1)}, u32[]{:S(2)}, u32[]{:S(2)}) %collective-permute-start) | collective-permute-done | bytes 524320 | tf_op jit(solution)/shard_map/ppermute | solution.py:21
  19.0 0.0 collective-permute-start.3
  19.0 0.0 copy-done.3
  19.0 0.1 select_reduce_fusion
  19.1 0.1 copy.13
  19.2 0.7 subtract_add_fusion.refs_1_
  19.9 0.0 collective-permute-done.1.refs_5_
  19.9 0.0 collective-permute-done.2.refs_6_
  19.9 3.0 %collective-permute-done.4.refs_9_ = bf16[256,1152]{1,0:T(8,128)(2,1)S(1)} collective-permute-done((bf16[256,1152]{1,0:T(8,128)(2,1)S(1)}, bf16[256,1152]{1,0:T(8,128)(2,1)S(1)}, u32[]{:S(2)}, u32[]{:S(2)}) %collective-permute-start.4) | collective-permute-done | bytes 589856 | tf_op jit(solution)/shard_map/ppermute | solution.py:26
  22.9 0.0 collective-permute-done.3.refs_7_
  22.9 0.0 copy-done.6
  22.9 0.0 copy-done.7
  22.9 0.8 copy-done.4
  23.7 8.8 %shard_map.93 = (bf16[256,1024]{1,0:T(8,128)(2,1)}, bf16[256,1024]{1,0:T(8,128)(2,1)}, bf16[256,1024]{1,0:T(8,128)(2,1)}, f32[256,1024]{1,0:T(8,128)}, f32[256,1024]{1,0:T(8,128)}) custom-call(s32[1]{0:T(128)} %bitcast.refs_0_, s32[256,1]{1,0:T(8,128)} %subtract_add_fusion.refs_1_, bf16[256,1024]{1,0:T(8,128)(2,1)} %bitcast.20, bf16[256,1024]{1,0:T(8,128)(2,1)} %bitcast.21, ...), custom_call_target="tpu_custom_call" | custom-call | flops 2684354560 | bytes 7864320 | tf_op jit(solution)/shard_map/pallas_call | solution.py:160
  32.6 0.7 collective-permute-start.7
  33.3 1.3 %collective-permute-start.5 = (bf16[256,1024]{1,0:T(8,128)(2,1)}, bf16[256,1024]{1,0:T(8,128)(2,1)S(1)}, u32[]{:S(2)}, u32[]{:S(2)}) collective-permute-start(bf16[256,1024]{1,0:T(8,128)(2,1)} %get-tuple-element.11), channel_id=1, source_target_pairs={{1,0},{3,2},{5,4},{7,6},{9,8},{11,10},{13,12},{15,14},{17,16},{19,... | collective-permute-start | bytes 1572872 | tf_op jit(solution)/shard_map/ppermute | solution.py:21
  34.6 0.7 collective-permute-start.6
  35.3 0.0 collective-permute-done.7
  35.3 1.4 %add_convert_fusion.1 = bf16[256,1024]{1,0:T(8,128)(2,1)S(1)} fusion(f32[256,1024]{1,0:T(8,128)} %get-tuple-element.12, bf16[256,1024]{1,0:T(8,128)(2,1)S(1)} %collective-permute-done.7), kind=kLoop, calls=%fused_computation.10 | loop fusion | flops 786432 | bytes 2097152 | tf_op jit(solution)/shard_map/convert_element_type | solution.py:229
  36.7 1.3 %collective-permute-start.8 = (bf16[256,1024]{1,0:T(8,128)(2,1)S(1)}, bf16[256,1024]{1,0:T(8,128)(2,1)S(1)}, u32[]{:S(2)}, u32[]{:S(2)}) collective-permute-start(bf16[256,1024]{1,0:T(8,128)(2,1)S(1)} %add_convert_fusion.1), channel_id=1, source_target_pairs={{4,0},{8,4},{12,8},{5,1},{9,5},{13,9},{6,2},{10,6},{14,10},{7,3},{... | collective-permute-start | bytes 1572872 | tf_op jit(solution)/shard_map/ppermute | solution.py:21
  38.0 0.0 collective-permute-done.5
  38.0 0.0 collective-permute-done.6
  38.0 22.5 %collective-permute-done.8 = bf16[256,1024]{1,0:T(8,128)(2,1)S(1)} collective-permute-done((bf16[256,1024]{1,0:T(8,128)(2,1)S(1)}, bf16[256,1024]{1,0:T(8,128)(2,1)S(1)}, u32[]{:S(2)}, u32[]{:S(2)}) %collective-permute-start.8) | collective-permute-done | bytes 524320 | tf_op jit(solution)/shard_map/ppermute | solution.py:21
  60.5 0.0 copy-done.1
  60.5 0.3 add_convert_fusion
  60.8 0.9 fusion.9
  61.7 1.5 %collective-permute-start.9 = (bf16[256,512]{1,0:T(8,128)(2,1)S(1)}, bf16[256,512]{1,0:T(8,128)(2,1)S(1)}, u32[]{:S(2)}, u32[]{:S(2)}) collective-permute-start(bf16[256,512]{1,0:T(8,128)(2,1)S(1)} %get-tuple-element.23), channel_id=1, source_target_pairs={{0,2},{2,0},{1,3},{3,1},{4,6},{6,4},{5,7},{7,5},{8,10},{10,8},{9,1... | collective-permute-start | bytes 786440 | tf_op jit(solution)/shard_map/ppermute | solution.py:26
  63.2 6.8 %collective-permute-done.9 = bf16[256,512]{1,0:T(8,128)(2,1)S(1)} collective-permute-done((bf16[256,512]{1,0:T(8,128)(2,1)S(1)}, bf16[256,512]{1,0:T(8,128)(2,1)S(1)}, u32[]{:S(2)}, u32[]{:S(2)}) %collective-permute-start.9) | collective-permute-done | bytes 262176 | tf_op jit(solution)/shard_map/ppermute | solution.py:26
  70.0 0.8 convolution_multiply_fusion
  70.8 0.0 copy-start
  70.9 1.4 %copy-done = f32[1152,512]{1,0:T(8,128)} copy-done((f32[1152,512]{1,0:T(8,128)}, f32[1152,512]{1,0:T(8,128)S(1)}, u32[]{:S(2)}) %copy-start) | copy-done | bytes 2359320
  72.3 0.1 dynamic-slice_convert_fusion
  72.3 0.1 collective-permute-start.10
  72.5 1.9 %collective-permute-done.10 = bf16[576,512]{1,0:T(8,128)(2,1)S(1)} collective-permute-done((bf16[576,512]{1,0:T(8,128)(2,1)S(1)}, bf16[576,512]{1,0:T(8,128)(2,1)S(1)}, u32[]{:S(2)}, u32[]{:S(2)}) %collective-permute-start.10) | collective-permute-done | bytes 589856 | tf_op jit(solution)/shard_map/ppermute | solution.py:26
  74.4 1.4 %convert_add_fusion = f32[576,512]{1,0:T(8,128)S(1)} fusion(bf16[576,512]{1,0:T(8,128)(2,1)S(1)} %collective-permute-done.10, f32[1152,512]{1,0:T(8,128)} %copy-done, s32[]{:T(128)S(6)} %select_n.90), kind=kLoop, calls=%fused_computation.7 | loop fusion | flops 589824 | bytes 2949124 | tf_op jit(solution)/shard_map/add | solution.py:271
  75.9 0.1 dynamic-slice_convert_fusion.3
  75.9 5.6 %collective-permute-start.11 = (bf16[144,512]{1,0:T(8,128)(2,1)S(1)}, bf16[144,512]{1,0:T(8,128)(2,1)S(1)}, u32[]{:S(2)}, u32[]{:S(2)}) collective-permute-start(bf16[144,512]{1,0:T(8,128)(2,1)S(1)} %get-tuple-element.18), channel_id=1, source_target_pairs={{0,4},{4,8},{8,12},{12,0},{1,5},{5,9},{9,13},{13,1},{2,6},{6,10},{... | collective-permute-start | bytes 442376 | tf_op jit(solution)/shard_map/ppermute | solution.py:26
  81.6 0.0 collective-permute-start.12
  81.6 2.4 %collective-permute-start.13 = (bf16[144,512]{1,0:T(8,128)(2,1)S(1)}, bf16[144,512]{1,0:T(8,128)(2,1)S(1)}, u32[]{:S(2)}, u32[]{:S(2)}) collective-permute-start(bf16[144,512]{1,0:T(8,128)(2,1)S(1)} %get-tuple-element.19), channel_id=1, source_target_pairs={{0,12},{4,0},{8,4},{12,8},{1,13},{5,1},{9,5},{13,9},{2,14},{6,2},{... | collective-permute-start | bytes 442376 | tf_op jit(solution)/shard_map/ppermute | solution.py:26
  84.0 1.8 %collective-permute-done.11 = bf16[144,512]{1,0:T(8,128)(2,1)S(1)} collective-permute-done((bf16[144,512]{1,0:T(8,128)(2,1)S(1)}, bf16[144,512]{1,0:T(8,128)(2,1)S(1)}, u32[]{:S(2)}, u32[]{:S(2)}) %collective-permute-start.11) | collective-permute-done | bytes 147488 | tf_op jit(solution)/shard_map/ppermute | solution.py:26
  85.8 5.3 %collective-permute-done.12 = bf16[144,512]{1,0:T(8,128)(2,1)S(1)} collective-permute-done((bf16[144,512]{1,0:T(8,128)(2,1)S(1)}, bf16[144,512]{1,0:T(8,128)(2,1)S(1)}, u32[]{:S(2)}, u32[]{:S(2)}) %collective-permute-start.12) | collective-permute-done | bytes 147488 | tf_op jit(solution)/shard_map/ppermute | solution.py:26
  91.1 0.2 collective-permute-done.13
  91.3 0.1 broadcast_in_dim.28
  91.5 0.1 fusion.6
  91.6 3.5 %collective-permute-start.14 = (bf16[144,512]{1,0:T(8,128)(2,1)S(1)}, bf16[144,512]{1,0:T(8,128)(2,1)S(1)}, u32[]{:S(2)}, u32[]{:S(2)}) collective-permute-start(bf16[144,512]{1,0:T(8,128)(2,1)S(1)} %get-tuple-element.16), channel_id=1, source_target_pairs={{0,4},{4,8},{8,12},{12,0},{1,5},{5,9},{9,13},{13,1},{2,6},{6,10},{... | collective-permute-start | bytes 442376 | tf_op jit(solution)/shard_map/ppermute | solution.py:26
  95.0 3.4 %collective-permute-start.15 = (bf16[144,512]{1,0:T(8,128)(2,1)S(1)}, bf16[144,512]{1,0:T(8,128)(2,1)S(1)}, u32[]{:S(2)}, u32[]{:S(2)}) collective-permute-start(bf16[144,512]{1,0:T(8,128)(2,1)S(1)} %get-tuple-element.16), channel_id=1, source_target_pairs={{0,8},{4,12},{8,0},{12,4},{1,9},{5,13},{9,1},{13,5},{2,10},{6,14},... | collective-permute-start | bytes 442376 | tf_op jit(solution)/shard_map/ppermute | solution.py:26
  98.4 0.0 collective-permute-start.16
  98.4 4.2 %collective-permute-done.14 = bf16[144,512]{1,0:T(8,128)(2,1)S(1)} collective-permute-done((bf16[144,512]{1,0:T(8,128)(2,1)S(1)}, bf16[144,512]{1,0:T(8,128)(2,1)S(1)}, u32[]{:S(2)}, u32[]{:S(2)}) %collective-permute-start.14) | collective-permute-done | bytes 147488 | tf_op jit(solution)/shard_map/ppermute | solution.py:26
  102.7 5.2 %collective-permute-done.15 = bf16[144,512]{1,0:T(8,128)(2,1)S(1)} collective-permute-done((bf16[144,512]{1,0:T(8,128)(2,1)S(1)}, bf16[144,512]{1,0:T(8,128)(2,1)S(1)}, u32[]{:S(2)}, u32[]{:S(2)}) %collective-permute-start.15) | collective-permute-done | bytes 147488 | tf_op jit(solution)/shard_map/ppermute | solution.py:26
  107.9 0.0 collective-permute-done.16
  108.0 0.1 convert_element_type.78
  108.0 0.1 collective-permute-start.17
  108.1 2.0 %collective-permute-done.17 = bf16[576,512]{1,0:T(8,128)(2,1)S(1)} collective-permute-done((bf16[576,512]{1,0:T(8,128)(2,1)S(1)}, bf16[576,512]{1,0:T(8,128)(2,1)S(1)}, u32[]{:S(2)}, u32[]{:S(2)}) %collective-permute-start.17) | collective-permute-done | bytes 589856 | tf_op jit(solution)/shard_map/ppermute | solution.py:26
  110.1 0.3 convert_select_fusion.1
  110.4 1.6 %pad_maximum_fusion = f32[1152,512]{1,0:T(8,128)} fusion(f32[576,512]{1,0:T(8,128)S(1)} %get-tuple-element.15, f32[576,512]{1,0:T(8,128)S(1)} %get-tuple-element.14), kind=kLoop, calls=%fused_computation.1 | loop fusion | flops 589824 | bytes 4718592 | tf_op jit(solution)/shard_map/concatenate | solution.py:277
  (10 shorter events, 0.1 us)
Async XLA Ops:
  1.7 9.2 %copy-start.2 = (bf16[256,1024]{1,0:T(8,128)(2,1)}, bf16[256,1024]{1,0:T(8,128)(2,1)S(1)}, u32[]{:S(2)}) copy-start(bf16[256,1024]{1,0:T(8,128)(2,1)S(1)} %pad_maximum_fusion.1.refs_8_) | copy-start | bytes 1572868
  1.7 17.2 %collective-permute-start = (bf16[256,1024]{1,0:T(8,128)(2,1)S(1)}, bf16[256,1024]{1,0:T(8,128)(2,1)S(1)}, u32[]{:S(2)}, u32[]{:S(2)}) collective-permute-start(bf16[256,1024]{1,0:T(8,128)(2,1)S(1)} %pad_maximum_fusion.1.refs_8_), channel_id=1, source_target_pairs={{0,4},{4,8},{8,12},{1,5},{5,9},{9,13},{2,6},{6,10},{10,14},{3,7},{... | collective-permute-start | bytes 1572872 | tf_op jit(solution)/shard_map/ppermute | solution.py:21
  6.7 12.3 %copy-start.3 = (s32[1,12]{1,0:T(1,128)S(1)}, s32[1,12]{1,0:T(1,128)}, u32[]{:S(2)}) copy-start(s32[1,12]{1,0:T(1,128)} %param.11) | copy-start | bytes 148
  8.1 14.9 %collective-permute-start.4 = (bf16[256,1152]{1,0:T(8,128)(2,1)S(1)}, bf16[256,1152]{1,0:T(8,128)(2,1)S(1)}, u32[]{:S(2)}, u32[]{:S(2)}) collective-permute-start(bf16[256,1152]{1,0:T(8,128)(2,1)S(1)} %get-tuple-element.22), channel_id=1, source_target_pairs={{0,2},{2,0},{1,3},{3,1},{4,6},{6,4},{5,7},{7,5},{8,10},{10,8},{9,1... | collective-permute-start | bytes 1769480 | tf_op jit(solution)/shard_map/ppermute | solution.py:26
  9.6 10.3 %collective-permute-start.1 = (bf16[256,1024]{1,0:T(8,128)(2,1)S(1)}, bf16[256,1024]{1,0:T(8,128)(2,1)S(1)}, u32[]{:S(2)}, u32[]{:S(2)}) collective-permute-start(bf16[256,1024]{1,0:T(8,128)(2,1)S(1)} %pad_maximum_fusion.1.refs_8_), channel_id=1, source_target_pairs={{0,1},{2,3},{4,5},{6,7},{8,9},{10,11},{12,13},{14,15},{16,17},{18,... | collective-permute-start | bytes 1572872 | tf_op jit(solution)/shard_map/ppermute | solution.py:21
  11.0 9.0 %collective-permute-start.2 = (bf16[256,1024]{1,0:T(8,128)(2,1)S(1)}, bf16[256,1024]{1,0:T(8,128)(2,1)}, u32[]{:S(2)}, u32[]{:S(2)}) collective-permute-start(bf16[256,1024]{1,0:T(8,128)(2,1)S(1)} %pad_maximum_fusion.1.refs_8_), channel_id=1, source_target_pairs={{1,8},{5,12},{3,10},{7,14},{17,24},{21,28},{19,26},{23,30}} | collective-permute-start | bytes 1572872 | tf_op jit(solution)/shard_map/ppermute | solution.py:210
  19.0 4.0 %copy-start.6 = (bf16[256,1024]{1,0:T(8,128)(2,1)}, bf16[256,1024]{1,0:T(8,128)(2,1)S(1)}, u32[]{:S(2)}) copy-start(bf16[256,1024]{1,0:T(8,128)(2,1)S(1)} %collective-permute-done.refs_4_) | copy-start | bytes 1572868
  19.0 4.0 %collective-permute-start.3 = (bf16[256,1024]{1,0:T(8,128)(2,1)S(1)}, bf16[256,1024]{1,0:T(8,128)(2,1)}, u32[]{:S(2)}, u32[]{:S(2)}) collective-permute-start(bf16[256,1024]{1,0:T(8,128)(2,1)S(1)} %collective-permute-done.refs_4_), channel_id=1, source_target_pairs={{0,1},{1,0},{2,3},{3,2},{4,5},{5,4},{6,7},{7,6},{8,9},{9,8},{10,11... | collective-permute-start | bytes 1572872 | tf_op jit(solution)/shard_map/ppermute | solution.py:26
  19.9 3.0 %copy-start.7 = (bf16[256,1024]{1,0:T(8,128)(2,1)}, bf16[256,1024]{1,0:T(8,128)(2,1)S(1)}, u32[]{:S(2)}) copy-start(bf16[256,1024]{1,0:T(8,128)(2,1)S(1)} %collective-permute-done.1.refs_5_) | copy-start | bytes 1572868
  22.9 0.8 copy-start.4
  32.6 27.9 %copy-start.1 = (f32[256,1024]{1,0:T(8,128)S(1)}, f32[256,1024]{1,0:T(8,128)}, u32[]{:S(2)}) copy-start(f32[256,1024]{1,0:T(8,128)} %get-tuple-element.10) | copy-start | bytes 3145732
  32.6 2.7 %collective-permute-start.7 = (bf16[256,1024]{1,0:T(8,128)(2,1)}, bf16[256,1024]{1,0:T(8,128)(2,1)S(1)}, u32[]{:S(2)}, u32[]{:S(2)}) collective-permute-start(bf16[256,1024]{1,0:T(8,128)(2,1)} %get-tuple-element.13), channel_id=1, source_target_pairs={{0,1},{1,0},{2,3},{3,2},{4,5},{5,4},{6,7},{7,6},{8,9},{9,8},{10,11... | collective-permute-start | bytes 1572872 | tf_op jit(solution)/shard_map/ppermute | solution.py:26
  33.3 4.7 %collective-permute-start.5 = (bf16[256,1024]{1,0:T(8,128)(2,1)}, bf16[256,1024]{1,0:T(8,128)(2,1)S(1)}, u32[]{:S(2)}, u32[]{:S(2)}) collective-permute-start(bf16[256,1024]{1,0:T(8,128)(2,1)} %get-tuple-element.11), channel_id=1, source_target_pairs={{1,0},{3,2},{5,4},{7,6},{9,8},{11,10},{13,12},{15,14},{17,16},{19,... | collective-permute-start | bytes 1572872 | tf_op jit(solution)/shard_map/ppermute | solution.py:21
  34.6 3.4 %collective-permute-start.6 = (bf16[256,1024]{1,0:T(8,128)(2,1)}, bf16[256,1024]{1,0:T(8,128)(2,1)S(1)}, u32[]{:S(2)}, u32[]{:S(2)}) collective-permute-start(bf16[256,1024]{1,0:T(8,128)(2,1)} %get-tuple-element.11), channel_id=1, source_target_pairs={{8,1},{12,5},{10,3},{14,7},{24,17},{28,21},{26,19},{30,23}} | collective-permute-start | bytes 1572872 | tf_op jit(solution)/shard_map/ppermute | solution.py:234
  36.7 23.8 %collective-permute-start.8 = (bf16[256,1024]{1,0:T(8,128)(2,1)S(1)}, bf16[256,1024]{1,0:T(8,128)(2,1)S(1)}, u32[]{:S(2)}, u32[]{:S(2)}) collective-permute-start(bf16[256,1024]{1,0:T(8,128)(2,1)S(1)} %add_convert_fusion.1), channel_id=1, source_target_pairs={{4,0},{8,4},{12,8},{5,1},{9,5},{13,9},{6,2},{10,6},{14,10},{7,3},{... | collective-permute-start | bytes 1572872 | tf_op jit(solution)/shard_map/ppermute | solution.py:21
  60.8 9.2 %copy-start.5 = (bf16[256,1152]{1,0:T(8,128)(2,1)S(1)}, bf16[256,1152]{1,0:T(8,128)(2,1)}, u32[]{:S(2)}) copy-start(bf16[256,1152]{1,0:T(8,128)(2,1)} %copy-done.4) | copy-start | bytes 1769476
  61.7 8.3 %collective-permute-start.9 = (bf16[256,512]{1,0:T(8,128)(2,1)S(1)}, bf16[256,512]{1,0:T(8,128)(2,1)S(1)}, u32[]{:S(2)}, u32[]{:S(2)}) collective-permute-start(bf16[256,512]{1,0:T(8,128)(2,1)S(1)} %get-tuple-element.23), channel_id=1, source_target_pairs={{0,2},{2,0},{1,3},{3,1},{4,6},{6,4},{5,7},{7,5},{8,10},{10,8},{9,1... | collective-permute-start | bytes 786440 | tf_op jit(solution)/shard_map/ppermute | solution.py:26
  70.8 1.4 %copy-start = (f32[1152,512]{1,0:T(8,128)}, f32[1152,512]{1,0:T(8,128)S(1)}, u32[]{:S(2)}) copy-start(f32[1152,512]{1,0:T(8,128)S(1)} %convolution_multiply_fusion) | copy-start | bytes 7077892
  72.3 2.1 %collective-permute-start.10 = (bf16[576,512]{1,0:T(8,128)(2,1)S(1)}, bf16[576,512]{1,0:T(8,128)(2,1)S(1)}, u32[]{:S(2)}, u32[]{:S(2)}) collective-permute-start(bf16[576,512]{1,0:T(8,128)(2,1)S(1)} %dynamic-slice_convert_fusion), channel_id=1, source_target_pairs={{0,1},{1,0},{2,3},{3,2},{4,5},{5,4},{6,7},{7,6},{8,9},{9,8},{10,11... | collective-permute-start | bytes 1769480 | tf_op jit(solution)/shard_map/ppermute | solution.py:26
  75.9 9.8 %collective-permute-start.11 = (bf16[144,512]{1,0:T(8,128)(2,1)S(1)}, bf16[144,512]{1,0:T(8,128)(2,1)S(1)}, u32[]{:S(2)}, u32[]{:S(2)}) collective-permute-start(bf16[144,512]{1,0:T(8,128)(2,1)S(1)} %get-tuple-element.18), channel_id=1, source_target_pairs={{0,4},{4,8},{8,12},{12,0},{1,5},{5,9},{9,13},{13,1},{2,6},{6,10},{... | collective-permute-start | bytes 442376 | tf_op jit(solution)/shard_map/ppermute | solution.py:26
  81.6 9.6 %collective-permute-start.12 = (bf16[144,512]{1,0:T(8,128)(2,1)S(1)}, bf16[144,512]{1,0:T(8,128)(2,1)S(1)}, u32[]{:S(2)}, u32[]{:S(2)}) collective-permute-start(bf16[144,512]{1,0:T(8,128)(2,1)S(1)} %get-tuple-element.20), channel_id=1, source_target_pairs={{0,8},{4,12},{8,0},{12,4},{1,9},{5,13},{9,1},{13,5},{2,10},{6,14},... | collective-permute-start | bytes 442376 | tf_op jit(solution)/shard_map/ppermute | solution.py:26
  81.6 9.8 %collective-permute-start.13 = (bf16[144,512]{1,0:T(8,128)(2,1)S(1)}, bf16[144,512]{1,0:T(8,128)(2,1)S(1)}, u32[]{:S(2)}, u32[]{:S(2)}) collective-permute-start(bf16[144,512]{1,0:T(8,128)(2,1)S(1)} %get-tuple-element.19), channel_id=1, source_target_pairs={{0,12},{4,0},{8,4},{12,8},{1,13},{5,1},{9,5},{13,9},{2,14},{6,2},{... | collective-permute-start | bytes 442376 | tf_op jit(solution)/shard_map/ppermute | solution.py:26
  91.6 11.1 %collective-permute-start.14 = (bf16[144,512]{1,0:T(8,128)(2,1)S(1)}, bf16[144,512]{1,0:T(8,128)(2,1)S(1)}, u32[]{:S(2)}, u32[]{:S(2)}) collective-permute-start(bf16[144,512]{1,0:T(8,128)(2,1)S(1)} %get-tuple-element.16), channel_id=1, source_target_pairs={{0,4},{4,8},{8,12},{12,0},{1,5},{5,9},{9,13},{13,1},{2,6},{6,10},{... | collective-permute-start | bytes 442376 | tf_op jit(solution)/shard_map/ppermute | solution.py:26
  95.0 12.9 %collective-permute-start.15 = (bf16[144,512]{1,0:T(8,128)(2,1)S(1)}, bf16[144,512]{1,0:T(8,128)(2,1)S(1)}, u32[]{:S(2)}, u32[]{:S(2)}) collective-permute-start(bf16[144,512]{1,0:T(8,128)(2,1)S(1)} %get-tuple-element.16), channel_id=1, source_target_pairs={{0,8},{4,12},{8,0},{12,4},{1,9},{5,13},{9,1},{13,5},{2,10},{6,14},... | collective-permute-start | bytes 442376 | tf_op jit(solution)/shard_map/ppermute | solution.py:26
  98.4 9.5 %collective-permute-start.16 = (bf16[144,512]{1,0:T(8,128)(2,1)S(1)}, bf16[144,512]{1,0:T(8,128)(2,1)S(1)}, u32[]{:S(2)}, u32[]{:S(2)}) collective-permute-start(bf16[144,512]{1,0:T(8,128)(2,1)S(1)} %get-tuple-element.16), channel_id=1, source_target_pairs={{0,12},{4,0},{8,4},{12,8},{1,13},{5,1},{9,5},{13,9},{2,14},{6,2},{... | collective-permute-start | bytes 442376 | tf_op jit(solution)/shard_map/ppermute | solution.py:26
  108.0 2.1 %collective-permute-start.17 = (bf16[576,512]{1,0:T(8,128)(2,1)S(1)}, bf16[576,512]{1,0:T(8,128)(2,1)S(1)}, u32[]{:S(2)}, u32[]{:S(2)}) collective-permute-start(bf16[576,512]{1,0:T(8,128)(2,1)S(1)} %convert_element_type.78), channel_id=1, source_target_pairs={{0,1},{1,0},{2,3},{3,2},{4,5},{5,4},{6,7},{7,6},{8,9},{9,8},{10,11... | collective-permute-start | bytes 1769480 | tf_op jit(solution)/shard_map/ppermute | solution.py:26

commit v8 on v7

--- a/solution.py
+++ b/solution.py
@@ -194,7 +194,6 @@
         outgoing = lax.dynamic_slice_in_dim(own_input, target * shard_rows, shard_rows, axis=1)
         inputs.append(rotated(outgoing, "fsdp", steps))
 
-    own_kv = jnp.concatenate([key_heads[0], value_heads[0]], axis=1)
     query_pos = first_row + jnp.arange(block_rows, dtype=jnp.int32)
     lowest = jnp.maximum(doc_start_of(doc_starts[0], query_pos), query_pos - window + 1)
     lo_rel = (lowest - first_row + margin).astype(jnp.int32)[:, None]
@@ -202,53 +201,69 @@
     sub_at = lax.axis_index("sub")
     flag = jnp.reshape(sub_at, (1,)).astype(jnp.int32)
     chip_route = sub_count == 2 and reach == 3
-    if chip_route:
-        ring_count = lax.axis_size(RING)
-        across = [(2 * chip - 3, 2 * chip) for chip in range(2, ring_count // 2)]
-        two_back = passed_along(own_kv, "ctx", 1)
-        one_back_high = passed_along(own_kv, "sub", 1)
-        three_back_low = lax.ppermute(own_kv, RING, across)
-        swapped = rotated(two_back, "sub", 1)
-        kv_blocks = [two_back, one_back_high, three_back_low, swapped, own_kv]
-        slots = [(2, 3), (0, 0), (3, 1), (4, 4)]
-    else:
+    ring_count = lax.axis_size(RING)
+    across = [(2 * chip - 3, 2 * chip) for chip in range(2, ring_count // 2)]
+    back = [(target, source) for source, target in across]
+    per_group = heads // kv_heads
+
+    def low(value):
+        return value.astype(jnp.bfloat16)
+
+    def forward_halo(own_kv):
+        if chip_route:
+            two_back = passed_along(own_kv, "ctx", 1)
+            one_back_high = passed_along(own_kv, "sub", 1)
+            three_back_low = lax.ppermute(own_kv, RING, across)
+            swapped = rotated(two_back, "sub", 1)
+            return [two_back, one_back_high, three_back_low, swapped, own_kv]
         arrived = []
         moving = own_kv
         for _ in range(reach):
             moving = passed_along(moving, RING, 1)
             arrived.append(moving)
-        kv_blocks = arrived[::-1] + [own_kv]
+        return arrived[::-1] + [own_kv]
+
+    if chip_route:
+        slots = [(2, 3), (0, 0), (3, 1), (4, 4)]
+    else:
         slots = [(index, index) for index in range(reach + 1)]
-    grad_q, *grad_pieces = attention(
-        flag, lo_rel, query_heads[0], grad_out[0], kv_blocks, slots, heads, kv_heads, margin,
-        inputs[1:],
-        chip_route,
-    )
-
-    def low(value):
-        return value.astype(jnp.bfloat16)
-
-    if chip_route:
-        back = [(target, source) for source, target in across]
-        to_mate, to_other, g2, g0 = grad_pieces
-        from_far = lax.ppermute(to_other, RING, back).astype(jnp.float32)
-        from_mate = rotated(to_mate, "sub", 1).astype(jnp.float32)
-        from_high = passed_along(to_other, "sub", -1).astype(jnp.float32)
-        two_back_sum = g2 + from_mate
-        from_next = passed_along(low(two_back_sum), "ctx", -1).astype(jnp.float32)
-        total = g0 + from_high + from_far + from_next
-    else:
-
-        def own_piece(distance):
-            return grad_pieces[reach - distance]
-
-        total = own_piece(reach)
+
+    def backward_halo(grad_pieces):
+        if chip_route:
+            to_mate, to_other, g2, g0 = grad_pieces
+            from_far = lax.ppermute(to_other, RING, back).astype(jnp.float32)
+            from_mate = rotated(to_mate, "sub", 1).astype(jnp.float32)
+            from_high = passed_along(to_other, "sub", -1).astype(jnp.float32)
+            two_back_sum = g2 + from_mate
+            from_next = passed_along(low(two_back_sum), "ctx", -1).astype(jnp.float32)
+            return g0 + from_high + from_far + from_next
+        total = grad_pieces[0]
         for distance in range(reach - 1, -1, -1):
             moved = passed_along(low(total), RING, -1).astype(jnp.float32)
-            total = moved + own_piece(distance)
-    grad_kv = total.astype(jnp.bfloat16)
-    grad_key = grad_kv[:, :kv_width]
-    grad_value = grad_kv[:, kv_width:]
+            total = moved + grad_pieces[reach - distance]
+        return total
+
+    grad_q_parts, key_parts, value_parts = [], [], []
+    previous = None
+    for group in range(kv_heads):
+        k_cols = slice(group * HEAD_DIM, (group + 1) * HEAD_DIM)
+        q_cols = slice(group * per_group * HEAD_DIM, (group + 1) * per_group * HEAD_DIM)
+        own_kv = jnp.concatenate([key_heads[0][:, k_cols], value_heads[0][:, k_cols]], axis=1)
+        if previous is not None:
+            own_kv, _ = lax.optimization_barrier((own_kv, previous))
+        kv_blocks = forward_halo(own_kv)
+        previous = kv_blocks[:-1]
+        grad_q_g, *grad_pieces = attention(
+            flag, lo_rel, query_heads[0][:, q_cols], grad_out[0][:, q_cols], kv_blocks, slots,
+            per_group, 1, margin, inputs[1:] if group == 0 else [], chip_route,
+        )
+        total = low(backward_halo(grad_pieces))
+        grad_q_parts.append(grad_q_g)
+        key_parts.append(total[:, :HEAD_DIM])
+        value_parts.append(total[:, HEAD_DIM:])
+    grad_q = jnp.concatenate(grad_q_parts, axis=1)
+    grad_key = jnp.concatenate(key_parts, axis=1)
+    grad_value = jnp.concatenate(value_parts, axis=1)
 
     values = [grad_value]
     for steps in range(1, fsdp_count):
@@ -261,8 +276,6 @@
     if scale_early:
         shard = shard * token_scale
 
-    sub_count = lax.axis_size("sub")
-    sub_at = lax.axis_index("sub")
     piece_rows = shard_rows // sub_count
     mine = lax.dynamic_slice_in_dim(shard, sub_at * piece_rows, piece_rows, axis=0)
     for steps in range(1, sub_count):

time: 113 us -> 128 us (1.13)
  starting transfers between devices: 29.8 us -> 51.7 us
  waiting for transfers between devices: 59.6 us -> 46.7 us
  local copies, waits for them, and re-layouts: 4.83 us -> 6.55 us
  other arithmetic: 7.16 us -> 8.85 us
  Pallas kernels: 8.83 us -> 10.5 us
    ppermute x4 -> x8, starting transfers between devices: 8.84 us -> 26.5 us  [passed_along(): lax.ppermute(value, axis, [(source, source + steps) for source in range(f...]
    ppermute x4 -> x8, waiting for transfers between devices: 29 us -> 16.3 us  [passed_along(): lax.ppermute(value, axis, [(source, source + steps) for source in range(f...]
    ppermute x12 -> x14, starting transfers between devices: 18.8 us -> 21.7 us  [rotated(): lax.ppermute(value, axis, [(source, (source + steps) % count) for source...]
    slice x1 -> x4, local copies, waits for them, and re-layouts: 0.85 us -> 2.9 us  [the longest x1 1.88 us: body(): key_heads[0][:, k_cols]]
    pallas_call x1 -> x2, Pallas kernels: 8.83 us -> 10.5 us  [attention(): pl.pallas_call(kernel, out_shape=(jax.ShapeDtypeStruct((rows, width), jnp...]
    broadcast_in_dim x0 -> x2, other arithmetic: none -> 1.58 us  [body(): return (grad_q[None], grad_key[None], grad_value[None], weight_v)]
    ppermute x2 -> x4, starting transfers between devices: 2.17 us -> 3.52 us  [the longest x2 2.05 us: forward_halo(): three_back_low = lax.ppermute(own_kv, RING, across)]
    concatenate x1 -> x3, other arithmetic: 1.08 us -> 2.39 us  [the longest x2 1.65 us: body(): jnp.concatenate([key_heads[0][:, k_cols], value_heads[0][:, k_cols]], axi...]
  transfers between devices with their start and end apart: 18 -> 26, of which waited for: 11 -> 12; matrix products, arithmetic and copies ran while one was open for 3% -> 4% of each run, Pallas kernels for 0% -> 8%
where the time goes in v8:
time: 128 us; the launch traced here: 127 us
  starting transfers between devices  51.7 us (40%)
  waiting for transfers between devices  46.7 us (36%)
  Pallas kernels  10.5 us (8%)
  other arithmetic  8.85 us (7%)
  local copies, waits for them, and re-layouts  6.55 us (5%)
  matrix products  1.87 us (1%)
    ppermute x14, waiting for transfers between devices, rotated(): lax.ppermute(value, axis, [(source, (source + steps) % count) for source...  30.4 us
    ppermute x8, starting transfers between devices, passed_along(): lax.ppermute(value, axis, [(source, source + steps) for source in range(f...  26.5 us
    ppermute x14, starting transfers between devices, rotated(): lax.ppermute(value, axis, [(source, (source + steps) % count) for source...  21.7 us
    ppermute x8, waiting for transfers between devices, passed_along(): lax.ppermute(value, axis, [(source, source + steps) for source in range(f...  16.3 us
    pallas_call x2, Pallas kernels, attention(): pl.pallas_call(kernel, out_shape=(jax.ShapeDtypeStruct((rows, width), jnp...  10.5 us
    unnamed x36, local copies, waits for them, and re-layouts  3.08 us
  transfers between devices with their start and end apart: 26, of which 12 were waited for; matrix products, arithmetic and copies ran while one was open for 4% of the time, Pallas kernels for 8%

profile of v8, /device:TPU:0, one launch (start us, length us, event | category | flops | bytes accessed | tf_op | source)
XLA Modules:
  0.0 127.3 jit_solution(3744255038256903113)
XLA Ops:
  0.6 1.9 %fusion.16 = (bf16[256,256]{1,0:T(8,128)(2,1)S(1)}, bf16[256,256]{1,0:T(8,128)(2,1)S(1)}, bf16[256,256]{1,0:T(8,128)(2,1)}, bf16[256,256]{1,0:T(8,128)(2,1)S(1)}) fusion(bf16[256,512]{1,0:T(8,128)(2,1)} %bitcast.19, bf16[256,512]{1,0:T(8,128)(2,1)} %bitcast.20), kind=kLoop, calls=%fused_computation.43 | loop fusion | bytes 1048576 | tf_op jit(solution)/shard_map/slice | solution.py:251
  2.5 0.7 pad_maximum_fusion.1.refs_8_
  3.2 1.4 %collective-permute-start.2 = (bf16[256,512]{1,0:T(8,128)(2,1)}, bf16[256,512]{1,0:T(8,128)(2,1)}, u32[]{:S(2)}, u32[]{:S(2)}) collective-permute-start(bf16[256,512]{1,0:T(8,128)(2,1)} %pad_maximum_fusion.1.refs_8_), channel_id=1, source_target_pairs={{1,8},{5,12},{3,10},{7,14},{17,24},{21,28},{19,26},{23,30}} | collective-permute-start | bytes 786440 | tf_op jit(solution)/shard_map/ppermute | solution.py:216
  4.6 8.0 %collective-permute-start.1 = (bf16[256,512]{1,0:T(8,128)(2,1)}, bf16[256,512]{1,0:T(8,128)(2,1)}, u32[]{:S(2)}, u32[]{:S(2)}) collective-permute-start(bf16[256,512]{1,0:T(8,128)(2,1)} %pad_maximum_fusion.1.refs_8_), channel_id=1, source_target_pairs={{0,1},{2,3},{4,5},{6,7},{8,9},{10,11},{12,13},{14,15},{16,17},{18,... | collective-permute-start | bytes 786440 | tf_op jit(solution)/shard_map/ppermute | solution.py:21
  12.6 4.2 %collective-permute-start = (bf16[256,512]{1,0:T(8,128)(2,1)}, bf16[256,512]{1,0:T(8,128)(2,1)}, u32[]{:S(2)}, u32[]{:S(2)}) collective-permute-start(bf16[256,512]{1,0:T(8,128)(2,1)} %pad_maximum_fusion.1.refs_8_), channel_id=1, source_target_pairs={{0,4},{4,8},{8,12},{1,5},{5,9},{9,13},{2,6},{6,10},{10,14},{3,7},{... | collective-permute-start | bytes 786440 | tf_op jit(solution)/shard_map/ppermute | solution.py:21
  16.8 0.2 dynamic-slice_bitcast_fusion
  17.0 1.5 %collective-permute-start.4 = (bf16[256,1152]{1,0:T(8,128)(2,1)S(1)}, bf16[256,1152]{1,0:T(8,128)(2,1)}, u32[]{:S(2)}, u32[]{:S(2)}) collective-permute-start(bf16[256,1152]{1,0:T(8,128)(2,1)S(1)} %get-tuple-element.34), channel_id=1, source_target_pairs={{0,2},{2,0},{1,3},{3,1},{4,6},{6,4},{5,7},{7,5},{8,10},{10,8},{9,1... | collective-permute-start | bytes 1769480 | tf_op jit(solution)/shard_map/ppermute | solution.py:26
  18.5 2.4 %collective-permute-done.refs_4_ = bf16[256,512]{1,0:T(8,128)(2,1)} collective-permute-done((bf16[256,512]{1,0:T(8,128)(2,1)}, bf16[256,512]{1,0:T(8,128)(2,1)}, u32[]{:S(2)}, u32[]{:S(2)}) %collective-permute-start) | collective-permute-done | bytes 262176 | tf_op jit(solution)/shard_map/ppermute | solution.py:21
  20.8 0.1 select_reduce_fusion
  20.9 0.1 copy.13
  21.1 0.9 pad_maximum_fusion.2.refs_8_
  22.0 0.5 collective-permute-done.3.refs_7_
  22.6 4.4 %collective-permute-start.5 = (bf16[256,512]{1,0:T(8,128)(2,1)S(1)}, bf16[256,512]{1,0:T(8,128)(2,1)S(1)}, u32[]{:S(2)}, u32[]{:S(2)}) collective-permute-start(bf16[256,512]{1,0:T(8,128)(2,1)S(1)} %pad_maximum_fusion.2.refs_8_), channel_id=1, source_target_pairs={{0,4},{4,8},{8,12},{1,5},{5,9},{9,13},{2,6},{6,10},{10,14},{3,7},{... | collective-permute-start | bytes 786440 | tf_op jit(solution)/shard_map/ppermute | solution.py:21
  27.0 1.0 fusion.12
  28.0 0.7 collective-permute-start.7
  28.6 4.6 %collective-permute-start.6 = (bf16[256,512]{1,0:T(8,128)(2,1)S(1)}, bf16[256,512]{1,0:T(8,128)(2,1)S(1)}, u32[]{:S(2)}, u32[]{:S(2)}) collective-permute-start(bf16[256,512]{1,0:T(8,128)(2,1)S(1)} %pad_maximum_fusion.2.refs_8_), channel_id=1, source_target_pairs={{0,1},{2,3},{4,5},{6,7},{8,9},{10,11},{12,13},{14,15},{16,17},{18,... | collective-permute-start | bytes 786440 | tf_op jit(solution)/shard_map/ppermute | solution.py:21
  33.3 0.3 collective-permute-done.5.refs_4_
  33.6 0.8 subtract_add_fusion.refs_1_
  34.4 5.2 %shard_map.93 = (bf16[256,512]{1,0:T(8,128)(2,1)}, bf16[256,512]{1,0:T(8,128)(2,1)}, bf16[256,512]{1,0:T(8,128)(2,1)}, f32[256,512]{1,0:T(8,128)}, f32[256,512]{1,0:T(8,128)}) custom-call(s32[1]{0:T(128)} %bitcast.refs_0_, s32[256,1]{1,0:T(8,128)} %subtract_add_fusion.refs_1_, bf16[256,512]{1,0:T(8,128)(2,1)} %get-tuple-element.52.refs_2_, ...), custom_call_target="tpu_custom_call" | custom-call | flops 1342177280 | bytes 3932160 | tf_op jit(solution)/shard_map/pallas_call | solution.py:160
  39.6 0.5 collective-permute-start.11
  40.1 0.7 copy-done.15
  40.9 0.1 copy-done.17
  41.0 5.3 %shard_map.94 = (bf16[256,512]{1,0:T(8,128)(2,1)}, bf16[256,512]{1,0:T(8,128)(2,1)}, bf16[256,512]{1,0:T(8,128)(2,1)}, f32[256,512]{1,0:T(8,128)}, f32[256,512]{1,0:T(8,128)}) custom-call(s32[1]{0:T(128)} %bitcast.refs_0_, s32[256,1]{1,0:T(8,128)} %subtract_add_fusion.refs_1_, bf16[256,512]{1,0:T(8,128)(2,1)} %get-tuple-element.51.refs_2_, ...), custom_call_target="tpu_custom_call" | custom-call | flops 1342177280 | bytes 3932160 | tf_op jit(solution)/shard_map/pallas_call | solution.py:160
  46.2 0.1 collective-permute-start.15
  46.4 0.8 collective-permute-start.10
  47.2 1.3 %collective-permute-start.9 = (bf16[256,512]{1,0:T(8,128)(2,1)S(1)}, bf16[256,512]{1,0:T(8,128)(2,1)S(1)}, u32[]{:S(2)}, u32[]{:S(2)}) collective-permute-start(bf16[256,512]{1,0:T(8,128)(2,1)S(1)} %copy-done.12), channel_id=1, source_target_pairs={{1,0},{3,2},{5,4},{7,6},{9,8},{11,10},{13,12},{15,14},{17,16},{19,... | collective-permute-start | bytes 786440 | tf_op jit(solution)/shard_map/ppermute | solution.py:21
  48.5 0.1 add_convert_fusion.3
  48.6 1.3 %collective-permute-start.12 = (bf16[256,512]{1,0:T(8,128)(2,1)S(1)}, bf16[256,512]{1,0:T(8,128)(2,1)S(1)}, u32[]{:S(2)}, u32[]{:S(2)}) collective-permute-start(bf16[256,512]{1,0:T(8,128)(2,1)S(1)} %add_convert_fusion.3), channel_id=1, source_target_pairs={{4,0},{8,4},{12,8},{5,1},{9,5},{13,9},{6,2},{10,6},{14,10},{7,3},{... | collective-permute-start | bytes 786440 | tf_op jit(solution)/shard_map/ppermute | solution.py:21
  49.9 0.7 collective-permute-start.14
  50.6 1.3 %collective-permute-start.13 = (bf16[256,512]{1,0:T(8,128)(2,1)}, bf16[256,512]{1,0:T(8,128)(2,1)S(1)}, u32[]{:S(2)}, u32[]{:S(2)}) collective-permute-start(bf16[256,512]{1,0:T(8,128)(2,1)} %get-tuple-element.23), channel_id=1, source_target_pairs={{1,0},{3,2},{5,4},{7,6},{9,8},{11,10},{13,12},{15,14},{17,16},{19,... | collective-permute-start | bytes 786440 | tf_op jit(solution)/shard_map/ppermute | solution.py:21
  52.0 1.4 %collective-permute-start.16 = (bf16[256,512]{1,0:T(8,128)(2,1)S(1)}, bf16[256,512]{1,0:T(8,128)(2,1)S(1)}, u32[]{:S(2)}, u32[]{:S(2)}) collective-permute-start(bf16[256,512]{1,0:T(8,128)(2,1)S(1)} %add_convert_fusion.1), channel_id=1, source_target_pairs={{4,0},{8,4},{12,8},{5,1},{9,5},{13,9},{6,2},{10,6},{14,10},{7,3},{... | collective-permute-start | bytes 786440 | tf_op jit(solution)/shard_map/ppermute | solution.py:21
  53.4 10.8 %collective-permute-done.12 = bf16[256,512]{1,0:T(8,128)(2,1)S(1)} collective-permute-done((bf16[256,512]{1,0:T(8,128)(2,1)S(1)}, bf16[256,512]{1,0:T(8,128)(2,1)S(1)}, u32[]{:S(2)}, u32[]{:S(2)}) %collective-permute-start.12) | collective-permute-done | bytes 262176 | tf_op jit(solution)/shard_map/ppermute | solution.py:21
  64.2 0.1 add_convert_fusion.2
  64.4 2.8 %collective-permute-done.16 = bf16[256,512]{1,0:T(8,128)(2,1)S(1)} collective-permute-done((bf16[256,512]{1,0:T(8,128)(2,1)S(1)}, bf16[256,512]{1,0:T(8,128)(2,1)S(1)}, u32[]{:S(2)}, u32[]{:S(2)}) %collective-permute-start.16) | collective-permute-done | bytes 262176 | tf_op jit(solution)/shard_map/ppermute | solution.py:21
  67.2 0.1 add_convert_fusion
  67.4 0.7 pad_maximum_fusion.3
  68.1 1.5 %collective-permute-start.17 = (bf16[256,512]{1,0:T(8,128)(2,1)S(1)}, bf16[256,512]{1,0:T(8,128)(2,1)S(1)}, u32[]{:S(2)}, u32[]{:S(2)}) collective-permute-start(bf16[256,512]{1,0:T(8,128)(2,1)S(1)} %get-tuple-element.39), channel_id=1, source_target_pairs={{0,2},{2,0},{1,3},{3,1},{4,6},{6,4},{5,7},{7,5},{8,10},{10,8},{9,1... | collective-permute-start | bytes 786440 | tf_op jit(solution)/shard_map/ppermute | solution.py:26
  69.6 4.9 %collective-permute-done.17 = bf16[256,512]{1,0:T(8,128)(2,1)S(1)} collective-permute-done((bf16[256,512]{1,0:T(8,128)(2,1)S(1)}, bf16[256,512]{1,0:T(8,128)(2,1)S(1)}, u32[]{:S(2)}, u32[]{:S(2)}) %collective-permute-start.17) | collective-permute-done | bytes 262176 | tf_op jit(solution)/shard_map/ppermute | solution.py:26
  74.5 1.9 %convolution_multiply_fusion = f32[1152,512]{1,0:T(8,128)S(1)} fusion(bf16[256,1152]{1,0:T(8,128)(2,1)} %collective-permute-done.4.refs_9_, bf16[256,1152]{1,0:T(8,128)(2,1)S(1)} %get-tuple-element.33, bf16[256,512]{1,0:T(8,128)(2,1)S(1)} %collective-permute-done.17, bf16[256,256]{1,0:T(8,128)(2,1)S(1)} %get-tuple-element.43, ...), kind=kOutput, calls=%fused_computation | convolution fusion | flops 608501760 | bytes 4063232 | tf_op jit(solution)/shard_map/dot_general | solution.py:273
  76.4 1.4 %copy-done = f32[1152,512]{1,0:T(8,128)} copy-done((f32[1152,512]{1,0:T(8,128)}, f32[1152,512]{1,0:T(8,128)S(1)}, u32[]{:S(2)}) %copy-start) | copy-done | bytes 2359320
  77.8 0.1 dynamic-slice_convert_fusion
  77.8 7.2 %collective-permute-start.18 = (bf16[576,512]{1,0:T(8,128)(2,1)S(1)}, bf16[576,512]{1,0:T(8,128)(2,1)S(1)}, u32[]{:S(2)}, u32[]{:S(2)}) collective-permute-start(bf16[576,512]{1,0:T(8,128)(2,1)S(1)} %dynamic-slice_convert_fusion), channel_id=1, source_target_pairs={{0,1},{1,0},{2,3},{3,2},{4,5},{5,4},{6,7},{7,6},{8,9},{9,8},{10,11... | collective-permute-start | bytes 1769480 | tf_op jit(solution)/shard_map/ppermute | solution.py:26
  85.0 1.6 %collective-permute-done.18 = bf16[576,512]{1,0:T(8,128)(2,1)S(1)} collective-permute-done((bf16[576,512]{1,0:T(8,128)(2,1)S(1)}, bf16[576,512]{1,0:T(8,128)(2,1)S(1)}, u32[]{:S(2)}, u32[]{:S(2)}) %collective-permute-start.18) | collective-permute-done | bytes 589856 | tf_op jit(solution)/shard_map/ppermute | solution.py:26
  86.7 1.4 %convert_add_fusion = f32[576,512]{1,0:T(8,128)S(1)} fusion(bf16[576,512]{1,0:T(8,128)(2,1)S(1)} %collective-permute-done.18, f32[1152,512]{1,0:T(8,128)} %copy-done, s32[]{:T(128)S(6)} %select_n.90), kind=kLoop, calls=%fused_computation.7 | loop fusion | flops 589824 | bytes 2949124 | tf_op jit(solution)/shard_map/add | solution.py:284
  88.2 5.1 %collective-permute-start.19 = (bf16[144,512]{1,0:T(8,128)(2,1)S(1)}, bf16[144,512]{1,0:T(8,128)(2,1)S(1)}, u32[]{:S(2)}, u32[]{:S(2)}) collective-permute-start(bf16[144,512]{1,0:T(8,128)(2,1)S(1)} %get-tuple-element.30), channel_id=1, source_target_pairs={{0,4},{4,8},{8,12},{12,0},{1,5},{5,9},{9,13},{13,1},{2,6},{6,10},{... | collective-permute-start | bytes 442376 | tf_op jit(solution)/shard_map/ppermute | solution.py:26
  93.3 1.5 %collective-permute-start.20 = (bf16[144,512]{1,0:T(8,128)(2,1)S(1)}, bf16[144,512]{1,0:T(8,128)(2,1)S(1)}, u32[]{:S(2)}, u32[]{:S(2)}) collective-permute-start(bf16[144,512]{1,0:T(8,128)(2,1)S(1)} %get-tuple-element.32), channel_id=1, source_target_pairs={{0,8},{4,12},{8,0},{12,4},{1,9},{5,13},{9,1},{13,5},{2,10},{6,14},... | collective-permute-start | bytes 442376 | tf_op jit(solution)/shard_map/ppermute | solution.py:26
  94.8 2.7 %collective-permute-done.19 = bf16[144,512]{1,0:T(8,128)(2,1)S(1)} collective-permute-done((bf16[144,512]{1,0:T(8,128)(2,1)S(1)}, bf16[144,512]{1,0:T(8,128)(2,1)S(1)}, u32[]{:S(2)}, u32[]{:S(2)}) %collective-permute-start.19) | collective-permute-done | bytes 147488 | tf_op jit(solution)/shard_map/ppermute | solution.py:26
  97.5 3.2 %collective-permute-done.21 = bf16[144,512]{1,0:T(8,128)(2,1)S(1)} collective-permute-done((bf16[144,512]{1,0:T(8,128)(2,1)S(1)}, bf16[144,512]{1,0:T(8,128)(2,1)S(1)}, u32[]{:S(2)}, u32[]{:S(2)}) %collective-permute-start.21) | collective-permute-done | bytes 147488 | tf_op jit(solution)/shard_map/ppermute | solution.py:26
  100.7 4.9 %collective-permute-done.20 = bf16[144,512]{1,0:T(8,128)(2,1)S(1)} collective-permute-done((bf16[144,512]{1,0:T(8,128)(2,1)S(1)}, bf16[144,512]{1,0:T(8,128)(2,1)S(1)}, u32[]{:S(2)}, u32[]{:S(2)}) %collective-permute-start.20) | collective-permute-done | bytes 147488 | tf_op jit(solution)/shard_map/ppermute | solution.py:26
  105.6 0.1 broadcast_in_dim.28
  105.8 0.1 fusion.8
  105.9 0.9 collective-permute-start.22
  106.8 3.0 %collective-permute-start.24 = (bf16[144,512]{1,0:T(8,128)(2,1)S(1)}, bf16[144,512]{1,0:T(8,128)(2,1)S(1)}, u32[]{:S(2)}, u32[]{:S(2)}) collective-permute-start(bf16[144,512]{1,0:T(8,128)(2,1)S(1)} %get-tuple-element.28), channel_id=1, source_target_pairs={{0,12},{4,0},{8,4},{12,8},{1,13},{5,1},{9,5},{13,9},{2,14},{6,2},{... | collective-permute-start | bytes 442376 | tf_op jit(solution)/shard_map/ppermute | solution.py:26
  109.7 0.4 collective-permute-start.23
  110.1 4.4 %collective-permute-done.22 = bf16[144,512]{1,0:T(8,128)(2,1)S(1)} collective-permute-done((bf16[144,512]{1,0:T(8,128)(2,1)S(1)}, bf16[144,512]{1,0:T(8,128)(2,1)S(1)}, u32[]{:S(2)}, u32[]{:S(2)}) %collective-permute-start.22) | collective-permute-done | bytes 147488 | tf_op jit(solution)/shard_map/ppermute | solution.py:26
  114.5 8.2 %collective-permute-done.23 = bf16[144,512]{1,0:T(8,128)(2,1)S(1)} collective-permute-done((bf16[144,512]{1,0:T(8,128)(2,1)S(1)}, bf16[144,512]{1,0:T(8,128)(2,1)S(1)}, u32[]{:S(2)}, u32[]{:S(2)}) %collective-permute-start.23) | collective-permute-done | bytes 147488 | tf_op jit(solution)/shard_map/ppermute | solution.py:26
  122.8 0.1 convert_element_type.102
  122.9 0.1 collective-permute-start.25
  123.0 0.7 copy-done.9
  123.7 0.1 copy-done.10
  123.8 0.9 maximum_bitcast_fusion
  124.6 0.7 maximum_bitcast_fusion.1
  125.4 0.3 convert_select_fusion.1
  125.7 1.6 %pad_maximum_fusion = f32[1152,512]{1,0:T(8,128)} fusion(f32[576,512]{1,0:T(8,128)S(1)} %get-tuple-element.27, f32[576,512]{1,0:T(8,128)S(1)} %get-tuple-element.26), kind=kLoop, calls=%fused_computation.1 | loop fusion | flops 589824 | bytes 4718592 | tf_op jit(solution)/shard_map/concatenate | solution.py:290
  (56 shorter events, 0.4 us)
Async XLA Ops:
  0.6 16.2 %copy-start.1 = (bf16[1,256,2304]{2,1,0:T(8,128)(2,1)S(1)}, bf16[1,256,2304]{2,1,0:T(8,128)(2,1)}, u32[]{:S(2)}) copy-start(bf16[1,256,2304]{2,1,0:T(8,128)(2,1)} %param.6) | copy-start | bytes 3538948
  3.2 18.8 %collective-permute-start.2 = (bf16[256,512]{1,0:T(8,128)(2,1)}, bf16[256,512]{1,0:T(8,128)(2,1)}, u32[]{:S(2)}, u32[]{:S(2)}) collective-permute-start(bf16[256,512]{1,0:T(8,128)(2,1)} %pad_maximum_fusion.1.refs_8_), channel_id=1, source_target_pairs={{1,8},{5,12},{3,10},{7,14},{17,24},{21,28},{19,26},{23,30}} | collective-permute-start | bytes 786440 | tf_op jit(solution)/shard_map/ppermute | solution.py:216
  4.6 17.4 %collective-permute-start.1 = (bf16[256,512]{1,0:T(8,128)(2,1)}, bf16[256,512]{1,0:T(8,128)(2,1)}, u32[]{:S(2)}, u32[]{:S(2)}) collective-permute-start(bf16[256,512]{1,0:T(8,128)(2,1)} %pad_maximum_fusion.1.refs_8_), channel_id=1, source_target_pairs={{0,1},{2,3},{4,5},{6,7},{8,9},{10,11},{12,13},{14,15},{16,17},{18,... | collective-permute-start | bytes 786440 | tf_op jit(solution)/shard_map/ppermute | solution.py:21
  12.6 8.2 %collective-permute-start = (bf16[256,512]{1,0:T(8,128)(2,1)}, bf16[256,512]{1,0:T(8,128)(2,1)}, u32[]{:S(2)}, u32[]{:S(2)}) collective-permute-start(bf16[256,512]{1,0:T(8,128)(2,1)} %pad_maximum_fusion.1.refs_8_), channel_id=1, source_target_pairs={{0,4},{4,8},{8,12},{1,5},{5,9},{9,13},{2,6},{6,10},{10,14},{3,7},{... | collective-permute-start | bytes 786440 | tf_op jit(solution)/shard_map/ppermute | solution.py:21
  16.8 4.0 %copy-start.11 = (s32[1,12]{1,0:T(1,128)S(1)}, s32[1,12]{1,0:T(1,128)}, u32[]{:S(2)}) copy-start(s32[1,12]{1,0:T(1,128)} %param.11) | copy-start | bytes 148
  16.8 10.2 %copy-start.6 = (bf16[1,256,1024]{2,1,0:T(8,128)(2,1)S(1)}, bf16[1,256,1024]{2,1,0:T(8,128)(2,1)}, u32[]{:S(2)}) copy-start(bf16[1,256,1024]{2,1,0:T(8,128)(2,1)} %param.10) | copy-start | bytes 1572868
  16.8 10.2 %copy-start.7 = (bf16[1,256,1024]{2,1,0:T(8,128)(2,1)S(1)}, bf16[1,256,1024]{2,1,0:T(8,128)(2,1)}, u32[]{:S(2)}) copy-start(bf16[1,256,1024]{2,1,0:T(8,128)(2,1)} %param.7) | copy-start | bytes 1572868
  17.0 17.4 %collective-permute-start.4 = (bf16[256,1152]{1,0:T(8,128)(2,1)S(1)}, bf16[256,1152]{1,0:T(8,128)(2,1)}, u32[]{:S(2)}, u32[]{:S(2)}) collective-permute-start(bf16[256,1152]{1,0:T(8,128)(2,1)S(1)} %get-tuple-element.34), channel_id=1, source_target_pairs={{0,2},{2,0},{1,3},{3,1},{4,6},{6,4},{5,7},{7,5},{8,10},{10,8},{9,1... | collective-permute-start | bytes 1769480 | tf_op jit(solution)/shard_map/ppermute | solution.py:26
  20.8 1.7 %collective-permute-start.3 = (bf16[256,512]{1,0:T(8,128)(2,1)}, bf16[256,512]{1,0:T(8,128)(2,1)S(1)}, u32[]{:S(2)}, u32[]{:S(2)}) collective-permute-start(bf16[256,512]{1,0:T(8,128)(2,1)} %collective-permute-done.refs_4_), channel_id=1, source_target_pairs={{0,1},{1,0},{2,3},{3,2},{4,5},{5,4},{6,7},{7,6},{8,9},{9,8},{10,11... | collective-permute-start | bytes 786440 | tf_op jit(solution)/shard_map/ppermute | solution.py:26
  22.0 12.4 %copy-start.8 = (bf16[256,512]{1,0:T(8,128)(2,1)}, bf16[256,512]{1,0:T(8,128)(2,1)S(1)}, u32[]{:S(2)}) copy-start(bf16[256,512]{1,0:T(8,128)(2,1)S(1)} %pad_maximum_fusion.2.refs_8_) | copy-start | bytes 786436
  22.6 11.8 %copy-start.14 = (bf16[256,512]{1,0:T(8,128)(2,1)}, bf16[256,512]{1,0:T(8,128)(2,1)S(1)}, u32[]{:S(2)}) copy-start(bf16[256,512]{1,0:T(8,128)(2,1)S(1)} %collective-permute-done.3.refs_7_) | copy-start | bytes 786436
  22.6 11.0 %collective-permute-start.5 = (bf16[256,512]{1,0:T(8,128)(2,1)S(1)}, bf16[256,512]{1,0:T(8,128)(2,1)S(1)}, u32[]{:S(2)}, u32[]{:S(2)}) collective-permute-start(bf16[256,512]{1,0:T(8,128)(2,1)S(1)} %pad_maximum_fusion.2.refs_8_), channel_id=1, source_target_pairs={{0,4},{4,8},{8,12},{1,5},{5,9},{9,13},{2,6},{6,10},{10,14},{3,7},{... | collective-permute-start | bytes 786440 | tf_op jit(solution)/shard_map/ppermute | solution.py:21
  28.0 12.1 %collective-permute-start.7 = (bf16[256,512]{1,0:T(8,128)(2,1)S(1)}, bf16[256,512]{1,0:T(8,128)(2,1)S(1)}, u32[]{:S(2)}, u32[]{:S(2)}) collective-permute-start(bf16[256,512]{1,0:T(8,128)(2,1)S(1)} %pad_maximum_fusion.2.refs_8_), channel_id=1, source_target_pairs={{1,8},{5,12},{3,10},{7,14},{17,24},{21,28},{19,26},{23,30}} | collective-permute-start | bytes 786440 | tf_op jit(solution)/shard_map/ppermute | solution.py:216
  28.6 11.4 %collective-permute-start.6 = (bf16[256,512]{1,0:T(8,128)(2,1)S(1)}, bf16[256,512]{1,0:T(8,128)(2,1)S(1)}, u32[]{:S(2)}, u32[]{:S(2)}) collective-permute-start(bf16[256,512]{1,0:T(8,128)(2,1)S(1)} %pad_maximum_fusion.2.refs_8_), channel_id=1, source_target_pairs={{0,1},{2,3},{4,5},{6,7},{8,9},{10,11},{12,13},{14,15},{16,17},{18,... | collective-permute-start | bytes 786440 | tf_op jit(solution)/shard_map/ppermute | solution.py:21
  33.6 6.0 %copy-start.13 = (bf16[256,512]{1,0:T(8,128)(2,1)}, bf16[256,512]{1,0:T(8,128)(2,1)S(1)}, u32[]{:S(2)}) copy-start(bf16[256,512]{1,0:T(8,128)(2,1)S(1)} %collective-permute-done.5.refs_4_) | copy-start | bytes 786436
  33.6 6.5 %collective-permute-start.8 = (bf16[256,512]{1,0:T(8,128)(2,1)S(1)}, bf16[256,512]{1,0:T(8,128)(2,1)S(1)}, u32[]{:S(2)}, u32[]{:S(2)}) collective-permute-start(bf16[256,512]{1,0:T(8,128)(2,1)S(1)} %collective-permute-done.5.refs_4_), channel_id=1, source_target_pairs={{0,1},{1,0},{2,3},{3,2},{4,5},{5,4},{6,7},{7,6},{8,9},{9,8},{10,11... | collective-permute-start | bytes 786440 | tf_op jit(solution)/shard_map/ppermute | solution.py:26
  39.6 8.9 %collective-permute-start.11 = (bf16[256,512]{1,0:T(8,128)(2,1)}, bf16[256,512]{1,0:T(8,128)(2,1)S(1)}, u32[]{:S(2)}, u32[]{:S(2)}) collective-permute-start(bf16[256,512]{1,0:T(8,128)(2,1)} %get-tuple-element.21), channel_id=1, source_target_pairs={{0,1},{1,0},{2,3},{3,2},{4,5},{5,4},{6,7},{7,6},{8,9},{9,8},{10,11... | collective-permute-start | bytes 786440 | tf_op jit(solution)/shard_map/ppermute | solution.py:26
  40.1 0.7 copy-start.15
  40.1 0.8 copy-start.16
  40.1 0.8 copy-start.17
  41.0 5.4 %copy-start.12 = (bf16[256,512]{1,0:T(8,128)(2,1)S(1)}, bf16[256,512]{1,0:T(8,128)(2,1)}, u32[]{:S(2)}) copy-start(bf16[256,512]{1,0:T(8,128)(2,1)} %get-tuple-element.19) | copy-start | bytes 786436
  41.0 7.5 %copy-start.4 = (f32[256,512]{1,0:T(8,128)S(1)}, f32[256,512]{1,0:T(8,128)}, u32[]{:S(2)}) copy-start(f32[256,512]{1,0:T(8,128)} %get-tuple-element.20) | copy-start | bytes 1572868
  46.2 5.6 %copy-start.5 = (f32[256,512]{1,0:T(8,128)S(1)}, f32[256,512]{1,0:T(8,128)}, u32[]{:S(2)}) copy-start(f32[256,512]{1,0:T(8,128)} %get-tuple-element.24) | copy-start | bytes 1572868
  46.2 18.0 %copy-start.2 = (f32[256,512]{1,0:T(8,128)S(1)}, f32[256,512]{1,0:T(8,128)}, u32[]{:S(2)}) copy-start(f32[256,512]{1,0:T(8,128)} %get-tuple-element.18) | copy-start | bytes 1572868
  46.2 4.3 %collective-permute-start.15 = (bf16[256,512]{1,0:T(8,128)(2,1)}, bf16[256,512]{1,0:T(8,128)(2,1)S(1)}, u32[]{:S(2)}, u32[]{:S(2)}) collective-permute-start(bf16[256,512]{1,0:T(8,128)(2,1)} %get-tuple-element.25), channel_id=1, source_target_pairs={{0,1},{1,0},{2,3},{3,2},{4,5},{5,4},{6,7},{7,6},{8,9},{9,8},{10,11... | collective-permute-start | bytes 786440 | tf_op jit(solution)/shard_map/ppermute | solution.py:26
  46.4 5.6 %collective-permute-start.10 = (bf16[256,512]{1,0:T(8,128)(2,1)S(1)}, bf16[256,512]{1,0:T(8,128)(2,1)S(1)}, u32[]{:S(2)}, u32[]{:S(2)}) collective-permute-start(bf16[256,512]{1,0:T(8,128)(2,1)S(1)} %copy-done.12), channel_id=1, source_target_pairs={{8,1},{12,5},{10,3},{14,7},{24,17},{28,21},{26,19},{30,23}} | collective-permute-start | bytes 786440 | tf_op jit(solution)/shard_map/ppermute | solution.py:234
  47.2 6.2 %collective-permute-start.9 = (bf16[256,512]{1,0:T(8,128)(2,1)S(1)}, bf16[256,512]{1,0:T(8,128)(2,1)S(1)}, u32[]{:S(2)}, u32[]{:S(2)}) collective-permute-start(bf16[256,512]{1,0:T(8,128)(2,1)S(1)} %copy-done.12), channel_id=1, source_target_pairs={{1,0},{3,2},{5,4},{7,6},{9,8},{11,10},{13,12},{15,14},{17,16},{19,... | collective-permute-start | bytes 786440 | tf_op jit(solution)/shard_map/ppermute | solution.py:21
  48.6 15.6 %collective-permute-start.12 = (bf16[256,512]{1,0:T(8,128)(2,1)S(1)}, bf16[256,512]{1,0:T(8,128)(2,1)S(1)}, u32[]{:S(2)}, u32[]{:S(2)}) collective-permute-start(bf16[256,512]{1,0:T(8,128)(2,1)S(1)} %add_convert_fusion.3), channel_id=1, source_target_pairs={{4,0},{8,4},{12,8},{5,1},{9,5},{13,9},{6,2},{10,6},{14,10},{7,3},{... | collective-permute-start | bytes 786440 | tf_op jit(solution)/shard_map/ppermute | solution.py:21
  49.9 14.5 %collective-permute-start.14 = (bf16[256,512]{1,0:T(8,128)(2,1)}, bf16[256,512]{1,0:T(8,128)(2,1)S(1)}, u32[]{:S(2)}, u32[]{:S(2)}) collective-permute-start(bf16[256,512]{1,0:T(8,128)(2,1)} %get-tuple-element.23), channel_id=1, source_target_pairs={{8,1},{12,5},{10,3},{14,7},{24,17},{28,21},{26,19},{30,23}} | collective-permute-start | bytes 786440 | tf_op jit(solution)/shard_map/ppermute | solution.py:234
  50.6 13.8 %collective-permute-start.13 = (bf16[256,512]{1,0:T(8,128)(2,1)}, bf16[256,512]{1,0:T(8,128)(2,1)S(1)}, u32[]{:S(2)}, u32[]{:S(2)}) collective-permute-start(bf16[256,512]{1,0:T(8,128)(2,1)} %get-tuple-element.23), channel_id=1, source_target_pairs={{1,0},{3,2},{5,4},{7,6},{9,8},{11,10},{13,12},{15,14},{17,16},{19,... | collective-permute-start | bytes 786440 | tf_op jit(solution)/shard_map/ppermute | solution.py:21
  52.0 15.2 %copy-start.3 = (f32[256,512]{1,0:T(8,128)S(1)}, f32[256,512]{1,0:T(8,128)}, u32[]{:S(2)}) copy-start(f32[256,512]{1,0:T(8,128)} %get-tuple-element.22) | copy-start | bytes 1572868
  52.0 15.2 %collective-permute-start.16 = (bf16[256,512]{1,0:T(8,128)(2,1)S(1)}, bf16[256,512]{1,0:T(8,128)(2,1)S(1)}, u32[]{:S(2)}, u32[]{:S(2)}) collective-permute-start(bf16[256,512]{1,0:T(8,128)(2,1)S(1)} %add_convert_fusion.1), channel_id=1, source_target_pairs={{4,0},{8,4},{12,8},{5,1},{9,5},{13,9},{6,2},{10,6},{14,10},{7,3},{... | collective-permute-start | bytes 786440 | tf_op jit(solution)/shard_map/ppermute | solution.py:21
  68.1 6.4 %collective-permute-start.17 = (bf16[256,512]{1,0:T(8,128)(2,1)S(1)}, bf16[256,512]{1,0:T(8,128)(2,1)S(1)}, u32[]{:S(2)}, u32[]{:S(2)}) collective-permute-start(bf16[256,512]{1,0:T(8,128)(2,1)S(1)} %get-tuple-element.39), channel_id=1, source_target_pairs={{0,2},{2,0},{1,3},{3,1},{4,6},{6,4},{5,7},{7,5},{8,10},{10,8},{9,1... | collective-permute-start | bytes 786440 | tf_op jit(solution)/shard_map/ppermute | solution.py:26
  76.4 1.4 %copy-start = (f32[1152,512]{1,0:T(8,128)}, f32[1152,512]{1,0:T(8,128)S(1)}, u32[]{:S(2)}) copy-start(f32[1152,512]{1,0:T(8,128)S(1)} %convolution_multiply_fusion) | copy-start | bytes 7077892
  77.8 8.8 %collective-permute-start.18 = (bf16[576,512]{1,0:T(8,128)(2,1)S(1)}, bf16[576,512]{1,0:T(8,128)(2,1)S(1)}, u32[]{:S(2)}, u32[]{:S(2)}) collective-permute-start(bf16[576,512]{1,0:T(8,128)(2,1)S(1)} %dynamic-slice_convert_fusion), channel_id=1, source_target_pairs={{0,1},{1,0},{2,3},{3,2},{4,5},{5,4},{6,7},{7,6},{8,9},{9,8},{10,11... | collective-permute-start | bytes 1769480 | tf_op jit(solution)/shard_map/ppermute | solution.py:26
  88.2 9.3 %collective-permute-start.19 = (bf16[144,512]{1,0:T(8,128)(2,1)S(1)}, bf16[144,512]{1,0:T(8,128)(2,1)S(1)}, u32[]{:S(2)}, u32[]{:S(2)}) collective-permute-start(bf16[144,512]{1,0:T(8,128)(2,1)S(1)} %get-tuple-element.30), channel_id=1, source_target_pairs={{0,4},{4,8},{8,12},{12,0},{1,5},{5,9},{9,13},{13,1},{2,6},{6,10},{... | collective-permute-start | bytes 442376 | tf_op jit(solution)/shard_map/ppermute | solution.py:26
  93.3 7.4 %collective-permute-start.21 = (bf16[144,512]{1,0:T(8,128)(2,1)S(1)}, bf16[144,512]{1,0:T(8,128)(2,1)S(1)}, u32[]{:S(2)}, u32[]{:S(2)}) collective-permute-start(bf16[144,512]{1,0:T(8,128)(2,1)S(1)} %get-tuple-element.31), channel_id=1, source_target_pairs={{0,12},{4,0},{8,4},{12,8},{1,13},{5,1},{9,5},{13,9},{2,14},{6,2},{... | collective-permute-start | bytes 442376 | tf_op jit(solution)/shard_map/ppermute | solution.py:26
  93.3 12.3 %collective-permute-start.20 = (bf16[144,512]{1,0:T(8,128)(2,1)S(1)}, bf16[144,512]{1,0:T(8,128)(2,1)S(1)}, u32[]{:S(2)}, u32[]{:S(2)}) collective-permute-start(bf16[144,512]{1,0:T(8,128)(2,1)S(1)} %get-tuple-element.32), channel_id=1, source_target_pairs={{0,8},{4,12},{8,0},{12,4},{1,9},{5,13},{9,1},{13,5},{2,10},{6,14},... | collective-permute-start | bytes 442376 | tf_op jit(solution)/shard_map/ppermute | solution.py:26
  105.9 8.6 %collective-permute-start.22 = (bf16[144,512]{1,0:T(8,128)(2,1)S(1)}, bf16[144,512]{1,0:T(8,128)(2,1)S(1)}, u32[]{:S(2)}, u32[]{:S(2)}) collective-permute-start(bf16[144,512]{1,0:T(8,128)(2,1)S(1)} %get-tuple-element.28), channel_id=1, source_target_pairs={{0,4},{4,8},{8,12},{12,0},{1,5},{5,9},{9,13},{13,1},{2,6},{6,10},{... | collective-permute-start | bytes 442376 | tf_op jit(solution)/shard_map/ppermute | solution.py:26
  106.8 16.0 %collective-permute-start.24 = (bf16[144,512]{1,0:T(8,128)(2,1)S(1)}, bf16[144,512]{1,0:T(8,128)(2,1)S(1)}, u32[]{:S(2)}, u32[]{:S(2)}) collective-permute-start(bf16[144,512]{1,0:T(8,128)(2,1)S(1)} %get-tuple-element.28), channel_id=1, source_target_pairs={{0,12},{4,0},{8,4},{12,8},{1,13},{5,1},{9,5},{13,9},{2,14},{6,2},{... | collective-permute-start | bytes 442376 | tf_op jit(solution)/shard_map/ppermute | solution.py:26
  109.7 13.0 %collective-permute-start.23 = (bf16[144,512]{1,0:T(8,128)(2,1)S(1)}, bf16[144,512]{1,0:T(8,128)(2,1)S(1)}, u32[]{:S(2)}, u32[]{:S(2)}) collective-permute-start(bf16[144,512]{1,0:T(8,128)(2,1)S(1)} %get-tuple-element.28), channel_id=1, source_target_pairs={{0,8},{4,12},{8,0},{12,4},{1,9},{5,13},{9,1},{13,5},{2,10},{6,14},... | collective-permute-start | bytes 442376 | tf_op jit(solution)/shard_map/ppermute | solution.py:26
  122.8 1.0 copy-start.9
  122.8 1.0 copy-start.10
  122.9 2.5 %collective-permute-start.25 = (bf16[576,512]{1,0:T(8,128)(2,1)S(1)}, bf16[576,512]{1,0:T(8,128)(2,1)S(1)}, u32[]{:S(2)}, u32[]{:S(2)}) collective-permute-start(bf16[576,512]{1,0:T(8,128)(2,1)S(1)} %convert_element_type.102), channel_id=1, source_target_pairs={{0,1},{1,0},{2,3},{3,2},{4,5},{5,4},{6,7},{7,6},{8,9},{9,8},{10,11... | collective-permute-start | bytes 1769480 | tf_op jit(solution)/shard_map/ppermute | solution.py:26

commit v9 on v8

--- a/solution.py
+++ b/solution.py
@@ -252,11 +252,13 @@
         if previous is not None:
             own_kv, _ = lax.optimization_barrier((own_kv, previous))
         kv_blocks = forward_halo(own_kv)
-        previous = kv_blocks[:-1]
+        if key_parts:
+            kv_blocks, _ = lax.optimization_barrier((kv_blocks, (key_parts[-1], value_parts[-1])))
         grad_q_g, *grad_pieces = attention(
             flag, lo_rel, query_heads[0][:, q_cols], grad_out[0][:, q_cols], kv_blocks, slots,
             per_group, 1, margin, inputs[1:] if group == 0 else [], chip_route,
         )
+        previous = grad_q_g
         total = low(backward_halo(grad_pieces))
         grad_q_parts.append(grad_q_g)
         key_parts.append(total[:, :HEAD_DIM])

time: 128 us -> 130 us (1.016)
  waiting for transfers between devices: 46.7 us -> 51.2 us
  starting transfers between devices: 51.7 us -> 48.9 us
    ppermute x14, waiting for transfers between devices: 30.4 us -> 38.8 us  [rotated(): lax.ppermute(value, axis, [(source, (source + steps) % count) for source...]
    ppermute x8, starting transfers between devices: 26.5 us -> 18.5 us  [passed_along(): lax.ppermute(value, axis, [(source, source + steps) for source in range(f...]
    ppermute x14, starting transfers between devices: 21.7 us -> 27 us  [rotated(): lax.ppermute(value, axis, [(source, (source + steps) % count) for source...]
    ppermute x8, waiting for transfers between devices: 16.3 us -> 12.3 us  [passed_along(): lax.ppermute(value, axis, [(source, source + steps) for source in range(f...]
    convert_element_type x4, other arithmetic: 0.42 us -> 2.52 us  [low(): return value.astype(jnp.bfloat16)]
  transfers between devices with their start and end apart: 26 -> 26, of which waited for: 12 -> 11; matrix products, arithmetic and copies ran while one was open for 4% -> 5% of each run, Pallas kernels for 8% -> 0%
where the time goes in v9:
time: 130 us
  waiting for transfers between devices  51.2 us (39%)
  starting transfers between devices  48.9 us (38%)
  Pallas kernels  10.5 us (8%)
  other arithmetic  9.97 us (8%)
  local copies, waits for them, and re-layouts  7.24 us (6%)
    ppermute x14, waiting for transfers between devices, rotated(): lax.ppermute(value, axis, [(source, (source + steps) % count) for source...  38.8 us
    ppermute x14, starting transfers between devices, rotated(): lax.ppermute(value, axis, [(source, (source + steps) % count) for source...  27 us
    ppermute x8, starting transfers between devices, passed_along(): lax.ppermute(value, axis, [(source, source + steps) for source in range(f...  18.5 us
    ppermute x8, waiting for transfers between devices, passed_along(): lax.ppermute(value, axis, [(source, source + steps) for source in range(f...  12.3 us
    pallas_call x2, Pallas kernels, attention(): pl.pallas_call(kernel, out_shape=(jax.ShapeDtypeStruct((rows, width), jnp...  10.5 us
    unnamed x36, local copies, waits for them, and re-layouts  3.78 us
  transfers between devices with their start and end apart: 26, of which 11 were waited for; matrix products, arithmetic and copies ran while one was open for 5% of the time, Pallas kernels for 0%

profile of v9, /device:TPU:0, one launch (start us, length us, event | category | flops | bytes accessed | tf_op | source)
XLA Modules:
  0.0 129.7 jit_solution(1238077048914023743)
XLA Ops:
  0.6 1.9 %fusion.16 = (bf16[256,256]{1,0:T(8,128)(2,1)S(1)}, bf16[256,256]{1,0:T(8,128)(2,1)S(1)}, bf16[256,256]{1,0:T(8,128)(2,1)}, bf16[256,256]{1,0:T(8,128)(2,1)S(1)}) fusion(bf16[256,512]{1,0:T(8,128)(2,1)} %bitcast.19, bf16[256,512]{1,0:T(8,128)(2,1)} %bitcast.20), kind=kLoop, calls=%fused_computation.43 | loop fusion | bytes 1048576 | tf_op jit(solution)/shard_map/slice | solution.py:251
  2.5 0.7 pad_maximum_fusion.1.refs_8_
  3.2 5.6 %collective-permute-start = (bf16[256,512]{1,0:T(8,128)(2,1)}, bf16[256,512]{1,0:T(8,128)(2,1)}, u32[]{:S(2)}, u32[]{:S(2)}) collective-permute-start(bf16[256,512]{1,0:T(8,128)(2,1)} %pad_maximum_fusion.1.refs_8_), channel_id=1, source_target_pairs={{0,4},{4,8},{8,12},{1,5},{5,9},{9,13},{2,6},{6,10},{10,14},{3,7},{... | collective-permute-start | bytes 786440 | tf_op jit(solution)/shard_map/ppermute | solution.py:21
  8.9 2.1 %collective-permute-start.1 = (bf16[256,512]{1,0:T(8,128)(2,1)}, bf16[256,512]{1,0:T(8,128)(2,1)}, u32[]{:S(2)}, u32[]{:S(2)}) collective-permute-start(bf16[256,512]{1,0:T(8,128)(2,1)} %pad_maximum_fusion.1.refs_8_), channel_id=1, source_target_pairs={{0,1},{2,3},{4,5},{6,7},{8,9},{10,11},{12,13},{14,15},{16,17},{18,... | collective-permute-start | bytes 786440 | tf_op jit(solution)/shard_map/ppermute | solution.py:21
  11.0 1.4 %collective-permute-start.2 = (bf16[256,512]{1,0:T(8,128)(2,1)}, bf16[256,512]{1,0:T(8,128)(2,1)}, u32[]{:S(2)}, u32[]{:S(2)}) collective-permute-start(bf16[256,512]{1,0:T(8,128)(2,1)} %pad_maximum_fusion.1.refs_8_), channel_id=1, source_target_pairs={{1,8},{5,12},{3,10},{7,14},{17,24},{21,28},{19,26},{23,30}} | collective-permute-start | bytes 786440 | tf_op jit(solution)/shard_map/ppermute | solution.py:216
  12.4 0.2 dynamic-slice_bitcast_fusion
  12.5 1.5 %collective-permute-start.4 = (bf16[256,1152]{1,0:T(8,128)(2,1)S(1)}, bf16[256,1152]{1,0:T(8,128)(2,1)S(1)}, u32[]{:S(2)}, u32[]{:S(2)}) collective-permute-start(bf16[256,1152]{1,0:T(8,128)(2,1)S(1)} %get-tuple-element.44), channel_id=1, source_target_pairs={{0,2},{2,0},{1,3},{3,1},{4,6},{6,4},{5,7},{7,5},{8,10},{10,8},{9,1... | collective-permute-start | bytes 1769480 | tf_op jit(solution)/shard_map/ppermute | solution.py:26
  14.1 0.1 select_reduce_fusion
  14.1 0.1 copy.13
  14.3 0.7 subtract_add_fusion.refs_1_
  15.0 3.0 %collective-permute-start.3 = (bf16[256,512]{1,0:T(8,128)(2,1)}, bf16[256,512]{1,0:T(8,128)(2,1)S(1)}, u32[]{:S(2)}, u32[]{:S(2)}) collective-permute-start(bf16[256,512]{1,0:T(8,128)(2,1)} %collective-permute-done.refs_4_), channel_id=1, source_target_pairs={{0,1},{1,0},{2,3},{3,2},{4,5},{5,4},{6,7},{7,6},{8,9},{9,8},{10,11... | collective-permute-start | bytes 786440 | tf_op jit(solution)/shard_map/ppermute | solution.py:26
  18.0 1.0 fusion.12
  19.0 0.4 collective-permute-done.3.refs_7_
  19.4 7.1 %collective-permute-done.4.refs_9_ = bf16[256,1152]{1,0:T(8,128)(2,1)S(1)} collective-permute-done((bf16[256,1152]{1,0:T(8,128)(2,1)S(1)}, bf16[256,1152]{1,0:T(8,128)(2,1)S(1)}, u32[]{:S(2)}, u32[]{:S(2)}) %collective-permute-start.4) | collective-permute-done | bytes 589856 | tf_op jit(solution)/shard_map/ppermute | solution.py:26
  26.5 0.8 copy-done.11
  27.3 5.3 %shard_map.93 = (bf16[256,512]{1,0:T(8,128)(2,1)}, bf16[256,512]{1,0:T(8,128)(2,1)}, bf16[256,512]{1,0:T(8,128)(2,1)}, f32[256,512]{1,0:T(8,128)}, f32[256,512]{1,0:T(8,128)}) custom-call(s32[1]{0:T(128)} %bitcast.refs_0_, s32[256,1]{1,0:T(8,128)} %subtract_add_fusion.refs_1_, bf16[256,512]{1,0:T(8,128)(2,1)} %get-tuple-element.62.refs_2_, ...), custom_call_target="tpu_custom_call" | custom-call | flops 1342177280 | bytes 3932160 | tf_op jit(solution)/shard_map/pallas_call | solution.py:160
  32.5 2.2 %collective-permute-start.11 = (bf16[256,512]{1,0:T(8,128)(2,1)}, bf16[256,512]{1,0:T(8,128)(2,1)S(1)}, u32[]{:S(2)}, u32[]{:S(2)}) collective-permute-start(bf16[256,512]{1,0:T(8,128)(2,1)} %get-tuple-element.25), channel_id=1, source_target_pairs={{0,1},{1,0},{2,3},{3,2},{4,5},{5,4},{6,7},{7,6},{8,9},{9,8},{10,11... | collective-permute-start | bytes 786440 | tf_op jit(solution)/shard_map/ppermute | solution.py:26
  34.8 0.7 collective-permute-start.10
  35.4 1.3 collective-permute-start.9
  36.7 2.8 %collective-permute-start.5 = (bf16[256,512]{1,0:T(8,128)(2,1)S(1)}, bf16[256,512]{1,0:T(8,128)(2,1)S(1)}, u32[]{:S(2)}, u32[]{:S(2)}) collective-permute-start(bf16[256,512]{1,0:T(8,128)(2,1)S(1)} %pad_maximum_fusion.2.refs_8_), channel_id=1, source_target_pairs={{0,4},{4,8},{8,12},{1,5},{5,9},{9,13},{2,6},{6,10},{10,14},{3,7},{... | collective-permute-start | bytes 786440 | tf_op jit(solution)/shard_map/ppermute | solution.py:21
  39.6 1.1 add_convert_fusion.3
  40.7 1.3 collective-permute-start.12
  42.0 2.8 %collective-permute-start.6 = (bf16[256,512]{1,0:T(8,128)(2,1)S(1)}, bf16[256,512]{1,0:T(8,128)(2,1)S(1)}, u32[]{:S(2)}, u32[]{:S(2)}) collective-permute-start(bf16[256,512]{1,0:T(8,128)(2,1)S(1)} %pad_maximum_fusion.2.refs_8_), channel_id=1, source_target_pairs={{0,1},{2,3},{4,5},{6,7},{8,9},{10,11},{12,13},{14,15},{16,17},{18,... | collective-permute-start | bytes 786440 | tf_op jit(solution)/shard_map/ppermute | solution.py:21
  44.8 1.3 collective-permute-done.5.refs_4_
  46.1 0.7 collective-permute-start.7
  46.7 6.9 %collective-permute-start.8 = (bf16[256,512]{1,0:T(8,128)(2,1)S(1)}, bf16[256,512]{1,0:T(8,128)(2,1)S(1)}, u32[]{:S(2)}, u32[]{:S(2)}) collective-permute-start(bf16[256,512]{1,0:T(8,128)(2,1)S(1)} %collective-permute-done.5.refs_4_), channel_id=1, source_target_pairs={{0,1},{1,0},{2,3},{3,2},{4,5},{5,4},{6,7},{7,6},{8,9},{9,8},{10,11... | collective-permute-start | bytes 786440 | tf_op jit(solution)/shard_map/ppermute | solution.py:26
  53.7 0.1 add_convert_fusion.2
  53.9 0.9 collective-permute-done.8.refs_7_
  54.9 0.7 copy-done.16
  55.6 5.2 %shard_map.94 = (bf16[256,512]{1,0:T(8,128)(2,1)}, bf16[256,512]{1,0:T(8,128)(2,1)}, bf16[256,512]{1,0:T(8,128)(2,1)}, f32[256,512]{1,0:T(8,128)}, f32[256,512]{1,0:T(8,128)}) custom-call(s32[1]{0:T(128)} %bitcast.refs_0_, s32[256,1]{1,0:T(8,128)} %subtract_add_fusion.refs_1_, bf16[256,512]{1,0:T(8,128)(2,1)} %get-tuple-element.61.refs_2_, ...), custom_call_target="tpu_custom_call" | custom-call | flops 1342177280 | bytes 3932160 | tf_op jit(solution)/shard_map/pallas_call | solution.py:160
  60.8 2.2 %collective-permute-start.15 = (bf16[256,512]{1,0:T(8,128)(2,1)}, bf16[256,512]{1,0:T(8,128)(2,1)S(1)}, u32[]{:S(2)}, u32[]{:S(2)}) collective-permute-start(bf16[256,512]{1,0:T(8,128)(2,1)} %get-tuple-element.35), channel_id=1, source_target_pairs={{0,1},{1,0},{2,3},{3,2},{4,5},{5,4},{6,7},{7,6},{8,9},{9,8},{10,11... | collective-permute-start | bytes 786440 | tf_op jit(solution)/shard_map/ppermute | solution.py:26
  63.0 0.7 collective-permute-start.14
  63.6 1.3 collective-permute-start.13
  65.0 1.1 add_convert_fusion.1
  66.1 1.3 collective-permute-start.16
  67.4 11.0 %collective-permute-done.16 = bf16[256,512]{1,0:T(8,128)(2,1)S(1)} collective-permute-done((bf16[256,512]{1,0:T(8,128)(2,1)S(1)}, bf16[256,512]{1,0:T(8,128)(2,1)S(1)}, u32[]{:S(2)}, u32[]{:S(2)}) %collective-permute-start.16) | collective-permute-done | bytes 262176 | tf_op jit(solution)/shard_map/ppermute | solution.py:21
  78.4 0.1 add_convert_fusion
  78.6 0.7 pad_maximum_fusion.3
  79.3 1.4 %collective-permute-start.17 = (bf16[256,512]{1,0:T(8,128)(2,1)S(1)}, bf16[256,512]{1,0:T(8,128)(2,1)S(1)}, u32[]{:S(2)}, u32[]{:S(2)}) collective-permute-start(bf16[256,512]{1,0:T(8,128)(2,1)S(1)} %get-tuple-element.49), channel_id=1, source_target_pairs={{0,2},{2,0},{1,3},{3,1},{4,6},{6,4},{5,7},{7,5},{8,10},{10,8},{9,1... | collective-permute-start | bytes 786440 | tf_op jit(solution)/shard_map/ppermute | solution.py:26
  80.8 7.0 %collective-permute-done.17 = bf16[256,512]{1,0:T(8,128)(2,1)S(1)} collective-permute-done((bf16[256,512]{1,0:T(8,128)(2,1)S(1)}, bf16[256,512]{1,0:T(8,128)(2,1)S(1)}, u32[]{:S(2)}, u32[]{:S(2)}) %collective-permute-start.17) | collective-permute-done | bytes 262176 | tf_op jit(solution)/shard_map/ppermute | solution.py:26
  87.7 0.8 convolution_multiply_fusion
  88.6 1.4 %copy-done = f32[1152,512]{1,0:T(8,128)} copy-done((f32[1152,512]{1,0:T(8,128)}, f32[1152,512]{1,0:T(8,128)S(1)}, u32[]{:S(2)}) %copy-start) | copy-done | bytes 2359320
  90.0 0.1 dynamic-slice_convert_fusion
  90.0 0.1 collective-permute-start.18
  90.2 1.9 %collective-permute-done.18 = bf16[576,512]{1,0:T(8,128)(2,1)S(1)} collective-permute-done((bf16[576,512]{1,0:T(8,128)(2,1)S(1)}, bf16[576,512]{1,0:T(8,128)(2,1)S(1)}, u32[]{:S(2)}, u32[]{:S(2)}) %collective-permute-start.18) | collective-permute-done | bytes 589856 | tf_op jit(solution)/shard_map/ppermute | solution.py:26
  92.1 1.4 %convert_add_fusion = f32[576,512]{1,0:T(8,128)S(1)} fusion(bf16[576,512]{1,0:T(8,128)(2,1)S(1)} %collective-permute-done.18, f32[1152,512]{1,0:T(8,128)} %copy-done, s32[]{:T(128)S(6)} %select_n.90), kind=kLoop, calls=%fused_computation.7 | loop fusion | flops 589824 | bytes 2949124 | tf_op jit(solution)/shard_map/add | solution.py:286
  93.6 2.7 %collective-permute-start.21 = (bf16[144,512]{1,0:T(8,128)(2,1)S(1)}, bf16[144,512]{1,0:T(8,128)(2,1)S(1)}, u32[]{:S(2)}, u32[]{:S(2)}) collective-permute-start(bf16[144,512]{1,0:T(8,128)(2,1)S(1)} %get-tuple-element.41), channel_id=1, source_target_pairs={{0,12},{4,0},{8,4},{12,8},{1,13},{5,1},{9,5},{13,9},{2,14},{6,2},{... | collective-permute-start | bytes 442376 | tf_op jit(solution)/shard_map/ppermute | solution.py:26
  96.4 1.7 %collective-permute-start.20 = (bf16[144,512]{1,0:T(8,128)(2,1)S(1)}, bf16[144,512]{1,0:T(8,128)(2,1)S(1)}, u32[]{:S(2)}, u32[]{:S(2)}) collective-permute-start(bf16[144,512]{1,0:T(8,128)(2,1)S(1)} %get-tuple-element.42), channel_id=1, source_target_pairs={{0,8},{4,12},{8,0},{12,4},{1,9},{5,13},{9,1},{13,5},{2,10},{6,14},... | collective-permute-start | bytes 442376 | tf_op jit(solution)/shard_map/ppermute | solution.py:26
  98.1 1.0 collective-permute-start.19
  99.1 1.7 %collective-permute-done.21 = bf16[144,512]{1,0:T(8,128)(2,1)S(1)} collective-permute-done((bf16[144,512]{1,0:T(8,128)(2,1)S(1)}, bf16[144,512]{1,0:T(8,128)(2,1)S(1)}, u32[]{:S(2)}, u32[]{:S(2)}) %collective-permute-start.21) | collective-permute-done | bytes 147488 | tf_op jit(solution)/shard_map/ppermute | solution.py:26
  100.8 10.7 %collective-permute-done.20 = bf16[144,512]{1,0:T(8,128)(2,1)S(1)} collective-permute-done((bf16[144,512]{1,0:T(8,128)(2,1)S(1)}, bf16[144,512]{1,0:T(8,128)(2,1)S(1)}, u32[]{:S(2)}, u32[]{:S(2)}) %collective-permute-start.20) | collective-permute-done | bytes 147488 | tf_op jit(solution)/shard_map/ppermute | solution.py:26
  111.5 0.1 broadcast_in_dim.28
  111.6 0.1 fusion.8
  111.8 1.3 collective-permute-start.23
  113.1 2.8 %collective-permute-start.24 = (bf16[144,512]{1,0:T(8,128)(2,1)S(1)}, bf16[144,512]{1,0:T(8,128)(2,1)S(1)}, u32[]{:S(2)}, u32[]{:S(2)}) collective-permute-start(bf16[144,512]{1,0:T(8,128)(2,1)S(1)} %get-tuple-element.38), channel_id=1, source_target_pairs={{0,12},{4,0},{8,4},{12,8},{1,13},{5,1},{9,5},{13,9},{2,14},{6,2},{... | collective-permute-start | bytes 442376 | tf_op jit(solution)/shard_map/ppermute | solution.py:26
  115.9 4.5 %collective-permute-done.22 = bf16[144,512]{1,0:T(8,128)(2,1)S(1)} collective-permute-done((bf16[144,512]{1,0:T(8,128)(2,1)S(1)}, bf16[144,512]{1,0:T(8,128)(2,1)S(1)}, u32[]{:S(2)}, u32[]{:S(2)}) %collective-permute-start.22) | collective-permute-done | bytes 147488 | tf_op jit(solution)/shard_map/ppermute | solution.py:26
  120.4 4.7 %collective-permute-done.23 = bf16[144,512]{1,0:T(8,128)(2,1)S(1)} collective-permute-done((bf16[144,512]{1,0:T(8,128)(2,1)S(1)}, bf16[144,512]{1,0:T(8,128)(2,1)S(1)}, u32[]{:S(2)}, u32[]{:S(2)}) %collective-permute-start.23) | collective-permute-done | bytes 147488 | tf_op jit(solution)/shard_map/ppermute | solution.py:26
  125.2 0.1 convert_element_type.102
  125.3 0.7 copy-done.8
  126.1 0.1 copy-done.9
  126.1 0.9 maximum_bitcast_fusion
  127.0 0.7 maximum_bitcast_fusion.1
  127.7 0.3 convert_select_fusion.1
  128.0 1.6 %pad_maximum_fusion = f32[1152,512]{1,0:T(8,128)} fusion(f32[576,512]{1,0:T(8,128)S(1)} %get-tuple-element.37, f32[576,512]{1,0:T(8,128)S(1)} %get-tuple-element.36), kind=kLoop, calls=%fused_computation.1 | loop fusion | flops 589824 | bytes 4718592 | tf_op jit(solution)/shard_map/concatenate | solution.py:292
  (56 shorter events, 0.4 us)
Async XLA Ops:
  0.6 11.7 %copy-start.1 = (bf16[1,256,2304]{2,1,0:T(8,128)(2,1)S(1)}, bf16[1,256,2304]{2,1,0:T(8,128)(2,1)}, u32[]{:S(2)}) copy-start(bf16[1,256,2304]{2,1,0:T(8,128)(2,1)} %param.6) | copy-start | bytes 3538948
  3.2 11.8 %collective-permute-start = (bf16[256,512]{1,0:T(8,128)(2,1)}, bf16[256,512]{1,0:T(8,128)(2,1)}, u32[]{:S(2)}, u32[]{:S(2)}) collective-permute-start(bf16[256,512]{1,0:T(8,128)(2,1)} %pad_maximum_fusion.1.refs_8_), channel_id=1, source_target_pairs={{0,4},{4,8},{8,12},{1,5},{5,9},{9,13},{2,6},{6,10},{10,14},{3,7},{... | collective-permute-start | bytes 786440 | tf_op jit(solution)/shard_map/ppermute | solution.py:21
  8.9 10.1 %collective-permute-start.1 = (bf16[256,512]{1,0:T(8,128)(2,1)}, bf16[256,512]{1,0:T(8,128)(2,1)}, u32[]{:S(2)}, u32[]{:S(2)}) collective-permute-start(bf16[256,512]{1,0:T(8,128)(2,1)} %pad_maximum_fusion.1.refs_8_), channel_id=1, source_target_pairs={{0,1},{2,3},{4,5},{6,7},{8,9},{10,11},{12,13},{14,15},{16,17},{18,... | collective-permute-start | bytes 786440 | tf_op jit(solution)/shard_map/ppermute | solution.py:21
  11.0 7.9 %collective-permute-start.2 = (bf16[256,512]{1,0:T(8,128)(2,1)}, bf16[256,512]{1,0:T(8,128)(2,1)}, u32[]{:S(2)}, u32[]{:S(2)}) collective-permute-start(bf16[256,512]{1,0:T(8,128)(2,1)} %pad_maximum_fusion.1.refs_8_), channel_id=1, source_target_pairs={{1,8},{5,12},{3,10},{7,14},{17,24},{21,28},{19,26},{23,30}} | collective-permute-start | bytes 786440 | tf_op jit(solution)/shard_map/ppermute | solution.py:216
  12.4 1.7 %copy-start.10 = (s32[1,12]{1,0:T(1,128)S(1)}, s32[1,12]{1,0:T(1,128)}, u32[]{:S(2)}) copy-start(s32[1,12]{1,0:T(1,128)} %param.11) | copy-start | bytes 148
  12.4 5.6 %copy-start.4 = (bf16[1,256,1024]{2,1,0:T(8,128)(2,1)S(1)}, bf16[1,256,1024]{2,1,0:T(8,128)(2,1)}, u32[]{:S(2)}) copy-start(bf16[1,256,1024]{2,1,0:T(8,128)(2,1)} %param.10) | copy-start | bytes 1572868
  12.4 5.6 %copy-start.5 = (bf16[1,256,1024]{2,1,0:T(8,128)(2,1)S(1)}, bf16[1,256,1024]{2,1,0:T(8,128)(2,1)}, u32[]{:S(2)}) copy-start(bf16[1,256,1024]{2,1,0:T(8,128)(2,1)} %param.7) | copy-start | bytes 1572868
  12.5 13.9 %collective-permute-start.4 = (bf16[256,1152]{1,0:T(8,128)(2,1)S(1)}, bf16[256,1152]{1,0:T(8,128)(2,1)S(1)}, u32[]{:S(2)}, u32[]{:S(2)}) collective-permute-start(bf16[256,1152]{1,0:T(8,128)(2,1)S(1)} %get-tuple-element.44), channel_id=1, source_target_pairs={{0,2},{2,0},{1,3},{3,1},{4,6},{6,4},{5,7},{7,5},{8,10},{10,8},{9,1... | collective-permute-start | bytes 1769480 | tf_op jit(solution)/shard_map/ppermute | solution.py:26
  15.0 4.3 %collective-permute-start.3 = (bf16[256,512]{1,0:T(8,128)(2,1)}, bf16[256,512]{1,0:T(8,128)(2,1)S(1)}, u32[]{:S(2)}, u32[]{:S(2)}) collective-permute-start(bf16[256,512]{1,0:T(8,128)(2,1)} %collective-permute-done.refs_4_), channel_id=1, source_target_pairs={{0,1},{1,0},{2,3},{3,2},{4,5},{5,4},{6,7},{7,6},{8,9},{9,8},{10,11... | collective-permute-start | bytes 786440 | tf_op jit(solution)/shard_map/ppermute | solution.py:26
  19.3 7.1 %copy-start.17 = (bf16[256,512]{1,0:T(8,128)(2,1)}, bf16[256,512]{1,0:T(8,128)(2,1)S(1)}, u32[]{:S(2)}) copy-start(bf16[256,512]{1,0:T(8,128)(2,1)S(1)} %collective-permute-done.3.refs_7_) | copy-start | bytes 786436
  26.5 0.8 copy-start.11
  27.3 7.4 %copy-start.6 = (bf16[256,256]{1,0:T(8,128)(2,1)S(1)}, bf16[256,256]{1,0:T(8,128)(2,1)}, u32[]{:S(2)}) copy-start(bf16[256,256]{1,0:T(8,128)(2,1)} %get-tuple-element.59) | copy-start | bytes 393220
  32.5 21.2 %copy-start.2 = (f32[256,512]{1,0:T(8,128)S(1)}, f32[256,512]{1,0:T(8,128)}, u32[]{:S(2)}) copy-start(f32[256,512]{1,0:T(8,128)} %get-tuple-element.22) | copy-start | bytes 1572868
  32.5 7.0 %collective-permute-start.11 = (bf16[256,512]{1,0:T(8,128)(2,1)}, bf16[256,512]{1,0:T(8,128)(2,1)S(1)}, u32[]{:S(2)}, u32[]{:S(2)}) collective-permute-start(bf16[256,512]{1,0:T(8,128)(2,1)} %get-tuple-element.25), channel_id=1, source_target_pairs={{0,1},{1,0},{2,3},{3,2},{4,5},{5,4},{6,7},{7,6},{8,9},{9,8},{10,11... | collective-permute-start | bytes 786440 | tf_op jit(solution)/shard_map/ppermute | solution.py:26
  34.8 19.1 %copy-start.7 = (bf16[256,512]{1,0:T(8,128)(2,1)}, bf16[256,512]{1,0:T(8,128)(2,1)S(1)}, u32[]{:S(2)}) copy-start(bf16[256,512]{1,0:T(8,128)(2,1)S(1)} %pad_maximum_fusion.2.refs_8_) | copy-start | bytes 786436
  34.8 12.0 %collective-permute-start.10 = (bf16[256,512]{1,0:T(8,128)(2,1)}, bf16[256,512]{1,0:T(8,128)(2,1)S(1)}, u32[]{:S(2)}, u32[]{:S(2)}) collective-permute-start(bf16[256,512]{1,0:T(8,128)(2,1)} %get-tuple-element.23), channel_id=1, source_target_pairs={{8,1},{12,5},{10,3},{14,7},{24,17},{28,21},{26,19},{30,23}} | collective-permute-start | bytes 786440 | tf_op jit(solution)/shard_map/ppermute | solution.py:234
  35.4 18.2 %collective-permute-start.9 = (bf16[256,512]{1,0:T(8,128)(2,1)}, bf16[256,512]{1,0:T(8,128)(2,1)S(1)}, u32[]{:S(2)}, u32[]{:S(2)}) collective-permute-start(bf16[256,512]{1,0:T(8,128)(2,1)} %get-tuple-element.23), channel_id=1, source_target_pairs={{1,0},{3,2},{5,4},{7,6},{9,8},{11,10},{13,12},{15,14},{17,16},{19,... | collective-permute-start | bytes 786440 | tf_op jit(solution)/shard_map/ppermute | solution.py:21
  36.7 9.3 %collective-permute-start.5 = (bf16[256,512]{1,0:T(8,128)(2,1)S(1)}, bf16[256,512]{1,0:T(8,128)(2,1)S(1)}, u32[]{:S(2)}, u32[]{:S(2)}) collective-permute-start(bf16[256,512]{1,0:T(8,128)(2,1)S(1)} %pad_maximum_fusion.2.refs_8_), channel_id=1, source_target_pairs={{0,4},{4,8},{8,12},{1,5},{5,9},{9,13},{2,6},{6,10},{10,14},{3,7},{... | collective-permute-start | bytes 786440 | tf_op jit(solution)/shard_map/ppermute | solution.py:21
  40.7 13.0 %collective-permute-start.12 = (bf16[256,512]{1,0:T(8,128)(2,1)S(1)}, bf16[256,512]{1,0:T(8,128)(2,1)S(1)}, u32[]{:S(2)}, u32[]{:S(2)}) collective-permute-start(bf16[256,512]{1,0:T(8,128)(2,1)S(1)} %add_convert_fusion.3), channel_id=1, source_target_pairs={{4,0},{8,4},{12,8},{5,1},{9,5},{13,9},{6,2},{10,6},{14,10},{7,3},{... | collective-permute-start | bytes 786440 | tf_op jit(solution)/shard_map/ppermute | solution.py:21
  42.0 11.9 %collective-permute-start.6 = (bf16[256,512]{1,0:T(8,128)(2,1)S(1)}, bf16[256,512]{1,0:T(8,128)(2,1)S(1)}, u32[]{:S(2)}, u32[]{:S(2)}) collective-permute-start(bf16[256,512]{1,0:T(8,128)(2,1)S(1)} %pad_maximum_fusion.2.refs_8_), channel_id=1, source_target_pairs={{0,1},{2,3},{4,5},{6,7},{8,9},{10,11},{12,13},{14,15},{16,17},{18,... | collective-permute-start | bytes 786440 | tf_op jit(solution)/shard_map/ppermute | solution.py:21
  46.1 8.8 %copy-start.13 = (bf16[256,512]{1,0:T(8,128)(2,1)}, bf16[256,512]{1,0:T(8,128)(2,1)S(1)}, u32[]{:S(2)}) copy-start(bf16[256,512]{1,0:T(8,128)(2,1)S(1)} %collective-permute-done.5.refs_4_) | copy-start | bytes 786436
  46.1 7.8 %collective-permute-start.7 = (bf16[256,512]{1,0:T(8,128)(2,1)S(1)}, bf16[256,512]{1,0:T(8,128)(2,1)S(1)}, u32[]{:S(2)}, u32[]{:S(2)}) collective-permute-start(bf16[256,512]{1,0:T(8,128)(2,1)S(1)} %pad_maximum_fusion.2.refs_8_), channel_id=1, source_target_pairs={{1,8},{5,12},{3,10},{7,14},{17,24},{21,28},{19,26},{23,30}} | collective-permute-start | bytes 786440 | tf_op jit(solution)/shard_map/ppermute | solution.py:216
  46.7 8.1 %collective-permute-start.8 = (bf16[256,512]{1,0:T(8,128)(2,1)S(1)}, bf16[256,512]{1,0:T(8,128)(2,1)S(1)}, u32[]{:S(2)}, u32[]{:S(2)}) collective-permute-start(bf16[256,512]{1,0:T(8,128)(2,1)S(1)} %collective-permute-done.5.refs_4_), channel_id=1, source_target_pairs={{0,1},{1,0},{2,3},{3,2},{4,5},{5,4},{6,7},{7,6},{8,9},{9,8},{10,11... | collective-permute-start | bytes 786440 | tf_op jit(solution)/shard_map/ppermute | solution.py:26
  53.9 1.0 copy-start.14
  53.9 0.9 copy-start.15
  54.8 0.7 copy-start.16
  60.8 17.6 %copy-start.3 = (f32[256,512]{1,0:T(8,128)S(1)}, f32[256,512]{1,0:T(8,128)}, u32[]{:S(2)}) copy-start(f32[256,512]{1,0:T(8,128)} %get-tuple-element.32) | copy-start | bytes 1572868
  60.8 4.2 %collective-permute-start.15 = (bf16[256,512]{1,0:T(8,128)(2,1)}, bf16[256,512]{1,0:T(8,128)(2,1)S(1)}, u32[]{:S(2)}, u32[]{:S(2)}) collective-permute-start(bf16[256,512]{1,0:T(8,128)(2,1)} %get-tuple-element.35), channel_id=1, source_target_pairs={{0,1},{1,0},{2,3},{3,2},{4,5},{5,4},{6,7},{7,6},{8,9},{9,8},{10,11... | collective-permute-start | bytes 786440 | tf_op jit(solution)/shard_map/ppermute | solution.py:26
  63.0 4.4 %collective-permute-start.14 = (bf16[256,512]{1,0:T(8,128)(2,1)}, bf16[256,512]{1,0:T(8,128)(2,1)S(1)}, u32[]{:S(2)}, u32[]{:S(2)}) collective-permute-start(bf16[256,512]{1,0:T(8,128)(2,1)} %get-tuple-element.33), channel_id=1, source_target_pairs={{8,1},{12,5},{10,3},{14,7},{24,17},{28,21},{26,19},{30,23}} | collective-permute-start | bytes 786440 | tf_op jit(solution)/shard_map/ppermute | solution.py:234
  63.6 3.8 %collective-permute-start.13 = (bf16[256,512]{1,0:T(8,128)(2,1)}, bf16[256,512]{1,0:T(8,128)(2,1)S(1)}, u32[]{:S(2)}, u32[]{:S(2)}) collective-permute-start(bf16[256,512]{1,0:T(8,128)(2,1)} %get-tuple-element.33), channel_id=1, source_target_pairs={{1,0},{3,2},{5,4},{7,6},{9,8},{11,10},{13,12},{15,14},{17,16},{19,... | collective-permute-start | bytes 786440 | tf_op jit(solution)/shard_map/ppermute | solution.py:21
  66.1 12.3 %collective-permute-start.16 = (bf16[256,512]{1,0:T(8,128)(2,1)S(1)}, bf16[256,512]{1,0:T(8,128)(2,1)S(1)}, u32[]{:S(2)}, u32[]{:S(2)}) collective-permute-start(bf16[256,512]{1,0:T(8,128)(2,1)S(1)} %add_convert_fusion.1), channel_id=1, source_target_pairs={{4,0},{8,4},{12,8},{5,1},{9,5},{13,9},{6,2},{10,6},{14,10},{7,3},{... | collective-permute-start | bytes 786440 | tf_op jit(solution)/shard_map/ppermute | solution.py:21
  78.4 9.3 %copy-start.12 = (bf16[256,1152]{1,0:T(8,128)(2,1)S(1)}, bf16[256,1152]{1,0:T(8,128)(2,1)}, u32[]{:S(2)}) copy-start(bf16[256,1152]{1,0:T(8,128)(2,1)} %copy-done.11) | copy-start | bytes 1769476
  79.3 8.4 %collective-permute-start.17 = (bf16[256,512]{1,0:T(8,128)(2,1)S(1)}, bf16[256,512]{1,0:T(8,128)(2,1)S(1)}, u32[]{:S(2)}, u32[]{:S(2)}) collective-permute-start(bf16[256,512]{1,0:T(8,128)(2,1)S(1)} %get-tuple-element.49), channel_id=1, source_target_pairs={{0,2},{2,0},{1,3},{3,1},{4,6},{6,4},{5,7},{7,5},{8,10},{10,8},{9,1... | collective-permute-start | bytes 786440 | tf_op jit(solution)/shard_map/ppermute | solution.py:26
  88.6 1.4 %copy-start = (f32[1152,512]{1,0:T(8,128)}, f32[1152,512]{1,0:T(8,128)S(1)}, u32[]{:S(2)}) copy-start(f32[1152,512]{1,0:T(8,128)S(1)} %convolution_multiply_fusion) | copy-start | bytes 7077892
  90.0 2.1 %collective-permute-start.18 = (bf16[576,512]{1,0:T(8,128)(2,1)S(1)}, bf16[576,512]{1,0:T(8,128)(2,1)S(1)}, u32[]{:S(2)}, u32[]{:S(2)}) collective-permute-start(bf16[576,512]{1,0:T(8,128)(2,1)S(1)} %dynamic-slice_convert_fusion), channel_id=1, source_target_pairs={{0,1},{1,0},{2,3},{3,2},{4,5},{5,4},{6,7},{7,6},{8,9},{9,8},{10,11... | collective-permute-start | bytes 1769480 | tf_op jit(solution)/shard_map/ppermute | solution.py:26
  93.6 7.2 %collective-permute-start.21 = (bf16[144,512]{1,0:T(8,128)(2,1)S(1)}, bf16[144,512]{1,0:T(8,128)(2,1)S(1)}, u32[]{:S(2)}, u32[]{:S(2)}) collective-permute-start(bf16[144,512]{1,0:T(8,128)(2,1)S(1)} %get-tuple-element.41), channel_id=1, source_target_pairs={{0,12},{4,0},{8,4},{12,8},{1,13},{5,1},{9,5},{13,9},{2,14},{6,2},{... | collective-permute-start | bytes 442376 | tf_op jit(solution)/shard_map/ppermute | solution.py:26
  96.4 15.1 %collective-permute-start.20 = (bf16[144,512]{1,0:T(8,128)(2,1)S(1)}, bf16[144,512]{1,0:T(8,128)(2,1)S(1)}, u32[]{:S(2)}, u32[]{:S(2)}) collective-permute-start(bf16[144,512]{1,0:T(8,128)(2,1)S(1)} %get-tuple-element.42), channel_id=1, source_target_pairs={{0,8},{4,12},{8,0},{12,4},{1,9},{5,13},{9,1},{13,5},{2,10},{6,14},... | collective-permute-start | bytes 442376 | tf_op jit(solution)/shard_map/ppermute | solution.py:26
  98.1 13.3 %collective-permute-start.19 = (bf16[144,512]{1,0:T(8,128)(2,1)S(1)}, bf16[144,512]{1,0:T(8,128)(2,1)S(1)}, u32[]{:S(2)}, u32[]{:S(2)}) collective-permute-start(bf16[144,512]{1,0:T(8,128)(2,1)S(1)} %get-tuple-element.40), channel_id=1, source_target_pairs={{0,4},{4,8},{8,12},{12,0},{1,5},{5,9},{9,13},{13,1},{2,6},{6,10},{... | collective-permute-start | bytes 442376 | tf_op jit(solution)/shard_map/ppermute | solution.py:26
  111.7 8.6 %collective-permute-start.22 = (bf16[144,512]{1,0:T(8,128)(2,1)S(1)}, bf16[144,512]{1,0:T(8,128)(2,1)S(1)}, u32[]{:S(2)}, u32[]{:S(2)}) collective-permute-start(bf16[144,512]{1,0:T(8,128)(2,1)S(1)} %get-tuple-element.38), channel_id=1, source_target_pairs={{0,4},{4,8},{8,12},{12,0},{1,5},{5,9},{9,13},{13,1},{2,6},{6,10},{... | collective-permute-start | bytes 442376 | tf_op jit(solution)/shard_map/ppermute | solution.py:26
  111.8 13.3 %collective-permute-start.23 = (bf16[144,512]{1,0:T(8,128)(2,1)S(1)}, bf16[144,512]{1,0:T(8,128)(2,1)S(1)}, u32[]{:S(2)}, u32[]{:S(2)}) collective-permute-start(bf16[144,512]{1,0:T(8,128)(2,1)S(1)} %get-tuple-element.38), channel_id=1, source_target_pairs={{0,8},{4,12},{8,0},{12,4},{1,9},{5,13},{9,1},{13,5},{2,10},{6,14},... | collective-permute-start | bytes 442376 | tf_op jit(solution)/shard_map/ppermute | solution.py:26
  113.1 12.0 %collective-permute-start.24 = (bf16[144,512]{1,0:T(8,128)(2,1)S(1)}, bf16[144,512]{1,0:T(8,128)(2,1)S(1)}, u32[]{:S(2)}, u32[]{:S(2)}) collective-permute-start(bf16[144,512]{1,0:T(8,128)(2,1)S(1)} %get-tuple-element.38), channel_id=1, source_target_pairs={{0,12},{4,0},{8,4},{12,8},{1,13},{5,1},{9,5},{13,9},{2,14},{6,2},{... | collective-permute-start | bytes 442376 | tf_op jit(solution)/shard_map/ppermute | solution.py:26
  125.1 1.0 copy-start.8
  125.1 1.0 copy-start.9
  125.3 2.5 %collective-permute-start.25 = (bf16[576,512]{1,0:T(8,128)(2,1)S(1)}, bf16[576,512]{1,0:T(8,128)(2,1)S(1)}, u32[]{:S(2)}, u32[]{:S(2)}) collective-permute-start(bf16[576,512]{1,0:T(8,128)(2,1)S(1)} %convert_element_type.102), channel_id=1, source_target_pairs={{0,1},{1,0},{2,3},{3,2},{4,5},{5,4},{6,7},{7,6},{8,9},{9,8},{10,11... | collective-permute-start | bytes 1769480 | tf_op jit(solution)/shard_map/ppermute | solution.py:26

commit v10 on v7

--- a/solution.py
+++ b/solution.py
@@ -11,6 +11,7 @@
 HEAD_DIM = 256
 SPAN = 768
 RING = ("ctx", "sub")
+TRADE = ("fsdp", "sub")
 NT = (((1,), (1,)), ((), ()))
 TN = (((0,), (0,)), ((), ()))
 
@@ -184,15 +185,17 @@
     first_row = lax.axis_index(RING) * block_rows
 
     fsdp_count = lax.axis_size("fsdp")
-    fsdp_at = lax.axis_index("fsdp")
     model_width = layer_input.shape[2]
     shard_rows = model_width // fsdp_count
+    trade_count = lax.axis_size(TRADE)
+    trade_at = lax.axis_index(TRADE)
+    piece_rows = model_width // trade_count
     own_input = layer_input[0]
-    inputs = [lax.dynamic_slice_in_dim(own_input, fsdp_at * shard_rows, shard_rows, axis=1)]
-    for steps in range(1, fsdp_count):
-        target = (fsdp_at + steps) % fsdp_count
-        outgoing = lax.dynamic_slice_in_dim(own_input, target * shard_rows, shard_rows, axis=1)
-        inputs.append(rotated(outgoing, "fsdp", steps))
+    inputs = [lax.dynamic_slice_in_dim(own_input, trade_at * piece_rows, piece_rows, axis=1)]
+    for steps in range(1, trade_count):
+        target = (trade_at + steps) % trade_count
+        outgoing = lax.dynamic_slice_in_dim(own_input, target * piece_rows, piece_rows, axis=1)
+        inputs.append(rotated(outgoing, TRADE, steps))
 
     own_kv = jnp.concatenate([key_heads[0], value_heads[0]], axis=1)
     query_pos = first_row + jnp.arange(block_rows, dtype=jnp.int32)
@@ -251,24 +254,16 @@
     grad_value = grad_kv[:, kv_width:]
 
     values = [grad_value]
-    for steps in range(1, fsdp_count):
-        values.append(rotated(grad_value, "fsdp", steps))
+    for steps in range(1, trade_count):
+        values.append(rotated(grad_value, TRADE, steps))
     stacked_inputs = jnp.concatenate(inputs, axis=0)
     stacked_values = jnp.concatenate(values, axis=0)
-    shard = lax.dot_general(stacked_inputs, stacked_values, TN, preferred_element_type=jnp.float32)
+    mine = lax.dot_general(stacked_inputs, stacked_values, TN, preferred_element_type=jnp.float32)
     token_scale = float(fsdp_count * lax.axis_size(RING) * block_rows) ** (-0.5)
     scale_early = token_scale == 2.0 ** round(math.log2(token_scale))
     if scale_early:
-        shard = shard * token_scale
-
-    sub_count = lax.axis_size("sub")
-    sub_at = lax.axis_index("sub")
-    piece_rows = shard_rows // sub_count
-    mine = lax.dynamic_slice_in_dim(shard, sub_at * piece_rows, piece_rows, axis=0)
-    for steps in range(1, sub_count):
-        target = (sub_at + steps) % sub_count
-        outgoing = lax.dynamic_slice_in_dim(shard, target * piece_rows, piece_rows, axis=0)
-        mine = mine + rotated(outgoing.astype(jnp.bfloat16), "sub", steps).astype(jnp.float32)
+        mine = mine * token_scale
+
     reduced = ring_sum(mine, "ctx")
     if sub_count == 2:
         other = rotated(reduced.astype(jnp.bfloat16), "sub", 1).astype(jnp.float32)

time: 113 us -> 128 us (1.13)
  waiting for transfers between devices: 59.6 us -> 71.3 us
  starting transfers between devices: 29.8 us -> 33.9 us
  other arithmetic: 7.16 us -> 5.71 us
    ppermute x12 -> x15, waiting for transfers between devices: 30.5 us -> 40.3 us  [rotated(): lax.ppermute(value, axis, [(source, (source + steps) % count) for source...]
    ppermute x12 -> x15, starting transfers between devices: 18.8 us -> 21.5 us  [rotated(): lax.ppermute(value, axis, [(source, (source + steps) % count) for source...]
    ppermute x4, starting transfers between devices: 8.84 us -> 11.1 us  [passed_along(): lax.ppermute(value, axis, [(source, source + steps) for source in range(f...]
    ppermute x4, waiting for transfers between devices: 29 us -> 31 us  [passed_along(): lax.ppermute(value, axis, [(source, source + steps) for source in range(f...]
    add x1 -> x0, other arithmetic: 1.45 us -> none  [body(): mine + rotated(outgoing.astype(jnp.bfloat16), 'sub', steps).astype(jnp.fl...]
  transfers between devices with their start and end apart: 18 -> 21, of which waited for: 11 -> 13; matrix products, arithmetic and copies ran while one was open for 3% -> 3% of each run, Pallas kernels for 0% -> 0%
where the time goes in v10:
time: 128 us; the launch traced here: 127 us
  waiting for transfers between devices  71.3 us (56%)
  starting transfers between devices  33.9 us (26%)
  Pallas kernels  8.83 us (7%)
  other arithmetic  5.71 us (4%)
  local copies, waits for them, and re-layouts  4.09 us (3%)
  matrix products  1.97 us (2%)
    ppermute x15, waiting for transfers between devices, rotated(): lax.ppermute(value, axis, [(source, (source + steps) % count) for source...  40.3 us
    ppermute x4, waiting for transfers between devices, passed_along(): lax.ppermute(value, axis, [(source, source + steps) for source in range(f...  31 us
    ppermute x15, starting transfers between devices, rotated(): lax.ppermute(value, axis, [(source, (source + steps) % count) for source...  21.5 us
    ppermute x4, starting transfers between devices, passed_along(): lax.ppermute(value, axis, [(source, source + steps) for source in range(f...  11.1 us
    pallas_call x1, Pallas kernels, attention(): pl.pallas_call(kernel, out_shape=(jax.ShapeDtypeStruct((rows, width), jnp...  8.83 us
  transfers between devices with their start and end apart: 21, of which 13 were waited for; matrix products, arithmetic and copies ran while one was open for 3% of the time, Pallas kernels for 0%

profile of v10, /device:TPU:0, one launch (start us, length us, event | category | flops | bytes accessed | tf_op | source)
XLA Modules:
  0.0 126.8 jit_solution(11997627626477687842)
XLA Ops:
  0.6 1.1 pad_maximum_fusion.1.refs_8_
  1.7 0.0 copy-start.1
  1.7 5.0 %collective-permute-start = (bf16[256,1024]{1,0:T(8,128)(2,1)S(1)}, bf16[256,1024]{1,0:T(8,128)(2,1)S(1)}, u32[]{:S(2)}, u32[]{:S(2)}) collective-permute-start(bf16[256,1024]{1,0:T(8,128)(2,1)S(1)} %pad_maximum_fusion.1.refs_8_), channel_id=1, source_target_pairs={{0,4},{4,8},{8,12},{1,5},{5,9},{9,13},{2,6},{6,10},{10,14},{3,7},{... | collective-permute-start | bytes 1572872 | tf_op jit(solution)/shard_map/ppermute | solution.py:22
  6.7 0.0 copy-start.2
  6.8 1.9 %dynamic-slice_bitcast_fusion = (bf16[256,576]{1,0:T(8,128)(2,1)S(1)}, bf16[256,576]{1,0:T(8,128)(2,1)S(1)}, bf16[256,576]{1,0:T(8,128)(2,1)S(1)}, bf16[256,576]{1,0:T(8,128)(2,1)S(1)}) fusion(bf16[1,256,2304]{2,1,0:T(8,128)(2,1)} %param.6, s32[]{:T(128)S(6)} %select_n.97, s32[]{:T(128)S(6)} %select_n.93, s32[]{:T(128)S(6)} %select_n.91, s32[]{:T(128)S(6)} %select_n.95), kind=kLoop, calls=%fused_computation.21 | loop fusion | bytes 2359312 | tf_op jit(solution)/shard_map/dynamic_slice | solution.py:194
  8.7 0.1 collective-permute-start.4
  8.8 3.5 %collective-permute-start.1 = (bf16[256,1024]{1,0:T(8,128)(2,1)S(1)}, bf16[256,1024]{1,0:T(8,128)(2,1)S(1)}, u32[]{:S(2)}, u32[]{:S(2)}) collective-permute-start(bf16[256,1024]{1,0:T(8,128)(2,1)S(1)} %pad_maximum_fusion.1.refs_8_), channel_id=1, source_target_pairs={{0,1},{2,3},{4,5},{6,7},{8,9},{10,11},{12,13},{14,15},{16,17},{18,... | collective-permute-start | bytes 1572872 | tf_op jit(solution)/shard_map/ppermute | solution.py:22
  12.3 0.0 copy-done.1
  12.3 0.7 collective-permute-start.2
  13.0 5.3 %collective-permute-done.refs_4_ = bf16[256,1024]{1,0:T(8,128)(2,1)S(1)} collective-permute-done((bf16[256,1024]{1,0:T(8,128)(2,1)S(1)}, bf16[256,1024]{1,0:T(8,128)(2,1)S(1)}, u32[]{:S(2)}, u32[]{:S(2)}) %collective-permute-start) | collective-permute-done | bytes 524320 | tf_op jit(solution)/shard_map/ppermute | solution.py:22
  18.3 0.0 collective-permute-start.3
  18.3 2.1 %collective-permute-start.5 = (bf16[256,576]{1,0:T(8,128)(2,1)S(1)}, bf16[256,576]{1,0:T(8,128)(2,1)}, u32[]{:S(2)}, u32[]{:S(2)}) collective-permute-start(bf16[256,576]{1,0:T(8,128)(2,1)S(1)} %get-tuple-element.22), channel_id=1, source_target_pairs={{0,2},{1,3},{2,0},{3,1},{4,6},{5,7},{6,4},{7,5},{8,10},{9,11},{10,... | collective-permute-start | bytes 884744 | tf_op jit(solution)/shard_map/ppermute | solution.py:27
  20.5 0.0 collective-permute-done.4.refs_9_
  20.5 0.2 collective-permute-start.6
  20.6 0.1 select_reduce_fusion
  20.7 0.1 copy.13
  20.9 0.7 subtract_add_fusion.refs_1_
  21.6 7.4 %collective-permute-done.5.refs_10_ = bf16[256,576]{1,0:T(8,128)(2,1)} collective-permute-done((bf16[256,576]{1,0:T(8,128)(2,1)S(1)}, bf16[256,576]{1,0:T(8,128)(2,1)}, u32[]{:S(2)}, u32[]{:S(2)}) %collective-permute-start.5) | collective-permute-done | bytes 294944 | tf_op jit(solution)/shard_map/ppermute | solution.py:27
  29.0 2.7 %collective-permute-done.6.refs_11_ = bf16[256,576]{1,0:T(8,128)(2,1)} collective-permute-done((bf16[256,576]{1,0:T(8,128)(2,1)S(1)}, bf16[256,576]{1,0:T(8,128)(2,1)}, u32[]{:S(2)}, u32[]{:S(2)}) %collective-permute-start.6) | collective-permute-done | bytes 294944 | tf_op jit(solution)/shard_map/ppermute | solution.py:27
  31.6 0.0 collective-permute-done.1.refs_5_
  31.6 0.0 collective-permute-done.2.refs_6_
  31.6 0.0 collective-permute-done.3.refs_7_
  31.6 0.0 copy-done.3
  31.7 0.8 copy-done.4
  32.4 0.2 copy-done.5
  32.6 8.8 %shard_map.93 = (bf16[256,1024]{1,0:T(8,128)(2,1)}, bf16[256,1024]{1,0:T(8,128)(2,1)}, bf16[256,1024]{1,0:T(8,128)(2,1)}, f32[256,1024]{1,0:T(8,128)}, f32[256,1024]{1,0:T(8,128)}) custom-call(s32[1]{0:T(128)} %bitcast.refs_0_, s32[256,1]{1,0:T(8,128)} %subtract_add_fusion.refs_1_, bf16[256,1024]{1,0:T(8,128)(2,1)} %bitcast.24, bf16[256,1024]{1,0:T(8,128)(2,1)} %bitcast.25, ...), custom_call_target="tpu_custom_call" | custom-call | flops 2684354560 | bytes 7864320 | tf_op jit(solution)/shard_map/pallas_call | solution.py:161
  41.4 0.7 collective-permute-start.9
  42.1 1.3 %collective-permute-start.7 = (bf16[256,1024]{1,0:T(8,128)(2,1)}, bf16[256,1024]{1,0:T(8,128)(2,1)S(1)}, u32[]{:S(2)}, u32[]{:S(2)}) collective-permute-start(bf16[256,1024]{1,0:T(8,128)(2,1)} %get-tuple-element.11), channel_id=1, source_target_pairs={{1,0},{3,2},{5,4},{7,6},{9,8},{11,10},{13,12},{15,14},{17,16},{19,... | collective-permute-start | bytes 1572872 | tf_op jit(solution)/shard_map/ppermute | solution.py:22
  43.4 0.7 collective-permute-start.8
  44.1 0.0 collective-permute-done.9
  44.1 1.4 %add_convert_fusion.1 = bf16[256,1024]{1,0:T(8,128)(2,1)S(1)} fusion(f32[256,1024]{1,0:T(8,128)} %get-tuple-element.12, bf16[256,1024]{1,0:T(8,128)(2,1)S(1)} %collective-permute-done.9), kind=kLoop, calls=%fused_computation.19 | loop fusion | flops 786432 | bytes 2097152 | tf_op jit(solution)/shard_map/convert_element_type | solution.py:232
  45.5 1.3 %collective-permute-start.10 = (bf16[256,1024]{1,0:T(8,128)(2,1)S(1)}, bf16[256,1024]{1,0:T(8,128)(2,1)S(1)}, u32[]{:S(2)}, u32[]{:S(2)}) collective-permute-start(bf16[256,1024]{1,0:T(8,128)(2,1)S(1)} %add_convert_fusion.1), channel_id=1, source_target_pairs={{4,0},{8,4},{12,8},{5,1},{9,5},{13,9},{6,2},{10,6},{14,10},{7,3},{... | collective-permute-start | bytes 1572872 | tf_op jit(solution)/shard_map/ppermute | solution.py:22
  46.8 0.0 collective-permute-done.7
  46.8 0.0 collective-permute-done.8
  46.8 25.7 %collective-permute-done.10 = bf16[256,1024]{1,0:T(8,128)(2,1)S(1)} collective-permute-done((bf16[256,1024]{1,0:T(8,128)(2,1)S(1)}, bf16[256,1024]{1,0:T(8,128)(2,1)S(1)}, u32[]{:S(2)}, u32[]{:S(2)}) %collective-permute-start.10) | collective-permute-done | bytes 524320 | tf_op jit(solution)/shard_map/ppermute | solution.py:22
  72.6 0.3 add_convert_fusion
  72.9 0.9 fusion.17
  73.8 0.1 collective-permute-start.11
  73.9 1.5 %collective-permute-start.12 = (bf16[256,512]{1,0:T(8,128)(2,1)S(1)}, bf16[256,512]{1,0:T(8,128)(2,1)S(1)}, u32[]{:S(2)}, u32[]{:S(2)}) collective-permute-start(bf16[256,512]{1,0:T(8,128)(2,1)S(1)} %get-tuple-element.25), channel_id=1, source_target_pairs={{0,2},{1,3},{2,0},{3,1},{4,6},{5,7},{6,4},{7,5},{8,10},{9,11},{10,... | collective-permute-start | bytes 786440 | tf_op jit(solution)/shard_map/ppermute | solution.py:27
  75.4 1.4 %collective-permute-start.13 = (bf16[256,512]{1,0:T(8,128)(2,1)S(1)}, bf16[256,512]{1,0:T(8,128)(2,1)S(1)}, u32[]{:S(2)}, u32[]{:S(2)}) collective-permute-start(bf16[256,512]{1,0:T(8,128)(2,1)S(1)} %get-tuple-element.25), channel_id=1, source_target_pairs={{0,3},{1,0},{2,1},{3,2},{4,7},{5,4},{6,5},{7,6},{8,11},{9,8},{10,9... | collective-permute-start | bytes 786440 | tf_op jit(solution)/shard_map/ppermute | solution.py:27
  76.7 5.0 %collective-permute-done.11 = bf16[256,512]{1,0:T(8,128)(2,1)S(1)} collective-permute-done((bf16[256,512]{1,0:T(8,128)(2,1)S(1)}, bf16[256,512]{1,0:T(8,128)(2,1)S(1)}, u32[]{:S(2)}, u32[]{:S(2)}) %collective-permute-start.11) | collective-permute-done | bytes 262176 | tf_op jit(solution)/shard_map/ppermute | solution.py:27
  81.7 1.3 %collective-permute-done.12 = bf16[256,512]{1,0:T(8,128)(2,1)S(1)} collective-permute-done((bf16[256,512]{1,0:T(8,128)(2,1)S(1)}, bf16[256,512]{1,0:T(8,128)(2,1)S(1)}, u32[]{:S(2)}, u32[]{:S(2)}) %collective-permute-start.12) | collective-permute-done | bytes 262176 | tf_op jit(solution)/shard_map/ppermute | solution.py:27
  83.0 4.0 %collective-permute-done.13 = bf16[256,512]{1,0:T(8,128)(2,1)S(1)} collective-permute-done((bf16[256,512]{1,0:T(8,128)(2,1)S(1)}, bf16[256,512]{1,0:T(8,128)(2,1)S(1)}, u32[]{:S(2)}, u32[]{:S(2)}) %collective-permute-start.13) | collective-permute-done | bytes 262176 | tf_op jit(solution)/shard_map/ppermute | solution.py:27
  87.0 2.0 %convolution_multiply_fusion = f32[576,512]{1,0:T(8,128)S(1)} fusion(bf16[256,576]{1,0:T(8,128)(2,1)} %collective-permute-done.6.refs_11_, bf16[256,576]{1,0:T(8,128)(2,1)} %collective-permute-done.5.refs_10_, bf16[256,576]{1,0:T(8,128)(2,1)} %collective-permute-done.4.refs_9_, bf16[256,576]{1,0:T(8,128)(2,1)S(1)} %get-tuple-element.21, ...), kind=kOutput, calls=%fused_computation.3 | convolution fusion | flops 613187584 | bytes 3407872 | tf_op jit(solution)/shard_map/dot_general | solution.py:261
  89.0 0.1 dynamic-slice_convert_fusion.2
  89.0 6.3 %collective-permute-start.14 = (bf16[144,512]{1,0:T(8,128)(2,1)S(1)}, bf16[144,512]{1,0:T(8,128)(2,1)S(1)}, u32[]{:S(2)}, u32[]{:S(2)}) collective-permute-start(bf16[144,512]{1,0:T(8,128)(2,1)S(1)} %get-tuple-element.18), channel_id=1, source_target_pairs={{0,4},{4,8},{8,12},{12,0},{1,5},{5,9},{9,13},{13,1},{2,6},{6,10},{... | collective-permute-start | bytes 442376 | tf_op jit(solution)/shard_map/ppermute | solution.py:27
  95.4 0.0 collective-permute-start.15
  95.4 2.4 %collective-permute-start.16 = (bf16[144,512]{1,0:T(8,128)(2,1)S(1)}, bf16[144,512]{1,0:T(8,128)(2,1)S(1)}, u32[]{:S(2)}, u32[]{:S(2)}) collective-permute-start(bf16[144,512]{1,0:T(8,128)(2,1)S(1)} %get-tuple-element.19), channel_id=1, source_target_pairs={{0,12},{4,0},{8,4},{12,8},{1,13},{5,1},{9,5},{13,9},{2,14},{6,2},{... | collective-permute-start | bytes 442376 | tf_op jit(solution)/shard_map/ppermute | solution.py:27
  97.8 1.8 %collective-permute-done.14 = bf16[144,512]{1,0:T(8,128)(2,1)S(1)} collective-permute-done((bf16[144,512]{1,0:T(8,128)(2,1)S(1)}, bf16[144,512]{1,0:T(8,128)(2,1)S(1)}, u32[]{:S(2)}, u32[]{:S(2)}) %collective-permute-start.14) | collective-permute-done | bytes 147488 | tf_op jit(solution)/shard_map/ppermute | solution.py:27
  99.6 5.9 %collective-permute-done.15 = bf16[144,512]{1,0:T(8,128)(2,1)S(1)} collective-permute-done((bf16[144,512]{1,0:T(8,128)(2,1)S(1)}, bf16[144,512]{1,0:T(8,128)(2,1)S(1)}, u32[]{:S(2)}, u32[]{:S(2)}) %collective-permute-start.15) | collective-permute-done | bytes 147488 | tf_op jit(solution)/shard_map/ppermute | solution.py:27
  105.6 0.3 collective-permute-done.16
  105.8 0.1 broadcast_in_dim.28
  106.0 0.1 fusion.14
  106.1 3.5 %collective-permute-start.17 = (bf16[144,512]{1,0:T(8,128)(2,1)S(1)}, bf16[144,512]{1,0:T(8,128)(2,1)S(1)}, u32[]{:S(2)}, u32[]{:S(2)}) collective-permute-start(bf16[144,512]{1,0:T(8,128)(2,1)S(1)} %get-tuple-element.16), channel_id=1, source_target_pairs={{0,4},{4,8},{8,12},{12,0},{1,5},{5,9},{9,13},{13,1},{2,6},{6,10},{... | collective-permute-start | bytes 442376 | tf_op jit(solution)/shard_map/ppermute | solution.py:27
  109.5 3.1 %collective-permute-start.18 = (bf16[144,512]{1,0:T(8,128)(2,1)S(1)}, bf16[144,512]{1,0:T(8,128)(2,1)S(1)}, u32[]{:S(2)}, u32[]{:S(2)}) collective-permute-start(bf16[144,512]{1,0:T(8,128)(2,1)S(1)} %get-tuple-element.16), channel_id=1, source_target_pairs={{0,8},{4,12},{8,0},{12,4},{1,9},{5,13},{9,1},{13,5},{2,10},{6,14},... | collective-permute-start | bytes 442376 | tf_op jit(solution)/shard_map/ppermute | solution.py:27
  112.6 0.0 collective-permute-start.19
  112.6 4.2 %collective-permute-done.17 = bf16[144,512]{1,0:T(8,128)(2,1)S(1)} collective-permute-done((bf16[144,512]{1,0:T(8,128)(2,1)S(1)}, bf16[144,512]{1,0:T(8,128)(2,1)S(1)}, u32[]{:S(2)}, u32[]{:S(2)}) %collective-permute-start.17) | collective-permute-done | bytes 147488 | tf_op jit(solution)/shard_map/ppermute | solution.py:27
  116.8 5.8 %collective-permute-done.18 = bf16[144,512]{1,0:T(8,128)(2,1)S(1)} collective-permute-done((bf16[144,512]{1,0:T(8,128)(2,1)S(1)}, bf16[144,512]{1,0:T(8,128)(2,1)S(1)}, u32[]{:S(2)}, u32[]{:S(2)}) %collective-permute-start.18) | collective-permute-done | bytes 147488 | tf_op jit(solution)/shard_map/ppermute | solution.py:27
  122.6 0.0 collective-permute-done.19
  122.7 0.1 convert_element_type.70
  122.8 0.1 collective-permute-start.20
  122.8 2.0 %collective-permute-done.20 = bf16[576,512]{1,0:T(8,128)(2,1)S(1)} collective-permute-done((bf16[576,512]{1,0:T(8,128)(2,1)S(1)}, bf16[576,512]{1,0:T(8,128)(2,1)S(1)}, u32[]{:S(2)}, u32[]{:S(2)}) %collective-permute-start.20) | collective-permute-done | bytes 589856 | tf_op jit(solution)/shard_map/ppermute | solution.py:27
  124.8 0.3 convert_select_fusion.1
  125.1 1.6 %pad_maximum_fusion = f32[1152,512]{1,0:T(8,128)} fusion(f32[576,512]{1,0:T(8,128)S(1)} %get-tuple-element.15, f32[576,512]{1,0:T(8,128)S(1)} %get-tuple-element.14), kind=kLoop, calls=%fused_computation | loop fusion | flops 589824 | bytes 4718592 | tf_op jit(solution)/shard_map/concatenate | solution.py:272
  (10 shorter events, 0.1 us)
Async XLA Ops:
  1.7 10.6 %copy-start.1 = (bf16[256,1024]{1,0:T(8,128)(2,1)}, bf16[256,1024]{1,0:T(8,128)(2,1)S(1)}, u32[]{:S(2)}) copy-start(bf16[256,1024]{1,0:T(8,128)(2,1)S(1)} %pad_maximum_fusion.1.refs_8_) | copy-start | bytes 1572868
  1.7 16.6 %collective-permute-start = (bf16[256,1024]{1,0:T(8,128)(2,1)S(1)}, bf16[256,1024]{1,0:T(8,128)(2,1)S(1)}, u32[]{:S(2)}, u32[]{:S(2)}) collective-permute-start(bf16[256,1024]{1,0:T(8,128)(2,1)S(1)} %pad_maximum_fusion.1.refs_8_), channel_id=1, source_target_pairs={{0,4},{4,8},{8,12},{1,5},{5,9},{9,13},{2,6},{6,10},{10,14},{3,7},{... | collective-permute-start | bytes 1572872 | tf_op jit(solution)/shard_map/ppermute | solution.py:22
  6.7 13.9 %copy-start.2 = (s32[1,12]{1,0:T(1,128)S(1)}, s32[1,12]{1,0:T(1,128)}, u32[]{:S(2)}) copy-start(s32[1,12]{1,0:T(1,128)} %param.11) | copy-start | bytes 148
  8.7 11.8 %collective-permute-start.4 = (bf16[256,576]{1,0:T(8,128)(2,1)S(1)}, bf16[256,576]{1,0:T(8,128)(2,1)}, u32[]{:S(2)}, u32[]{:S(2)}) collective-permute-start(bf16[256,576]{1,0:T(8,128)(2,1)S(1)} %get-tuple-element.23), channel_id=1, source_target_pairs={{0,1},{1,2},{2,3},{3,0},{4,5},{5,6},{6,7},{7,4},{8,9},{9,10},{10,1... | collective-permute-start | bytes 884744 | tf_op jit(solution)/shard_map/ppermute | solution.py:27
  8.8 22.9 %collective-permute-start.1 = (bf16[256,1024]{1,0:T(8,128)(2,1)S(1)}, bf16[256,1024]{1,0:T(8,128)(2,1)S(1)}, u32[]{:S(2)}, u32[]{:S(2)}) collective-permute-start(bf16[256,1024]{1,0:T(8,128)(2,1)S(1)} %pad_maximum_fusion.1.refs_8_), channel_id=1, source_target_pairs={{0,1},{2,3},{4,5},{6,7},{8,9},{10,11},{12,13},{14,15},{16,17},{18,... | collective-permute-start | bytes 1572872 | tf_op jit(solution)/shard_map/ppermute | solution.py:22
  12.3 19.3 %collective-permute-start.2 = (bf16[256,1024]{1,0:T(8,128)(2,1)S(1)}, bf16[256,1024]{1,0:T(8,128)(2,1)S(1)}, u32[]{:S(2)}, u32[]{:S(2)}) collective-permute-start(bf16[256,1024]{1,0:T(8,128)(2,1)S(1)} %pad_maximum_fusion.1.refs_8_), channel_id=1, source_target_pairs={{1,8},{5,12},{3,10},{7,14},{17,24},{21,28},{19,26},{23,30}} | collective-permute-start | bytes 1572872 | tf_op jit(solution)/shard_map/ppermute | solution.py:213
  18.3 13.3 %copy-start.3 = (bf16[256,1024]{1,0:T(8,128)(2,1)}, bf16[256,1024]{1,0:T(8,128)(2,1)S(1)}, u32[]{:S(2)}) copy-start(bf16[256,1024]{1,0:T(8,128)(2,1)S(1)} %collective-permute-done.refs_4_) | copy-start | bytes 1572868
  18.3 13.3 %collective-permute-start.3 = (bf16[256,1024]{1,0:T(8,128)(2,1)S(1)}, bf16[256,1024]{1,0:T(8,128)(2,1)}, u32[]{:S(2)}, u32[]{:S(2)}) collective-permute-start(bf16[256,1024]{1,0:T(8,128)(2,1)S(1)} %collective-permute-done.refs_4_), channel_id=1, source_target_pairs={{0,1},{1,0},{2,3},{3,2},{4,5},{5,4},{6,7},{7,6},{8,9},{9,8},{10,11... | collective-permute-start | bytes 1572872 | tf_op jit(solution)/shard_map/ppermute | solution.py:27
  18.3 10.6 %collective-permute-start.5 = (bf16[256,576]{1,0:T(8,128)(2,1)S(1)}, bf16[256,576]{1,0:T(8,128)(2,1)}, u32[]{:S(2)}, u32[]{:S(2)}) collective-permute-start(bf16[256,576]{1,0:T(8,128)(2,1)S(1)} %get-tuple-element.22), channel_id=1, source_target_pairs={{0,2},{1,3},{2,0},{3,1},{4,6},{5,7},{6,4},{7,5},{8,10},{9,11},{10,... | collective-permute-start | bytes 884744 | tf_op jit(solution)/shard_map/ppermute | solution.py:27
  20.5 11.1 %collective-permute-start.6 = (bf16[256,576]{1,0:T(8,128)(2,1)S(1)}, bf16[256,576]{1,0:T(8,128)(2,1)}, u32[]{:S(2)}, u32[]{:S(2)}) collective-permute-start(bf16[256,576]{1,0:T(8,128)(2,1)S(1)} %get-tuple-element.24), channel_id=1, source_target_pairs={{0,3},{1,0},{2,1},{3,2},{4,7},{5,4},{6,5},{7,6},{8,11},{9,8},{10,9... | collective-permute-start | bytes 884744 | tf_op jit(solution)/shard_map/ppermute | solution.py:27
  31.6 0.8 copy-start.4
  31.6 1.0 copy-start.5
  41.4 31.1 %copy-start = (f32[256,1024]{1,0:T(8,128)S(1)}, f32[256,1024]{1,0:T(8,128)}, u32[]{:S(2)}) copy-start(f32[256,1024]{1,0:T(8,128)} %get-tuple-element.10) | copy-start | bytes 3145732
  41.4 2.7 %collective-permute-start.9 = (bf16[256,1024]{1,0:T(8,128)(2,1)}, bf16[256,1024]{1,0:T(8,128)(2,1)S(1)}, u32[]{:S(2)}, u32[]{:S(2)}) collective-permute-start(bf16[256,1024]{1,0:T(8,128)(2,1)} %get-tuple-element.13), channel_id=1, source_target_pairs={{0,1},{1,0},{2,3},{3,2},{4,5},{5,4},{6,7},{7,6},{8,9},{9,8},{10,11... | collective-permute-start | bytes 1572872 | tf_op jit(solution)/shard_map/ppermute | solution.py:27
  42.1 4.7 %collective-permute-start.7 = (bf16[256,1024]{1,0:T(8,128)(2,1)}, bf16[256,1024]{1,0:T(8,128)(2,1)S(1)}, u32[]{:S(2)}, u32[]{:S(2)}) collective-permute-start(bf16[256,1024]{1,0:T(8,128)(2,1)} %get-tuple-element.11), channel_id=1, source_target_pairs={{1,0},{3,2},{5,4},{7,6},{9,8},{11,10},{13,12},{15,14},{17,16},{19,... | collective-permute-start | bytes 1572872 | tf_op jit(solution)/shard_map/ppermute | solution.py:22
  43.4 3.4 %collective-permute-start.8 = (bf16[256,1024]{1,0:T(8,128)(2,1)}, bf16[256,1024]{1,0:T(8,128)(2,1)S(1)}, u32[]{:S(2)}, u32[]{:S(2)}) collective-permute-start(bf16[256,1024]{1,0:T(8,128)(2,1)} %get-tuple-element.11), channel_id=1, source_target_pairs={{8,1},{12,5},{10,3},{14,7},{24,17},{28,21},{26,19},{30,23}} | collective-permute-start | bytes 1572872 | tf_op jit(solution)/shard_map/ppermute | solution.py:237
  45.5 27.1 %collective-permute-start.10 = (bf16[256,1024]{1,0:T(8,128)(2,1)S(1)}, bf16[256,1024]{1,0:T(8,128)(2,1)S(1)}, u32[]{:S(2)}, u32[]{:S(2)}) collective-permute-start(bf16[256,1024]{1,0:T(8,128)(2,1)S(1)} %add_convert_fusion.1), channel_id=1, source_target_pairs={{4,0},{8,4},{12,8},{5,1},{9,5},{13,9},{6,2},{10,6},{14,10},{7,3},{... | collective-permute-start | bytes 1572872 | tf_op jit(solution)/shard_map/ppermute | solution.py:22
  73.8 8.0 %collective-permute-start.11 = (bf16[256,512]{1,0:T(8,128)(2,1)S(1)}, bf16[256,512]{1,0:T(8,128)(2,1)S(1)}, u32[]{:S(2)}, u32[]{:S(2)}) collective-permute-start(bf16[256,512]{1,0:T(8,128)(2,1)S(1)} %get-tuple-element.25), channel_id=1, source_target_pairs={{0,1},{1,2},{2,3},{3,0},{4,5},{5,6},{6,7},{7,4},{8,9},{9,10},{10,1... | collective-permute-start | bytes 786440 | tf_op jit(solution)/shard_map/ppermute | solution.py:27
  73.9 9.1 %collective-permute-start.12 = (bf16[256,512]{1,0:T(8,128)(2,1)S(1)}, bf16[256,512]{1,0:T(8,128)(2,1)S(1)}, u32[]{:S(2)}, u32[]{:S(2)}) collective-permute-start(bf16[256,512]{1,0:T(8,128)(2,1)S(1)} %get-tuple-element.25), channel_id=1, source_target_pairs={{0,2},{1,3},{2,0},{3,1},{4,6},{5,7},{6,4},{7,5},{8,10},{9,11},{10,... | collective-permute-start | bytes 786440 | tf_op jit(solution)/shard_map/ppermute | solution.py:27
  75.4 11.6 %collective-permute-start.13 = (bf16[256,512]{1,0:T(8,128)(2,1)S(1)}, bf16[256,512]{1,0:T(8,128)(2,1)S(1)}, u32[]{:S(2)}, u32[]{:S(2)}) collective-permute-start(bf16[256,512]{1,0:T(8,128)(2,1)S(1)} %get-tuple-element.25), channel_id=1, source_target_pairs={{0,3},{1,0},{2,1},{3,2},{4,7},{5,4},{6,5},{7,6},{8,11},{9,8},{10,9... | collective-permute-start | bytes 786440 | tf_op jit(solution)/shard_map/ppermute | solution.py:27
  89.0 10.6 %collective-permute-start.14 = (bf16[144,512]{1,0:T(8,128)(2,1)S(1)}, bf16[144,512]{1,0:T(8,128)(2,1)S(1)}, u32[]{:S(2)}, u32[]{:S(2)}) collective-permute-start(bf16[144,512]{1,0:T(8,128)(2,1)S(1)} %get-tuple-element.18), channel_id=1, source_target_pairs={{0,4},{4,8},{8,12},{12,0},{1,5},{5,9},{9,13},{13,1},{2,6},{6,10},{... | collective-permute-start | bytes 442376 | tf_op jit(solution)/shard_map/ppermute | solution.py:27
  95.4 10.2 %collective-permute-start.15 = (bf16[144,512]{1,0:T(8,128)(2,1)S(1)}, bf16[144,512]{1,0:T(8,128)(2,1)S(1)}, u32[]{:S(2)}, u32[]{:S(2)}) collective-permute-start(bf16[144,512]{1,0:T(8,128)(2,1)S(1)} %get-tuple-element.20), channel_id=1, source_target_pairs={{0,8},{4,12},{8,0},{12,4},{1,9},{5,13},{9,1},{13,5},{2,10},{6,14},... | collective-permute-start | bytes 442376 | tf_op jit(solution)/shard_map/ppermute | solution.py:27
  95.4 10.5 %collective-permute-start.16 = (bf16[144,512]{1,0:T(8,128)(2,1)S(1)}, bf16[144,512]{1,0:T(8,128)(2,1)S(1)}, u32[]{:S(2)}, u32[]{:S(2)}) collective-permute-start(bf16[144,512]{1,0:T(8,128)(2,1)S(1)} %get-tuple-element.19), channel_id=1, source_target_pairs={{0,12},{4,0},{8,4},{12,8},{1,13},{5,1},{9,5},{13,9},{2,14},{6,2},{... | collective-permute-start | bytes 442376 | tf_op jit(solution)/shard_map/ppermute | solution.py:27
  106.1 10.7 %collective-permute-start.17 = (bf16[144,512]{1,0:T(8,128)(2,1)S(1)}, bf16[144,512]{1,0:T(8,128)(2,1)S(1)}, u32[]{:S(2)}, u32[]{:S(2)}) collective-permute-start(bf16[144,512]{1,0:T(8,128)(2,1)S(1)} %get-tuple-element.16), channel_id=1, source_target_pairs={{0,4},{4,8},{8,12},{12,0},{1,5},{5,9},{9,13},{13,1},{2,6},{6,10},{... | collective-permute-start | bytes 442376 | tf_op jit(solution)/shard_map/ppermute | solution.py:27
  109.5 13.1 %collective-permute-start.18 = (bf16[144,512]{1,0:T(8,128)(2,1)S(1)}, bf16[144,512]{1,0:T(8,128)(2,1)S(1)}, u32[]{:S(2)}, u32[]{:S(2)}) collective-permute-start(bf16[144,512]{1,0:T(8,128)(2,1)S(1)} %get-tuple-element.16), channel_id=1, source_target_pairs={{0,8},{4,12},{8,0},{12,4},{1,9},{5,13},{9,1},{13,5},{2,10},{6,14},... | collective-permute-start | bytes 442376 | tf_op jit(solution)/shard_map/ppermute | solution.py:27
  112.6 10.0 %collective-permute-start.19 = (bf16[144,512]{1,0:T(8,128)(2,1)S(1)}, bf16[144,512]{1,0:T(8,128)(2,1)S(1)}, u32[]{:S(2)}, u32[]{:S(2)}) collective-permute-start(bf16[144,512]{1,0:T(8,128)(2,1)S(1)} %get-tuple-element.16), channel_id=1, source_target_pairs={{0,12},{4,0},{8,4},{12,8},{1,13},{5,1},{9,5},{13,9},{2,14},{6,2},{... | collective-permute-start | bytes 442376 | tf_op jit(solution)/shard_map/ppermute | solution.py:27
  122.8 2.1 %collective-permute-start.20 = (bf16[576,512]{1,0:T(8,128)(2,1)S(1)}, bf16[576,512]{1,0:T(8,128)(2,1)S(1)}, u32[]{:S(2)}, u32[]{:S(2)}) collective-permute-start(bf16[576,512]{1,0:T(8,128)(2,1)S(1)} %convert_element_type.70), channel_id=1, source_target_pairs={{0,1},{1,0},{2,3},{3,2},{4,5},{5,4},{6,7},{7,6},{8,9},{9,8},{10,11... | collective-permute-start | bytes 1769480 | tf_op jit(solution)/shard_map/ppermute | solution.py:27

commit v11 on v7

--- a/solution.py
+++ b/solution.py
@@ -230,13 +230,21 @@
 
     if chip_route:
         back = [(target, source) for source, target in across]
-        to_mate, to_other, g2, g0 = grad_pieces
-        from_far = lax.ppermute(to_other, RING, back).astype(jnp.float32)
-        from_mate = rotated(to_mate, "sub", 1).astype(jnp.float32)
-        from_high = passed_along(to_other, "sub", -1).astype(jnp.float32)
-        two_back_sum = g2 + from_mate
-        from_next = passed_along(low(two_back_sum), "ctx", -1).astype(jnp.float32)
-        total = g0 + from_high + from_far + from_next
+
+        def returned(to_mate, to_other, g2, g0):
+            from_far = lax.ppermute(to_other, RING, back).astype(jnp.float32)
+            from_mate = rotated(to_mate, "sub", 1).astype(jnp.float32)
+            from_high = passed_along(to_other, "sub", -1).astype(jnp.float32)
+            two_back_sum = g2 + from_mate
+            from_next = passed_along(low(two_back_sum), "ctx", -1).astype(jnp.float32)
+            return g0 + from_high + from_far + from_next
+
+        total_v = returned(*[piece[:, kv_width:] for piece in grad_pieces])
+        total_v, key_pieces = lax.optimization_barrier(
+            (total_v, [piece[:, :kv_width] for piece in grad_pieces])
+        )
+        total_k = returned(*key_pieces)
+        total = jnp.concatenate([total_k, total_v], axis=1)
     else:
 
         def own_piece(distance):
@@ -269,6 +277,8 @@
         target = (sub_at + steps) % sub_count
         outgoing = lax.dynamic_slice_in_dim(shard, target * piece_rows, piece_rows, axis=0)
         mine = mine + rotated(outgoing.astype(jnp.bfloat16), "sub", steps).astype(jnp.float32)
+    if chip_route:
+        mine, _ = lax.optimization_barrier((mine, total_k))
     reduced = ring_sum(mine, "ctx")
     if sub_count == 2:
         other = rotated(reduced.astype(jnp.bfloat16), "sub", 1).astype(jnp.float32)

time: 113 us -> 114 us (level)
    ppermute x12 -> x13, waiting for transfers between devices: 30.5 us -> 25.7 us  [rotated(): lax.ppermute(value, axis, [(source, (source + steps) % count) for source...]
    ppermute x4 -> x6, waiting for transfers between devices: 29 us -> 33.1 us  [passed_along(): lax.ppermute(value, axis, [(source, source + steps) for source in range(f...]
    ppermute x12 -> x13, starting transfers between devices: 18.8 us -> 15.5 us  [rotated(): lax.ppermute(value, axis, [(source, (source + steps) % count) for source...]
    ppermute x4 -> x6, starting transfers between devices: 8.84 us -> 11.6 us  [passed_along(): lax.ppermute(value, axis, [(source, source + steps) for source in range(f...]
    slice x1 -> x3, local copies, waits for them, and re-layouts: 0.85 us -> 2.96 us  [body(): piece[:, :kv_width]]
    unnamed x16, local copies, waits for them, and re-layouts: 2.23 us -> 0.31 us
  transfers between devices with their start and end apart: 18 -> 22, of which waited for: 11 -> 10; matrix products, arithmetic and copies ran while one was open for 3% -> 7% of each run, Pallas kernels for 0% -> 0%
where the time goes in v11:
time: 114 us; the launch traced here: 113 us
  waiting for transfers between devices  58.8 us (52%)
  starting transfers between devices  29.8 us (26%)
  Pallas kernels  8.84 us (8%)
  other arithmetic  7.6 us (7%)
  local copies, waits for them, and re-layouts  5.02 us (4%)
  matrix products  1.87 us (2%)
    ppermute x6, waiting for transfers between devices, passed_along(): lax.ppermute(value, axis, [(source, source + steps) for source in range(f...  33.1 us
    ppermute x13, waiting for transfers between devices, rotated(): lax.ppermute(value, axis, [(source, (source + steps) % count) for source...  25.7 us
    ppermute x13, starting transfers between devices, rotated(): lax.ppermute(value, axis, [(source, (source + steps) % count) for source...  15.5 us
    ppermute x6, starting transfers between devices, passed_along(): lax.ppermute(value, axis, [(source, source + steps) for source in range(f...  11.6 us
    pallas_call x1, Pallas kernels, attention(): pl.pallas_call(kernel, out_shape=(jax.ShapeDtypeStruct((rows, width), jnp...  8.84 us
    slice x3, local copies, waits for them, and re-layouts, body(): piece[:, :kv_width]  2.96 us
  transfers between devices with their start and end apart: 22, of which 10 were waited for; matrix products, arithmetic and copies ran while one was open for 7% of the time, Pallas kernels for 0%

profile of v11, /device:TPU:0, one launch (start us, length us, event | category | flops | bytes accessed | tf_op | source)
XLA Modules:
  0.0 113.1 jit_solution(14752339290773934686)
XLA Ops:
  0.6 1.1 pad_maximum_fusion.1.refs_8_
  1.7 5.0 %collective-permute-start = (bf16[256,1024]{1,0:T(8,128)(2,1)S(1)}, bf16[256,1024]{1,0:T(8,128)(2,1)S(1)}, u32[]{:S(2)}, u32[]{:S(2)}) collective-permute-start(bf16[256,1024]{1,0:T(8,128)(2,1)S(1)} %pad_maximum_fusion.1.refs_8_), channel_id=1, source_target_pairs={{0,4},{4,8},{8,12},{1,5},{5,9},{9,13},{2,6},{6,10},{10,14},{3,7},{... | collective-permute-start | bytes 1572872 | tf_op jit(solution)/shard_map/ppermute | solution.py:21
  6.7 0.0 copy-start.5
  6.7 1.3 %dynamic-slice_bitcast_fusion = (bf16[256,1152]{1,0:T(8,128)(2,1)S(1)}, bf16[256,1152]{1,0:T(8,128)(2,1)S(1)}) fusion(bf16[1,256,2304]{2,1,0:T(8,128)(2,1)} %param.6, s32[]{:T(128)S(6)} %select_n.89, s32[]{:T(128)S(6)} %select_n.87), kind=kLoop, calls=%fused_computation.9 | loop fusion | bytes 2359304 | tf_op jit(solution)/shard_map/dynamic_slice | solution.py:191
  8.1 1.6 %collective-permute-start.4 = (bf16[256,1152]{1,0:T(8,128)(2,1)S(1)}, bf16[256,1152]{1,0:T(8,128)(2,1)}, u32[]{:S(2)}, u32[]{:S(2)}) collective-permute-start(bf16[256,1152]{1,0:T(8,128)(2,1)S(1)} %get-tuple-element.34), channel_id=1, source_target_pairs={{0,2},{2,0},{1,3},{3,1},{4,6},{6,4},{5,7},{7,5},{8,10},{10,8},{9,1... | collective-permute-start | bytes 1769480 | tf_op jit(solution)/shard_map/ppermute | solution.py:26
  9.6 1.3 %collective-permute-start.1 = (bf16[256,1024]{1,0:T(8,128)(2,1)S(1)}, bf16[256,1024]{1,0:T(8,128)(2,1)S(1)}, u32[]{:S(2)}, u32[]{:S(2)}) collective-permute-start(bf16[256,1024]{1,0:T(8,128)(2,1)S(1)} %pad_maximum_fusion.1.refs_8_), channel_id=1, source_target_pairs={{0,1},{2,3},{4,5},{6,7},{8,9},{10,11},{12,13},{14,15},{16,17},{18,... | collective-permute-start | bytes 1572872 | tf_op jit(solution)/shard_map/ppermute | solution.py:21
  11.0 1.5 %collective-permute-start.2 = (bf16[256,1024]{1,0:T(8,128)(2,1)S(1)}, bf16[256,1024]{1,0:T(8,128)(2,1)}, u32[]{:S(2)}, u32[]{:S(2)}) collective-permute-start(bf16[256,1024]{1,0:T(8,128)(2,1)S(1)} %pad_maximum_fusion.1.refs_8_), channel_id=1, source_target_pairs={{1,8},{5,12},{3,10},{7,14},{17,24},{21,28},{19,26},{23,30}} | collective-permute-start | bytes 1572872 | tf_op jit(solution)/shard_map/ppermute | solution.py:210
  12.4 6.6 %collective-permute-done.refs_4_ = bf16[256,1024]{1,0:T(8,128)(2,1)S(1)} collective-permute-done((bf16[256,1024]{1,0:T(8,128)(2,1)S(1)}, bf16[256,1024]{1,0:T(8,128)(2,1)S(1)}, u32[]{:S(2)}, u32[]{:S(2)}) %collective-permute-start) | collective-permute-done | bytes 524320 | tf_op jit(solution)/shard_map/ppermute | solution.py:21
  19.0 0.0 collective-permute-start.3
  19.0 0.1 select_reduce_fusion
  19.1 0.1 copy.13
  19.2 0.7 subtract_add_fusion.refs_1_
  19.9 0.0 collective-permute-done.1.refs_5_
  19.9 0.0 collective-permute-done.2.refs_6_
  19.9 3.1 %collective-permute-done.4.refs_9_ = bf16[256,1152]{1,0:T(8,128)(2,1)} collective-permute-done((bf16[256,1152]{1,0:T(8,128)(2,1)S(1)}, bf16[256,1152]{1,0:T(8,128)(2,1)}, u32[]{:S(2)}, u32[]{:S(2)}) %collective-permute-start.4) | collective-permute-done | bytes 589856 | tf_op jit(solution)/shard_map/ppermute | solution.py:26
  23.0 8.8 %shard_map.93 = (bf16[256,1024]{1,0:T(8,128)(2,1)}, bf16[256,1024]{1,0:T(8,128)(2,1)}, bf16[256,1024]{1,0:T(8,128)(2,1)}, f32[256,1024]{1,0:T(8,128)}, f32[256,1024]{1,0:T(8,128)}) custom-call(s32[1]{0:T(128)} %bitcast.refs_0_, s32[256,1]{1,0:T(8,128)} %subtract_add_fusion.refs_1_, bf16[256,1024]{1,0:T(8,128)(2,1)} %bitcast.22, bf16[256,1024]{1,0:T(8,128)(2,1)} %bitcast.23, ...), custom_call_target="tpu_custom_call" | custom-call | flops 2684354560 | bytes 7864320 | tf_op jit(solution)/shard_map/pallas_call | solution.py:160
  31.9 1.9 %fusion.11 = (bf16[256,512]{1,0:T(8,128)(2,1)}, bf16[256,512]{1,0:T(8,128)(2,1)S(1)}) fusion(bf16[256,1024]{1,0:T(8,128)(2,1)} %get-tuple-element.19), kind=kLoop, calls=%fused_computation.35 | loop fusion | bytes 1048576 | tf_op jit(solution)/shard_map/slice | solution.py:244
  33.7 0.6 collective-permute-start.7
  34.4 1.1 fusion.10
  35.4 1.4 %collective-permute-start.5 = (bf16[256,512]{1,0:T(8,128)(2,1)S(1)}, bf16[256,512]{1,0:T(8,128)(2,1)S(1)}, u32[]{:S(2)}, u32[]{:S(2)}) collective-permute-start(bf16[256,512]{1,0:T(8,128)(2,1)S(1)} %get-tuple-element.38), channel_id=1, source_target_pairs={{1,0},{3,2},{5,4},{7,6},{9,8},{11,10},{13,12},{15,14},{17,16},{19,... | collective-permute-start | bytes 786440 | tf_op jit(solution)/shard_map/ppermute | solution.py:21
  36.9 0.7 collective-permute-start.6
  37.6 0.1 fusion.9
  37.7 1.3 %collective-permute-start.8 = (bf16[256,512]{1,0:T(8,128)(2,1)S(1)}, bf16[256,512]{1,0:T(8,128)(2,1)S(1)}, u32[]{:S(2)}, u32[]{:S(2)}) collective-permute-start(bf16[256,512]{1,0:T(8,128)(2,1)S(1)} %get-tuple-element.36), channel_id=1, source_target_pairs={{4,0},{8,4},{12,8},{5,1},{9,5},{13,9},{6,2},{10,6},{14,10},{7,3},{... | collective-permute-start | bytes 786440 | tf_op jit(solution)/shard_map/ppermute | solution.py:21
  39.1 0.0 collective-permute-done.5
  39.1 0.0 collective-permute-done.6
  39.1 15.6 %collective-permute-done.8 = bf16[256,512]{1,0:T(8,128)(2,1)S(1)} collective-permute-done((bf16[256,512]{1,0:T(8,128)(2,1)S(1)}, bf16[256,512]{1,0:T(8,128)(2,1)S(1)}, u32[]{:S(2)}, u32[]{:S(2)}) %collective-permute-start.8) | collective-permute-done | bytes 262176 | tf_op jit(solution)/shard_map/ppermute | solution.py:21
  54.6 0.1 convert_add_fusion.2
  54.8 0.0 copy-start.4
  54.8 1.5 %collective-permute-start.13 = (bf16[256,512]{1,0:T(8,128)(2,1)S(1)}, bf16[256,512]{1,0:T(8,128)(2,1)S(1)}, u32[]{:S(2)}, u32[]{:S(2)}) collective-permute-start(bf16[256,512]{1,0:T(8,128)(2,1)S(1)} %convert_add_fusion.2), channel_id=1, source_target_pairs={{0,2},{2,0},{1,3},{3,1},{4,6},{6,4},{5,7},{7,5},{8,10},{10,8},{9,1... | collective-permute-start | bytes 786440 | tf_op jit(solution)/shard_map/ppermute | solution.py:26
  56.3 0.7 collective-permute-start.10
  57.0 1.3 %collective-permute-start.9 = (bf16[256,512]{1,0:T(8,128)(2,1)S(1)}, bf16[256,512]{1,0:T(8,128)(2,1)S(1)}, u32[]{:S(2)}, u32[]{:S(2)}) collective-permute-start(bf16[256,512]{1,0:T(8,128)(2,1)S(1)} %get-tuple-element.21), channel_id=1, source_target_pairs={{1,0},{3,2},{5,4},{7,6},{9,8},{11,10},{13,12},{15,14},{17,16},{19,... | collective-permute-start | bytes 786440 | tf_op jit(solution)/shard_map/ppermute | solution.py:21
  58.3 1.2 %collective-permute-start.11 = (bf16[256,512]{1,0:T(8,128)(2,1)}, bf16[256,512]{1,0:T(8,128)(2,1)S(1)}, u32[]{:S(2)}, u32[]{:S(2)}) collective-permute-start(bf16[256,512]{1,0:T(8,128)(2,1)} %get-tuple-element.23), channel_id=1, source_target_pairs={{0,1},{1,0},{2,3},{3,2},{4,5},{5,4},{6,7},{7,6},{8,9},{9,8},{10,11... | collective-permute-start | bytes 786440 | tf_op jit(solution)/shard_map/ppermute | solution.py:26
  59.5 3.7 %collective-permute-done.13 = bf16[256,512]{1,0:T(8,128)(2,1)S(1)} collective-permute-done((bf16[256,512]{1,0:T(8,128)(2,1)S(1)}, bf16[256,512]{1,0:T(8,128)(2,1)S(1)}, u32[]{:S(2)}, u32[]{:S(2)}) %collective-permute-start.13) | collective-permute-done | bytes 262176 | tf_op jit(solution)/shard_map/ppermute | solution.py:26
  63.2 1.9 %convolution_multiply_fusion = f32[1152,512]{1,0:T(8,128)S(1)} fusion(bf16[256,1152]{1,0:T(8,128)(2,1)} %collective-permute-done.4.refs_9_, bf16[256,1152]{1,0:T(8,128)(2,1)S(1)} %get-tuple-element.33, bf16[256,512]{1,0:T(8,128)(2,1)S(1)} %collective-permute-done.13, bf16[256,512]{1,0:T(8,128)(2,1)S(1)} %convert_add_fusion.2), kind=kOutput, calls=%fused_computation | convolution fusion | flops 607977472 | bytes 4063232 | tf_op jit(solution)/shard_map/dot_general | solution.py:266
  65.1 0.0 copy-start
  65.1 0.1 dynamic-slice_convert_fusion
  65.2 0.1 collective-permute-start.14
  65.3 1.0 add_convert_fusion
  66.3 0.3 copy-done
  66.6 1.3 %collective-permute-start.12 = (bf16[256,512]{1,0:T(8,128)(2,1)}, bf16[256,512]{1,0:T(8,128)(2,1)S(1)}, u32[]{:S(2)}, u32[]{:S(2)}) collective-permute-start(bf16[256,512]{1,0:T(8,128)(2,1)} %add_convert_fusion), channel_id=1, source_target_pairs={{4,0},{8,4},{12,8},{5,1},{9,5},{13,9},{6,2},{10,6},{14,10},{7,3},{... | collective-permute-start | bytes 786440 | tf_op jit(solution)/shard_map/ppermute | solution.py:21
  67.9 0.0 collective-permute-done.10
  67.9 0.0 collective-permute-done.9
  67.9 11.0 %collective-permute-done.12 = bf16[256,512]{1,0:T(8,128)(2,1)S(1)} collective-permute-done((bf16[256,512]{1,0:T(8,128)(2,1)}, bf16[256,512]{1,0:T(8,128)(2,1)S(1)}, u32[]{:S(2)}, u32[]{:S(2)}) %collective-permute-start.12) | collective-permute-done | bytes 262176 | tf_op jit(solution)/shard_map/ppermute | solution.py:21
  78.9 0.8 convert_add_fusion.1
  79.8 1.4 %convert_add_fusion = f32[576,512]{1,0:T(8,128)S(1)} fusion(bf16[576,512]{1,0:T(8,128)(2,1)S(1)} %collective-permute-done.14, f32[1152,512]{1,0:T(8,128)} %copy-done, s32[]{:T(128)S(6)} %select_n.90), kind=kLoop, calls=%fused_computation.7 | loop fusion | flops 589824 | bytes 2949124 | tf_op jit(solution)/shard_map/add | solution.py:279
  81.2 0.1 dynamic-slice_convert_fusion.3
  81.3 1.8 %collective-permute-start.15 = (bf16[144,512]{1,0:T(8,128)(2,1)S(1)}, bf16[144,512]{1,0:T(8,128)(2,1)S(1)}, u32[]{:S(2)}, u32[]{:S(2)}) collective-permute-start(bf16[144,512]{1,0:T(8,128)(2,1)S(1)} %get-tuple-element.30), channel_id=1, source_target_pairs={{0,4},{4,8},{8,12},{12,0},{1,5},{5,9},{9,13},{13,1},{2,6},{6,10},{... | collective-permute-start | bytes 442376 | tf_op jit(solution)/shard_map/ppermute | solution.py:26
  83.1 2.4 %collective-permute-start.17 = (bf16[144,512]{1,0:T(8,128)(2,1)S(1)}, bf16[144,512]{1,0:T(8,128)(2,1)S(1)}, u32[]{:S(2)}, u32[]{:S(2)}) collective-permute-start(bf16[144,512]{1,0:T(8,128)(2,1)S(1)} %get-tuple-element.31), channel_id=1, source_target_pairs={{0,12},{4,0},{8,4},{12,8},{1,13},{5,1},{9,5},{13,9},{2,14},{6,2},{... | collective-permute-start | bytes 442376 | tf_op jit(solution)/shard_map/ppermute | solution.py:26
  85.5 4.5 %collective-permute-done.15 = bf16[144,512]{1,0:T(8,128)(2,1)S(1)} collective-permute-done((bf16[144,512]{1,0:T(8,128)(2,1)S(1)}, bf16[144,512]{1,0:T(8,128)(2,1)S(1)}, u32[]{:S(2)}, u32[]{:S(2)}) %collective-permute-start.15) | collective-permute-done | bytes 147488 | tf_op jit(solution)/shard_map/ppermute | solution.py:26
  90.0 4.7 %collective-permute-done.16 = bf16[144,512]{1,0:T(8,128)(2,1)S(1)} collective-permute-done((bf16[144,512]{1,0:T(8,128)(2,1)S(1)}, bf16[144,512]{1,0:T(8,128)(2,1)S(1)}, u32[]{:S(2)}, u32[]{:S(2)}) %collective-permute-start.16) | collective-permute-done | bytes 147488 | tf_op jit(solution)/shard_map/ppermute | solution.py:26
  94.7 0.0 collective-permute-done.17
  94.8 0.1 broadcast_in_dim.28
  94.9 0.1 fusion.6
  95.0 3.7 %collective-permute-start.18 = (bf16[144,512]{1,0:T(8,128)(2,1)S(1)}, bf16[144,512]{1,0:T(8,128)(2,1)S(1)}, u32[]{:S(2)}, u32[]{:S(2)}) collective-permute-start(bf16[144,512]{1,0:T(8,128)(2,1)S(1)} %get-tuple-element.28), channel_id=1, source_target_pairs={{0,4},{4,8},{8,12},{12,0},{1,5},{5,9},{9,13},{13,1},{2,6},{6,10},{... | collective-permute-start | bytes 442376 | tf_op jit(solution)/shard_map/ppermute | solution.py:26
  98.7 0.2 collective-permute-start.19
  98.9 2.3 %collective-permute-start.20 = (bf16[144,512]{1,0:T(8,128)(2,1)S(1)}, bf16[144,512]{1,0:T(8,128)(2,1)S(1)}, u32[]{:S(2)}, u32[]{:S(2)}) collective-permute-start(bf16[144,512]{1,0:T(8,128)(2,1)S(1)} %get-tuple-element.28), channel_id=1, source_target_pairs={{0,12},{4,0},{8,4},{12,8},{1,13},{5,1},{9,5},{13,9},{2,14},{6,2},{... | collective-permute-start | bytes 442376 | tf_op jit(solution)/shard_map/ppermute | solution.py:26
  101.2 2.1 %collective-permute-done.18 = bf16[144,512]{1,0:T(8,128)(2,1)S(1)} collective-permute-done((bf16[144,512]{1,0:T(8,128)(2,1)S(1)}, bf16[144,512]{1,0:T(8,128)(2,1)S(1)}, u32[]{:S(2)}, u32[]{:S(2)}) %collective-permute-start.18) | collective-permute-done | bytes 147488 | tf_op jit(solution)/shard_map/ppermute | solution.py:26
  103.3 5.6 %collective-permute-done.19 = bf16[144,512]{1,0:T(8,128)(2,1)S(1)} collective-permute-done((bf16[144,512]{1,0:T(8,128)(2,1)S(1)}, bf16[144,512]{1,0:T(8,128)(2,1)S(1)}, u32[]{:S(2)}, u32[]{:S(2)}) %collective-permute-start.19) | collective-permute-done | bytes 147488 | tf_op jit(solution)/shard_map/ppermute | solution.py:26
  109.0 0.0 collective-permute-done.20
  109.0 0.1 convert_element_type.95
  109.1 0.1 collective-permute-start.21
  109.2 2.0 %collective-permute-done.21 = bf16[576,512]{1,0:T(8,128)(2,1)S(1)} collective-permute-done((bf16[576,512]{1,0:T(8,128)(2,1)S(1)}, bf16[576,512]{1,0:T(8,128)(2,1)S(1)}, u32[]{:S(2)}, u32[]{:S(2)}) %collective-permute-start.21) | collective-permute-done | bytes 589856 | tf_op jit(solution)/shard_map/ppermute | solution.py:26
  111.1 0.3 convert_select_fusion.1
  111.5 1.6 %pad_maximum_fusion = f32[1152,512]{1,0:T(8,128)} fusion(f32[576,512]{1,0:T(8,128)S(1)} %get-tuple-element.27, f32[576,512]{1,0:T(8,128)S(1)} %get-tuple-element.26), kind=kLoop, calls=%fused_computation.1 | loop fusion | flops 589824 | bytes 4718592 | tf_op jit(solution)/shard_map/concatenate | solution.py:287
  (22 shorter events, 0.2 us)
Async XLA Ops:
  1.7 9.2 %copy-start.3 = (bf16[256,1024]{1,0:T(8,128)(2,1)}, bf16[256,1024]{1,0:T(8,128)(2,1)S(1)}, u32[]{:S(2)}) copy-start(bf16[256,1024]{1,0:T(8,128)(2,1)S(1)} %pad_maximum_fusion.1.refs_8_) | copy-start | bytes 1572868
  1.7 17.2 %collective-permute-start = (bf16[256,1024]{1,0:T(8,128)(2,1)S(1)}, bf16[256,1024]{1,0:T(8,128)(2,1)S(1)}, u32[]{:S(2)}, u32[]{:S(2)}) collective-permute-start(bf16[256,1024]{1,0:T(8,128)(2,1)S(1)} %pad_maximum_fusion.1.refs_8_), channel_id=1, source_target_pairs={{0,4},{4,8},{8,12},{1,5},{5,9},{9,13},{2,6},{6,10},{10,14},{3,7},{... | collective-permute-start | bytes 1572872 | tf_op jit(solution)/shard_map/ppermute | solution.py:21
  6.7 12.3 %copy-start.5 = (s32[1,12]{1,0:T(1,128)S(1)}, s32[1,12]{1,0:T(1,128)}, u32[]{:S(2)}) copy-start(s32[1,12]{1,0:T(1,128)} %param.11) | copy-start | bytes 148
  8.1 15.0 %collective-permute-start.4 = (bf16[256,1152]{1,0:T(8,128)(2,1)S(1)}, bf16[256,1152]{1,0:T(8,128)(2,1)}, u32[]{:S(2)}, u32[]{:S(2)}) collective-permute-start(bf16[256,1152]{1,0:T(8,128)(2,1)S(1)} %get-tuple-element.34), channel_id=1, source_target_pairs={{0,2},{2,0},{1,3},{3,1},{4,6},{6,4},{5,7},{7,5},{8,10},{10,8},{9,1... | collective-permute-start | bytes 1769480 | tf_op jit(solution)/shard_map/ppermute | solution.py:26
  9.6 10.3 %collective-permute-start.1 = (bf16[256,1024]{1,0:T(8,128)(2,1)S(1)}, bf16[256,1024]{1,0:T(8,128)(2,1)S(1)}, u32[]{:S(2)}, u32[]{:S(2)}) collective-permute-start(bf16[256,1024]{1,0:T(8,128)(2,1)S(1)} %pad_maximum_fusion.1.refs_8_), channel_id=1, source_target_pairs={{0,1},{2,3},{4,5},{6,7},{8,9},{10,11},{12,13},{14,15},{16,17},{18,... | collective-permute-start | bytes 1572872 | tf_op jit(solution)/shard_map/ppermute | solution.py:21
  11.0 9.0 %collective-permute-start.2 = (bf16[256,1024]{1,0:T(8,128)(2,1)S(1)}, bf16[256,1024]{1,0:T(8,128)(2,1)}, u32[]{:S(2)}, u32[]{:S(2)}) collective-permute-start(bf16[256,1024]{1,0:T(8,128)(2,1)S(1)} %pad_maximum_fusion.1.refs_8_), channel_id=1, source_target_pairs={{1,8},{5,12},{3,10},{7,14},{17,24},{21,28},{19,26},{23,30}} | collective-permute-start | bytes 1572872 | tf_op jit(solution)/shard_map/ppermute | solution.py:210
  19.0 4.1 %copy-start.6 = (bf16[256,1024]{1,0:T(8,128)(2,1)}, bf16[256,1024]{1,0:T(8,128)(2,1)S(1)}, u32[]{:S(2)}) copy-start(bf16[256,1024]{1,0:T(8,128)(2,1)S(1)} %collective-permute-done.refs_4_) | copy-start | bytes 1572868
  19.0 4.1 %collective-permute-start.3 = (bf16[256,1024]{1,0:T(8,128)(2,1)S(1)}, bf16[256,1024]{1,0:T(8,128)(2,1)}, u32[]{:S(2)}, u32[]{:S(2)}) collective-permute-start(bf16[256,1024]{1,0:T(8,128)(2,1)S(1)} %collective-permute-done.refs_4_), channel_id=1, source_target_pairs={{0,1},{1,0},{2,3},{3,2},{4,5},{5,4},{6,7},{7,6},{8,9},{9,8},{10,11... | collective-permute-start | bytes 1572872 | tf_op jit(solution)/shard_map/ppermute | solution.py:26
  19.9 3.1 %copy-start.7 = (bf16[256,1024]{1,0:T(8,128)(2,1)}, bf16[256,1024]{1,0:T(8,128)(2,1)S(1)}, u32[]{:S(2)}) copy-start(bf16[256,1024]{1,0:T(8,128)(2,1)S(1)} %collective-permute-done.1.refs_5_) | copy-start | bytes 1572868
  31.9 5.7 %copy-start.2 = (f32[256,1024]{1,0:T(8,128)S(1)}, f32[256,1024]{1,0:T(8,128)}, u32[]{:S(2)}) copy-start(f32[256,1024]{1,0:T(8,128)} %get-tuple-element.18) | copy-start | bytes 3145732
  33.7 3.8 %collective-permute-start.7 = (bf16[256,512]{1,0:T(8,128)(2,1)S(1)}, bf16[256,512]{1,0:T(8,128)(2,1)S(1)}, u32[]{:S(2)}, u32[]{:S(2)}) collective-permute-start(bf16[256,512]{1,0:T(8,128)(2,1)S(1)} %get-tuple-element.40), channel_id=1, source_target_pairs={{0,1},{1,0},{2,3},{3,2},{4,5},{5,4},{6,7},{7,6},{8,9},{9,8},{10,11... | collective-permute-start | bytes 786440 | tf_op jit(solution)/shard_map/ppermute | solution.py:26
  35.4 3.6 %copy-start.1 = (f32[256,1024]{1,0:T(8,128)S(1)}, f32[256,1024]{1,0:T(8,128)}, u32[]{:S(2)}) copy-start(f32[256,1024]{1,0:T(8,128)} %get-tuple-element.16) | copy-start | bytes 3145732
  35.4 3.6 %collective-permute-start.5 = (bf16[256,512]{1,0:T(8,128)(2,1)S(1)}, bf16[256,512]{1,0:T(8,128)(2,1)S(1)}, u32[]{:S(2)}, u32[]{:S(2)}) collective-permute-start(bf16[256,512]{1,0:T(8,128)(2,1)S(1)} %get-tuple-element.38), channel_id=1, source_target_pairs={{1,0},{3,2},{5,4},{7,6},{9,8},{11,10},{13,12},{15,14},{17,16},{19,... | collective-permute-start | bytes 786440 | tf_op jit(solution)/shard_map/ppermute | solution.py:21
  36.9 2.2 %collective-permute-start.6 = (bf16[256,512]{1,0:T(8,128)(2,1)S(1)}, bf16[256,512]{1,0:T(8,128)(2,1)S(1)}, u32[]{:S(2)}, u32[]{:S(2)}) collective-permute-start(bf16[256,512]{1,0:T(8,128)(2,1)S(1)} %get-tuple-element.38), channel_id=1, source_target_pairs={{8,1},{12,5},{10,3},{14,7},{24,17},{28,21},{26,19},{30,23}} | collective-permute-start | bytes 786440 | tf_op jit(solution)/shard_map/ppermute | solution.py:235
  37.7 16.9 %collective-permute-start.8 = (bf16[256,512]{1,0:T(8,128)(2,1)S(1)}, bf16[256,512]{1,0:T(8,128)(2,1)S(1)}, u32[]{:S(2)}, u32[]{:S(2)}) collective-permute-start(bf16[256,512]{1,0:T(8,128)(2,1)S(1)} %get-tuple-element.36), channel_id=1, source_target_pairs={{4,0},{8,4},{12,8},{5,1},{9,5},{13,9},{6,2},{10,6},{14,10},{7,3},{... | collective-permute-start | bytes 786440 | tf_op jit(solution)/shard_map/ppermute | solution.py:21
  54.8 10.3 %copy-start.4 = (bf16[256,512]{1,0:T(8,128)(2,1)}, bf16[256,512]{1,0:T(8,128)(2,1)S(1)}, u32[]{:S(2)}) copy-start(bf16[256,512]{1,0:T(8,128)(2,1)S(1)} %convert_add_fusion.2) | copy-start | bytes 786436
  54.8 8.4 %collective-permute-start.13 = (bf16[256,512]{1,0:T(8,128)(2,1)S(1)}, bf16[256,512]{1,0:T(8,128)(2,1)S(1)}, u32[]{:S(2)}, u32[]{:S(2)}) collective-permute-start(bf16[256,512]{1,0:T(8,128)(2,1)S(1)} %convert_add_fusion.2), channel_id=1, source_target_pairs={{0,2},{2,0},{1,3},{3,1},{4,6},{6,4},{5,7},{7,5},{8,10},{10,8},{9,1... | collective-permute-start | bytes 786440 | tf_op jit(solution)/shard_map/ppermute | solution.py:26
  56.3 11.6 %collective-permute-start.10 = (bf16[256,512]{1,0:T(8,128)(2,1)S(1)}, bf16[256,512]{1,0:T(8,128)(2,1)S(1)}, u32[]{:S(2)}, u32[]{:S(2)}) collective-permute-start(bf16[256,512]{1,0:T(8,128)(2,1)S(1)} %get-tuple-element.21), channel_id=1, source_target_pairs={{8,1},{12,5},{10,3},{14,7},{24,17},{28,21},{26,19},{30,23}} | collective-permute-start | bytes 786440 | tf_op jit(solution)/shard_map/ppermute | solution.py:235
  57.0 10.9 %collective-permute-start.9 = (bf16[256,512]{1,0:T(8,128)(2,1)S(1)}, bf16[256,512]{1,0:T(8,128)(2,1)S(1)}, u32[]{:S(2)}, u32[]{:S(2)}) collective-permute-start(bf16[256,512]{1,0:T(8,128)(2,1)S(1)} %get-tuple-element.21), channel_id=1, source_target_pairs={{1,0},{3,2},{5,4},{7,6},{9,8},{11,10},{13,12},{15,14},{17,16},{19,... | collective-permute-start | bytes 786440 | tf_op jit(solution)/shard_map/ppermute | solution.py:21
  58.3 6.9 %collective-permute-start.11 = (bf16[256,512]{1,0:T(8,128)(2,1)}, bf16[256,512]{1,0:T(8,128)(2,1)S(1)}, u32[]{:S(2)}, u32[]{:S(2)}) collective-permute-start(bf16[256,512]{1,0:T(8,128)(2,1)} %get-tuple-element.23), channel_id=1, source_target_pairs={{0,1},{1,0},{2,3},{3,2},{4,5},{5,4},{6,7},{7,6},{8,9},{9,8},{10,11... | collective-permute-start | bytes 786440 | tf_op jit(solution)/shard_map/ppermute | solution.py:26
  65.1 1.5 %copy-start = (f32[1152,512]{1,0:T(8,128)}, f32[1152,512]{1,0:T(8,128)S(1)}, u32[]{:S(2)}) copy-start(f32[1152,512]{1,0:T(8,128)S(1)} %convolution_multiply_fusion) | copy-start | bytes 7077892
  65.2 14.6 %collective-permute-start.14 = (bf16[576,512]{1,0:T(8,128)(2,1)S(1)}, bf16[576,512]{1,0:T(8,128)(2,1)S(1)}, u32[]{:S(2)}, u32[]{:S(2)}) collective-permute-start(bf16[576,512]{1,0:T(8,128)(2,1)S(1)} %dynamic-slice_convert_fusion), channel_id=1, source_target_pairs={{0,1},{1,0},{2,3},{3,2},{4,5},{5,4},{6,7},{7,6},{8,9},{9,8},{10,11... | collective-permute-start | bytes 1769480 | tf_op jit(solution)/shard_map/ppermute | solution.py:26
  66.6 12.4 %collective-permute-start.12 = (bf16[256,512]{1,0:T(8,128)(2,1)}, bf16[256,512]{1,0:T(8,128)(2,1)S(1)}, u32[]{:S(2)}, u32[]{:S(2)}) collective-permute-start(bf16[256,512]{1,0:T(8,128)(2,1)} %add_convert_fusion), channel_id=1, source_target_pairs={{4,0},{8,4},{12,8},{5,1},{9,5},{13,9},{6,2},{10,6},{14,10},{7,3},{... | collective-permute-start | bytes 786440 | tf_op jit(solution)/shard_map/ppermute | solution.py:21
  81.3 8.7 %collective-permute-start.15 = (bf16[144,512]{1,0:T(8,128)(2,1)S(1)}, bf16[144,512]{1,0:T(8,128)(2,1)S(1)}, u32[]{:S(2)}, u32[]{:S(2)}) collective-permute-start(bf16[144,512]{1,0:T(8,128)(2,1)S(1)} %get-tuple-element.30), channel_id=1, source_target_pairs={{0,4},{4,8},{8,12},{12,0},{1,5},{5,9},{9,13},{13,1},{2,6},{6,10},{... | collective-permute-start | bytes 442376 | tf_op jit(solution)/shard_map/ppermute | solution.py:26
  83.1 11.7 %collective-permute-start.16 = (bf16[144,512]{1,0:T(8,128)(2,1)S(1)}, bf16[144,512]{1,0:T(8,128)(2,1)S(1)}, u32[]{:S(2)}, u32[]{:S(2)}) collective-permute-start(bf16[144,512]{1,0:T(8,128)(2,1)S(1)} %get-tuple-element.32), channel_id=1, source_target_pairs={{0,8},{4,12},{8,0},{12,4},{1,9},{5,13},{9,1},{13,5},{2,10},{6,14},... | collective-permute-start | bytes 442376 | tf_op jit(solution)/shard_map/ppermute | solution.py:26
  83.1 11.7 %collective-permute-start.17 = (bf16[144,512]{1,0:T(8,128)(2,1)S(1)}, bf16[144,512]{1,0:T(8,128)(2,1)S(1)}, u32[]{:S(2)}, u32[]{:S(2)}) collective-permute-start(bf16[144,512]{1,0:T(8,128)(2,1)S(1)} %get-tuple-element.31), channel_id=1, source_target_pairs={{0,12},{4,0},{8,4},{12,8},{1,13},{5,1},{9,5},{13,9},{2,14},{6,2},{... | collective-permute-start | bytes 442376 | tf_op jit(solution)/shard_map/ppermute | solution.py:26
  95.0 8.3 %collective-permute-start.18 = (bf16[144,512]{1,0:T(8,128)(2,1)S(1)}, bf16[144,512]{1,0:T(8,128)(2,1)S(1)}, u32[]{:S(2)}, u32[]{:S(2)}) collective-permute-start(bf16[144,512]{1,0:T(8,128)(2,1)S(1)} %get-tuple-element.28), channel_id=1, source_target_pairs={{0,4},{4,8},{8,12},{12,0},{1,5},{5,9},{9,13},{13,1},{2,6},{6,10},{... | collective-permute-start | bytes 442376 | tf_op jit(solution)/shard_map/ppermute | solution.py:26
  98.7 10.3 %collective-permute-start.19 = (bf16[144,512]{1,0:T(8,128)(2,1)S(1)}, bf16[144,512]{1,0:T(8,128)(2,1)S(1)}, u32[]{:S(2)}, u32[]{:S(2)}) collective-permute-start(bf16[144,512]{1,0:T(8,128)(2,1)S(1)} %get-tuple-element.28), channel_id=1, source_target_pairs={{0,8},{4,12},{8,0},{12,4},{1,9},{5,13},{9,1},{13,5},{2,10},{6,14},... | collective-permute-start | bytes 442376 | tf_op jit(solution)/shard_map/ppermute | solution.py:26
  98.9 10.1 %collective-permute-start.20 = (bf16[144,512]{1,0:T(8,128)(2,1)S(1)}, bf16[144,512]{1,0:T(8,128)(2,1)S(1)}, u32[]{:S(2)}, u32[]{:S(2)}) collective-permute-start(bf16[144,512]{1,0:T(8,128)(2,1)S(1)} %get-tuple-element.28), channel_id=1, source_target_pairs={{0,12},{4,0},{8,4},{12,8},{1,13},{5,1},{9,5},{13,9},{2,14},{6,2},{... | collective-permute-start | bytes 442376 | tf_op jit(solution)/shard_map/ppermute | solution.py:26
  109.1 2.1 %collective-permute-start.21 = (bf16[576,512]{1,0:T(8,128)(2,1)S(1)}, bf16[576,512]{1,0:T(8,128)(2,1)S(1)}, u32[]{:S(2)}, u32[]{:S(2)}) collective-permute-start(bf16[576,512]{1,0:T(8,128)(2,1)S(1)} %convert_element_type.95), channel_id=1, source_target_pairs={{0,1},{1,0},{2,3},{3,2},{4,5},{5,4},{6,7},{7,6},{8,9},{9,8},{10,11... | collective-permute-start | bytes 1769480 | tf_op jit(solution)/shard_map/ppermute | solution.py:26

commit v12 on v7

--- a/solution.py
+++ b/solution.py
@@ -221,7 +221,7 @@
         slots = [(index, index) for index in range(reach + 1)]
     grad_q, *grad_pieces = attention(
         flag, lo_rel, query_heads[0], grad_out[0], kv_blocks, slots, heads, kv_heads, margin,
-        inputs[1:],
+        [],
         chip_route,
     )
 

time: 113 us -> 115 us (1.018)
  other arithmetic: 7.16 us -> 9.71 us
    ppermute x12, waiting for transfers between devices: 30.5 us -> 28.3 us  [rotated(): lax.ppermute(value, axis, [(source, (source + steps) % count) for source...]
    ppermute x12, starting transfers between devices: 18.8 us -> 20.5 us  [rotated(): lax.ppermute(value, axis, [(source, (source + steps) % count) for source...]
    dynamic_slice x1, local copies, waits for them, and re-layouts: 1.34 us -> 0.16 us  [body(): lax.dynamic_slice_in_dim(own_input, fsdp_at * shard_rows, shard_rows, axi...]
  transfers between devices with their start and end apart: 18 -> 18, of which waited for: 11 -> 11; matrix products, arithmetic and copies ran while one was open for 3% -> 5% of each run, Pallas kernels for 0% -> 0%
where the time goes in v12:
time: 115 us; the launch traced here: 113 us
  waiting for transfers between devices  58.5 us (51%)
  starting transfers between devices  30.9 us (27%)
  other arithmetic  9.71 us (8%)
  Pallas kernels  8.84 us (8%)
  local copies, waits for them, and re-layouts  3.68 us (3%)
    ppermute x4, waiting for transfers between devices, passed_along(): lax.ppermute(value, axis, [(source, source + steps) for source in range(f...  30.2 us
    ppermute x12, waiting for transfers between devices, rotated(): lax.ppermute(value, axis, [(source, (source + steps) % count) for source...  28.3 us
    ppermute x12, starting transfers between devices, rotated(): lax.ppermute(value, axis, [(source, (source + steps) % count) for source...  20.5 us
    ppermute x4, starting transfers between devices, passed_along(): lax.ppermute(value, axis, [(source, source + steps) for source in range(f...  9.01 us
    pallas_call x1, Pallas kernels, attention(): pl.pallas_call(kernel, out_shape=(jax.ShapeDtypeStruct((rows, width), jnp...  8.84 us
  transfers between devices with their start and end apart: 18, of which 11 were waited for; matrix products, arithmetic and copies ran while one was open for 5% of the time, Pallas kernels for 0%

profile of v12, /device:TPU:0, one launch (start us, length us, event | category | flops | bytes accessed | tf_op | source)
XLA Modules:
  0.0 113.3 jit_solution(11865437192293685322)
XLA Ops:
  0.6 1.1 pad_maximum_fusion.1.refs_8_
  1.7 0.0 copy-start.3
  1.7 5.0 %collective-permute-start = (bf16[256,1024]{1,0:T(8,128)(2,1)S(1)}, bf16[256,1024]{1,0:T(8,128)(2,1)S(1)}, u32[]{:S(2)}, u32[]{:S(2)}) collective-permute-start(bf16[256,1024]{1,0:T(8,128)(2,1)S(1)} %pad_maximum_fusion.1.refs_8_), channel_id=1, source_target_pairs={{0,4},{4,8},{8,12},{1,5},{5,9},{9,13},{2,6},{6,10},{10,14},{3,7},{... | collective-permute-start | bytes 1572872 | tf_op jit(solution)/shard_map/ppermute | solution.py:21
  6.7 1.5 %collective-permute-start.1 = (bf16[256,1024]{1,0:T(8,128)(2,1)S(1)}, bf16[256,1024]{1,0:T(8,128)(2,1)S(1)}, u32[]{:S(2)}, u32[]{:S(2)}) collective-permute-start(bf16[256,1024]{1,0:T(8,128)(2,1)S(1)} %pad_maximum_fusion.1.refs_8_), channel_id=1, source_target_pairs={{0,1},{2,3},{4,5},{6,7},{8,9},{10,11},{12,13},{14,15},{16,17},{18,... | collective-permute-start | bytes 1572872 | tf_op jit(solution)/shard_map/ppermute | solution.py:21
  8.2 0.7 collective-permute-start.2
  8.9 10.1 %collective-permute-done.refs_4_ = bf16[256,1024]{1,0:T(8,128)(2,1)S(1)} collective-permute-done((bf16[256,1024]{1,0:T(8,128)(2,1)S(1)}, bf16[256,1024]{1,0:T(8,128)(2,1)S(1)}, u32[]{:S(2)}, u32[]{:S(2)}) %collective-permute-start) | collective-permute-done | bytes 524320 | tf_op jit(solution)/shard_map/ppermute | solution.py:21
  19.0 0.0 collective-permute-start.3
  19.0 0.8 select_reduce_fusion
  19.7 0.1 copy.13
  19.9 0.7 subtract_add_fusion.refs_1_
  20.6 0.0 collective-permute-done.1.refs_5_
  20.6 0.0 collective-permute-done.2.refs_6_
  20.6 0.0 copy-start.6
  20.6 0.3 collective-permute-done.3.refs_7_
  20.9 0.0 copy-done.3
  20.9 0.0 copy-done.4
  20.9 0.5 copy-done.5
  21.4 0.2 copy-done.6
  21.6 0.2 copy-done.7
  21.7 8.8 %shard_map.93 = (bf16[256,1024]{1,0:T(8,128)(2,1)}, bf16[256,1024]{1,0:T(8,128)(2,1)}, bf16[256,1024]{1,0:T(8,128)(2,1)}, f32[256,1024]{1,0:T(8,128)}, f32[256,1024]{1,0:T(8,128)}) custom-call(s32[1]{0:T(128)} %bitcast.refs_0_, s32[256,1]{1,0:T(8,128)} %subtract_add_fusion.refs_1_, bf16[256,1024]{1,0:T(8,128)(2,1)} %bitcast.20, bf16[256,1024]{1,0:T(8,128)(2,1)} %bitcast.21, ...), custom_call_target="tpu_custom_call" | custom-call | flops 2684354560 | bytes 7864320 | tf_op jit(solution)/shard_map/pallas_call | solution.py:160
  30.6 2.9 %collective-permute-start.6 = (bf16[256,1024]{1,0:T(8,128)(2,1)}, bf16[256,1024]{1,0:T(8,128)(2,1)S(1)}, u32[]{:S(2)}, u32[]{:S(2)}) collective-permute-start(bf16[256,1024]{1,0:T(8,128)(2,1)} %get-tuple-element.13), channel_id=1, source_target_pairs={{0,1},{1,0},{2,3},{3,2},{4,5},{5,4},{6,7},{7,6},{8,9},{9,8},{10,11... | collective-permute-start | bytes 1572872 | tf_op jit(solution)/shard_map/ppermute | solution.py:26
  33.4 1.3 %collective-permute-start.4 = (bf16[256,1024]{1,0:T(8,128)(2,1)}, bf16[256,1024]{1,0:T(8,128)(2,1)S(1)}, u32[]{:S(2)}, u32[]{:S(2)}) collective-permute-start(bf16[256,1024]{1,0:T(8,128)(2,1)} %get-tuple-element.11), channel_id=1, source_target_pairs={{1,0},{3,2},{5,4},{7,6},{9,8},{11,10},{13,12},{15,14},{17,16},{19,... | collective-permute-start | bytes 1572872 | tf_op jit(solution)/shard_map/ppermute | solution.py:21
  34.7 0.7 collective-permute-start.5
  35.4 0.0 collective-permute-done.6
  35.4 2.2 %add_convert_fusion.1 = bf16[256,1024]{1,0:T(8,128)(2,1)} fusion(f32[256,1024]{1,0:T(8,128)} %get-tuple-element.12, bf16[256,1024]{1,0:T(8,128)(2,1)S(1)} %collective-permute-done.6), kind=kLoop, calls=%fused_computation.10 | loop fusion | flops 786432 | bytes 2097152 | tf_op jit(solution)/shard_map/convert_element_type | solution.py:229
  37.6 1.3 %collective-permute-start.7 = (bf16[256,1024]{1,0:T(8,128)(2,1)}, bf16[256,1024]{1,0:T(8,128)(2,1)}, u32[]{:S(2)}, u32[]{:S(2)}) collective-permute-start(bf16[256,1024]{1,0:T(8,128)(2,1)} %add_convert_fusion.1), channel_id=1, source_target_pairs={{4,0},{8,4},{12,8},{5,1},{9,5},{13,9},{6,2},{10,6},{14,10},{7,3},{... | collective-permute-start | bytes 1572872 | tf_op jit(solution)/shard_map/ppermute | solution.py:21
  38.9 0.0 copy-done.1
  39.0 0.2 dynamic-slice_bitcast_fusion.1
  39.1 1.5 %collective-permute-start.8 = (bf16[256,1152]{1,0:T(8,128)(2,1)S(1)}, bf16[256,1152]{1,0:T(8,128)(2,1)S(1)}, u32[]{:S(2)}, u32[]{:S(2)}) collective-permute-start(bf16[256,1152]{1,0:T(8,128)(2,1)S(1)} %get-tuple-element.22), channel_id=1, source_target_pairs={{0,2},{2,0},{1,3},{3,1},{4,6},{6,4},{5,7},{7,5},{8,10},{10,8},{9,1... | collective-permute-start | bytes 1769480 | tf_op jit(solution)/shard_map/ppermute | solution.py:26
  40.6 0.0 collective-permute-done.4
  40.6 0.0 collective-permute-done.5
  40.6 20.1 %collective-permute-done.7 = bf16[256,1024]{1,0:T(8,128)(2,1)} collective-permute-done((bf16[256,1024]{1,0:T(8,128)(2,1)}, bf16[256,1024]{1,0:T(8,128)(2,1)}, u32[]{:S(2)}, u32[]{:S(2)}) %collective-permute-start.7) | collective-permute-done | bytes 524320 | tf_op jit(solution)/shard_map/ppermute | solution.py:21
  60.7 1.4 %add_convert_fusion = bf16[256,1024]{1,0:T(8,128)(2,1)S(1)} fusion(bf16[256,1024]{1,0:T(8,128)(2,1)} %collective-permute-done.7, bf16[256,1024]{1,0:T(8,128)(2,1)S(1)} %collective-permute-done.5, f32[256,1024]{1,0:T(8,128)S(1)} %copy-done.2, bf16[256,1024]{1,0:T(8,128)(2,1)S(1)} %collective-permute-done.4), kind=kLoop, calls=%fused_computation.9 | loop fusion | flops 1835008 | bytes 3145728 | tf_op jit(solution)/shard_map/convert_element_type | solution.py:249
  62.1 0.9 fusion.9
  63.0 1.5 %collective-permute-start.9 = (bf16[256,512]{1,0:T(8,128)(2,1)S(1)}, bf16[256,512]{1,0:T(8,128)(2,1)S(1)}, u32[]{:S(2)}, u32[]{:S(2)}) collective-permute-start(bf16[256,512]{1,0:T(8,128)(2,1)S(1)} %get-tuple-element.23), channel_id=1, source_target_pairs={{0,2},{2,0},{1,3},{3,1},{4,6},{6,4},{5,7},{7,5},{8,10},{10,8},{9,1... | collective-permute-start | bytes 786440 | tf_op jit(solution)/shard_map/ppermute | solution.py:26
  64.5 0.0 collective-permute-done.8
  64.5 7.3 %collective-permute-done.9 = bf16[256,512]{1,0:T(8,128)(2,1)S(1)} collective-permute-done((bf16[256,512]{1,0:T(8,128)(2,1)S(1)}, bf16[256,512]{1,0:T(8,128)(2,1)S(1)}, u32[]{:S(2)}, u32[]{:S(2)}) %collective-permute-start.9) | collective-permute-done | bytes 262176 | tf_op jit(solution)/shard_map/ppermute | solution.py:26
  71.8 0.8 convolution_multiply_fusion
  72.6 0.0 copy-start
  72.6 1.4 %copy-done = f32[1152,512]{1,0:T(8,128)} copy-done((f32[1152,512]{1,0:T(8,128)}, f32[1152,512]{1,0:T(8,128)S(1)}, u32[]{:S(2)}) %copy-start) | copy-done | bytes 2359320
  74.0 0.1 dynamic-slice_convert_fusion
  74.1 0.1 collective-permute-start.10
  74.2 1.9 %collective-permute-done.10 = bf16[576,512]{1,0:T(8,128)(2,1)S(1)} collective-permute-done((bf16[576,512]{1,0:T(8,128)(2,1)S(1)}, bf16[576,512]{1,0:T(8,128)(2,1)S(1)}, u32[]{:S(2)}, u32[]{:S(2)}) %collective-permute-start.10) | collective-permute-done | bytes 589856 | tf_op jit(solution)/shard_map/ppermute | solution.py:26
  76.1 1.4 %convert_add_fusion = f32[576,512]{1,0:T(8,128)S(1)} fusion(bf16[576,512]{1,0:T(8,128)(2,1)S(1)} %collective-permute-done.10, f32[1152,512]{1,0:T(8,128)} %copy-done, s32[]{:T(128)S(6)} %select_n.90), kind=kLoop, calls=%fused_computation.7 | loop fusion | flops 589824 | bytes 2949124 | tf_op jit(solution)/shard_map/add | solution.py:271
  77.6 0.1 dynamic-slice_convert_fusion.3
  77.7 5.2 %collective-permute-start.11 = (bf16[144,512]{1,0:T(8,128)(2,1)S(1)}, bf16[144,512]{1,0:T(8,128)(2,1)S(1)}, u32[]{:S(2)}, u32[]{:S(2)}) collective-permute-start(bf16[144,512]{1,0:T(8,128)(2,1)S(1)} %get-tuple-element.18), channel_id=1, source_target_pairs={{0,4},{4,8},{8,12},{12,0},{1,5},{5,9},{9,13},{13,1},{2,6},{6,10},{... | collective-permute-start | bytes 442376 | tf_op jit(solution)/shard_map/ppermute | solution.py:26
  82.8 0.0 collective-permute-start.12
  82.9 2.4 %collective-permute-start.13 = (bf16[144,512]{1,0:T(8,128)(2,1)S(1)}, bf16[144,512]{1,0:T(8,128)(2,1)S(1)}, u32[]{:S(2)}, u32[]{:S(2)}) collective-permute-start(bf16[144,512]{1,0:T(8,128)(2,1)S(1)} %get-tuple-element.19), channel_id=1, source_target_pairs={{0,12},{4,0},{8,4},{12,8},{1,13},{5,1},{9,5},{13,9},{2,14},{6,2},{... | collective-permute-start | bytes 442376 | tf_op jit(solution)/shard_map/ppermute | solution.py:26
  85.3 1.8 %collective-permute-done.11 = bf16[144,512]{1,0:T(8,128)(2,1)S(1)} collective-permute-done((bf16[144,512]{1,0:T(8,128)(2,1)S(1)}, bf16[144,512]{1,0:T(8,128)(2,1)S(1)}, u32[]{:S(2)}, u32[]{:S(2)}) %collective-permute-start.11) | collective-permute-done | bytes 147488 | tf_op jit(solution)/shard_map/ppermute | solution.py:26
  87.1 5.3 %collective-permute-done.12 = bf16[144,512]{1,0:T(8,128)(2,1)S(1)} collective-permute-done((bf16[144,512]{1,0:T(8,128)(2,1)S(1)}, bf16[144,512]{1,0:T(8,128)(2,1)S(1)}, u32[]{:S(2)}, u32[]{:S(2)}) %collective-permute-start.12) | collective-permute-done | bytes 147488 | tf_op jit(solution)/shard_map/ppermute | solution.py:26
  92.4 0.2 collective-permute-done.13
  92.6 0.1 broadcast_in_dim.28
  92.8 0.1 fusion.6
  92.8 3.5 %collective-permute-start.14 = (bf16[144,512]{1,0:T(8,128)(2,1)S(1)}, bf16[144,512]{1,0:T(8,128)(2,1)S(1)}, u32[]{:S(2)}, u32[]{:S(2)}) collective-permute-start(bf16[144,512]{1,0:T(8,128)(2,1)S(1)} %get-tuple-element.16), channel_id=1, source_target_pairs={{0,4},{4,8},{8,12},{12,0},{1,5},{5,9},{9,13},{13,1},{2,6},{6,10},{... | collective-permute-start | bytes 442376 | tf_op jit(solution)/shard_map/ppermute | solution.py:26
  96.3 3.4 %collective-permute-start.15 = (bf16[144,512]{1,0:T(8,128)(2,1)S(1)}, bf16[144,512]{1,0:T(8,128)(2,1)S(1)}, u32[]{:S(2)}, u32[]{:S(2)}) collective-permute-start(bf16[144,512]{1,0:T(8,128)(2,1)S(1)} %get-tuple-element.16), channel_id=1, source_target_pairs={{0,8},{4,12},{8,0},{12,4},{1,9},{5,13},{9,1},{13,5},{2,10},{6,14},... | collective-permute-start | bytes 442376 | tf_op jit(solution)/shard_map/ppermute | solution.py:26
  99.7 0.0 collective-permute-start.16
  99.7 4.2 %collective-permute-done.14 = bf16[144,512]{1,0:T(8,128)(2,1)S(1)} collective-permute-done((bf16[144,512]{1,0:T(8,128)(2,1)S(1)}, bf16[144,512]{1,0:T(8,128)(2,1)S(1)}, u32[]{:S(2)}, u32[]{:S(2)}) %collective-permute-start.14) | collective-permute-done | bytes 147488 | tf_op jit(solution)/shard_map/ppermute | solution.py:26
  104.0 5.2 %collective-permute-done.15 = bf16[144,512]{1,0:T(8,128)(2,1)S(1)} collective-permute-done((bf16[144,512]{1,0:T(8,128)(2,1)S(1)}, bf16[144,512]{1,0:T(8,128)(2,1)S(1)}, u32[]{:S(2)}, u32[]{:S(2)}) %collective-permute-start.15) | collective-permute-done | bytes 147488 | tf_op jit(solution)/shard_map/ppermute | solution.py:26
  109.2 0.0 collective-permute-done.16
  109.3 0.1 convert_element_type.78
  109.3 0.1 collective-permute-start.17
  109.4 2.0 %collective-permute-done.17 = bf16[576,512]{1,0:T(8,128)(2,1)S(1)} collective-permute-done((bf16[576,512]{1,0:T(8,128)(2,1)S(1)}, bf16[576,512]{1,0:T(8,128)(2,1)S(1)}, u32[]{:S(2)}, u32[]{:S(2)}) %collective-permute-start.17) | collective-permute-done | bytes 589856 | tf_op jit(solution)/shard_map/ppermute | solution.py:26
  111.4 0.3 convert_select_fusion.1
  111.7 1.6 %pad_maximum_fusion = f32[1152,512]{1,0:T(8,128)} fusion(f32[576,512]{1,0:T(8,128)S(1)} %get-tuple-element.15, f32[576,512]{1,0:T(8,128)S(1)} %get-tuple-element.14), kind=kLoop, calls=%fused_computation.1 | loop fusion | flops 589824 | bytes 4718592 | tf_op jit(solution)/shard_map/concatenate | solution.py:277
  (10 shorter events, 0.1 us)
Async XLA Ops:
  1.7 19.2 %copy-start.3 = (bf16[256,1024]{1,0:T(8,128)(2,1)}, bf16[256,1024]{1,0:T(8,128)(2,1)S(1)}, u32[]{:S(2)}) copy-start(bf16[256,1024]{1,0:T(8,128)(2,1)S(1)} %pad_maximum_fusion.1.refs_8_) | copy-start | bytes 1572868
  1.7 17.2 %collective-permute-start = (bf16[256,1024]{1,0:T(8,128)(2,1)S(1)}, bf16[256,1024]{1,0:T(8,128)(2,1)S(1)}, u32[]{:S(2)}, u32[]{:S(2)}) collective-permute-start(bf16[256,1024]{1,0:T(8,128)(2,1)S(1)} %pad_maximum_fusion.1.refs_8_), channel_id=1, source_target_pairs={{0,4},{4,8},{8,12},{1,5},{5,9},{9,13},{2,6},{6,10},{10,14},{3,7},{... | collective-permute-start | bytes 1572872 | tf_op jit(solution)/shard_map/ppermute | solution.py:21
  6.7 13.9 %collective-permute-start.1 = (bf16[256,1024]{1,0:T(8,128)(2,1)S(1)}, bf16[256,1024]{1,0:T(8,128)(2,1)S(1)}, u32[]{:S(2)}, u32[]{:S(2)}) collective-permute-start(bf16[256,1024]{1,0:T(8,128)(2,1)S(1)} %pad_maximum_fusion.1.refs_8_), channel_id=1, source_target_pairs={{0,1},{2,3},{4,5},{6,7},{8,9},{10,11},{12,13},{14,15},{16,17},{18,... | collective-permute-start | bytes 1572872 | tf_op jit(solution)/shard_map/ppermute | solution.py:21
  8.2 12.4 %collective-permute-start.2 = (bf16[256,1024]{1,0:T(8,128)(2,1)S(1)}, bf16[256,1024]{1,0:T(8,128)(2,1)S(1)}, u32[]{:S(2)}, u32[]{:S(2)}) collective-permute-start(bf16[256,1024]{1,0:T(8,128)(2,1)S(1)} %pad_maximum_fusion.1.refs_8_), channel_id=1, source_target_pairs={{1,8},{5,12},{3,10},{7,14},{17,24},{21,28},{19,26},{23,30}} | collective-permute-start | bytes 1572872 | tf_op jit(solution)/shard_map/ppermute | solution.py:210
  19.0 1.9 %copy-start.4 = (bf16[256,1024]{1,0:T(8,128)(2,1)}, bf16[256,1024]{1,0:T(8,128)(2,1)S(1)}, u32[]{:S(2)}) copy-start(bf16[256,1024]{1,0:T(8,128)(2,1)S(1)} %collective-permute-done.refs_4_) | copy-start | bytes 1572868
  19.0 1.9 %collective-permute-start.3 = (bf16[256,1024]{1,0:T(8,128)(2,1)S(1)}, bf16[256,1024]{1,0:T(8,128)(2,1)S(1)}, u32[]{:S(2)}, u32[]{:S(2)}) collective-permute-start(bf16[256,1024]{1,0:T(8,128)(2,1)S(1)} %collective-permute-done.refs_4_), channel_id=1, source_target_pairs={{0,1},{1,0},{2,3},{3,2},{4,5},{5,4},{6,7},{7,6},{8,9},{9,8},{10,11... | collective-permute-start | bytes 1572872 | tf_op jit(solution)/shard_map/ppermute | solution.py:26
  20.6 0.8 copy-start.5
  20.6 1.0 copy-start.6
  20.9 0.8 copy-start.7
  30.6 8.4 %copy-start.1 = (bf16[1,256,2304]{2,1,0:T(8,128)(2,1)S(1)}, bf16[1,256,2304]{2,1,0:T(8,128)(2,1)}, u32[]{:S(2)}) copy-start(bf16[1,256,2304]{2,1,0:T(8,128)(2,1)} %param.6) | copy-start | bytes 3538948
  30.6 4.9 %collective-permute-start.6 = (bf16[256,1024]{1,0:T(8,128)(2,1)}, bf16[256,1024]{1,0:T(8,128)(2,1)S(1)}, u32[]{:S(2)}, u32[]{:S(2)}) collective-permute-start(bf16[256,1024]{1,0:T(8,128)(2,1)} %get-tuple-element.13), channel_id=1, source_target_pairs={{0,1},{1,0},{2,3},{3,2},{4,5},{5,4},{6,7},{7,6},{8,9},{9,8},{10,11... | collective-permute-start | bytes 1572872 | tf_op jit(solution)/shard_map/ppermute | solution.py:26
  33.4 7.2 %collective-permute-start.4 = (bf16[256,1024]{1,0:T(8,128)(2,1)}, bf16[256,1024]{1,0:T(8,128)(2,1)S(1)}, u32[]{:S(2)}, u32[]{:S(2)}) collective-permute-start(bf16[256,1024]{1,0:T(8,128)(2,1)} %get-tuple-element.11), channel_id=1, source_target_pairs={{1,0},{3,2},{5,4},{7,6},{9,8},{11,10},{13,12},{15,14},{17,16},{19,... | collective-permute-start | bytes 1572872 | tf_op jit(solution)/shard_map/ppermute | solution.py:21
  34.7 5.9 %collective-permute-start.5 = (bf16[256,1024]{1,0:T(8,128)(2,1)}, bf16[256,1024]{1,0:T(8,128)(2,1)S(1)}, u32[]{:S(2)}, u32[]{:S(2)}) collective-permute-start(bf16[256,1024]{1,0:T(8,128)(2,1)} %get-tuple-element.11), channel_id=1, source_target_pairs={{8,1},{12,5},{10,3},{14,7},{24,17},{28,21},{26,19},{30,23}} | collective-permute-start | bytes 1572872 | tf_op jit(solution)/shard_map/ppermute | solution.py:234
  37.6 23.1 %collective-permute-start.7 = (bf16[256,1024]{1,0:T(8,128)(2,1)}, bf16[256,1024]{1,0:T(8,128)(2,1)}, u32[]{:S(2)}, u32[]{:S(2)}) collective-permute-start(bf16[256,1024]{1,0:T(8,128)(2,1)} %add_convert_fusion.1), channel_id=1, source_target_pairs={{4,0},{8,4},{12,8},{5,1},{9,5},{13,9},{6,2},{10,6},{14,10},{7,3},{... | collective-permute-start | bytes 1572872 | tf_op jit(solution)/shard_map/ppermute | solution.py:21
  38.9 21.8 %copy-start.2 = (f32[256,1024]{1,0:T(8,128)S(1)}, f32[256,1024]{1,0:T(8,128)}, u32[]{:S(2)}) copy-start(f32[256,1024]{1,0:T(8,128)} %get-tuple-element.10) | copy-start | bytes 3145732
  39.1 25.4 %collective-permute-start.8 = (bf16[256,1152]{1,0:T(8,128)(2,1)S(1)}, bf16[256,1152]{1,0:T(8,128)(2,1)S(1)}, u32[]{:S(2)}, u32[]{:S(2)}) collective-permute-start(bf16[256,1152]{1,0:T(8,128)(2,1)S(1)} %get-tuple-element.22), channel_id=1, source_target_pairs={{0,2},{2,0},{1,3},{3,1},{4,6},{6,4},{5,7},{7,5},{8,10},{10,8},{9,1... | collective-permute-start | bytes 1769480 | tf_op jit(solution)/shard_map/ppermute | solution.py:26
  63.0 8.8 %collective-permute-start.9 = (bf16[256,512]{1,0:T(8,128)(2,1)S(1)}, bf16[256,512]{1,0:T(8,128)(2,1)S(1)}, u32[]{:S(2)}, u32[]{:S(2)}) collective-permute-start(bf16[256,512]{1,0:T(8,128)(2,1)S(1)} %get-tuple-element.23), channel_id=1, source_target_pairs={{0,2},{2,0},{1,3},{3,1},{4,6},{6,4},{5,7},{7,5},{8,10},{10,8},{9,1... | collective-permute-start | bytes 786440 | tf_op jit(solution)/shard_map/ppermute | solution.py:26
  72.6 1.4 %copy-start = (f32[1152,512]{1,0:T(8,128)}, f32[1152,512]{1,0:T(8,128)S(1)}, u32[]{:S(2)}) copy-start(f32[1152,512]{1,0:T(8,128)S(1)} %convolution_multiply_fusion) | copy-start | bytes 7077892
  74.1 2.1 %collective-permute-start.10 = (bf16[576,512]{1,0:T(8,128)(2,1)S(1)}, bf16[576,512]{1,0:T(8,128)(2,1)S(1)}, u32[]{:S(2)}, u32[]{:S(2)}) collective-permute-start(bf16[576,512]{1,0:T(8,128)(2,1)S(1)} %dynamic-slice_convert_fusion), channel_id=1, source_target_pairs={{0,1},{1,0},{2,3},{3,2},{4,5},{5,4},{6,7},{7,6},{8,9},{9,8},{10,11... | collective-permute-start | bytes 1769480 | tf_op jit(solution)/shard_map/ppermute | solution.py:26
  77.7 9.4 %collective-permute-start.11 = (bf16[144,512]{1,0:T(8,128)(2,1)S(1)}, bf16[144,512]{1,0:T(8,128)(2,1)S(1)}, u32[]{:S(2)}, u32[]{:S(2)}) collective-permute-start(bf16[144,512]{1,0:T(8,128)(2,1)S(1)} %get-tuple-element.18), channel_id=1, source_target_pairs={{0,4},{4,8},{8,12},{12,0},{1,5},{5,9},{9,13},{13,1},{2,6},{6,10},{... | collective-permute-start | bytes 442376 | tf_op jit(solution)/shard_map/ppermute | solution.py:26
  82.8 9.6 %collective-permute-start.12 = (bf16[144,512]{1,0:T(8,128)(2,1)S(1)}, bf16[144,512]{1,0:T(8,128)(2,1)S(1)}, u32[]{:S(2)}, u32[]{:S(2)}) collective-permute-start(bf16[144,512]{1,0:T(8,128)(2,1)S(1)} %get-tuple-element.20), channel_id=1, source_target_pairs={{0,8},{4,12},{8,0},{12,4},{1,9},{5,13},{9,1},{13,5},{2,10},{6,14},... | collective-permute-start | bytes 442376 | tf_op jit(solution)/shard_map/ppermute | solution.py:26
  82.9 9.8 %collective-permute-start.13 = (bf16[144,512]{1,0:T(8,128)(2,1)S(1)}, bf16[144,512]{1,0:T(8,128)(2,1)S(1)}, u32[]{:S(2)}, u32[]{:S(2)}) collective-permute-start(bf16[144,512]{1,0:T(8,128)(2,1)S(1)} %get-tuple-element.19), channel_id=1, source_target_pairs={{0,12},{4,0},{8,4},{12,8},{1,13},{5,1},{9,5},{13,9},{2,14},{6,2},{... | collective-permute-start | bytes 442376 | tf_op jit(solution)/shard_map/ppermute | solution.py:26
  92.8 11.1 %collective-permute-start.14 = (bf16[144,512]{1,0:T(8,128)(2,1)S(1)}, bf16[144,512]{1,0:T(8,128)(2,1)S(1)}, u32[]{:S(2)}, u32[]{:S(2)}) collective-permute-start(bf16[144,512]{1,0:T(8,128)(2,1)S(1)} %get-tuple-element.16), channel_id=1, source_target_pairs={{0,4},{4,8},{8,12},{12,0},{1,5},{5,9},{9,13},{13,1},{2,6},{6,10},{... | collective-permute-start | bytes 442376 | tf_op jit(solution)/shard_map/ppermute | solution.py:26
  96.3 12.9 %collective-permute-start.15 = (bf16[144,512]{1,0:T(8,128)(2,1)S(1)}, bf16[144,512]{1,0:T(8,128)(2,1)S(1)}, u32[]{:S(2)}, u32[]{:S(2)}) collective-permute-start(bf16[144,512]{1,0:T(8,128)(2,1)S(1)} %get-tuple-element.16), channel_id=1, source_target_pairs={{0,8},{4,12},{8,0},{12,4},{1,9},{5,13},{9,1},{13,5},{2,10},{6,14},... | collective-permute-start | bytes 442376 | tf_op jit(solution)/shard_map/ppermute | solution.py:26
  99.7 9.5 %collective-permute-start.16 = (bf16[144,512]{1,0:T(8,128)(2,1)S(1)}, bf16[144,512]{1,0:T(8,128)(2,1)S(1)}, u32[]{:S(2)}, u32[]{:S(2)}) collective-permute-start(bf16[144,512]{1,0:T(8,128)(2,1)S(1)} %get-tuple-element.16), channel_id=1, source_target_pairs={{0,12},{4,0},{8,4},{12,8},{1,13},{5,1},{9,5},{13,9},{2,14},{6,2},{... | collective-permute-start | bytes 442376 | tf_op jit(solution)/shard_map/ppermute | solution.py:26
  109.3 2.1 %collective-permute-start.17 = (bf16[576,512]{1,0:T(8,128)(2,1)S(1)}, bf16[576,512]{1,0:T(8,128)(2,1)S(1)}, u32[]{:S(2)}, u32[]{:S(2)}) collective-permute-start(bf16[576,512]{1,0:T(8,128)(2,1)S(1)} %convert_element_type.78), channel_id=1, source_target_pairs={{0,1},{1,0},{2,3},{3,2},{4,5},{5,4},{6,7},{7,6},{8,9},{9,8},{10,11... | collective-permute-start | bytes 1769480 | tf_op jit(solution)/shard_map/ppermute | solution.py:26

commit v13 on v7

--- a/solution.py
+++ b/solution.py
@@ -78,9 +78,9 @@
     scale = HEAD_DIM ** (-0.5)
     kv_width = kv_heads * HEAD_DIM
     per_group = heads // kv_heads
-    col = lax.broadcasted_iota(jnp.int32, (rows, keys), 1)
-    row = lax.broadcasted_iota(jnp.int32, (rows, keys), 0)
-    allowed = (col >= lo_ref[...]) & (col <= row + margin)
+    query_at = lax.broadcasted_iota(jnp.int32, (keys, rows), 1)
+    key_at = lax.broadcasted_iota(jnp.int32, (keys, rows), 0)
+    allowed = (key_at >= lo_ref[...]) & (key_at <= query_at + margin)
     for group in range(kv_heads):
         k_cols = pl.ds(group * HEAD_DIM, HEAD_DIM)
         v_cols = pl.ds(kv_width + group * HEAD_DIM, HEAD_DIM)
@@ -92,20 +92,20 @@
             q_cols = pl.ds((group * per_group + member) * HEAD_DIM, HEAD_DIM)
             query_h = q_ref[:, q_cols]
             grad_h = do_ref[:, q_cols]
-            scores = lax.dot_general(query_h, key_g, NT, preferred_element_type=jnp.float32) * scale
+            scores = lax.dot_general(key_g, query_h, NT, preferred_element_type=jnp.float32) * scale
             scores = jnp.where(allowed, scores, -1e30)
-            largest = jnp.max(scores, axis=1, keepdims=True)
+            largest = jnp.max(scores, axis=0, keepdims=True)
             raised = jnp.exp(scores - largest)
-            probs = raised * (1.0 / jnp.sum(raised, axis=1, keepdims=True))
-            grad_probs = lax.dot_general(grad_h, value_g, NT, preferred_element_type=jnp.float32)
-            row_dot = jnp.sum(probs * grad_probs, axis=1, keepdims=True)
+            probs = raised * (1.0 / jnp.sum(raised, axis=0, keepdims=True))
+            grad_probs = lax.dot_general(value_g, grad_h, NT, preferred_element_type=jnp.float32)
+            row_dot = jnp.sum(probs * grad_probs, axis=0, keepdims=True)
             grad_scores = (probs * (grad_probs - row_dot) * scale).astype(jnp.bfloat16)
             probs_low = probs.astype(jnp.bfloat16)
-            dq_ref[:, q_cols] = jnp.dot(
-                grad_scores, key_g, preferred_element_type=jnp.float32
+            dq_ref[:, q_cols] = lax.dot_general(
+                grad_scores, key_g, TN, preferred_element_type=jnp.float32
             ).astype(dq_ref.dtype)
-            term_k = lax.dot_general(grad_scores, query_h, TN, preferred_element_type=jnp.float32)
-            term_v = lax.dot_general(probs_low, grad_h, TN, preferred_element_type=jnp.float32)
+            term_k = jnp.dot(grad_scores, query_h, preferred_element_type=jnp.float32)
+            term_v = jnp.dot(probs_low, grad_h, preferred_element_type=jnp.float32)
             grad_k = term_k if grad_k is None else grad_k + term_k
             grad_v = term_v if grad_v is None else grad_v + term_v
         dkv_ref[:, k_cols] = grad_k
@@ -197,7 +197,7 @@
     own_kv = jnp.concatenate([key_heads[0], value_heads[0]], axis=1)
     query_pos = first_row + jnp.arange(block_rows, dtype=jnp.int32)
     lowest = jnp.maximum(doc_start_of(doc_starts[0], query_pos), query_pos - window + 1)
-    lo_rel = (lowest - first_row + margin).astype(jnp.int32)[:, None]
+    lo_rel = (lowest - first_row + margin).astype(jnp.int32)[None, :]
     sub_count = lax.axis_size("sub")
     sub_at = lax.axis_index("sub")
     flag = jnp.reshape(sub_at, (1,)).astype(jnp.int32)

time: 113 us -> 114 us (level)
  no operation moved by 1% of the time
where the time goes in v13:
time: 114 us; the launch traced here: 112 us
  waiting for transfers between devices  59.7 us (52%)
  starting transfers between devices  30 us (26%)
  Pallas kernels  9.19 us (8%)
  other arithmetic  7.09 us (6%)
  local copies, waits for them, and re-layouts  4.69 us (4%)
    ppermute x12, waiting for transfers between devices, rotated(): lax.ppermute(value, axis, [(source, (source + steps) % count) for source...  30.8 us
    ppermute x4, waiting for transfers between devices, passed_along(): lax.ppermute(value, axis, [(source, source + steps) for source in range(f...  28.9 us
    ppermute x12, starting transfers between devices, rotated(): lax.ppermute(value, axis, [(source, (source + steps) % count) for source...  19 us
    pallas_call x1, Pallas kernels, attention(): pl.pallas_call(kernel, out_shape=(jax.ShapeDtypeStruct((rows, width), jnp...  9.19 us
    ppermute x4, starting transfers between devices, passed_along(): lax.ppermute(value, axis, [(source, source + steps) for source in range(f...  8.84 us
  transfers between devices with their start and end apart: 18, of which 11 were waited for; matrix products, arithmetic and copies ran while one was open for 3% of the time, Pallas kernels for 0%

profile of v13, /device:TPU:0, one launch (start us, length us, event | category | flops | bytes accessed | tf_op | source)
XLA Modules:
  0.0 112.4 jit_solution(10564238358201935197)
XLA Ops:
  0.6 1.1 pad_maximum_fusion.1.refs_8_
  1.7 0.0 copy-start.2
  1.7 5.0 %collective-permute-start = (bf16[256,1024]{1,0:T(8,128)(2,1)S(1)}, bf16[256,1024]{1,0:T(8,128)(2,1)S(1)}, u32[]{:S(2)}, u32[]{:S(2)}) collective-permute-start(bf16[256,1024]{1,0:T(8,128)(2,1)S(1)} %pad_maximum_fusion.1.refs_8_), channel_id=1, source_target_pairs={{0,4},{4,8},{8,12},{1,5},{5,9},{9,13},{2,6},{6,10},{10,14},{3,7},{... | collective-permute-start | bytes 1572872 | tf_op jit(solution)/shard_map/ppermute | solution.py:21
  6.7 0.0 copy-start.3
  6.7 1.3 %dynamic-slice_bitcast_fusion = (bf16[256,1152]{1,0:T(8,128)(2,1)S(1)}, bf16[256,1152]{1,0:T(8,128)(2,1)S(1)}) fusion(bf16[1,256,2304]{2,1,0:T(8,128)(2,1)} %param.6, s32[]{:T(128)S(6)} %select_n.89, s32[]{:T(128)S(6)} %select_n.87), kind=kLoop, calls=%fused_computation.11 | loop fusion | bytes 2359304 | tf_op jit(solution)/shard_map/dynamic_slice | solution.py:191
  8.1 1.6 %collective-permute-start.4 = (bf16[256,1152]{1,0:T(8,128)(2,1)S(1)}, bf16[256,1152]{1,0:T(8,128)(2,1)S(1)}, u32[]{:S(2)}, u32[]{:S(2)}) collective-permute-start(bf16[256,1152]{1,0:T(8,128)(2,1)S(1)} %get-tuple-element.22), channel_id=1, source_target_pairs={{0,2},{2,0},{1,3},{3,1},{4,6},{6,4},{5,7},{7,5},{8,10},{10,8},{9,1... | collective-permute-start | bytes 1769480 | tf_op jit(solution)/shard_map/ppermute | solution.py:26
  9.6 1.3 %collective-permute-start.1 = (bf16[256,1024]{1,0:T(8,128)(2,1)S(1)}, bf16[256,1024]{1,0:T(8,128)(2,1)S(1)}, u32[]{:S(2)}, u32[]{:S(2)}) collective-permute-start(bf16[256,1024]{1,0:T(8,128)(2,1)S(1)} %pad_maximum_fusion.1.refs_8_), channel_id=1, source_target_pairs={{0,1},{2,3},{4,5},{6,7},{8,9},{10,11},{12,13},{14,15},{16,17},{18,... | collective-permute-start | bytes 1572872 | tf_op jit(solution)/shard_map/ppermute | solution.py:21
  10.9 0.0 copy-done.2
  11.0 1.5 %collective-permute-start.2 = (bf16[256,1024]{1,0:T(8,128)(2,1)S(1)}, bf16[256,1024]{1,0:T(8,128)(2,1)}, u32[]{:S(2)}, u32[]{:S(2)}) collective-permute-start(bf16[256,1024]{1,0:T(8,128)(2,1)S(1)} %pad_maximum_fusion.1.refs_8_), channel_id=1, source_target_pairs={{1,8},{5,12},{3,10},{7,14},{17,24},{21,28},{19,26},{23,30}} | collective-permute-start | bytes 1572872 | tf_op jit(solution)/shard_map/ppermute | solution.py:210
  12.4 6.5 %collective-permute-done.refs_4_ = bf16[256,1024]{1,0:T(8,128)(2,1)S(1)} collective-permute-done((bf16[256,1024]{1,0:T(8,128)(2,1)S(1)}, bf16[256,1024]{1,0:T(8,128)(2,1)S(1)}, u32[]{:S(2)}, u32[]{:S(2)}) %collective-permute-start) | collective-permute-done | bytes 524320 | tf_op jit(solution)/shard_map/ppermute | solution.py:21
  19.0 0.0 collective-permute-start.3
  19.0 0.0 copy-done.3
  19.0 0.1 select_reduce_fusion
  19.1 0.6 subtract_add_fusion.refs_1_
  19.7 0.0 collective-permute-done.1.refs_5_
  19.7 0.0 collective-permute-done.2.refs_6_
  19.7 3.2 %collective-permute-done.4.refs_9_ = bf16[256,1152]{1,0:T(8,128)(2,1)S(1)} collective-permute-done((bf16[256,1152]{1,0:T(8,128)(2,1)S(1)}, bf16[256,1152]{1,0:T(8,128)(2,1)S(1)}, u32[]{:S(2)}, u32[]{:S(2)}) %collective-permute-start.4) | collective-permute-done | bytes 589856 | tf_op jit(solution)/shard_map/ppermute | solution.py:26
  22.9 0.0 collective-permute-done.3.refs_7_
  22.9 0.0 copy-done.6
  22.9 0.0 copy-done.7
  22.9 0.8 copy-done.4
  23.7 9.2 %shard_map.93 = (bf16[256,1024]{1,0:T(8,128)(2,1)}, bf16[256,1024]{1,0:T(8,128)(2,1)}, bf16[256,1024]{1,0:T(8,128)(2,1)}, f32[256,1024]{1,0:T(8,128)}, f32[256,1024]{1,0:T(8,128)}) custom-call(s32[1]{0:T(128)} %bitcast.refs_0_, s32[1,256]{1,0:T(1,128)} %subtract_add_fusion.refs_1_, bf16[256,1024]{1,0:T(8,128)(2,1)} %bitcast.20, bf16[256,1024]{1,0:T(8,128)(2,1)} %bitcast.21, ...), custom_call_target="tpu_custom_call" | custom-call | flops 2684354560 | bytes 7864320 | tf_op jit(solution)/shard_map/pallas_call | solution.py:160
  32.9 0.7 collective-permute-start.7
  33.7 1.3 %collective-permute-start.5 = (bf16[256,1024]{1,0:T(8,128)(2,1)}, bf16[256,1024]{1,0:T(8,128)(2,1)S(1)}, u32[]{:S(2)}, u32[]{:S(2)}) collective-permute-start(bf16[256,1024]{1,0:T(8,128)(2,1)} %get-tuple-element.11), channel_id=1, source_target_pairs={{1,0},{3,2},{5,4},{7,6},{9,8},{11,10},{13,12},{15,14},{17,16},{19,... | collective-permute-start | bytes 1572872 | tf_op jit(solution)/shard_map/ppermute | solution.py:21
  35.0 0.7 collective-permute-start.6
  35.7 0.0 collective-permute-done.7
  35.7 1.4 %add_convert_fusion.1 = bf16[256,1024]{1,0:T(8,128)(2,1)S(1)} fusion(f32[256,1024]{1,0:T(8,128)} %get-tuple-element.12, bf16[256,1024]{1,0:T(8,128)(2,1)S(1)} %collective-permute-done.7), kind=kLoop, calls=%fused_computation.10 | loop fusion | flops 786432 | bytes 2097152 | tf_op jit(solution)/shard_map/convert_element_type | solution.py:229
  37.0 1.3 %collective-permute-start.8 = (bf16[256,1024]{1,0:T(8,128)(2,1)S(1)}, bf16[256,1024]{1,0:T(8,128)(2,1)S(1)}, u32[]{:S(2)}, u32[]{:S(2)}) collective-permute-start(bf16[256,1024]{1,0:T(8,128)(2,1)S(1)} %add_convert_fusion.1), channel_id=1, source_target_pairs={{4,0},{8,4},{12,8},{5,1},{9,5},{13,9},{6,2},{10,6},{14,10},{7,3},{... | collective-permute-start | bytes 1572872 | tf_op jit(solution)/shard_map/ppermute | solution.py:21
  38.3 0.0 collective-permute-done.5
  38.4 0.0 collective-permute-done.6
  38.4 22.4 %collective-permute-done.8 = bf16[256,1024]{1,0:T(8,128)(2,1)S(1)} collective-permute-done((bf16[256,1024]{1,0:T(8,128)(2,1)S(1)}, bf16[256,1024]{1,0:T(8,128)(2,1)S(1)}, u32[]{:S(2)}, u32[]{:S(2)}) %collective-permute-start.8) | collective-permute-done | bytes 524320 | tf_op jit(solution)/shard_map/ppermute | solution.py:21
  60.7 0.0 copy-done.1
  60.7 0.3 add_convert_fusion
  61.1 0.0 copy-start.5
  61.1 0.9 fusion.9
  61.9 1.5 %collective-permute-start.9 = (bf16[256,512]{1,0:T(8,128)(2,1)S(1)}, bf16[256,512]{1,0:T(8,128)(2,1)S(1)}, u32[]{:S(2)}, u32[]{:S(2)}) collective-permute-start(bf16[256,512]{1,0:T(8,128)(2,1)S(1)} %get-tuple-element.23), channel_id=1, source_target_pairs={{0,2},{2,0},{1,3},{3,1},{4,6},{6,4},{5,7},{7,5},{8,10},{10,8},{9,1... | collective-permute-start | bytes 786440 | tf_op jit(solution)/shard_map/ppermute | solution.py:26
  63.4 6.8 %collective-permute-done.9 = bf16[256,512]{1,0:T(8,128)(2,1)S(1)} collective-permute-done((bf16[256,512]{1,0:T(8,128)(2,1)S(1)}, bf16[256,512]{1,0:T(8,128)(2,1)S(1)}, u32[]{:S(2)}, u32[]{:S(2)}) %collective-permute-start.9) | collective-permute-done | bytes 262176 | tf_op jit(solution)/shard_map/ppermute | solution.py:26
  70.2 0.8 convolution_multiply_fusion
  71.1 0.0 copy-start
  71.1 1.4 %copy-done = f32[1152,512]{1,0:T(8,128)} copy-done((f32[1152,512]{1,0:T(8,128)}, f32[1152,512]{1,0:T(8,128)S(1)}, u32[]{:S(2)}) %copy-start) | copy-done | bytes 2359320
  72.5 0.1 dynamic-slice_convert_fusion
  72.5 0.1 collective-permute-start.10
  72.7 1.9 %collective-permute-done.10 = bf16[576,512]{1,0:T(8,128)(2,1)S(1)} collective-permute-done((bf16[576,512]{1,0:T(8,128)(2,1)S(1)}, bf16[576,512]{1,0:T(8,128)(2,1)S(1)}, u32[]{:S(2)}, u32[]{:S(2)}) %collective-permute-start.10) | collective-permute-done | bytes 589856 | tf_op jit(solution)/shard_map/ppermute | solution.py:26
  74.6 1.4 %convert_add_fusion = f32[576,512]{1,0:T(8,128)S(1)} fusion(bf16[576,512]{1,0:T(8,128)(2,1)S(1)} %collective-permute-done.10, f32[1152,512]{1,0:T(8,128)} %copy-done, s32[]{:T(128)S(6)} %select_n.90), kind=kLoop, calls=%fused_computation.7 | loop fusion | flops 589824 | bytes 2949124 | tf_op jit(solution)/shard_map/add | solution.py:271
  76.1 0.1 dynamic-slice_convert_fusion.3
  76.1 5.8 %collective-permute-start.11 = (bf16[144,512]{1,0:T(8,128)(2,1)S(1)}, bf16[144,512]{1,0:T(8,128)(2,1)S(1)}, u32[]{:S(2)}, u32[]{:S(2)}) collective-permute-start(bf16[144,512]{1,0:T(8,128)(2,1)S(1)} %get-tuple-element.18), channel_id=1, source_target_pairs={{0,4},{4,8},{8,12},{12,0},{1,5},{5,9},{9,13},{13,1},{2,6},{6,10},{... | collective-permute-start | bytes 442376 | tf_op jit(solution)/shard_map/ppermute | solution.py:26
  81.9 0.0 collective-permute-start.12
  81.9 2.4 %collective-permute-start.13 = (bf16[144,512]{1,0:T(8,128)(2,1)S(1)}, bf16[144,512]{1,0:T(8,128)(2,1)S(1)}, u32[]{:S(2)}, u32[]{:S(2)}) collective-permute-start(bf16[144,512]{1,0:T(8,128)(2,1)S(1)} %get-tuple-element.19), channel_id=1, source_target_pairs={{0,12},{4,0},{8,4},{12,8},{1,13},{5,1},{9,5},{13,9},{2,14},{6,2},{... | collective-permute-start | bytes 442376 | tf_op jit(solution)/shard_map/ppermute | solution.py:26
  84.4 1.8 %collective-permute-done.11 = bf16[144,512]{1,0:T(8,128)(2,1)S(1)} collective-permute-done((bf16[144,512]{1,0:T(8,128)(2,1)S(1)}, bf16[144,512]{1,0:T(8,128)(2,1)S(1)}, u32[]{:S(2)}, u32[]{:S(2)}) %collective-permute-start.11) | collective-permute-done | bytes 147488 | tf_op jit(solution)/shard_map/ppermute | solution.py:26
  86.1 5.3 %collective-permute-done.12 = bf16[144,512]{1,0:T(8,128)(2,1)S(1)} collective-permute-done((bf16[144,512]{1,0:T(8,128)(2,1)S(1)}, bf16[144,512]{1,0:T(8,128)(2,1)S(1)}, u32[]{:S(2)}, u32[]{:S(2)}) %collective-permute-start.12) | collective-permute-done | bytes 147488 | tf_op jit(solution)/shard_map/ppermute | solution.py:26
  91.5 0.2 collective-permute-done.13
  91.7 0.1 broadcast_in_dim.28
  91.8 0.1 fusion.6
  91.9 3.5 %collective-permute-start.14 = (bf16[144,512]{1,0:T(8,128)(2,1)S(1)}, bf16[144,512]{1,0:T(8,128)(2,1)S(1)}, u32[]{:S(2)}, u32[]{:S(2)}) collective-permute-start(bf16[144,512]{1,0:T(8,128)(2,1)S(1)} %get-tuple-element.16), channel_id=1, source_target_pairs={{0,4},{4,8},{8,12},{12,0},{1,5},{5,9},{9,13},{13,1},{2,6},{6,10},{... | collective-permute-start | bytes 442376 | tf_op jit(solution)/shard_map/ppermute | solution.py:26
  95.4 3.4 %collective-permute-start.15 = (bf16[144,512]{1,0:T(8,128)(2,1)S(1)}, bf16[144,512]{1,0:T(8,128)(2,1)S(1)}, u32[]{:S(2)}, u32[]{:S(2)}) collective-permute-start(bf16[144,512]{1,0:T(8,128)(2,1)S(1)} %get-tuple-element.16), channel_id=1, source_target_pairs={{0,8},{4,12},{8,0},{12,4},{1,9},{5,13},{9,1},{13,5},{2,10},{6,14},... | collective-permute-start | bytes 442376 | tf_op jit(solution)/shard_map/ppermute | solution.py:26
  98.8 0.0 collective-permute-start.16
  98.8 4.2 %collective-permute-done.14 = bf16[144,512]{1,0:T(8,128)(2,1)S(1)} collective-permute-done((bf16[144,512]{1,0:T(8,128)(2,1)S(1)}, bf16[144,512]{1,0:T(8,128)(2,1)S(1)}, u32[]{:S(2)}, u32[]{:S(2)}) %collective-permute-start.14) | collective-permute-done | bytes 147488 | tf_op jit(solution)/shard_map/ppermute | solution.py:26
  103.0 5.2 %collective-permute-done.15 = bf16[144,512]{1,0:T(8,128)(2,1)S(1)} collective-permute-done((bf16[144,512]{1,0:T(8,128)(2,1)S(1)}, bf16[144,512]{1,0:T(8,128)(2,1)S(1)}, u32[]{:S(2)}, u32[]{:S(2)}) %collective-permute-start.15) | collective-permute-done | bytes 147488 | tf_op jit(solution)/shard_map/ppermute | solution.py:26
  108.3 0.0 collective-permute-done.16
  108.3 0.1 convert_element_type.78
  108.4 0.1 collective-permute-start.17
  108.5 2.0 %collective-permute-done.17 = bf16[576,512]{1,0:T(8,128)(2,1)S(1)} collective-permute-done((bf16[576,512]{1,0:T(8,128)(2,1)S(1)}, bf16[576,512]{1,0:T(8,128)(2,1)S(1)}, u32[]{:S(2)}, u32[]{:S(2)}) %collective-permute-start.17) | collective-permute-done | bytes 589856 | tf_op jit(solution)/shard_map/ppermute | solution.py:26
  110.5 0.3 convert_select_fusion.1
  110.8 1.6 %pad_maximum_fusion = f32[1152,512]{1,0:T(8,128)} fusion(f32[576,512]{1,0:T(8,128)S(1)} %get-tuple-element.15, f32[576,512]{1,0:T(8,128)S(1)} %get-tuple-element.14), kind=kLoop, calls=%fused_computation.1 | loop fusion | flops 589824 | bytes 4718592 | tf_op jit(solution)/shard_map/concatenate | solution.py:277
  (9 shorter events, 0.1 us)
Async XLA Ops:
  1.7 9.2 %copy-start.2 = (bf16[256,1024]{1,0:T(8,128)(2,1)}, bf16[256,1024]{1,0:T(8,128)(2,1)S(1)}, u32[]{:S(2)}) copy-start(bf16[256,1024]{1,0:T(8,128)(2,1)S(1)} %pad_maximum_fusion.1.refs_8_) | copy-start | bytes 1572868
  1.7 17.2 %collective-permute-start = (bf16[256,1024]{1,0:T(8,128)(2,1)S(1)}, bf16[256,1024]{1,0:T(8,128)(2,1)S(1)}, u32[]{:S(2)}, u32[]{:S(2)}) collective-permute-start(bf16[256,1024]{1,0:T(8,128)(2,1)S(1)} %pad_maximum_fusion.1.refs_8_), channel_id=1, source_target_pairs={{0,4},{4,8},{8,12},{1,5},{5,9},{9,13},{2,6},{6,10},{10,14},{3,7},{... | collective-permute-start | bytes 1572872 | tf_op jit(solution)/shard_map/ppermute | solution.py:21
  6.7 12.3 %copy-start.3 = (s32[1,12]{1,0:T(1,128)S(1)}, s32[1,12]{1,0:T(1,128)}, u32[]{:S(2)}) copy-start(s32[1,12]{1,0:T(1,128)} %param.11) | copy-start | bytes 148
  8.1 14.9 %collective-permute-start.4 = (bf16[256,1152]{1,0:T(8,128)(2,1)S(1)}, bf16[256,1152]{1,0:T(8,128)(2,1)S(1)}, u32[]{:S(2)}, u32[]{:S(2)}) collective-permute-start(bf16[256,1152]{1,0:T(8,128)(2,1)S(1)} %get-tuple-element.22), channel_id=1, source_target_pairs={{0,2},{2,0},{1,3},{3,1},{4,6},{6,4},{5,7},{7,5},{8,10},{10,8},{9,1... | collective-permute-start | bytes 1769480 | tf_op jit(solution)/shard_map/ppermute | solution.py:26
  9.6 10.1 %collective-permute-start.1 = (bf16[256,1024]{1,0:T(8,128)(2,1)S(1)}, bf16[256,1024]{1,0:T(8,128)(2,1)S(1)}, u32[]{:S(2)}, u32[]{:S(2)}) collective-permute-start(bf16[256,1024]{1,0:T(8,128)(2,1)S(1)} %pad_maximum_fusion.1.refs_8_), channel_id=1, source_target_pairs={{0,1},{2,3},{4,5},{6,7},{8,9},{10,11},{12,13},{14,15},{16,17},{18,... | collective-permute-start | bytes 1572872 | tf_op jit(solution)/shard_map/ppermute | solution.py:21
  11.0 8.8 %collective-permute-start.2 = (bf16[256,1024]{1,0:T(8,128)(2,1)S(1)}, bf16[256,1024]{1,0:T(8,128)(2,1)}, u32[]{:S(2)}, u32[]{:S(2)}) collective-permute-start(bf16[256,1024]{1,0:T(8,128)(2,1)S(1)} %pad_maximum_fusion.1.refs_8_), channel_id=1, source_target_pairs={{1,8},{5,12},{3,10},{7,14},{17,24},{21,28},{19,26},{23,30}} | collective-permute-start | bytes 1572872 | tf_op jit(solution)/shard_map/ppermute | solution.py:210
  19.0 4.0 %copy-start.6 = (bf16[256,1024]{1,0:T(8,128)(2,1)}, bf16[256,1024]{1,0:T(8,128)(2,1)S(1)}, u32[]{:S(2)}) copy-start(bf16[256,1024]{1,0:T(8,128)(2,1)S(1)} %collective-permute-done.refs_4_) | copy-start | bytes 1572868
  19.0 4.0 %collective-permute-start.3 = (bf16[256,1024]{1,0:T(8,128)(2,1)S(1)}, bf16[256,1024]{1,0:T(8,128)(2,1)}, u32[]{:S(2)}, u32[]{:S(2)}) collective-permute-start(bf16[256,1024]{1,0:T(8,128)(2,1)S(1)} %collective-permute-done.refs_4_), channel_id=1, source_target_pairs={{0,1},{1,0},{2,3},{3,2},{4,5},{5,4},{6,7},{7,6},{8,9},{9,8},{10,11... | collective-permute-start | bytes 1572872 | tf_op jit(solution)/shard_map/ppermute | solution.py:26
  19.7 3.2 %copy-start.7 = (bf16[256,1024]{1,0:T(8,128)(2,1)}, bf16[256,1024]{1,0:T(8,128)(2,1)S(1)}, u32[]{:S(2)}) copy-start(bf16[256,1024]{1,0:T(8,128)(2,1)S(1)} %collective-permute-done.1.refs_5_) | copy-start | bytes 1572868
  22.9 0.8 copy-start.4
  32.9 27.8 %copy-start.1 = (f32[256,1024]{1,0:T(8,128)S(1)}, f32[256,1024]{1,0:T(8,128)}, u32[]{:S(2)}) copy-start(f32[256,1024]{1,0:T(8,128)} %get-tuple-element.10) | copy-start | bytes 3145732
  32.9 2.7 %collective-permute-start.7 = (bf16[256,1024]{1,0:T(8,128)(2,1)}, bf16[256,1024]{1,0:T(8,128)(2,1)S(1)}, u32[]{:S(2)}, u32[]{:S(2)}) collective-permute-start(bf16[256,1024]{1,0:T(8,128)(2,1)} %get-tuple-element.13), channel_id=1, source_target_pairs={{0,1},{1,0},{2,3},{3,2},{4,5},{5,4},{6,7},{7,6},{8,9},{9,8},{10,11... | collective-permute-start | bytes 1572872 | tf_op jit(solution)/shard_map/ppermute | solution.py:26
  33.7 4.7 %collective-permute-start.5 = (bf16[256,1024]{1,0:T(8,128)(2,1)}, bf16[256,1024]{1,0:T(8,128)(2,1)S(1)}, u32[]{:S(2)}, u32[]{:S(2)}) collective-permute-start(bf16[256,1024]{1,0:T(8,128)(2,1)} %get-tuple-element.11), channel_id=1, source_target_pairs={{1,0},{3,2},{5,4},{7,6},{9,8},{11,10},{13,12},{15,14},{17,16},{19,... | collective-permute-start | bytes 1572872 | tf_op jit(solution)/shard_map/ppermute | solution.py:21
  35.0 3.4 %collective-permute-start.6 = (bf16[256,1024]{1,0:T(8,128)(2,1)}, bf16[256,1024]{1,0:T(8,128)(2,1)S(1)}, u32[]{:S(2)}, u32[]{:S(2)}) collective-permute-start(bf16[256,1024]{1,0:T(8,128)(2,1)} %get-tuple-element.11), channel_id=1, source_target_pairs={{8,1},{12,5},{10,3},{14,7},{24,17},{28,21},{26,19},{30,23}} | collective-permute-start | bytes 1572872 | tf_op jit(solution)/shard_map/ppermute | solution.py:234
  37.0 23.7 %collective-permute-start.8 = (bf16[256,1024]{1,0:T(8,128)(2,1)S(1)}, bf16[256,1024]{1,0:T(8,128)(2,1)S(1)}, u32[]{:S(2)}, u32[]{:S(2)}) collective-permute-start(bf16[256,1024]{1,0:T(8,128)(2,1)S(1)} %add_convert_fusion.1), channel_id=1, source_target_pairs={{4,0},{8,4},{12,8},{5,1},{9,5},{13,9},{6,2},{10,6},{14,10},{7,3},{... | collective-permute-start | bytes 1572872 | tf_op jit(solution)/shard_map/ppermute | solution.py:21
  61.1 9.2 %copy-start.5 = (bf16[256,1152]{1,0:T(8,128)(2,1)S(1)}, bf16[256,1152]{1,0:T(8,128)(2,1)}, u32[]{:S(2)}) copy-start(bf16[256,1152]{1,0:T(8,128)(2,1)} %copy-done.4) | copy-start | bytes 1769476
  61.9 8.3 %collective-permute-start.9 = (bf16[256,512]{1,0:T(8,128)(2,1)S(1)}, bf16[256,512]{1,0:T(8,128)(2,1)S(1)}, u32[]{:S(2)}, u32[]{:S(2)}) collective-permute-start(bf16[256,512]{1,0:T(8,128)(2,1)S(1)} %get-tuple-element.23), channel_id=1, source_target_pairs={{0,2},{2,0},{1,3},{3,1},{4,6},{6,4},{5,7},{7,5},{8,10},{10,8},{9,1... | collective-permute-start | bytes 786440 | tf_op jit(solution)/shard_map/ppermute | solution.py:26
  71.1 1.4 %copy-start = (f32[1152,512]{1,0:T(8,128)}, f32[1152,512]{1,0:T(8,128)S(1)}, u32[]{:S(2)}) copy-start(f32[1152,512]{1,0:T(8,128)S(1)} %convolution_multiply_fusion) | copy-start | bytes 7077892
  72.5 2.1 %collective-permute-start.10 = (bf16[576,512]{1,0:T(8,128)(2,1)S(1)}, bf16[576,512]{1,0:T(8,128)(2,1)S(1)}, u32[]{:S(2)}, u32[]{:S(2)}) collective-permute-start(bf16[576,512]{1,0:T(8,128)(2,1)S(1)} %dynamic-slice_convert_fusion), channel_id=1, source_target_pairs={{0,1},{1,0},{2,3},{3,2},{4,5},{5,4},{6,7},{7,6},{8,9},{9,8},{10,11... | collective-permute-start | bytes 1769480 | tf_op jit(solution)/shard_map/ppermute | solution.py:26
  76.1 10.0 %collective-permute-start.11 = (bf16[144,512]{1,0:T(8,128)(2,1)S(1)}, bf16[144,512]{1,0:T(8,128)(2,1)S(1)}, u32[]{:S(2)}, u32[]{:S(2)}) collective-permute-start(bf16[144,512]{1,0:T(8,128)(2,1)S(1)} %get-tuple-element.18), channel_id=1, source_target_pairs={{0,4},{4,8},{8,12},{12,0},{1,5},{5,9},{9,13},{13,1},{2,6},{6,10},{... | collective-permute-start | bytes 442376 | tf_op jit(solution)/shard_map/ppermute | solution.py:26
  81.9 9.6 %collective-permute-start.12 = (bf16[144,512]{1,0:T(8,128)(2,1)S(1)}, bf16[144,512]{1,0:T(8,128)(2,1)S(1)}, u32[]{:S(2)}, u32[]{:S(2)}) collective-permute-start(bf16[144,512]{1,0:T(8,128)(2,1)S(1)} %get-tuple-element.20), channel_id=1, source_target_pairs={{0,8},{4,12},{8,0},{12,4},{1,9},{5,13},{9,1},{13,5},{2,10},{6,14},... | collective-permute-start | bytes 442376 | tf_op jit(solution)/shard_map/ppermute | solution.py:26
  81.9 9.8 %collective-permute-start.13 = (bf16[144,512]{1,0:T(8,128)(2,1)S(1)}, bf16[144,512]{1,0:T(8,128)(2,1)S(1)}, u32[]{:S(2)}, u32[]{:S(2)}) collective-permute-start(bf16[144,512]{1,0:T(8,128)(2,1)S(1)} %get-tuple-element.19), channel_id=1, source_target_pairs={{0,12},{4,0},{8,4},{12,8},{1,13},{5,1},{9,5},{13,9},{2,14},{6,2},{... | collective-permute-start | bytes 442376 | tf_op jit(solution)/shard_map/ppermute | solution.py:26
  91.9 11.1 %collective-permute-start.14 = (bf16[144,512]{1,0:T(8,128)(2,1)S(1)}, bf16[144,512]{1,0:T(8,128)(2,1)S(1)}, u32[]{:S(2)}, u32[]{:S(2)}) collective-permute-start(bf16[144,512]{1,0:T(8,128)(2,1)S(1)} %get-tuple-element.16), channel_id=1, source_target_pairs={{0,4},{4,8},{8,12},{12,0},{1,5},{5,9},{9,13},{13,1},{2,6},{6,10},{... | collective-permute-start | bytes 442376 | tf_op jit(solution)/shard_map/ppermute | solution.py:26
  95.4 12.9 %collective-permute-start.15 = (bf16[144,512]{1,0:T(8,128)(2,1)S(1)}, bf16[144,512]{1,0:T(8,128)(2,1)S(1)}, u32[]{:S(2)}, u32[]{:S(2)}) collective-permute-start(bf16[144,512]{1,0:T(8,128)(2,1)S(1)} %get-tuple-element.16), channel_id=1, source_target_pairs={{0,8},{4,12},{8,0},{12,4},{1,9},{5,13},{9,1},{13,5},{2,10},{6,14},... | collective-permute-start | bytes 442376 | tf_op jit(solution)/shard_map/ppermute | solution.py:26
  98.8 9.5 %collective-permute-start.16 = (bf16[144,512]{1,0:T(8,128)(2,1)S(1)}, bf16[144,512]{1,0:T(8,128)(2,1)S(1)}, u32[]{:S(2)}, u32[]{:S(2)}) collective-permute-start(bf16[144,512]{1,0:T(8,128)(2,1)S(1)} %get-tuple-element.16), channel_id=1, source_target_pairs={{0,12},{4,0},{8,4},{12,8},{1,13},{5,1},{9,5},{13,9},{2,14},{6,2},{... | collective-permute-start | bytes 442376 | tf_op jit(solution)/shard_map/ppermute | solution.py:26
  108.4 2.1 %collective-permute-start.17 = (bf16[576,512]{1,0:T(8,128)(2,1)S(1)}, bf16[576,512]{1,0:T(8,128)(2,1)S(1)}, u32[]{:S(2)}, u32[]{:S(2)}) collective-permute-start(bf16[576,512]{1,0:T(8,128)(2,1)S(1)} %convert_element_type.78), channel_id=1, source_target_pairs={{0,1},{1,0},{2,3},{3,2},{4,5},{5,4},{6,7},{7,6},{8,9},{9,8},{10,11... | collective-permute-start | bytes 1769480 | tf_op jit(solution)/shard_map/ppermute | solution.py:26

commit v14 on v7

--- a/solution.py
+++ b/solution.py
@@ -272,9 +272,11 @@
     reduced = ring_sum(mine, "ctx")
     if sub_count == 2:
         other = rotated(reduced.astype(jnp.bfloat16), "sub", 1).astype(jnp.float32)
-        first = jnp.where(sub_at == 0, reduced, other)
-        second = jnp.where(sub_at == 0, other, reduced)
-        weight_v = jnp.concatenate([first, second], axis=0)
+        weight_v = jnp.zeros((shard_rows, reduced.shape[1]), jnp.float32)
+        weight_v = lax.dynamic_update_slice_in_dim(weight_v, reduced, sub_at * piece_rows, axis=0)
+        weight_v = lax.dynamic_update_slice_in_dim(
+            weight_v, other, (1 - sub_at) * piece_rows, axis=0
+        )
     else:
         weight_v = lax.all_gather(reduced, "sub", axis=0, tiled=True)
     if not scale_early:

time: 113 us -> 114 us (level)
  local copies, waits for them, and re-layouts: 4.83 us -> 6.51 us
    concatenate x1 -> x0, other arithmetic: 1.61 us -> none  [body(): weight_v = jnp.concatenate([first, second], axis=0)]
    unnamed x16 -> x18, local copies, waits for them, and re-layouts: 2.23 us -> 3.63 us
where the time goes in v14:
time: 114 us; the launch traced here: 113 us
  waiting for transfers between devices  59.8 us (52%)
  starting transfers between devices  29.8 us (26%)
  Pallas kernels  8.84 us (8%)
  local copies, waits for them, and re-layouts  6.51 us (6%)
  other arithmetic  6.33 us (6%)
    ppermute x12, waiting for transfers between devices, rotated(): lax.ppermute(value, axis, [(source, (source + steps) % count) for source...  30.8 us
    ppermute x4, waiting for transfers between devices, passed_along(): lax.ppermute(value, axis, [(source, source + steps) for source in range(f...  29 us
    ppermute x12, starting transfers between devices, rotated(): lax.ppermute(value, axis, [(source, (source + steps) % count) for source...  18.8 us
    ppermute x4, starting transfers between devices, passed_along(): lax.ppermute(value, axis, [(source, source + steps) for source in range(f...  8.84 us
    pallas_call x1, Pallas kernels, attention(): pl.pallas_call(kernel, out_shape=(jax.ShapeDtypeStruct((rows, width), jnp...  8.84 us
    unnamed x18, local copies, waits for them, and re-layouts  3.63 us
  transfers between devices with their start and end apart: 18, of which 11 were waited for; matrix products, arithmetic and copies ran while one was open for 3% of the time, Pallas kernels for 0%

profile of v14, /device:TPU:0, one launch (start us, length us, event | category | flops | bytes accessed | tf_op | source)
XLA Modules:
  0.0 113.1 jit_solution(3970450174288553121)
XLA Ops:
  0.6 1.1 pad_maximum_fusion.refs_8_
  1.7 0.0 copy-start.3
  1.7 5.0 %collective-permute-start = (bf16[256,1024]{1,0:T(8,128)(2,1)S(1)}, bf16[256,1024]{1,0:T(8,128)(2,1)S(1)}, u32[]{:S(2)}, u32[]{:S(2)}) collective-permute-start(bf16[256,1024]{1,0:T(8,128)(2,1)S(1)} %pad_maximum_fusion.refs_8_), channel_id=1, source_target_pairs={{0,4},{4,8},{8,12},{1,5},{5,9},{9,13},{2,6},{6,10},{10,14},{3,7},{... | collective-permute-start | bytes 1572872 | tf_op jit(solution)/shard_map/ppermute | solution.py:21
  6.7 0.0 copy-start.4
  6.7 1.3 %dynamic-slice_bitcast_fusion = (bf16[256,1152]{1,0:T(8,128)(2,1)S(1)}, bf16[256,1152]{1,0:T(8,128)(2,1)S(1)}) fusion(bf16[1,256,2304]{2,1,0:T(8,128)(2,1)} %param.6, s32[]{:T(128)S(6)} %select_n.80, s32[]{:T(128)S(6)} %select_n.79), kind=kLoop, calls=%fused_computation.9 | loop fusion | bytes 2359304 | tf_op jit(solution)/shard_map/dynamic_slice | solution.py:191
  8.1 1.6 %collective-permute-start.4 = (bf16[256,1152]{1,0:T(8,128)(2,1)S(1)}, bf16[256,1152]{1,0:T(8,128)(2,1)S(1)}, u32[]{:S(2)}, u32[]{:S(2)}) collective-permute-start(bf16[256,1152]{1,0:T(8,128)(2,1)S(1)} %get-tuple-element.22), channel_id=1, source_target_pairs={{0,2},{2,0},{1,3},{3,1},{4,6},{6,4},{5,7},{7,5},{8,10},{10,8},{9,1... | collective-permute-start | bytes 1769480 | tf_op jit(solution)/shard_map/ppermute | solution.py:26
  9.6 1.3 %collective-permute-start.1 = (bf16[256,1024]{1,0:T(8,128)(2,1)S(1)}, bf16[256,1024]{1,0:T(8,128)(2,1)S(1)}, u32[]{:S(2)}, u32[]{:S(2)}) collective-permute-start(bf16[256,1024]{1,0:T(8,128)(2,1)S(1)} %pad_maximum_fusion.refs_8_), channel_id=1, source_target_pairs={{0,1},{2,3},{4,5},{6,7},{8,9},{10,11},{12,13},{14,15},{16,17},{18,... | collective-permute-start | bytes 1572872 | tf_op jit(solution)/shard_map/ppermute | solution.py:21
  10.9 0.0 copy-done.3
  11.0 1.5 %collective-permute-start.2 = (bf16[256,1024]{1,0:T(8,128)(2,1)S(1)}, bf16[256,1024]{1,0:T(8,128)(2,1)}, u32[]{:S(2)}, u32[]{:S(2)}) collective-permute-start(bf16[256,1024]{1,0:T(8,128)(2,1)S(1)} %pad_maximum_fusion.refs_8_), channel_id=1, source_target_pairs={{1,8},{5,12},{3,10},{7,14},{17,24},{21,28},{19,26},{23,30}} | collective-permute-start | bytes 1572872 | tf_op jit(solution)/shard_map/ppermute | solution.py:210
  12.4 6.5 %collective-permute-done.refs_4_ = bf16[256,1024]{1,0:T(8,128)(2,1)S(1)} collective-permute-done((bf16[256,1024]{1,0:T(8,128)(2,1)S(1)}, bf16[256,1024]{1,0:T(8,128)(2,1)S(1)}, u32[]{:S(2)}, u32[]{:S(2)}) %collective-permute-start) | collective-permute-done | bytes 524320 | tf_op jit(solution)/shard_map/ppermute | solution.py:21
  19.0 0.0 collective-permute-start.3
  19.0 0.0 copy-done.4
  19.0 0.1 select_reduce_fusion
  19.1 0.1 copy.13
  19.2 0.7 subtract_add_fusion.refs_1_
  19.9 0.0 collective-permute-done.1.refs_5_
  19.9 0.0 collective-permute-done.2.refs_6_
  19.9 3.0 %collective-permute-done.4.refs_9_ = bf16[256,1152]{1,0:T(8,128)(2,1)S(1)} collective-permute-done((bf16[256,1152]{1,0:T(8,128)(2,1)S(1)}, bf16[256,1152]{1,0:T(8,128)(2,1)S(1)}, u32[]{:S(2)}, u32[]{:S(2)}) %collective-permute-start.4) | collective-permute-done | bytes 589856 | tf_op jit(solution)/shard_map/ppermute | solution.py:26
  22.9 0.0 collective-permute-done.3.refs_7_
  22.9 0.8 copy-done.5
  23.7 8.8 %shard_map.93 = (bf16[256,1024]{1,0:T(8,128)(2,1)}, bf16[256,1024]{1,0:T(8,128)(2,1)}, bf16[256,1024]{1,0:T(8,128)(2,1)}, f32[256,1024]{1,0:T(8,128)}, f32[256,1024]{1,0:T(8,128)}) custom-call(s32[1]{0:T(128)} %bitcast.refs_0_, s32[256,1]{1,0:T(8,128)} %subtract_add_fusion.refs_1_, bf16[256,1024]{1,0:T(8,128)(2,1)} %bitcast.20, bf16[256,1024]{1,0:T(8,128)(2,1)} %bitcast.21, ...), custom_call_target="tpu_custom_call" | custom-call | flops 2684354560 | bytes 7864320 | tf_op jit(solution)/shard_map/pallas_call | solution.py:160
  32.6 0.7 collective-permute-start.7
  33.3 1.3 %collective-permute-start.5 = (bf16[256,1024]{1,0:T(8,128)(2,1)}, bf16[256,1024]{1,0:T(8,128)(2,1)S(1)}, u32[]{:S(2)}, u32[]{:S(2)}) collective-permute-start(bf16[256,1024]{1,0:T(8,128)(2,1)} %get-tuple-element.11), channel_id=1, source_target_pairs={{1,0},{3,2},{5,4},{7,6},{9,8},{11,10},{13,12},{15,14},{17,16},{19,... | collective-permute-start | bytes 1572872 | tf_op jit(solution)/shard_map/ppermute | solution.py:21
  34.6 0.7 collective-permute-start.6
  35.3 0.0 collective-permute-done.7
  35.3 1.4 %add_convert_fusion.1 = bf16[256,1024]{1,0:T(8,128)(2,1)S(1)} fusion(f32[256,1024]{1,0:T(8,128)} %get-tuple-element.12, bf16[256,1024]{1,0:T(8,128)(2,1)S(1)} %collective-permute-done.7), kind=kLoop, calls=%fused_computation.8 | loop fusion | flops 786432 | bytes 2097152 | tf_op jit(solution)/shard_map/convert_element_type | solution.py:229
  36.7 1.3 %collective-permute-start.8 = (bf16[256,1024]{1,0:T(8,128)(2,1)S(1)}, bf16[256,1024]{1,0:T(8,128)(2,1)S(1)}, u32[]{:S(2)}, u32[]{:S(2)}) collective-permute-start(bf16[256,1024]{1,0:T(8,128)(2,1)S(1)} %add_convert_fusion.1), channel_id=1, source_target_pairs={{4,0},{8,4},{12,8},{5,1},{9,5},{13,9},{6,2},{10,6},{14,10},{7,3},{... | collective-permute-start | bytes 1572872 | tf_op jit(solution)/shard_map/ppermute | solution.py:21
  38.0 0.0 collective-permute-done.5
  38.0 0.0 collective-permute-done.6
  38.0 22.5 %collective-permute-done.8 = bf16[256,1024]{1,0:T(8,128)(2,1)S(1)} collective-permute-done((bf16[256,1024]{1,0:T(8,128)(2,1)S(1)}, bf16[256,1024]{1,0:T(8,128)(2,1)S(1)}, u32[]{:S(2)}, u32[]{:S(2)}) %collective-permute-start.8) | collective-permute-done | bytes 524320 | tf_op jit(solution)/shard_map/ppermute | solution.py:21
  60.5 0.3 add_convert_fusion
  60.9 0.9 fusion.10
  61.7 1.5 %collective-permute-start.9 = (bf16[256,512]{1,0:T(8,128)(2,1)S(1)}, bf16[256,512]{1,0:T(8,128)(2,1)S(1)}, u32[]{:S(2)}, u32[]{:S(2)}) collective-permute-start(bf16[256,512]{1,0:T(8,128)(2,1)S(1)} %get-tuple-element.23), channel_id=1, source_target_pairs={{0,2},{2,0},{1,3},{3,1},{4,6},{6,4},{5,7},{7,5},{8,10},{10,8},{9,1... | collective-permute-start | bytes 786440 | tf_op jit(solution)/shard_map/ppermute | solution.py:26
  63.2 6.8 %collective-permute-done.9 = bf16[256,512]{1,0:T(8,128)(2,1)S(1)} collective-permute-done((bf16[256,512]{1,0:T(8,128)(2,1)S(1)}, bf16[256,512]{1,0:T(8,128)(2,1)S(1)}, u32[]{:S(2)}, u32[]{:S(2)}) %collective-permute-start.9) | collective-permute-done | bytes 262176 | tf_op jit(solution)/shard_map/ppermute | solution.py:26
  70.0 0.0 copy-done.6
  70.0 0.8 convolution_multiply_fusion
  70.8 0.0 copy-start.1
  70.9 1.4 %copy-done.1 = f32[1152,512]{1,0:T(8,128)} copy-done((f32[1152,512]{1,0:T(8,128)}, f32[1152,512]{1,0:T(8,128)S(1)}, u32[]{:S(2)}) %copy-start.1) | copy-done | bytes 2359320
  72.3 0.1 dynamic-slice_convert_fusion
  72.3 0.1 collective-permute-start.10
  72.5 1.9 %collective-permute-done.10 = bf16[576,512]{1,0:T(8,128)(2,1)S(1)} collective-permute-done((bf16[576,512]{1,0:T(8,128)(2,1)S(1)}, bf16[576,512]{1,0:T(8,128)(2,1)S(1)}, u32[]{:S(2)}, u32[]{:S(2)}) %collective-permute-start.10) | collective-permute-done | bytes 589856 | tf_op jit(solution)/shard_map/ppermute | solution.py:26
  74.4 1.4 %convert_add_fusion = f32[576,512]{1,0:T(8,128)S(1)} fusion(bf16[576,512]{1,0:T(8,128)(2,1)S(1)} %collective-permute-done.10, f32[1152,512]{1,0:T(8,128)} %copy-done.1, s32[]{:T(128)S(6)} %select_n.81), kind=kLoop, calls=%fused_computation.5 | loop fusion | flops 589824 | bytes 2949124 | tf_op jit(solution)/shard_map/add | solution.py:271
  75.9 0.1 dynamic-slice_convert_fusion.3
  75.9 5.6 %collective-permute-start.11 = (bf16[144,512]{1,0:T(8,128)(2,1)S(1)}, bf16[144,512]{1,0:T(8,128)(2,1)S(1)}, u32[]{:S(2)}, u32[]{:S(2)}) collective-permute-start(bf16[144,512]{1,0:T(8,128)(2,1)S(1)} %get-tuple-element.18), channel_id=1, source_target_pairs={{0,4},{4,8},{8,12},{12,0},{1,5},{5,9},{9,13},{13,1},{2,6},{6,10},{... | collective-permute-start | bytes 442376 | tf_op jit(solution)/shard_map/ppermute | solution.py:26
  81.6 0.0 collective-permute-start.12
  81.6 2.4 %collective-permute-start.13 = (bf16[144,512]{1,0:T(8,128)(2,1)S(1)}, bf16[144,512]{1,0:T(8,128)(2,1)S(1)}, u32[]{:S(2)}, u32[]{:S(2)}) collective-permute-start(bf16[144,512]{1,0:T(8,128)(2,1)S(1)} %get-tuple-element.19), channel_id=1, source_target_pairs={{0,12},{4,0},{8,4},{12,8},{1,13},{5,1},{9,5},{13,9},{2,14},{6,2},{... | collective-permute-start | bytes 442376 | tf_op jit(solution)/shard_map/ppermute | solution.py:26
  84.0 1.8 %collective-permute-done.11 = bf16[144,512]{1,0:T(8,128)(2,1)S(1)} collective-permute-done((bf16[144,512]{1,0:T(8,128)(2,1)S(1)}, bf16[144,512]{1,0:T(8,128)(2,1)S(1)}, u32[]{:S(2)}, u32[]{:S(2)}) %collective-permute-start.11) | collective-permute-done | bytes 147488 | tf_op jit(solution)/shard_map/ppermute | solution.py:26
  85.8 5.3 %collective-permute-done.12 = bf16[144,512]{1,0:T(8,128)(2,1)S(1)} collective-permute-done((bf16[144,512]{1,0:T(8,128)(2,1)S(1)}, bf16[144,512]{1,0:T(8,128)(2,1)S(1)}, u32[]{:S(2)}, u32[]{:S(2)}) %collective-permute-start.12) | collective-permute-done | bytes 147488 | tf_op jit(solution)/shard_map/ppermute | solution.py:26
  91.1 0.2 collective-permute-done.13
  91.3 0.1 broadcast_in_dim.32
  91.5 0.1 fusion.6
  91.6 3.5 %collective-permute-start.14 = (bf16[144,512]{1,0:T(8,128)(2,1)S(1)}, bf16[144,512]{1,0:T(8,128)(2,1)S(1)}, u32[]{:S(2)}, u32[]{:S(2)}) collective-permute-start(bf16[144,512]{1,0:T(8,128)(2,1)S(1)} %get-tuple-element.14), channel_id=1, source_target_pairs={{0,4},{4,8},{8,12},{12,0},{1,5},{5,9},{9,13},{13,1},{2,6},{6,10},{... | collective-permute-start | bytes 442376 | tf_op jit(solution)/shard_map/ppermute | solution.py:26
  95.0 3.4 %collective-permute-start.15 = (bf16[144,512]{1,0:T(8,128)(2,1)S(1)}, bf16[144,512]{1,0:T(8,128)(2,1)S(1)}, u32[]{:S(2)}, u32[]{:S(2)}) collective-permute-start(bf16[144,512]{1,0:T(8,128)(2,1)S(1)} %get-tuple-element.14), channel_id=1, source_target_pairs={{0,8},{4,12},{8,0},{12,4},{1,9},{5,13},{9,1},{13,5},{2,10},{6,14},... | collective-permute-start | bytes 442376 | tf_op jit(solution)/shard_map/ppermute | solution.py:26
  98.4 0.0 collective-permute-start.16
  98.4 4.2 %collective-permute-done.14 = bf16[144,512]{1,0:T(8,128)(2,1)S(1)} collective-permute-done((bf16[144,512]{1,0:T(8,128)(2,1)S(1)}, bf16[144,512]{1,0:T(8,128)(2,1)S(1)}, u32[]{:S(2)}, u32[]{:S(2)}) %collective-permute-start.14) | collective-permute-done | bytes 147488 | tf_op jit(solution)/shard_map/ppermute | solution.py:26
  102.7 5.2 %collective-permute-done.15 = bf16[144,512]{1,0:T(8,128)(2,1)S(1)} collective-permute-done((bf16[144,512]{1,0:T(8,128)(2,1)S(1)}, bf16[144,512]{1,0:T(8,128)(2,1)S(1)}, u32[]{:S(2)}, u32[]{:S(2)}) %collective-permute-start.15) | collective-permute-done | bytes 147488 | tf_op jit(solution)/shard_map/ppermute | solution.py:26
  107.9 0.0 collective-permute-done.16
  108.0 0.3 broadcast_in_dim.31
  108.3 1.0 fusion.9
  109.3 0.0 collective-permute-start.17
  109.3 2.2 %collective-permute-done.17 = bf16[576,512]{1,0:T(8,128)(2,1)S(1)} collective-permute-done((bf16[576,512]{1,0:T(8,128)(2,1)}, bf16[576,512]{1,0:T(8,128)(2,1)S(1)}, u32[]{:S(2)}, u32[]{:S(2)}) %collective-permute-start.17) | collective-permute-done | bytes 589856 | tf_op jit(solution)/shard_map/ppermute | solution.py:26
  111.5 0.1 convert_dynamic-update-slice_fusion
  111.6 0.0 copy-start
  111.7 1.4 %copy-done = f32[1152,512]{1,0:T(8,128)} copy-done((f32[1152,512]{1,0:T(8,128)}, f32[1152,512]{1,0:T(8,128)S(1)}, u32[]{:S(2)}) %copy-start) | copy-done | bytes 2359320
  (12 shorter events, 0.1 us)
Async XLA Ops:
  1.7 9.2 %copy-start.3 = (bf16[256,1024]{1,0:T(8,128)(2,1)}, bf16[256,1024]{1,0:T(8,128)(2,1)S(1)}, u32[]{:S(2)}) copy-start(bf16[256,1024]{1,0:T(8,128)(2,1)S(1)} %pad_maximum_fusion.refs_8_) | copy-start | bytes 1572868
  1.7 17.2 %collective-permute-start = (bf16[256,1024]{1,0:T(8,128)(2,1)S(1)}, bf16[256,1024]{1,0:T(8,128)(2,1)S(1)}, u32[]{:S(2)}, u32[]{:S(2)}) collective-permute-start(bf16[256,1024]{1,0:T(8,128)(2,1)S(1)} %pad_maximum_fusion.refs_8_), channel_id=1, source_target_pairs={{0,4},{4,8},{8,12},{1,5},{5,9},{9,13},{2,6},{6,10},{10,14},{3,7},{... | collective-permute-start | bytes 1572872 | tf_op jit(solution)/shard_map/ppermute | solution.py:21
  6.7 12.3 %copy-start.4 = (s32[1,12]{1,0:T(1,128)S(1)}, s32[1,12]{1,0:T(1,128)}, u32[]{:S(2)}) copy-start(s32[1,12]{1,0:T(1,128)} %param.11) | copy-start | bytes 148
  8.1 14.9 %collective-permute-start.4 = (bf16[256,1152]{1,0:T(8,128)(2,1)S(1)}, bf16[256,1152]{1,0:T(8,128)(2,1)S(1)}, u32[]{:S(2)}, u32[]{:S(2)}) collective-permute-start(bf16[256,1152]{1,0:T(8,128)(2,1)S(1)} %get-tuple-element.22), channel_id=1, source_target_pairs={{0,2},{2,0},{1,3},{3,1},{4,6},{6,4},{5,7},{7,5},{8,10},{10,8},{9,1... | collective-permute-start | bytes 1769480 | tf_op jit(solution)/shard_map/ppermute | solution.py:26
  9.6 10.3 %collective-permute-start.1 = (bf16[256,1024]{1,0:T(8,128)(2,1)S(1)}, bf16[256,1024]{1,0:T(8,128)(2,1)S(1)}, u32[]{:S(2)}, u32[]{:S(2)}) collective-permute-start(bf16[256,1024]{1,0:T(8,128)(2,1)S(1)} %pad_maximum_fusion.refs_8_), channel_id=1, source_target_pairs={{0,1},{2,3},{4,5},{6,7},{8,9},{10,11},{12,13},{14,15},{16,17},{18,... | collective-permute-start | bytes 1572872 | tf_op jit(solution)/shard_map/ppermute | solution.py:21
  11.0 9.0 %collective-permute-start.2 = (bf16[256,1024]{1,0:T(8,128)(2,1)S(1)}, bf16[256,1024]{1,0:T(8,128)(2,1)}, u32[]{:S(2)}, u32[]{:S(2)}) collective-permute-start(bf16[256,1024]{1,0:T(8,128)(2,1)S(1)} %pad_maximum_fusion.refs_8_), channel_id=1, source_target_pairs={{1,8},{5,12},{3,10},{7,14},{17,24},{21,28},{19,26},{23,30}} | collective-permute-start | bytes 1572872 | tf_op jit(solution)/shard_map/ppermute | solution.py:210
  19.0 4.0 %copy-start.7 = (bf16[256,1024]{1,0:T(8,128)(2,1)}, bf16[256,1024]{1,0:T(8,128)(2,1)S(1)}, u32[]{:S(2)}) copy-start(bf16[256,1024]{1,0:T(8,128)(2,1)S(1)} %collective-permute-done.refs_4_) | copy-start | bytes 1572868
  19.0 4.0 %collective-permute-start.3 = (bf16[256,1024]{1,0:T(8,128)(2,1)S(1)}, bf16[256,1024]{1,0:T(8,128)(2,1)}, u32[]{:S(2)}, u32[]{:S(2)}) collective-permute-start(bf16[256,1024]{1,0:T(8,128)(2,1)S(1)} %collective-permute-done.refs_4_), channel_id=1, source_target_pairs={{0,1},{1,0},{2,3},{3,2},{4,5},{5,4},{6,7},{7,6},{8,9},{9,8},{10,11... | collective-permute-start | bytes 1572872 | tf_op jit(solution)/shard_map/ppermute | solution.py:26
  19.9 3.0 %copy-start.8 = (bf16[256,1024]{1,0:T(8,128)(2,1)}, bf16[256,1024]{1,0:T(8,128)(2,1)S(1)}, u32[]{:S(2)}) copy-start(bf16[256,1024]{1,0:T(8,128)(2,1)S(1)} %collective-permute-done.1.refs_5_) | copy-start | bytes 1572868
  22.9 0.8 copy-start.5
  32.6 27.9 %copy-start.2 = (f32[256,1024]{1,0:T(8,128)S(1)}, f32[256,1024]{1,0:T(8,128)}, u32[]{:S(2)}) copy-start(f32[256,1024]{1,0:T(8,128)} %get-tuple-element.10) | copy-start | bytes 3145732
  32.6 2.7 %collective-permute-start.7 = (bf16[256,1024]{1,0:T(8,128)(2,1)}, bf16[256,1024]{1,0:T(8,128)(2,1)S(1)}, u32[]{:S(2)}, u32[]{:S(2)}) collective-permute-start(bf16[256,1024]{1,0:T(8,128)(2,1)} %get-tuple-element.13), channel_id=1, source_target_pairs={{0,1},{1,0},{2,3},{3,2},{4,5},{5,4},{6,7},{7,6},{8,9},{9,8},{10,11... | collective-permute-start | bytes 1572872 | tf_op jit(solution)/shard_map/ppermute | solution.py:26
  33.3 4.7 %collective-permute-start.5 = (bf16[256,1024]{1,0:T(8,128)(2,1)}, bf16[256,1024]{1,0:T(8,128)(2,1)S(1)}, u32[]{:S(2)}, u32[]{:S(2)}) collective-permute-start(bf16[256,1024]{1,0:T(8,128)(2,1)} %get-tuple-element.11), channel_id=1, source_target_pairs={{1,0},{3,2},{5,4},{7,6},{9,8},{11,10},{13,12},{15,14},{17,16},{19,... | collective-permute-start | bytes 1572872 | tf_op jit(solution)/shard_map/ppermute | solution.py:21
  34.6 3.4 %collective-permute-start.6 = (bf16[256,1024]{1,0:T(8,128)(2,1)}, bf16[256,1024]{1,0:T(8,128)(2,1)S(1)}, u32[]{:S(2)}, u32[]{:S(2)}) collective-permute-start(bf16[256,1024]{1,0:T(8,128)(2,1)} %get-tuple-element.11), channel_id=1, source_target_pairs={{8,1},{12,5},{10,3},{14,7},{24,17},{28,21},{26,19},{30,23}} | collective-permute-start | bytes 1572872 | tf_op jit(solution)/shard_map/ppermute | solution.py:234
  36.7 23.8 %collective-permute-start.8 = (bf16[256,1024]{1,0:T(8,128)(2,1)S(1)}, bf16[256,1024]{1,0:T(8,128)(2,1)S(1)}, u32[]{:S(2)}, u32[]{:S(2)}) collective-permute-start(bf16[256,1024]{1,0:T(8,128)(2,1)S(1)} %add_convert_fusion.1), channel_id=1, source_target_pairs={{4,0},{8,4},{12,8},{5,1},{9,5},{13,9},{6,2},{10,6},{14,10},{7,3},{... | collective-permute-start | bytes 1572872 | tf_op jit(solution)/shard_map/ppermute | solution.py:21
  60.8 9.2 %copy-start.6 = (bf16[256,1152]{1,0:T(8,128)(2,1)S(1)}, bf16[256,1152]{1,0:T(8,128)(2,1)}, u32[]{:S(2)}) copy-start(bf16[256,1152]{1,0:T(8,128)(2,1)} %copy-done.5) | copy-start | bytes 1769476
  61.7 8.3 %collective-permute-start.9 = (bf16[256,512]{1,0:T(8,128)(2,1)S(1)}, bf16[256,512]{1,0:T(8,128)(2,1)S(1)}, u32[]{:S(2)}, u32[]{:S(2)}) collective-permute-start(bf16[256,512]{1,0:T(8,128)(2,1)S(1)} %get-tuple-element.23), channel_id=1, source_target_pairs={{0,2},{2,0},{1,3},{3,1},{4,6},{6,4},{5,7},{7,5},{8,10},{10,8},{9,1... | collective-permute-start | bytes 786440 | tf_op jit(solution)/shard_map/ppermute | solution.py:26
  70.8 1.4 %copy-start.1 = (f32[1152,512]{1,0:T(8,128)}, f32[1152,512]{1,0:T(8,128)S(1)}, u32[]{:S(2)}) copy-start(f32[1152,512]{1,0:T(8,128)S(1)} %convolution_multiply_fusion) | copy-start | bytes 7077892
  72.3 2.1 %collective-permute-start.10 = (bf16[576,512]{1,0:T(8,128)(2,1)S(1)}, bf16[576,512]{1,0:T(8,128)(2,1)S(1)}, u32[]{:S(2)}, u32[]{:S(2)}) collective-permute-start(bf16[576,512]{1,0:T(8,128)(2,1)S(1)} %dynamic-slice_convert_fusion), channel_id=1, source_target_pairs={{0,1},{1,0},{2,3},{3,2},{4,5},{5,4},{6,7},{7,6},{8,9},{9,8},{10,11... | collective-permute-start | bytes 1769480 | tf_op jit(solution)/shard_map/ppermute | solution.py:26
  75.9 9.8 %collective-permute-start.11 = (bf16[144,512]{1,0:T(8,128)(2,1)S(1)}, bf16[144,512]{1,0:T(8,128)(2,1)S(1)}, u32[]{:S(2)}, u32[]{:S(2)}) collective-permute-start(bf16[144,512]{1,0:T(8,128)(2,1)S(1)} %get-tuple-element.18), channel_id=1, source_target_pairs={{0,4},{4,8},{8,12},{12,0},{1,5},{5,9},{9,13},{13,1},{2,6},{6,10},{... | collective-permute-start | bytes 442376 | tf_op jit(solution)/shard_map/ppermute | solution.py:26
  81.6 9.6 %collective-permute-start.12 = (bf16[144,512]{1,0:T(8,128)(2,1)S(1)}, bf16[144,512]{1,0:T(8,128)(2,1)S(1)}, u32[]{:S(2)}, u32[]{:S(2)}) collective-permute-start(bf16[144,512]{1,0:T(8,128)(2,1)S(1)} %get-tuple-element.20), channel_id=1, source_target_pairs={{0,8},{4,12},{8,0},{12,4},{1,9},{5,13},{9,1},{13,5},{2,10},{6,14},... | collective-permute-start | bytes 442376 | tf_op jit(solution)/shard_map/ppermute | solution.py:26
  81.6 9.8 %collective-permute-start.13 = (bf16[144,512]{1,0:T(8,128)(2,1)S(1)}, bf16[144,512]{1,0:T(8,128)(2,1)S(1)}, u32[]{:S(2)}, u32[]{:S(2)}) collective-permute-start(bf16[144,512]{1,0:T(8,128)(2,1)S(1)} %get-tuple-element.19), channel_id=1, source_target_pairs={{0,12},{4,0},{8,4},{12,8},{1,13},{5,1},{9,5},{13,9},{2,14},{6,2},{... | collective-permute-start | bytes 442376 | tf_op jit(solution)/shard_map/ppermute | solution.py:26
  91.6 11.1 %collective-permute-start.14 = (bf16[144,512]{1,0:T(8,128)(2,1)S(1)}, bf16[144,512]{1,0:T(8,128)(2,1)S(1)}, u32[]{:S(2)}, u32[]{:S(2)}) collective-permute-start(bf16[144,512]{1,0:T(8,128)(2,1)S(1)} %get-tuple-element.14), channel_id=1, source_target_pairs={{0,4},{4,8},{8,12},{12,0},{1,5},{5,9},{9,13},{13,1},{2,6},{6,10},{... | collective-permute-start | bytes 442376 | tf_op jit(solution)/shard_map/ppermute | solution.py:26
  95.0 12.9 %collective-permute-start.15 = (bf16[144,512]{1,0:T(8,128)(2,1)S(1)}, bf16[144,512]{1,0:T(8,128)(2,1)S(1)}, u32[]{:S(2)}, u32[]{:S(2)}) collective-permute-start(bf16[144,512]{1,0:T(8,128)(2,1)S(1)} %get-tuple-element.14), channel_id=1, source_target_pairs={{0,8},{4,12},{8,0},{12,4},{1,9},{5,13},{9,1},{13,5},{2,10},{6,14},... | collective-permute-start | bytes 442376 | tf_op jit(solution)/shard_map/ppermute | solution.py:26
  98.4 9.5 %collective-permute-start.16 = (bf16[144,512]{1,0:T(8,128)(2,1)S(1)}, bf16[144,512]{1,0:T(8,128)(2,1)S(1)}, u32[]{:S(2)}, u32[]{:S(2)}) collective-permute-start(bf16[144,512]{1,0:T(8,128)(2,1)S(1)} %get-tuple-element.14), channel_id=1, source_target_pairs={{0,12},{4,0},{8,4},{12,8},{1,13},{5,1},{9,5},{13,9},{2,14},{6,2},{... | collective-permute-start | bytes 442376 | tf_op jit(solution)/shard_map/ppermute | solution.py:26
  109.3 2.2 %collective-permute-start.17 = (bf16[576,512]{1,0:T(8,128)(2,1)}, bf16[576,512]{1,0:T(8,128)(2,1)S(1)}, u32[]{:S(2)}, u32[]{:S(2)}) collective-permute-start(bf16[576,512]{1,0:T(8,128)(2,1)} %get-tuple-element.16), channel_id=1, source_target_pairs={{0,1},{1,0},{2,3},{3,2},{4,5},{5,4},{6,7},{7,6},{8,9},{9,8},{10,11... | collective-permute-start | bytes 1769480 | tf_op jit(solution)/shard_map/ppermute | solution.py:26
  111.6 1.4 %copy-start = (f32[1152,512]{1,0:T(8,128)}, f32[1152,512]{1,0:T(8,128)S(1)}, u32[]{:S(2)}) copy-start(f32[1152,512]{1,0:T(8,128)S(1)} %convert_dynamic-update-slice_fusion) | copy-start | bytes 7077892

commit v15 on v7

--- a/solution.py
+++ b/solution.py
@@ -78,38 +78,49 @@
     scale = HEAD_DIM ** (-0.5)
     kv_width = kv_heads * HEAD_DIM
     per_group = heads // kv_heads
-    col = lax.broadcasted_iota(jnp.int32, (rows, keys), 1)
-    row = lax.broadcasted_iota(jnp.int32, (rows, keys), 0)
-    allowed = (col >= lo_ref[...]) & (col <= row + margin)
+    half = rows // 2
+    reach_keys = keys - half
+    col = lax.broadcasted_iota(jnp.int32, (half, reach_keys), 1)
+    row = lax.broadcasted_iota(jnp.int32, (half, reach_keys), 0)
+    allowed = [
+        (col + part * half >= lo_ref[pl.ds(part * half, half), :])
+        & (col + part * half <= row + part * half + margin)
+        for part in range(2)
+    ]
     for group in range(kv_heads):
         k_cols = pl.ds(group * HEAD_DIM, HEAD_DIM)
         v_cols = pl.ds(kv_width + group * HEAD_DIM, HEAD_DIM)
-        key_g = kv_ref[:, k_cols]
-        value_g = kv_ref[:, v_cols]
-        grad_k = None
-        grad_v = None
+        sums_k = [None, None]
+        sums_v = [None, None]
         for member in range(per_group):
             q_cols = pl.ds((group * per_group + member) * HEAD_DIM, HEAD_DIM)
-            query_h = q_ref[:, q_cols]
-            grad_h = do_ref[:, q_cols]
-            scores = lax.dot_general(query_h, key_g, NT, preferred_element_type=jnp.float32) * scale
-            scores = jnp.where(allowed, scores, -1e30)
-            largest = jnp.max(scores, axis=1, keepdims=True)
-            raised = jnp.exp(scores - largest)
-            probs = raised * (1.0 / jnp.sum(raised, axis=1, keepdims=True))
-            grad_probs = lax.dot_general(grad_h, value_g, NT, preferred_element_type=jnp.float32)
-            row_dot = jnp.sum(probs * grad_probs, axis=1, keepdims=True)
-            grad_scores = (probs * (grad_probs - row_dot) * scale).astype(jnp.bfloat16)
-            probs_low = probs.astype(jnp.bfloat16)
-            dq_ref[:, q_cols] = jnp.dot(
-                grad_scores, key_g, preferred_element_type=jnp.float32
-            ).astype(dq_ref.dtype)
-            term_k = lax.dot_general(grad_scores, query_h, TN, preferred_element_type=jnp.float32)
-            term_v = lax.dot_general(probs_low, grad_h, TN, preferred_element_type=jnp.float32)
-            grad_k = term_k if grad_k is None else grad_k + term_k
-            grad_v = term_v if grad_v is None else grad_v + term_v
-        dkv_ref[:, k_cols] = grad_k
-        dkv_ref[:, v_cols] = grad_v
+            for part in range(2):
+                part_rows = pl.ds(part * half, half)
+                part_keys = pl.ds(part * half, reach_keys)
+                key_g = kv_ref[part_keys, k_cols]
+                value_g = kv_ref[part_keys, v_cols]
+                query_h = q_ref[part_rows, q_cols]
+                grad_h = do_ref[part_rows, q_cols]
+                scores = lax.dot_general(query_h, key_g, NT, preferred_element_type=jnp.float32) * scale
+                scores = jnp.where(allowed[part], scores, -1e30)
+                largest = jnp.max(scores, axis=1, keepdims=True)
+                raised = jnp.exp(scores - largest)
+                probs = raised * (1.0 / jnp.sum(raised, axis=1, keepdims=True))
+                grad_probs = lax.dot_general(grad_h, value_g, NT, preferred_element_type=jnp.float32)
+                row_dot = jnp.sum(probs * grad_probs, axis=1, keepdims=True)
+                grad_scores = (probs * (grad_probs - row_dot) * scale).astype(jnp.bfloat16)
+                probs_low = probs.astype(jnp.bfloat16)
+                dq_ref[part_rows, q_cols] = jnp.dot(
+                    grad_scores, key_g, preferred_element_type=jnp.float32
+                ).astype(dq_ref.dtype)
+                term_k = lax.dot_general(grad_scores, query_h, TN, preferred_element_type=jnp.float32)
+                term_v = lax.dot_general(probs_low, grad_h, TN, preferred_element_type=jnp.float32)
+                sums_k[part] = term_k if sums_k[part] is None else sums_k[part] + term_k
+                sums_v[part] = term_v if sums_v[part] is None else sums_v[part] + term_v
+        for cols, sums in ((k_cols, sums_k), (v_cols, sums_v)):
+            dkv_ref[pl.ds(0, half), cols] = sums[0][:half]
+            dkv_ref[pl.ds(half, reach_keys - half), cols] = sums[0][half:] + sums[1][: reach_keys - half]
+            dkv_ref[pl.ds(reach_keys, half), cols] = sums[1][reach_keys - half :]
     def slot_rows(index):
         return dkv_ref[pl.ds(index * block_rows, block_rows), :]
 

time: 113 us -> 116 us (1.027)
  Pallas kernels: 8.83 us -> 11.2 us
    pallas_call x1, Pallas kernels: 8.83 us -> 11.2 us  [attention(): pl.pallas_call(kernel, out_shape=(jax.ShapeDtypeStruct((rows, width), jnp...]
where the time goes in v15:
time: 116 us; the launch traced here: 114 us
  waiting for transfers between devices  59.6 us (51%)
  starting transfers between devices  29.8 us (26%)
  Pallas kernels  11.2 us (10%)
  other arithmetic  7.16 us (6%)
  local copies, waits for them, and re-layouts  4.83 us (4%)
    ppermute x12, waiting for transfers between devices, rotated(): lax.ppermute(value, axis, [(source, (source + steps) % count) for source...  30.6 us
    ppermute x4, waiting for transfers between devices, passed_along(): lax.ppermute(value, axis, [(source, source + steps) for source in range(f...  29 us
    ppermute x12, starting transfers between devices, rotated(): lax.ppermute(value, axis, [(source, (source + steps) % count) for source...  18.8 us
    pallas_call x1, Pallas kernels, attention(): pl.pallas_call(kernel, out_shape=(jax.ShapeDtypeStruct((rows, width), jnp...  11.2 us
    ppermute x4, starting transfers between devices, passed_along(): lax.ppermute(value, axis, [(source, source + steps) for source in range(f...  8.84 us
  transfers between devices with their start and end apart: 18, of which 11 were waited for; matrix products, arithmetic and copies ran while one was open for 3% of the time, Pallas kernels for 0%

profile of v15, /device:TPU:0, one launch (start us, length us, event | category | flops | bytes accessed | tf_op | source)
XLA Modules:
  0.0 114.4 jit_solution(8371899220556049709)
XLA Ops:
  0.6 1.1 pad_maximum_fusion.1.refs_8_
  1.7 0.0 copy-start.2
  1.7 5.0 %collective-permute-start = (bf16[256,1024]{1,0:T(8,128)(2,1)S(1)}, bf16[256,1024]{1,0:T(8,128)(2,1)S(1)}, u32[]{:S(2)}, u32[]{:S(2)}) collective-permute-start(bf16[256,1024]{1,0:T(8,128)(2,1)S(1)} %pad_maximum_fusion.1.refs_8_), channel_id=1, source_target_pairs={{0,4},{4,8},{8,12},{1,5},{5,9},{9,13},{2,6},{6,10},{10,14},{3,7},{... | collective-permute-start | bytes 1572872 | tf_op jit(solution)/shard_map/ppermute | solution.py:21
  6.7 0.0 copy-start.3
  6.7 1.3 %dynamic-slice_bitcast_fusion = (bf16[256,1152]{1,0:T(8,128)(2,1)S(1)}, bf16[256,1152]{1,0:T(8,128)(2,1)S(1)}) fusion(bf16[1,256,2304]{2,1,0:T(8,128)(2,1)} %param.6, s32[]{:T(128)S(6)} %select_n.89, s32[]{:T(128)S(6)} %select_n.87), kind=kLoop, calls=%fused_computation.11 | loop fusion | bytes 2359304 | tf_op jit(solution)/shard_map/dynamic_slice | solution.py:202
  8.1 1.6 %collective-permute-start.4 = (bf16[256,1152]{1,0:T(8,128)(2,1)S(1)}, bf16[256,1152]{1,0:T(8,128)(2,1)S(1)}, u32[]{:S(2)}, u32[]{:S(2)}) collective-permute-start(bf16[256,1152]{1,0:T(8,128)(2,1)S(1)} %get-tuple-element.22), channel_id=1, source_target_pairs={{0,2},{2,0},{1,3},{3,1},{4,6},{6,4},{5,7},{7,5},{8,10},{10,8},{9,1... | collective-permute-start | bytes 1769480 | tf_op jit(solution)/shard_map/ppermute | solution.py:26
  9.6 1.3 %collective-permute-start.1 = (bf16[256,1024]{1,0:T(8,128)(2,1)S(1)}, bf16[256,1024]{1,0:T(8,128)(2,1)S(1)}, u32[]{:S(2)}, u32[]{:S(2)}) collective-permute-start(bf16[256,1024]{1,0:T(8,128)(2,1)S(1)} %pad_maximum_fusion.1.refs_8_), channel_id=1, source_target_pairs={{0,1},{2,3},{4,5},{6,7},{8,9},{10,11},{12,13},{14,15},{16,17},{18,... | collective-permute-start | bytes 1572872 | tf_op jit(solution)/shard_map/ppermute | solution.py:21
  10.9 0.0 copy-done.2
  11.0 1.5 %collective-permute-start.2 = (bf16[256,1024]{1,0:T(8,128)(2,1)S(1)}, bf16[256,1024]{1,0:T(8,128)(2,1)}, u32[]{:S(2)}, u32[]{:S(2)}) collective-permute-start(bf16[256,1024]{1,0:T(8,128)(2,1)S(1)} %pad_maximum_fusion.1.refs_8_), channel_id=1, source_target_pairs={{1,8},{5,12},{3,10},{7,14},{17,24},{21,28},{19,26},{23,30}} | collective-permute-start | bytes 1572872 | tf_op jit(solution)/shard_map/ppermute | solution.py:221
  12.4 6.5 %collective-permute-done.refs_4_ = bf16[256,1024]{1,0:T(8,128)(2,1)S(1)} collective-permute-done((bf16[256,1024]{1,0:T(8,128)(2,1)S(1)}, bf16[256,1024]{1,0:T(8,128)(2,1)S(1)}, u32[]{:S(2)}, u32[]{:S(2)}) %collective-permute-start) | collective-permute-done | bytes 524320 | tf_op jit(solution)/shard_map/ppermute | solution.py:21
  19.0 0.0 collective-permute-start.3
  19.0 0.0 copy-done.3
  19.0 0.1 select_reduce_fusion
  19.1 0.1 copy.13
  19.2 0.7 subtract_add_fusion.refs_1_
  19.9 0.0 collective-permute-done.1.refs_5_
  19.9 0.0 collective-permute-done.2.refs_6_
  19.9 3.0 %collective-permute-done.4.refs_9_ = bf16[256,1152]{1,0:T(8,128)(2,1)S(1)} collective-permute-done((bf16[256,1152]{1,0:T(8,128)(2,1)S(1)}, bf16[256,1152]{1,0:T(8,128)(2,1)S(1)}, u32[]{:S(2)}, u32[]{:S(2)}) %collective-permute-start.4) | collective-permute-done | bytes 589856 | tf_op jit(solution)/shard_map/ppermute | solution.py:26
  22.9 0.0 collective-permute-done.3.refs_7_
  22.9 0.0 copy-done.6
  22.9 0.8 copy-done.4
  23.7 11.2 %shard_map.93 = (bf16[256,1024]{1,0:T(8,128)(2,1)}, bf16[256,1024]{1,0:T(8,128)(2,1)}, bf16[256,1024]{1,0:T(8,128)(2,1)}, f32[256,1024]{1,0:T(8,128)}, f32[256,1024]{1,0:T(8,128)}) custom-call(s32[1]{0:T(128)} %bitcast.refs_0_, s32[256,1]{1,0:T(8,128)} %subtract_add_fusion.refs_1_, bf16[256,1024]{1,0:T(8,128)(2,1)} %bitcast.20, bf16[256,1024]{1,0:T(8,128)(2,1)} %bitcast.21, ...), custom_call_target="tpu_custom_call" | custom-call | flops 2684354560 | bytes 7864320 | tf_op jit(solution)/shard_map/pallas_call | solution.py:171
  35.0 0.7 collective-permute-start.7
  35.7 1.3 %collective-permute-start.5 = (bf16[256,1024]{1,0:T(8,128)(2,1)}, bf16[256,1024]{1,0:T(8,128)(2,1)S(1)}, u32[]{:S(2)}, u32[]{:S(2)}) collective-permute-start(bf16[256,1024]{1,0:T(8,128)(2,1)} %get-tuple-element.11), channel_id=1, source_target_pairs={{1,0},{3,2},{5,4},{7,6},{9,8},{11,10},{13,12},{15,14},{17,16},{19,... | collective-permute-start | bytes 1572872 | tf_op jit(solution)/shard_map/ppermute | solution.py:21
  37.0 0.7 collective-permute-start.6
  37.7 0.0 collective-permute-done.7
  37.7 1.4 %add_convert_fusion.1 = bf16[256,1024]{1,0:T(8,128)(2,1)S(1)} fusion(f32[256,1024]{1,0:T(8,128)} %get-tuple-element.12, bf16[256,1024]{1,0:T(8,128)(2,1)S(1)} %collective-permute-done.7), kind=kLoop, calls=%fused_computation.10 | loop fusion | flops 786432 | bytes 2097152 | tf_op jit(solution)/shard_map/convert_element_type | solution.py:240
  39.1 1.3 %collective-permute-start.8 = (bf16[256,1024]{1,0:T(8,128)(2,1)S(1)}, bf16[256,1024]{1,0:T(8,128)(2,1)S(1)}, u32[]{:S(2)}, u32[]{:S(2)}) collective-permute-start(bf16[256,1024]{1,0:T(8,128)(2,1)S(1)} %add_convert_fusion.1), channel_id=1, source_target_pairs={{4,0},{8,4},{12,8},{5,1},{9,5},{13,9},{6,2},{10,6},{14,10},{7,3},{... | collective-permute-start | bytes 1572872 | tf_op jit(solution)/shard_map/ppermute | solution.py:21
  40.4 0.0 collective-permute-done.5
  40.4 0.0 collective-permute-done.6
  40.4 22.5 %collective-permute-done.8 = bf16[256,1024]{1,0:T(8,128)(2,1)S(1)} collective-permute-done((bf16[256,1024]{1,0:T(8,128)(2,1)S(1)}, bf16[256,1024]{1,0:T(8,128)(2,1)S(1)}, u32[]{:S(2)}, u32[]{:S(2)}) %collective-permute-start.8) | collective-permute-done | bytes 524320 | tf_op jit(solution)/shard_map/ppermute | solution.py:21
  62.9 0.0 copy-done.1
  62.9 0.3 add_convert_fusion
  63.2 0.0 copy-start.5
  63.2 0.9 fusion.9
  64.1 1.5 %collective-permute-start.9 = (bf16[256,512]{1,0:T(8,128)(2,1)S(1)}, bf16[256,512]{1,0:T(8,128)(2,1)S(1)}, u32[]{:S(2)}, u32[]{:S(2)}) collective-permute-start(bf16[256,512]{1,0:T(8,128)(2,1)S(1)} %get-tuple-element.23), channel_id=1, source_target_pairs={{0,2},{2,0},{1,3},{3,1},{4,6},{6,4},{5,7},{7,5},{8,10},{10,8},{9,1... | collective-permute-start | bytes 786440 | tf_op jit(solution)/shard_map/ppermute | solution.py:26
  65.6 6.8 %collective-permute-done.9 = bf16[256,512]{1,0:T(8,128)(2,1)S(1)} collective-permute-done((bf16[256,512]{1,0:T(8,128)(2,1)S(1)}, bf16[256,512]{1,0:T(8,128)(2,1)S(1)}, u32[]{:S(2)}, u32[]{:S(2)}) %collective-permute-start.9) | collective-permute-done | bytes 262176 | tf_op jit(solution)/shard_map/ppermute | solution.py:26
  72.4 0.8 convolution_multiply_fusion
  73.2 0.0 copy-start
  73.2 1.4 %copy-done = f32[1152,512]{1,0:T(8,128)} copy-done((f32[1152,512]{1,0:T(8,128)}, f32[1152,512]{1,0:T(8,128)S(1)}, u32[]{:S(2)}) %copy-start) | copy-done | bytes 2359320
  74.6 0.1 dynamic-slice_convert_fusion
  74.7 0.1 collective-permute-start.10
  74.8 1.9 %collective-permute-done.10 = bf16[576,512]{1,0:T(8,128)(2,1)S(1)} collective-permute-done((bf16[576,512]{1,0:T(8,128)(2,1)S(1)}, bf16[576,512]{1,0:T(8,128)(2,1)S(1)}, u32[]{:S(2)}, u32[]{:S(2)}) %collective-permute-start.10) | collective-permute-done | bytes 589856 | tf_op jit(solution)/shard_map/ppermute | solution.py:26
  76.8 1.4 %convert_add_fusion = f32[576,512]{1,0:T(8,128)S(1)} fusion(bf16[576,512]{1,0:T(8,128)(2,1)S(1)} %collective-permute-done.10, f32[1152,512]{1,0:T(8,128)} %copy-done, s32[]{:T(128)S(6)} %select_n.90), kind=kLoop, calls=%fused_computation.7 | loop fusion | flops 589824 | bytes 2949124 | tf_op jit(solution)/shard_map/add | solution.py:282
  78.2 0.1 dynamic-slice_convert_fusion.3
  78.3 5.6 %collective-permute-start.11 = (bf16[144,512]{1,0:T(8,128)(2,1)S(1)}, bf16[144,512]{1,0:T(8,128)(2,1)S(1)}, u32[]{:S(2)}, u32[]{:S(2)}) collective-permute-start(bf16[144,512]{1,0:T(8,128)(2,1)S(1)} %get-tuple-element.18), channel_id=1, source_target_pairs={{0,4},{4,8},{8,12},{12,0},{1,5},{5,9},{9,13},{13,1},{2,6},{6,10},{... | collective-permute-start | bytes 442376 | tf_op jit(solution)/shard_map/ppermute | solution.py:26
  83.9 0.0 collective-permute-start.12
  83.9 2.4 %collective-permute-start.13 = (bf16[144,512]{1,0:T(8,128)(2,1)S(1)}, bf16[144,512]{1,0:T(8,128)(2,1)S(1)}, u32[]{:S(2)}, u32[]{:S(2)}) collective-permute-start(bf16[144,512]{1,0:T(8,128)(2,1)S(1)} %get-tuple-element.19), channel_id=1, source_target_pairs={{0,12},{4,0},{8,4},{12,8},{1,13},{5,1},{9,5},{13,9},{2,14},{6,2},{... | collective-permute-start | bytes 442376 | tf_op jit(solution)/shard_map/ppermute | solution.py:26
  86.4 1.8 %collective-permute-done.11 = bf16[144,512]{1,0:T(8,128)(2,1)S(1)} collective-permute-done((bf16[144,512]{1,0:T(8,128)(2,1)S(1)}, bf16[144,512]{1,0:T(8,128)(2,1)S(1)}, u32[]{:S(2)}, u32[]{:S(2)}) %collective-permute-start.11) | collective-permute-done | bytes 147488 | tf_op jit(solution)/shard_map/ppermute | solution.py:26
  88.1 5.3 %collective-permute-done.12 = bf16[144,512]{1,0:T(8,128)(2,1)S(1)} collective-permute-done((bf16[144,512]{1,0:T(8,128)(2,1)S(1)}, bf16[144,512]{1,0:T(8,128)(2,1)S(1)}, u32[]{:S(2)}, u32[]{:S(2)}) %collective-permute-start.12) | collective-permute-done | bytes 147488 | tf_op jit(solution)/shard_map/ppermute | solution.py:26
  93.5 0.2 collective-permute-done.13
  93.7 0.1 broadcast_in_dim.28
  93.8 0.1 fusion.6
  93.9 3.5 %collective-permute-start.14 = (bf16[144,512]{1,0:T(8,128)(2,1)S(1)}, bf16[144,512]{1,0:T(8,128)(2,1)S(1)}, u32[]{:S(2)}, u32[]{:S(2)}) collective-permute-start(bf16[144,512]{1,0:T(8,128)(2,1)S(1)} %get-tuple-element.16), channel_id=1, source_target_pairs={{0,4},{4,8},{8,12},{12,0},{1,5},{5,9},{9,13},{13,1},{2,6},{6,10},{... | collective-permute-start | bytes 442376 | tf_op jit(solution)/shard_map/ppermute | solution.py:26
  97.4 3.4 %collective-permute-start.15 = (bf16[144,512]{1,0:T(8,128)(2,1)S(1)}, bf16[144,512]{1,0:T(8,128)(2,1)S(1)}, u32[]{:S(2)}, u32[]{:S(2)}) collective-permute-start(bf16[144,512]{1,0:T(8,128)(2,1)S(1)} %get-tuple-element.16), channel_id=1, source_target_pairs={{0,8},{4,12},{8,0},{12,4},{1,9},{5,13},{9,1},{13,5},{2,10},{6,14},... | collective-permute-start | bytes 442376 | tf_op jit(solution)/shard_map/ppermute | solution.py:26
  100.8 0.0 collective-permute-start.16
  100.8 4.2 %collective-permute-done.14 = bf16[144,512]{1,0:T(8,128)(2,1)S(1)} collective-permute-done((bf16[144,512]{1,0:T(8,128)(2,1)S(1)}, bf16[144,512]{1,0:T(8,128)(2,1)S(1)}, u32[]{:S(2)}, u32[]{:S(2)}) %collective-permute-start.14) | collective-permute-done | bytes 147488 | tf_op jit(solution)/shard_map/ppermute | solution.py:26
  105.0 5.2 %collective-permute-done.15 = bf16[144,512]{1,0:T(8,128)(2,1)S(1)} collective-permute-done((bf16[144,512]{1,0:T(8,128)(2,1)S(1)}, bf16[144,512]{1,0:T(8,128)(2,1)S(1)}, u32[]{:S(2)}, u32[]{:S(2)}) %collective-permute-start.15) | collective-permute-done | bytes 147488 | tf_op jit(solution)/shard_map/ppermute | solution.py:26
  110.3 0.0 collective-permute-done.16
  110.3 0.1 convert_element_type.78
  110.4 0.1 collective-permute-start.17
  110.5 2.0 %collective-permute-done.17 = bf16[576,512]{1,0:T(8,128)(2,1)S(1)} collective-permute-done((bf16[576,512]{1,0:T(8,128)(2,1)S(1)}, bf16[576,512]{1,0:T(8,128)(2,1)S(1)}, u32[]{:S(2)}, u32[]{:S(2)}) %collective-permute-start.17) | collective-permute-done | bytes 589856 | tf_op jit(solution)/shard_map/ppermute | solution.py:26
  112.5 0.3 convert_select_fusion.1
  112.8 1.6 %pad_maximum_fusion = f32[1152,512]{1,0:T(8,128)} fusion(f32[576,512]{1,0:T(8,128)S(1)} %get-tuple-element.15, f32[576,512]{1,0:T(8,128)S(1)} %get-tuple-element.14), kind=kLoop, calls=%fused_computation.1 | loop fusion | flops 589824 | bytes 4718592 | tf_op jit(solution)/shard_map/concatenate | solution.py:288
  (10 shorter events, 0.1 us)
Async XLA Ops:
  1.7 9.2 %copy-start.2 = (bf16[256,1024]{1,0:T(8,128)(2,1)}, bf16[256,1024]{1,0:T(8,128)(2,1)S(1)}, u32[]{:S(2)}) copy-start(bf16[256,1024]{1,0:T(8,128)(2,1)S(1)} %pad_maximum_fusion.1.refs_8_) | copy-start | bytes 1572868
  1.7 17.2 %collective-permute-start = (bf16[256,1024]{1,0:T(8,128)(2,1)S(1)}, bf16[256,1024]{1,0:T(8,128)(2,1)S(1)}, u32[]{:S(2)}, u32[]{:S(2)}) collective-permute-start(bf16[256,1024]{1,0:T(8,128)(2,1)S(1)} %pad_maximum_fusion.1.refs_8_), channel_id=1, source_target_pairs={{0,4},{4,8},{8,12},{1,5},{5,9},{9,13},{2,6},{6,10},{10,14},{3,7},{... | collective-permute-start | bytes 1572872 | tf_op jit(solution)/shard_map/ppermute | solution.py:21
  6.7 12.3 %copy-start.3 = (s32[1,12]{1,0:T(1,128)S(1)}, s32[1,12]{1,0:T(1,128)}, u32[]{:S(2)}) copy-start(s32[1,12]{1,0:T(1,128)} %param.11) | copy-start | bytes 148
  8.1 14.9 %collective-permute-start.4 = (bf16[256,1152]{1,0:T(8,128)(2,1)S(1)}, bf16[256,1152]{1,0:T(8,128)(2,1)S(1)}, u32[]{:S(2)}, u32[]{:S(2)}) collective-permute-start(bf16[256,1152]{1,0:T(8,128)(2,1)S(1)} %get-tuple-element.22), channel_id=1, source_target_pairs={{0,2},{2,0},{1,3},{3,1},{4,6},{6,4},{5,7},{7,5},{8,10},{10,8},{9,1... | collective-permute-start | bytes 1769480 | tf_op jit(solution)/shard_map/ppermute | solution.py:26
  9.6 10.3 %collective-permute-start.1 = (bf16[256,1024]{1,0:T(8,128)(2,1)S(1)}, bf16[256,1024]{1,0:T(8,128)(2,1)S(1)}, u32[]{:S(2)}, u32[]{:S(2)}) collective-permute-start(bf16[256,1024]{1,0:T(8,128)(2,1)S(1)} %pad_maximum_fusion.1.refs_8_), channel_id=1, source_target_pairs={{0,1},{2,3},{4,5},{6,7},{8,9},{10,11},{12,13},{14,15},{16,17},{18,... | collective-permute-start | bytes 1572872 | tf_op jit(solution)/shard_map/ppermute | solution.py:21
  11.0 9.0 %collective-permute-start.2 = (bf16[256,1024]{1,0:T(8,128)(2,1)S(1)}, bf16[256,1024]{1,0:T(8,128)(2,1)}, u32[]{:S(2)}, u32[]{:S(2)}) collective-permute-start(bf16[256,1024]{1,0:T(8,128)(2,1)S(1)} %pad_maximum_fusion.1.refs_8_), channel_id=1, source_target_pairs={{1,8},{5,12},{3,10},{7,14},{17,24},{21,28},{19,26},{23,30}} | collective-permute-start | bytes 1572872 | tf_op jit(solution)/shard_map/ppermute | solution.py:221
  19.0 4.0 %copy-start.6 = (bf16[256,1024]{1,0:T(8,128)(2,1)}, bf16[256,1024]{1,0:T(8,128)(2,1)S(1)}, u32[]{:S(2)}) copy-start(bf16[256,1024]{1,0:T(8,128)(2,1)S(1)} %collective-permute-done.refs_4_) | copy-start | bytes 1572868
  19.0 4.0 %collective-permute-start.3 = (bf16[256,1024]{1,0:T(8,128)(2,1)S(1)}, bf16[256,1024]{1,0:T(8,128)(2,1)}, u32[]{:S(2)}, u32[]{:S(2)}) collective-permute-start(bf16[256,1024]{1,0:T(8,128)(2,1)S(1)} %collective-permute-done.refs_4_), channel_id=1, source_target_pairs={{0,1},{1,0},{2,3},{3,2},{4,5},{5,4},{6,7},{7,6},{8,9},{9,8},{10,11... | collective-permute-start | bytes 1572872 | tf_op jit(solution)/shard_map/ppermute | solution.py:26
  19.9 3.0 %copy-start.7 = (bf16[256,1024]{1,0:T(8,128)(2,1)}, bf16[256,1024]{1,0:T(8,128)(2,1)S(1)}, u32[]{:S(2)}) copy-start(bf16[256,1024]{1,0:T(8,128)(2,1)S(1)} %collective-permute-done.1.refs_5_) | copy-start | bytes 1572868
  22.9 0.8 copy-start.4
  35.0 27.9 %copy-start.1 = (f32[256,1024]{1,0:T(8,128)S(1)}, f32[256,1024]{1,0:T(8,128)}, u32[]{:S(2)}) copy-start(f32[256,1024]{1,0:T(8,128)} %get-tuple-element.10) | copy-start | bytes 3145732
  35.0 2.7 %collective-permute-start.7 = (bf16[256,1024]{1,0:T(8,128)(2,1)}, bf16[256,1024]{1,0:T(8,128)(2,1)S(1)}, u32[]{:S(2)}, u32[]{:S(2)}) collective-permute-start(bf16[256,1024]{1,0:T(8,128)(2,1)} %get-tuple-element.13), channel_id=1, source_target_pairs={{0,1},{1,0},{2,3},{3,2},{4,5},{5,4},{6,7},{7,6},{8,9},{9,8},{10,11... | collective-permute-start | bytes 1572872 | tf_op jit(solution)/shard_map/ppermute | solution.py:26
  35.7 4.7 %collective-permute-start.5 = (bf16[256,1024]{1,0:T(8,128)(2,1)}, bf16[256,1024]{1,0:T(8,128)(2,1)S(1)}, u32[]{:S(2)}, u32[]{:S(2)}) collective-permute-start(bf16[256,1024]{1,0:T(8,128)(2,1)} %get-tuple-element.11), channel_id=1, source_target_pairs={{1,0},{3,2},{5,4},{7,6},{9,8},{11,10},{13,12},{15,14},{17,16},{19,... | collective-permute-start | bytes 1572872 | tf_op jit(solution)/shard_map/ppermute | solution.py:21
  37.0 3.4 %collective-permute-start.6 = (bf16[256,1024]{1,0:T(8,128)(2,1)}, bf16[256,1024]{1,0:T(8,128)(2,1)S(1)}, u32[]{:S(2)}, u32[]{:S(2)}) collective-permute-start(bf16[256,1024]{1,0:T(8,128)(2,1)} %get-tuple-element.11), channel_id=1, source_target_pairs={{8,1},{12,5},{10,3},{14,7},{24,17},{28,21},{26,19},{30,23}} | collective-permute-start | bytes 1572872 | tf_op jit(solution)/shard_map/ppermute | solution.py:245
  39.1 23.8 %collective-permute-start.8 = (bf16[256,1024]{1,0:T(8,128)(2,1)S(1)}, bf16[256,1024]{1,0:T(8,128)(2,1)S(1)}, u32[]{:S(2)}, u32[]{:S(2)}) collective-permute-start(bf16[256,1024]{1,0:T(8,128)(2,1)S(1)} %add_convert_fusion.1), channel_id=1, source_target_pairs={{4,0},{8,4},{12,8},{5,1},{9,5},{13,9},{6,2},{10,6},{14,10},{7,3},{... | collective-permute-start | bytes 1572872 | tf_op jit(solution)/shard_map/ppermute | solution.py:21
  63.2 9.2 %copy-start.5 = (bf16[256,1152]{1,0:T(8,128)(2,1)S(1)}, bf16[256,1152]{1,0:T(8,128)(2,1)}, u32[]{:S(2)}) copy-start(bf16[256,1152]{1,0:T(8,128)(2,1)} %copy-done.4) | copy-start | bytes 1769476
  64.1 8.3 %collective-permute-start.9 = (bf16[256,512]{1,0:T(8,128)(2,1)S(1)}, bf16[256,512]{1,0:T(8,128)(2,1)S(1)}, u32[]{:S(2)}, u32[]{:S(2)}) collective-permute-start(bf16[256,512]{1,0:T(8,128)(2,1)S(1)} %get-tuple-element.23), channel_id=1, source_target_pairs={{0,2},{2,0},{1,3},{3,1},{4,6},{6,4},{5,7},{7,5},{8,10},{10,8},{9,1... | collective-permute-start | bytes 786440 | tf_op jit(solution)/shard_map/ppermute | solution.py:26
  73.2 1.4 %copy-start = (f32[1152,512]{1,0:T(8,128)}, f32[1152,512]{1,0:T(8,128)S(1)}, u32[]{:S(2)}) copy-start(f32[1152,512]{1,0:T(8,128)S(1)} %convolution_multiply_fusion) | copy-start | bytes 7077892
  74.7 2.1 %collective-permute-start.10 = (bf16[576,512]{1,0:T(8,128)(2,1)S(1)}, bf16[576,512]{1,0:T(8,128)(2,1)S(1)}, u32[]{:S(2)}, u32[]{:S(2)}) collective-permute-start(bf16[576,512]{1,0:T(8,128)(2,1)S(1)} %dynamic-slice_convert_fusion), channel_id=1, source_target_pairs={{0,1},{1,0},{2,3},{3,2},{4,5},{5,4},{6,7},{7,6},{8,9},{9,8},{10,11... | collective-permute-start | bytes 1769480 | tf_op jit(solution)/shard_map/ppermute | solution.py:26
  78.3 9.8 %collective-permute-start.11 = (bf16[144,512]{1,0:T(8,128)(2,1)S(1)}, bf16[144,512]{1,0:T(8,128)(2,1)S(1)}, u32[]{:S(2)}, u32[]{:S(2)}) collective-permute-start(bf16[144,512]{1,0:T(8,128)(2,1)S(1)} %get-tuple-element.18), channel_id=1, source_target_pairs={{0,4},{4,8},{8,12},{12,0},{1,5},{5,9},{9,13},{13,1},{2,6},{6,10},{... | collective-permute-start | bytes 442376 | tf_op jit(solution)/shard_map/ppermute | solution.py:26
  83.9 9.6 %collective-permute-start.12 = (bf16[144,512]{1,0:T(8,128)(2,1)S(1)}, bf16[144,512]{1,0:T(8,128)(2,1)S(1)}, u32[]{:S(2)}, u32[]{:S(2)}) collective-permute-start(bf16[144,512]{1,0:T(8,128)(2,1)S(1)} %get-tuple-element.20), channel_id=1, source_target_pairs={{0,8},{4,12},{8,0},{12,4},{1,9},{5,13},{9,1},{13,5},{2,10},{6,14},... | collective-permute-start | bytes 442376 | tf_op jit(solution)/shard_map/ppermute | solution.py:26
  83.9 9.8 %collective-permute-start.13 = (bf16[144,512]{1,0:T(8,128)(2,1)S(1)}, bf16[144,512]{1,0:T(8,128)(2,1)S(1)}, u32[]{:S(2)}, u32[]{:S(2)}) collective-permute-start(bf16[144,512]{1,0:T(8,128)(2,1)S(1)} %get-tuple-element.19), channel_id=1, source_target_pairs={{0,12},{4,0},{8,4},{12,8},{1,13},{5,1},{9,5},{13,9},{2,14},{6,2},{... | collective-permute-start | bytes 442376 | tf_op jit(solution)/shard_map/ppermute | solution.py:26
  93.9 11.1 %collective-permute-start.14 = (bf16[144,512]{1,0:T(8,128)(2,1)S(1)}, bf16[144,512]{1,0:T(8,128)(2,1)S(1)}, u32[]{:S(2)}, u32[]{:S(2)}) collective-permute-start(bf16[144,512]{1,0:T(8,128)(2,1)S(1)} %get-tuple-element.16), channel_id=1, source_target_pairs={{0,4},{4,8},{8,12},{12,0},{1,5},{5,9},{9,13},{13,1},{2,6},{6,10},{... | collective-permute-start | bytes 442376 | tf_op jit(solution)/shard_map/ppermute | solution.py:26
  97.4 12.9 %collective-permute-start.15 = (bf16[144,512]{1,0:T(8,128)(2,1)S(1)}, bf16[144,512]{1,0:T(8,128)(2,1)S(1)}, u32[]{:S(2)}, u32[]{:S(2)}) collective-permute-start(bf16[144,512]{1,0:T(8,128)(2,1)S(1)} %get-tuple-element.16), channel_id=1, source_target_pairs={{0,8},{4,12},{8,0},{12,4},{1,9},{5,13},{9,1},{13,5},{2,10},{6,14},... | collective-permute-start | bytes 442376 | tf_op jit(solution)/shard_map/ppermute | solution.py:26
  100.8 9.5 %collective-permute-start.16 = (bf16[144,512]{1,0:T(8,128)(2,1)S(1)}, bf16[144,512]{1,0:T(8,128)(2,1)S(1)}, u32[]{:S(2)}, u32[]{:S(2)}) collective-permute-start(bf16[144,512]{1,0:T(8,128)(2,1)S(1)} %get-tuple-element.16), channel_id=1, source_target_pairs={{0,12},{4,0},{8,4},{12,8},{1,13},{5,1},{9,5},{13,9},{2,14},{6,2},{... | collective-permute-start | bytes 442376 | tf_op jit(solution)/shard_map/ppermute | solution.py:26
  110.4 2.1 %collective-permute-start.17 = (bf16[576,512]{1,0:T(8,128)(2,1)S(1)}, bf16[576,512]{1,0:T(8,128)(2,1)S(1)}, u32[]{:S(2)}, u32[]{:S(2)}) collective-permute-start(bf16[576,512]{1,0:T(8,128)(2,1)S(1)} %convert_element_type.78), channel_id=1, source_target_pairs={{0,1},{1,0},{2,3},{3,2},{4,5},{5,4},{6,7},{7,6},{8,9},{9,8},{10,11... | collective-permute-start | bytes 1769480 | tf_op jit(solution)/shard_map/ppermute | solution.py:26

commit v16 on v7

--- a/solution.py
+++ b/solution.py
@@ -53,8 +53,8 @@
 def attention_kernel(*refs, heads, kv_heads, margin, slots, blocks, chip_outputs):
     flag_ref, lo_ref, q_ref, do_ref = refs[:4]
     block_refs = refs[4 : 4 + blocks]
-    kv_ref, dkv_ref = refs[-2:]
-    outs = refs[-3 - len(slots) : -2]
+    kv_ref = refs[-1]
+    outs = refs[-2 - len(slots) : -1]
     dq_ref = outs[0]
     out_refs = outs[1:]
     block_rows = block_refs[0].shape[0]
@@ -81,6 +81,27 @@
     col = lax.broadcasted_iota(jnp.int32, (rows, keys), 1)
     row = lax.broadcasted_iota(jnp.int32, (rows, keys), 0)
     allowed = (col >= lo_ref[...]) & (col <= row + margin)
+
+    def emit(cols, full):
+        pieces = [full[index * block_rows : (index + 1) * block_rows] for index in range(len(slots))]
+        if not chip_outputs:
+            for out_ref, piece in zip(out_refs, pieces):
+                out_ref[:, cols] = piece
+            return
+        mate_ref, other_ref, two_ref, own_ref = out_refs
+        two_ref[:, cols] = pieces[1]
+        own_ref[:, cols] = pieces[3]
+
+        @pl.when(flag == 0)
+        def _():
+            mate_ref[:, cols] = pieces[2].astype(mate_ref.dtype)
+            other_ref[:, cols] = pieces[0].astype(other_ref.dtype)
+
+        @pl.when(flag != 0)
+        def _():
+            mate_ref[:, cols] = pieces[0].astype(mate_ref.dtype)
+            other_ref[:, cols] = pieces[2].astype(other_ref.dtype)
+
     for group in range(kv_heads):
         k_cols = pl.ds(group * HEAD_DIM, HEAD_DIM)
         v_cols = pl.ds(kv_width + group * HEAD_DIM, HEAD_DIM)
@@ -108,29 +129,8 @@
             term_v = lax.dot_general(probs_low, grad_h, TN, preferred_element_type=jnp.float32)
             grad_k = term_k if grad_k is None else grad_k + term_k
             grad_v = term_v if grad_v is None else grad_v + term_v
-        dkv_ref[:, k_cols] = grad_k
-        dkv_ref[:, v_cols] = grad_v
-    def slot_rows(index):
-        return dkv_ref[pl.ds(index * block_rows, block_rows), :]
-
-    if chip_outputs:
-        mate_ref, other_ref, two_ref, own_ref = out_refs
-        two_ref[...] = slot_rows(1)
-        own_ref[...] = slot_rows(3)
-
-        @pl.when(flag == 0)
-        def _():
-            mate_ref[...] = slot_rows(2).astype(mate_ref.dtype)
-            other_ref[...] = slot_rows(0).astype(other_ref.dtype)
-
-        @pl.when(flag != 0)
-        def _():
-            mate_ref[...] = slot_rows(0).astype(mate_ref.dtype)
-            other_ref[...] = slot_rows(2).astype(other_ref.dtype)
-
-    else:
-        for index, out_ref in enumerate(out_refs):
-            out_ref[...] = slot_rows(index)
+        emit(k_cols, grad_k)
+        emit(v_cols, grad_v)
 
 
 def attention(
@@ -163,10 +163,7 @@
         + tuple(jax.ShapeDtypeStruct((block_rows, kv_cols), kind) for kind in piece_types),
         in_specs=[smem] + [vmem] * (3 + blocks) + [pl.BlockSpec(memory_space=pl.ANY)] * len(early),
         out_specs=(vmem,) * (1 + len(slots)),
-        scratch_shapes=[
-            pltpu.VMEM((keys, kv_cols), kv_blocks[0].dtype),
-            pltpu.VMEM((keys, kv_cols), jnp.float32),
-        ],
+        scratch_shapes=[pltpu.VMEM((keys, kv_cols), kv_blocks[0].dtype)],
         cost_estimate=pl.CostEstimate(
             flops=flops, transcendentals=heads * rows * keys, bytes_accessed=moved
         ),

time: 113 us -> 114 us (level)
  no operation moved by 1% of the time
where the time goes in v16:
time: 114 us; the launch traced here: 112 us
  waiting for transfers between devices  59.6 us (52%)
  starting transfers between devices  29.8 us (26%)
  Pallas kernels  9.19 us (8%)
  other arithmetic  7.16 us (6%)
  local copies, waits for them, and re-layouts  4.83 us (4%)
    ppermute x12, waiting for transfers between devices, rotated(): lax.ppermute(value, axis, [(source, (source + steps) % count) for source...  30.5 us
    ppermute x4, waiting for transfers between devices, passed_along(): lax.ppermute(value, axis, [(source, source + steps) for source in range(f...  29 us
    ppermute x12, starting transfers between devices, rotated(): lax.ppermute(value, axis, [(source, (source + steps) % count) for source...  18.8 us
    pallas_call x1, Pallas kernels, attention(): pl.pallas_call(kernel, out_shape=(jax.ShapeDtypeStruct((rows, width), jnp...  9.19 us
    ppermute x4, starting transfers between devices, passed_along(): lax.ppermute(value, axis, [(source, source + steps) for source in range(f...  8.84 us
  transfers between devices with their start and end apart: 18, of which 11 were waited for; matrix products, arithmetic and copies ran while one was open for 3% of the time, Pallas kernels for 0%

profile of v16, /device:TPU:0, one launch (start us, length us, event | category | flops | bytes accessed | tf_op | source)
XLA Modules:
  0.0 112.4 jit_solution(15553379760674196845)
XLA Ops:
  0.6 1.1 pad_maximum_fusion.1.refs_8_
  1.7 0.0 copy-start.2
  1.7 5.0 %collective-permute-start = (bf16[256,1024]{1,0:T(8,128)(2,1)S(1)}, bf16[256,1024]{1,0:T(8,128)(2,1)S(1)}, u32[]{:S(2)}, u32[]{:S(2)}) collective-permute-start(bf16[256,1024]{1,0:T(8,128)(2,1)S(1)} %pad_maximum_fusion.1.refs_8_), channel_id=1, source_target_pairs={{0,4},{4,8},{8,12},{1,5},{5,9},{9,13},{2,6},{6,10},{10,14},{3,7},{... | collective-permute-start | bytes 1572872 | tf_op jit(solution)/shard_map/ppermute | solution.py:21
  6.7 0.0 copy-start.3
  6.7 1.3 %dynamic-slice_bitcast_fusion = (bf16[256,1152]{1,0:T(8,128)(2,1)S(1)}, bf16[256,1152]{1,0:T(8,128)(2,1)S(1)}) fusion(bf16[1,256,2304]{2,1,0:T(8,128)(2,1)} %param.6, s32[]{:T(128)S(6)} %select_n.89, s32[]{:T(128)S(6)} %select_n.87), kind=kLoop, calls=%fused_computation.11 | loop fusion | bytes 2359304 | tf_op jit(solution)/shard_map/dynamic_slice | solution.py:188
  8.1 1.6 %collective-permute-start.4 = (bf16[256,1152]{1,0:T(8,128)(2,1)S(1)}, bf16[256,1152]{1,0:T(8,128)(2,1)S(1)}, u32[]{:S(2)}, u32[]{:S(2)}) collective-permute-start(bf16[256,1152]{1,0:T(8,128)(2,1)S(1)} %get-tuple-element.22), channel_id=1, source_target_pairs={{0,2},{2,0},{1,3},{3,1},{4,6},{6,4},{5,7},{7,5},{8,10},{10,8},{9,1... | collective-permute-start | bytes 1769480 | tf_op jit(solution)/shard_map/ppermute | solution.py:26
  9.6 1.3 %collective-permute-start.1 = (bf16[256,1024]{1,0:T(8,128)(2,1)S(1)}, bf16[256,1024]{1,0:T(8,128)(2,1)S(1)}, u32[]{:S(2)}, u32[]{:S(2)}) collective-permute-start(bf16[256,1024]{1,0:T(8,128)(2,1)S(1)} %pad_maximum_fusion.1.refs_8_), channel_id=1, source_target_pairs={{0,1},{2,3},{4,5},{6,7},{8,9},{10,11},{12,13},{14,15},{16,17},{18,... | collective-permute-start | bytes 1572872 | tf_op jit(solution)/shard_map/ppermute | solution.py:21
  10.9 0.0 copy-done.2
  11.0 1.5 %collective-permute-start.2 = (bf16[256,1024]{1,0:T(8,128)(2,1)S(1)}, bf16[256,1024]{1,0:T(8,128)(2,1)}, u32[]{:S(2)}, u32[]{:S(2)}) collective-permute-start(bf16[256,1024]{1,0:T(8,128)(2,1)S(1)} %pad_maximum_fusion.1.refs_8_), channel_id=1, source_target_pairs={{1,8},{5,12},{3,10},{7,14},{17,24},{21,28},{19,26},{23,30}} | collective-permute-start | bytes 1572872 | tf_op jit(solution)/shard_map/ppermute | solution.py:207
  12.4 6.5 %collective-permute-done.refs_4_ = bf16[256,1024]{1,0:T(8,128)(2,1)S(1)} collective-permute-done((bf16[256,1024]{1,0:T(8,128)(2,1)S(1)}, bf16[256,1024]{1,0:T(8,128)(2,1)S(1)}, u32[]{:S(2)}, u32[]{:S(2)}) %collective-permute-start) | collective-permute-done | bytes 524320 | tf_op jit(solution)/shard_map/ppermute | solution.py:21
  19.0 0.0 collective-permute-start.3
  19.0 0.0 copy-done.3
  19.0 0.1 select_reduce_fusion
  19.1 0.1 copy.13
  19.2 0.7 subtract_add_fusion.refs_1_
  19.9 0.0 collective-permute-done.1.refs_5_
  19.9 0.0 collective-permute-done.2.refs_6_
  19.9 3.0 %collective-permute-done.4.refs_9_ = bf16[256,1152]{1,0:T(8,128)(2,1)S(1)} collective-permute-done((bf16[256,1152]{1,0:T(8,128)(2,1)S(1)}, bf16[256,1152]{1,0:T(8,128)(2,1)S(1)}, u32[]{:S(2)}, u32[]{:S(2)}) %collective-permute-start.4) | collective-permute-done | bytes 589856 | tf_op jit(solution)/shard_map/ppermute | solution.py:26
  22.9 0.0 collective-permute-done.3.refs_7_
  22.9 0.0 copy-done.6
  22.9 0.0 copy-done.7
  22.9 0.8 copy-done.4
  23.7 9.2 %shard_map.93 = (bf16[256,1024]{1,0:T(8,128)(2,1)}, bf16[256,1024]{1,0:T(8,128)(2,1)}, bf16[256,1024]{1,0:T(8,128)(2,1)}, f32[256,1024]{1,0:T(8,128)}, f32[256,1024]{1,0:T(8,128)}) custom-call(s32[1]{0:T(128)} %bitcast.refs_0_, s32[256,1]{1,0:T(8,128)} %subtract_add_fusion.refs_1_, bf16[256,1024]{1,0:T(8,128)(2,1)} %bitcast.20, bf16[256,1024]{1,0:T(8,128)(2,1)} %bitcast.21, ...), custom_call_target="tpu_custom_call" | custom-call | flops 2684354560 | bytes 7864320 | tf_op jit(solution)/shard_map/pallas_call | solution.py:160
  32.9 0.7 collective-permute-start.7
  33.6 1.3 %collective-permute-start.5 = (bf16[256,1024]{1,0:T(8,128)(2,1)}, bf16[256,1024]{1,0:T(8,128)(2,1)S(1)}, u32[]{:S(2)}, u32[]{:S(2)}) collective-permute-start(bf16[256,1024]{1,0:T(8,128)(2,1)} %get-tuple-element.11), channel_id=1, source_target_pairs={{1,0},{3,2},{5,4},{7,6},{9,8},{11,10},{13,12},{15,14},{17,16},{19,... | collective-permute-start | bytes 1572872 | tf_op jit(solution)/shard_map/ppermute | solution.py:21
  34.9 0.7 collective-permute-start.6
  35.6 0.0 collective-permute-done.7
  35.6 1.4 %add_convert_fusion.1 = bf16[256,1024]{1,0:T(8,128)(2,1)S(1)} fusion(f32[256,1024]{1,0:T(8,128)} %get-tuple-element.12, bf16[256,1024]{1,0:T(8,128)(2,1)S(1)} %collective-permute-done.7), kind=kLoop, calls=%fused_computation.10 | loop fusion | flops 786432 | bytes 2097152 | tf_op jit(solution)/shard_map/convert_element_type | solution.py:226
  37.0 1.3 %collective-permute-start.8 = (bf16[256,1024]{1,0:T(8,128)(2,1)S(1)}, bf16[256,1024]{1,0:T(8,128)(2,1)S(1)}, u32[]{:S(2)}, u32[]{:S(2)}) collective-permute-start(bf16[256,1024]{1,0:T(8,128)(2,1)S(1)} %add_convert_fusion.1), channel_id=1, source_target_pairs={{4,0},{8,4},{12,8},{5,1},{9,5},{13,9},{6,2},{10,6},{14,10},{7,3},{... | collective-permute-start | bytes 1572872 | tf_op jit(solution)/shard_map/ppermute | solution.py:21
  38.3 0.0 collective-permute-done.5
  38.3 0.0 collective-permute-done.6
  38.3 22.5 %collective-permute-done.8 = bf16[256,1024]{1,0:T(8,128)(2,1)S(1)} collective-permute-done((bf16[256,1024]{1,0:T(8,128)(2,1)S(1)}, bf16[256,1024]{1,0:T(8,128)(2,1)S(1)}, u32[]{:S(2)}, u32[]{:S(2)}) %collective-permute-start.8) | collective-permute-done | bytes 524320 | tf_op jit(solution)/shard_map/ppermute | solution.py:21
  60.8 0.0 copy-done.1
  60.8 0.3 add_convert_fusion
  61.2 0.9 fusion.9
  62.0 1.5 %collective-permute-start.9 = (bf16[256,512]{1,0:T(8,128)(2,1)S(1)}, bf16[256,512]{1,0:T(8,128)(2,1)S(1)}, u32[]{:S(2)}, u32[]{:S(2)}) collective-permute-start(bf16[256,512]{1,0:T(8,128)(2,1)S(1)} %get-tuple-element.23), channel_id=1, source_target_pairs={{0,2},{2,0},{1,3},{3,1},{4,6},{6,4},{5,7},{7,5},{8,10},{10,8},{9,1... | collective-permute-start | bytes 786440 | tf_op jit(solution)/shard_map/ppermute | solution.py:26
  63.5 6.8 %collective-permute-done.9 = bf16[256,512]{1,0:T(8,128)(2,1)S(1)} collective-permute-done((bf16[256,512]{1,0:T(8,128)(2,1)S(1)}, bf16[256,512]{1,0:T(8,128)(2,1)S(1)}, u32[]{:S(2)}, u32[]{:S(2)}) %collective-permute-start.9) | collective-permute-done | bytes 262176 | tf_op jit(solution)/shard_map/ppermute | solution.py:26
  70.3 0.8 convolution_multiply_fusion
  71.2 0.0 copy-start
  71.2 1.4 %copy-done = f32[1152,512]{1,0:T(8,128)} copy-done((f32[1152,512]{1,0:T(8,128)}, f32[1152,512]{1,0:T(8,128)S(1)}, u32[]{:S(2)}) %copy-start) | copy-done | bytes 2359320
  72.6 0.1 dynamic-slice_convert_fusion
  72.6 0.1 collective-permute-start.10
  72.8 1.9 %collective-permute-done.10 = bf16[576,512]{1,0:T(8,128)(2,1)S(1)} collective-permute-done((bf16[576,512]{1,0:T(8,128)(2,1)S(1)}, bf16[576,512]{1,0:T(8,128)(2,1)S(1)}, u32[]{:S(2)}, u32[]{:S(2)}) %collective-permute-start.10) | collective-permute-done | bytes 589856 | tf_op jit(solution)/shard_map/ppermute | solution.py:26
  74.7 1.4 %convert_add_fusion = f32[576,512]{1,0:T(8,128)S(1)} fusion(bf16[576,512]{1,0:T(8,128)(2,1)S(1)} %collective-permute-done.10, f32[1152,512]{1,0:T(8,128)} %copy-done, s32[]{:T(128)S(6)} %select_n.90), kind=kLoop, calls=%fused_computation.7 | loop fusion | flops 589824 | bytes 2949124 | tf_op jit(solution)/shard_map/add | solution.py:268
  76.2 0.1 dynamic-slice_convert_fusion.3
  76.2 5.6 %collective-permute-start.11 = (bf16[144,512]{1,0:T(8,128)(2,1)S(1)}, bf16[144,512]{1,0:T(8,128)(2,1)S(1)}, u32[]{:S(2)}, u32[]{:S(2)}) collective-permute-start(bf16[144,512]{1,0:T(8,128)(2,1)S(1)} %get-tuple-element.18), channel_id=1, source_target_pairs={{0,4},{4,8},{8,12},{12,0},{1,5},{5,9},{9,13},{13,1},{2,6},{6,10},{... | collective-permute-start | bytes 442376 | tf_op jit(solution)/shard_map/ppermute | solution.py:26
  81.9 0.0 collective-permute-start.12
  81.9 2.4 %collective-permute-start.13 = (bf16[144,512]{1,0:T(8,128)(2,1)S(1)}, bf16[144,512]{1,0:T(8,128)(2,1)S(1)}, u32[]{:S(2)}, u32[]{:S(2)}) collective-permute-start(bf16[144,512]{1,0:T(8,128)(2,1)S(1)} %get-tuple-element.19), channel_id=1, source_target_pairs={{0,12},{4,0},{8,4},{12,8},{1,13},{5,1},{9,5},{13,9},{2,14},{6,2},{... | collective-permute-start | bytes 442376 | tf_op jit(solution)/shard_map/ppermute | solution.py:26
  84.3 1.8 %collective-permute-done.11 = bf16[144,512]{1,0:T(8,128)(2,1)S(1)} collective-permute-done((bf16[144,512]{1,0:T(8,128)(2,1)S(1)}, bf16[144,512]{1,0:T(8,128)(2,1)S(1)}, u32[]{:S(2)}, u32[]{:S(2)}) %collective-permute-start.11) | collective-permute-done | bytes 147488 | tf_op jit(solution)/shard_map/ppermute | solution.py:26
  86.1 5.3 %collective-permute-done.12 = bf16[144,512]{1,0:T(8,128)(2,1)S(1)} collective-permute-done((bf16[144,512]{1,0:T(8,128)(2,1)S(1)}, bf16[144,512]{1,0:T(8,128)(2,1)S(1)}, u32[]{:S(2)}, u32[]{:S(2)}) %collective-permute-start.12) | collective-permute-done | bytes 147488 | tf_op jit(solution)/shard_map/ppermute | solution.py:26
  91.4 0.2 collective-permute-done.13
  91.7 0.1 broadcast_in_dim.28
  91.8 0.1 fusion.6
  91.9 3.5 %collective-permute-start.14 = (bf16[144,512]{1,0:T(8,128)(2,1)S(1)}, bf16[144,512]{1,0:T(8,128)(2,1)S(1)}, u32[]{:S(2)}, u32[]{:S(2)}) collective-permute-start(bf16[144,512]{1,0:T(8,128)(2,1)S(1)} %get-tuple-element.16), channel_id=1, source_target_pairs={{0,4},{4,8},{8,12},{12,0},{1,5},{5,9},{9,13},{13,1},{2,6},{6,10},{... | collective-permute-start | bytes 442376 | tf_op jit(solution)/shard_map/ppermute | solution.py:26
  95.4 3.4 %collective-permute-start.15 = (bf16[144,512]{1,0:T(8,128)(2,1)S(1)}, bf16[144,512]{1,0:T(8,128)(2,1)S(1)}, u32[]{:S(2)}, u32[]{:S(2)}) collective-permute-start(bf16[144,512]{1,0:T(8,128)(2,1)S(1)} %get-tuple-element.16), channel_id=1, source_target_pairs={{0,8},{4,12},{8,0},{12,4},{1,9},{5,13},{9,1},{13,5},{2,10},{6,14},... | collective-permute-start | bytes 442376 | tf_op jit(solution)/shard_map/ppermute | solution.py:26
  98.7 0.0 collective-permute-start.16
  98.7 4.2 %collective-permute-done.14 = bf16[144,512]{1,0:T(8,128)(2,1)S(1)} collective-permute-done((bf16[144,512]{1,0:T(8,128)(2,1)S(1)}, bf16[144,512]{1,0:T(8,128)(2,1)S(1)}, u32[]{:S(2)}, u32[]{:S(2)}) %collective-permute-start.14) | collective-permute-done | bytes 147488 | tf_op jit(solution)/shard_map/ppermute | solution.py:26
  103.0 5.2 %collective-permute-done.15 = bf16[144,512]{1,0:T(8,128)(2,1)S(1)} collective-permute-done((bf16[144,512]{1,0:T(8,128)(2,1)S(1)}, bf16[144,512]{1,0:T(8,128)(2,1)S(1)}, u32[]{:S(2)}, u32[]{:S(2)}) %collective-permute-start.15) | collective-permute-done | bytes 147488 | tf_op jit(solution)/shard_map/ppermute | solution.py:26
  108.2 0.0 collective-permute-done.16
  108.3 0.1 convert_element_type.78
  108.4 0.1 collective-permute-start.17
  108.5 2.0 %collective-permute-done.17 = bf16[576,512]{1,0:T(8,128)(2,1)S(1)} collective-permute-done((bf16[576,512]{1,0:T(8,128)(2,1)S(1)}, bf16[576,512]{1,0:T(8,128)(2,1)S(1)}, u32[]{:S(2)}, u32[]{:S(2)}) %collective-permute-start.17) | collective-permute-done | bytes 589856 | tf_op jit(solution)/shard_map/ppermute | solution.py:26
  110.4 0.3 convert_select_fusion.1
  110.8 1.6 %pad_maximum_fusion = f32[1152,512]{1,0:T(8,128)} fusion(f32[576,512]{1,0:T(8,128)S(1)} %get-tuple-element.15, f32[576,512]{1,0:T(8,128)S(1)} %get-tuple-element.14), kind=kLoop, calls=%fused_computation.1 | loop fusion | flops 589824 | bytes 4718592 | tf_op jit(solution)/shard_map/concatenate | solution.py:274
  (10 shorter events, 0.1 us)
Async XLA Ops:
  1.7 9.2 %copy-start.2 = (bf16[256,1024]{1,0:T(8,128)(2,1)}, bf16[256,1024]{1,0:T(8,128)(2,1)S(1)}, u32[]{:S(2)}) copy-start(bf16[256,1024]{1,0:T(8,128)(2,1)S(1)} %pad_maximum_fusion.1.refs_8_) | copy-start | bytes 1572868
  1.7 17.2 %collective-permute-start = (bf16[256,1024]{1,0:T(8,128)(2,1)S(1)}, bf16[256,1024]{1,0:T(8,128)(2,1)S(1)}, u32[]{:S(2)}, u32[]{:S(2)}) collective-permute-start(bf16[256,1024]{1,0:T(8,128)(2,1)S(1)} %pad_maximum_fusion.1.refs_8_), channel_id=1, source_target_pairs={{0,4},{4,8},{8,12},{1,5},{5,9},{9,13},{2,6},{6,10},{10,14},{3,7},{... | collective-permute-start | bytes 1572872 | tf_op jit(solution)/shard_map/ppermute | solution.py:21
  6.7 12.3 %copy-start.3 = (s32[1,12]{1,0:T(1,128)S(1)}, s32[1,12]{1,0:T(1,128)}, u32[]{:S(2)}) copy-start(s32[1,12]{1,0:T(1,128)} %param.11) | copy-start | bytes 148
  8.1 14.9 %collective-permute-start.4 = (bf16[256,1152]{1,0:T(8,128)(2,1)S(1)}, bf16[256,1152]{1,0:T(8,128)(2,1)S(1)}, u32[]{:S(2)}, u32[]{:S(2)}) collective-permute-start(bf16[256,1152]{1,0:T(8,128)(2,1)S(1)} %get-tuple-element.22), channel_id=1, source_target_pairs={{0,2},{2,0},{1,3},{3,1},{4,6},{6,4},{5,7},{7,5},{8,10},{10,8},{9,1... | collective-permute-start | bytes 1769480 | tf_op jit(solution)/shard_map/ppermute | solution.py:26
  9.6 10.3 %collective-permute-start.1 = (bf16[256,1024]{1,0:T(8,128)(2,1)S(1)}, bf16[256,1024]{1,0:T(8,128)(2,1)S(1)}, u32[]{:S(2)}, u32[]{:S(2)}) collective-permute-start(bf16[256,1024]{1,0:T(8,128)(2,1)S(1)} %pad_maximum_fusion.1.refs_8_), channel_id=1, source_target_pairs={{0,1},{2,3},{4,5},{6,7},{8,9},{10,11},{12,13},{14,15},{16,17},{18,... | collective-permute-start | bytes 1572872 | tf_op jit(solution)/shard_map/ppermute | solution.py:21
  11.0 9.0 %collective-permute-start.2 = (bf16[256,1024]{1,0:T(8,128)(2,1)S(1)}, bf16[256,1024]{1,0:T(8,128)(2,1)}, u32[]{:S(2)}, u32[]{:S(2)}) collective-permute-start(bf16[256,1024]{1,0:T(8,128)(2,1)S(1)} %pad_maximum_fusion.1.refs_8_), channel_id=1, source_target_pairs={{1,8},{5,12},{3,10},{7,14},{17,24},{21,28},{19,26},{23,30}} | collective-permute-start | bytes 1572872 | tf_op jit(solution)/shard_map/ppermute | solution.py:207
  19.0 4.0 %copy-start.6 = (bf16[256,1024]{1,0:T(8,128)(2,1)}, bf16[256,1024]{1,0:T(8,128)(2,1)S(1)}, u32[]{:S(2)}) copy-start(bf16[256,1024]{1,0:T(8,128)(2,1)S(1)} %collective-permute-done.refs_4_) | copy-start | bytes 1572868
  19.0 4.0 %collective-permute-start.3 = (bf16[256,1024]{1,0:T(8,128)(2,1)S(1)}, bf16[256,1024]{1,0:T(8,128)(2,1)}, u32[]{:S(2)}, u32[]{:S(2)}) collective-permute-start(bf16[256,1024]{1,0:T(8,128)(2,1)S(1)} %collective-permute-done.refs_4_), channel_id=1, source_target_pairs={{0,1},{1,0},{2,3},{3,2},{4,5},{5,4},{6,7},{7,6},{8,9},{9,8},{10,11... | collective-permute-start | bytes 1572872 | tf_op jit(solution)/shard_map/ppermute | solution.py:26
  19.9 3.0 %copy-start.7 = (bf16[256,1024]{1,0:T(8,128)(2,1)}, bf16[256,1024]{1,0:T(8,128)(2,1)S(1)}, u32[]{:S(2)}) copy-start(bf16[256,1024]{1,0:T(8,128)(2,1)S(1)} %collective-permute-done.1.refs_5_) | copy-start | bytes 1572868
  22.9 0.8 copy-start.4
  32.9 27.9 %copy-start.1 = (f32[256,1024]{1,0:T(8,128)S(1)}, f32[256,1024]{1,0:T(8,128)}, u32[]{:S(2)}) copy-start(f32[256,1024]{1,0:T(8,128)} %get-tuple-element.10) | copy-start | bytes 3145732
  32.9 2.7 %collective-permute-start.7 = (bf16[256,1024]{1,0:T(8,128)(2,1)}, bf16[256,1024]{1,0:T(8,128)(2,1)S(1)}, u32[]{:S(2)}, u32[]{:S(2)}) collective-permute-start(bf16[256,1024]{1,0:T(8,128)(2,1)} %get-tuple-element.13), channel_id=1, source_target_pairs={{0,1},{1,0},{2,3},{3,2},{4,5},{5,4},{6,7},{7,6},{8,9},{9,8},{10,11... | collective-permute-start | bytes 1572872 | tf_op jit(solution)/shard_map/ppermute | solution.py:26
  33.6 4.7 %collective-permute-start.5 = (bf16[256,1024]{1,0:T(8,128)(2,1)}, bf16[256,1024]{1,0:T(8,128)(2,1)S(1)}, u32[]{:S(2)}, u32[]{:S(2)}) collective-permute-start(bf16[256,1024]{1,0:T(8,128)(2,1)} %get-tuple-element.11), channel_id=1, source_target_pairs={{1,0},{3,2},{5,4},{7,6},{9,8},{11,10},{13,12},{15,14},{17,16},{19,... | collective-permute-start | bytes 1572872 | tf_op jit(solution)/shard_map/ppermute | solution.py:21
  34.9 3.4 %collective-permute-start.6 = (bf16[256,1024]{1,0:T(8,128)(2,1)}, bf16[256,1024]{1,0:T(8,128)(2,1)S(1)}, u32[]{:S(2)}, u32[]{:S(2)}) collective-permute-start(bf16[256,1024]{1,0:T(8,128)(2,1)} %get-tuple-element.11), channel_id=1, source_target_pairs={{8,1},{12,5},{10,3},{14,7},{24,17},{28,21},{26,19},{30,23}} | collective-permute-start | bytes 1572872 | tf_op jit(solution)/shard_map/ppermute | solution.py:231
  37.0 23.8 %collective-permute-start.8 = (bf16[256,1024]{1,0:T(8,128)(2,1)S(1)}, bf16[256,1024]{1,0:T(8,128)(2,1)S(1)}, u32[]{:S(2)}, u32[]{:S(2)}) collective-permute-start(bf16[256,1024]{1,0:T(8,128)(2,1)S(1)} %add_convert_fusion.1), channel_id=1, source_target_pairs={{4,0},{8,4},{12,8},{5,1},{9,5},{13,9},{6,2},{10,6},{14,10},{7,3},{... | collective-permute-start | bytes 1572872 | tf_op jit(solution)/shard_map/ppermute | solution.py:21
  61.2 9.2 %copy-start.5 = (bf16[256,1152]{1,0:T(8,128)(2,1)S(1)}, bf16[256,1152]{1,0:T(8,128)(2,1)}, u32[]{:S(2)}) copy-start(bf16[256,1152]{1,0:T(8,128)(2,1)} %copy-done.4) | copy-start | bytes 1769476
  62.0 8.3 %collective-permute-start.9 = (bf16[256,512]{1,0:T(8,128)(2,1)S(1)}, bf16[256,512]{1,0:T(8,128)(2,1)S(1)}, u32[]{:S(2)}, u32[]{:S(2)}) collective-permute-start(bf16[256,512]{1,0:T(8,128)(2,1)S(1)} %get-tuple-element.23), channel_id=1, source_target_pairs={{0,2},{2,0},{1,3},{3,1},{4,6},{6,4},{5,7},{7,5},{8,10},{10,8},{9,1... | collective-permute-start | bytes 786440 | tf_op jit(solution)/shard_map/ppermute | solution.py:26
  71.2 1.4 %copy-start = (f32[1152,512]{1,0:T(8,128)}, f32[1152,512]{1,0:T(8,128)S(1)}, u32[]{:S(2)}) copy-start(f32[1152,512]{1,0:T(8,128)S(1)} %convolution_multiply_fusion) | copy-start | bytes 7077892
  72.6 2.1 %collective-permute-start.10 = (bf16[576,512]{1,0:T(8,128)(2,1)S(1)}, bf16[576,512]{1,0:T(8,128)(2,1)S(1)}, u32[]{:S(2)}, u32[]{:S(2)}) collective-permute-start(bf16[576,512]{1,0:T(8,128)(2,1)S(1)} %dynamic-slice_convert_fusion), channel_id=1, source_target_pairs={{0,1},{1,0},{2,3},{3,2},{4,5},{5,4},{6,7},{7,6},{8,9},{9,8},{10,11... | collective-permute-start | bytes 1769480 | tf_op jit(solution)/shard_map/ppermute | solution.py:26
  76.2 9.8 %collective-permute-start.11 = (bf16[144,512]{1,0:T(8,128)(2,1)S(1)}, bf16[144,512]{1,0:T(8,128)(2,1)S(1)}, u32[]{:S(2)}, u32[]{:S(2)}) collective-permute-start(bf16[144,512]{1,0:T(8,128)(2,1)S(1)} %get-tuple-element.18), channel_id=1, source_target_pairs={{0,4},{4,8},{8,12},{12,0},{1,5},{5,9},{9,13},{13,1},{2,6},{6,10},{... | collective-permute-start | bytes 442376 | tf_op jit(solution)/shard_map/ppermute | solution.py:26
  81.9 9.6 %collective-permute-start.12 = (bf16[144,512]{1,0:T(8,128)(2,1)S(1)}, bf16[144,512]{1,0:T(8,128)(2,1)S(1)}, u32[]{:S(2)}, u32[]{:S(2)}) collective-permute-start(bf16[144,512]{1,0:T(8,128)(2,1)S(1)} %get-tuple-element.20), channel_id=1, source_target_pairs={{0,8},{4,12},{8,0},{12,4},{1,9},{5,13},{9,1},{13,5},{2,10},{6,14},... | collective-permute-start | bytes 442376 | tf_op jit(solution)/shard_map/ppermute | solution.py:26
  81.9 9.8 %collective-permute-start.13 = (bf16[144,512]{1,0:T(8,128)(2,1)S(1)}, bf16[144,512]{1,0:T(8,128)(2,1)S(1)}, u32[]{:S(2)}, u32[]{:S(2)}) collective-permute-start(bf16[144,512]{1,0:T(8,128)(2,1)S(1)} %get-tuple-element.19), channel_id=1, source_target_pairs={{0,12},{4,0},{8,4},{12,8},{1,13},{5,1},{9,5},{13,9},{2,14},{6,2},{... | collective-permute-start | bytes 442376 | tf_op jit(solution)/shard_map/ppermute | solution.py:26
  91.9 11.1 %collective-permute-start.14 = (bf16[144,512]{1,0:T(8,128)(2,1)S(1)}, bf16[144,512]{1,0:T(8,128)(2,1)S(1)}, u32[]{:S(2)}, u32[]{:S(2)}) collective-permute-start(bf16[144,512]{1,0:T(8,128)(2,1)S(1)} %get-tuple-element.16), channel_id=1, source_target_pairs={{0,4},{4,8},{8,12},{12,0},{1,5},{5,9},{9,13},{13,1},{2,6},{6,10},{... | collective-permute-start | bytes 442376 | tf_op jit(solution)/shard_map/ppermute | solution.py:26
  95.4 12.9 %collective-permute-start.15 = (bf16[144,512]{1,0:T(8,128)(2,1)S(1)}, bf16[144,512]{1,0:T(8,128)(2,1)S(1)}, u32[]{:S(2)}, u32[]{:S(2)}) collective-permute-start(bf16[144,512]{1,0:T(8,128)(2,1)S(1)} %get-tuple-element.16), channel_id=1, source_target_pairs={{0,8},{4,12},{8,0},{12,4},{1,9},{5,13},{9,1},{13,5},{2,10},{6,14},... | collective-permute-start | bytes 442376 | tf_op jit(solution)/shard_map/ppermute | solution.py:26
  98.7 9.5 %collective-permute-start.16 = (bf16[144,512]{1,0:T(8,128)(2,1)S(1)}, bf16[144,512]{1,0:T(8,128)(2,1)S(1)}, u32[]{:S(2)}, u32[]{:S(2)}) collective-permute-start(bf16[144,512]{1,0:T(8,128)(2,1)S(1)} %get-tuple-element.16), channel_id=1, source_target_pairs={{0,12},{4,0},{8,4},{12,8},{1,13},{5,1},{9,5},{13,9},{2,14},{6,2},{... | collective-permute-start | bytes 442376 | tf_op jit(solution)/shard_map/ppermute | solution.py:26
  108.4 2.1 %collective-permute-start.17 = (bf16[576,512]{1,0:T(8,128)(2,1)S(1)}, bf16[576,512]{1,0:T(8,128)(2,1)S(1)}, u32[]{:S(2)}, u32[]{:S(2)}) collective-permute-start(bf16[576,512]{1,0:T(8,128)(2,1)S(1)} %convert_element_type.78), channel_id=1, source_target_pairs={{0,1},{1,0},{2,3},{3,2},{4,5},{5,4},{6,7},{7,6},{8,9},{9,8},{10,11... | collective-permute-start | bytes 1769480 | tf_op jit(solution)/shard_map/ppermute | solution.py:26

commit v17 on v7

--- a/solution.py
+++ b/solution.py
@@ -35,10 +35,10 @@
         outgoing = lax.dynamic_slice_in_dim(piece, ((at + steps) % count) * rows, rows, axis=0)
         total = total + rotated(outgoing.astype(jnp.bfloat16), axis, steps).astype(jnp.float32)
     low = total.astype(jnp.bfloat16)
-    gathered = jnp.zeros(piece.shape, jnp.float32)
-    gathered = lax.dynamic_update_slice_in_dim(gathered, total, at * rows, axis=0)
+    gathered = jnp.zeros(piece.shape, jnp.bfloat16)
+    gathered = lax.dynamic_update_slice_in_dim(gathered, low, at * rows, axis=0)
     for steps in range(1, count):
-        arrived = rotated(low, axis, steps).astype(jnp.float32)
+        arrived = rotated(low, axis, steps)
         gathered = lax.dynamic_update_slice_in_dim(
             gathered, arrived, ((at - steps) % count) * rows, axis=0
         )
@@ -271,12 +271,12 @@
         mine = mine + rotated(outgoing.astype(jnp.bfloat16), "sub", steps).astype(jnp.float32)
     reduced = ring_sum(mine, "ctx")
     if sub_count == 2:
-        other = rotated(reduced.astype(jnp.bfloat16), "sub", 1).astype(jnp.float32)
+        other = rotated(reduced, "sub", 1)
         first = jnp.where(sub_at == 0, reduced, other)
         second = jnp.where(sub_at == 0, other, reduced)
-        weight_v = jnp.concatenate([first, second], axis=0)
-    else:
-        weight_v = lax.all_gather(reduced, "sub", axis=0, tiled=True)
+        weight_v = jnp.concatenate([first, second], axis=0).astype(jnp.float32)
+    else:
+        weight_v = lax.all_gather(reduced, "sub", axis=0, tiled=True).astype(jnp.float32)
     if not scale_early:
         weight_v = weight_v * token_scale
     return (

time: 113 us -> 113 us (level)
  local copies, waits for them, and re-layouts: 4.83 us -> 2.59 us
    unnamed x16 -> x12, local copies, waits for them, and re-layouts: 2.23 us -> 0.02 us
    concatenate x1 -> x0, other arithmetic: 1.61 us -> none  [body(): weight_v = jnp.concatenate([first, second], axis=0)]
    convert_element_type x2 -> x1, other arithmetic: 0.16 us -> 1.73 us  [body(): weight_v = jnp.concatenate([first, second], axis=0).astype(jnp.float32)]
where the time goes in v17:
time: 113 us; the launch traced here: 111 us
  waiting for transfers between devices  60.6 us (54%)
  starting transfers between devices  29.8 us (26%)
  Pallas kernels  8.86 us (8%)
  other arithmetic  6.7 us (6%)
  local copies, waits for them, and re-layouts  2.59 us (2%)
  matrix products  1.87 us (2%)
    ppermute x12, waiting for transfers between devices, rotated(): lax.ppermute(value, axis, [(source, (source + steps) % count) for source...  30.8 us
    ppermute x4, waiting for transfers between devices, passed_along(): lax.ppermute(value, axis, [(source, source + steps) for source in range(f...  29.8 us
    ppermute x12, starting transfers between devices, rotated(): lax.ppermute(value, axis, [(source, (source + steps) % count) for source...  19.5 us
    pallas_call x1, Pallas kernels, attention(): pl.pallas_call(kernel, out_shape=(jax.ShapeDtypeStruct((rows, width), jnp...  8.86 us
    ppermute x4, starting transfers between devices, passed_along(): lax.ppermute(value, axis, [(source, source + steps) for source in range(f...  8.84 us
  transfers between devices with their start and end apart: 18, of which 11 were waited for; matrix products, arithmetic and copies ran while one was open for 3% of the time, Pallas kernels for 0%

profile of v17, /device:TPU:0, one launch (start us, length us, event | category | flops | bytes accessed | tf_op | source)
XLA Modules:
  0.0 111.3 jit_solution(4389168250547548186)
XLA Ops:
  0.6 0.0 copy-start.2
  0.6 1.1 pad_maximum_fusion.refs_8_
  1.7 0.0 copy-start.1
  1.7 5.0 %collective-permute-start = (bf16[256,1024]{1,0:T(8,128)(2,1)S(1)}, bf16[256,1024]{1,0:T(8,128)(2,1)S(1)}, u32[]{:S(2)}, u32[]{:S(2)}) collective-permute-start(bf16[256,1024]{1,0:T(8,128)(2,1)S(1)} %pad_maximum_fusion.refs_8_), channel_id=1, source_target_pairs={{0,4},{4,8},{8,12},{1,5},{5,9},{9,13},{2,6},{6,10},{10,14},{3,7},{... | collective-permute-start | bytes 1572872 | tf_op jit(solution)/shard_map/ppermute | solution.py:21
  6.7 1.3 %dynamic-slice_bitcast_fusion = (bf16[256,1152]{1,0:T(8,128)(2,1)S(1)}, bf16[256,1152]{1,0:T(8,128)(2,1)S(1)}) fusion(bf16[1,256,2304]{2,1,0:T(8,128)(2,1)} %param.6, s32[]{:T(128)S(6)} %select_n.89, s32[]{:T(128)S(6)} %select_n.87), kind=kLoop, calls=%fused_computation.9 | loop fusion | bytes 2359304 | tf_op jit(solution)/shard_map/dynamic_slice | solution.py:191
  8.1 1.6 %collective-permute-start.4 = (bf16[256,1152]{1,0:T(8,128)(2,1)S(1)}, bf16[256,1152]{1,0:T(8,128)(2,1)}, u32[]{:S(2)}, u32[]{:S(2)}) collective-permute-start(bf16[256,1152]{1,0:T(8,128)(2,1)S(1)} %get-tuple-element.22), channel_id=1, source_target_pairs={{0,2},{2,0},{1,3},{3,1},{4,6},{6,4},{5,7},{7,5},{8,10},{10,8},{9,1... | collective-permute-start | bytes 1769480 | tf_op jit(solution)/shard_map/ppermute | solution.py:26
  9.6 1.3 %collective-permute-start.1 = (bf16[256,1024]{1,0:T(8,128)(2,1)S(1)}, bf16[256,1024]{1,0:T(8,128)(2,1)S(1)}, u32[]{:S(2)}, u32[]{:S(2)}) collective-permute-start(bf16[256,1024]{1,0:T(8,128)(2,1)S(1)} %pad_maximum_fusion.refs_8_), channel_id=1, source_target_pairs={{0,1},{2,3},{4,5},{6,7},{8,9},{10,11},{12,13},{14,15},{16,17},{18,... | collective-permute-start | bytes 1572872 | tf_op jit(solution)/shard_map/ppermute | solution.py:21
  10.9 0.7 collective-permute-start.2
  11.6 7.3 %collective-permute-done.refs_4_ = bf16[256,1024]{1,0:T(8,128)(2,1)S(1)} collective-permute-done((bf16[256,1024]{1,0:T(8,128)(2,1)S(1)}, bf16[256,1024]{1,0:T(8,128)(2,1)S(1)}, u32[]{:S(2)}, u32[]{:S(2)}) %collective-permute-start) | collective-permute-done | bytes 524320 | tf_op jit(solution)/shard_map/ppermute | solution.py:21
  19.0 0.0 copy-start.3
  19.0 0.0 collective-permute-start.3
  19.0 0.0 copy-done.2
  19.0 0.1 select_reduce_fusion
  19.1 0.1 copy.13
  19.2 0.7 subtract_add_fusion.refs_1_
  19.9 0.0 collective-permute-done.1.refs_5_
  19.9 0.0 copy-start.4
  19.9 0.0 collective-permute-done.2.refs_6_
  19.9 0.0 copy-start.5
  20.0 3.1 %collective-permute-done.4.refs_9_ = bf16[256,1152]{1,0:T(8,128)(2,1)} collective-permute-done((bf16[256,1152]{1,0:T(8,128)(2,1)S(1)}, bf16[256,1152]{1,0:T(8,128)(2,1)}, u32[]{:S(2)}, u32[]{:S(2)}) %collective-permute-start.4) | collective-permute-done | bytes 589856 | tf_op jit(solution)/shard_map/ppermute | solution.py:26
  23.0 0.0 collective-permute-done.3.refs_7_
  23.0 0.0 copy-done.1
  23.0 0.0 copy-done.3
  23.0 0.0 copy-done.4
  23.1 0.0 copy-done.5
  23.1 8.9 %shard_map.93 = (bf16[256,1024]{1,0:T(8,128)(2,1)}, bf16[256,1024]{1,0:T(8,128)(2,1)}, bf16[256,1024]{1,0:T(8,128)(2,1)}, f32[256,1024]{1,0:T(8,128)}, f32[256,1024]{1,0:T(8,128)}) custom-call(s32[1]{0:T(128)} %bitcast.refs_0_, s32[256,1]{1,0:T(8,128)} %subtract_add_fusion.refs_1_, bf16[256,1024]{1,0:T(8,128)(2,1)} %bitcast.20, bf16[256,1024]{1,0:T(8,128)(2,1)} %bitcast.21, ...), custom_call_target="tpu_custom_call" | custom-call | flops 2684354560 | bytes 7864320 | tf_op jit(solution)/shard_map/pallas_call | solution.py:160
  31.9 0.0 copy-start
  31.9 1.4 %collective-permute-start.7 = (bf16[256,1024]{1,0:T(8,128)(2,1)}, bf16[256,1024]{1,0:T(8,128)(2,1)S(1)}, u32[]{:S(2)}, u32[]{:S(2)}) collective-permute-start(bf16[256,1024]{1,0:T(8,128)(2,1)} %get-tuple-element.13), channel_id=1, source_target_pairs={{0,1},{1,0},{2,3},{3,2},{4,5},{5,4},{6,7},{7,6},{8,9},{9,8},{10,11... | collective-permute-start | bytes 1572872 | tf_op jit(solution)/shard_map/ppermute | solution.py:26
  33.3 1.3 %collective-permute-start.5 = (bf16[256,1024]{1,0:T(8,128)(2,1)}, bf16[256,1024]{1,0:T(8,128)(2,1)S(1)}, u32[]{:S(2)}, u32[]{:S(2)}) collective-permute-start(bf16[256,1024]{1,0:T(8,128)(2,1)} %get-tuple-element.11), channel_id=1, source_target_pairs={{1,0},{3,2},{5,4},{7,6},{9,8},{11,10},{13,12},{15,14},{17,16},{19,... | collective-permute-start | bytes 1572872 | tf_op jit(solution)/shard_map/ppermute | solution.py:21
  34.6 0.7 collective-permute-start.6
  35.3 0.0 collective-permute-done.7
  35.3 1.4 %add_convert_fusion.1 = bf16[256,1024]{1,0:T(8,128)(2,1)S(1)} fusion(f32[256,1024]{1,0:T(8,128)} %get-tuple-element.12, bf16[256,1024]{1,0:T(8,128)(2,1)S(1)} %collective-permute-done.7), kind=kLoop, calls=%fused_computation.8 | loop fusion | flops 786432 | bytes 2097152 | tf_op jit(solution)/shard_map/convert_element_type | solution.py:229
  36.7 1.3 %collective-permute-start.8 = (bf16[256,1024]{1,0:T(8,128)(2,1)S(1)}, bf16[256,1024]{1,0:T(8,128)(2,1)S(1)}, u32[]{:S(2)}, u32[]{:S(2)}) collective-permute-start(bf16[256,1024]{1,0:T(8,128)(2,1)S(1)} %add_convert_fusion.1), channel_id=1, source_target_pairs={{4,0},{8,4},{12,8},{5,1},{9,5},{13,9},{6,2},{10,6},{14,10},{7,3},{... | collective-permute-start | bytes 1572872 | tf_op jit(solution)/shard_map/ppermute | solution.py:21
  38.0 0.0 collective-permute-done.5
  38.0 0.0 collective-permute-done.6
  38.0 22.5 %collective-permute-done.8 = bf16[256,1024]{1,0:T(8,128)(2,1)S(1)} collective-permute-done((bf16[256,1024]{1,0:T(8,128)(2,1)S(1)}, bf16[256,1024]{1,0:T(8,128)(2,1)S(1)}, u32[]{:S(2)}, u32[]{:S(2)}) %collective-permute-start.8) | collective-permute-done | bytes 524320 | tf_op jit(solution)/shard_map/ppermute | solution.py:21
  60.5 0.0 copy-done
  60.5 0.3 add_convert_fusion
  60.8 0.9 fusion.7
  61.7 1.5 %collective-permute-start.9 = (bf16[256,512]{1,0:T(8,128)(2,1)S(1)}, bf16[256,512]{1,0:T(8,128)(2,1)S(1)}, u32[]{:S(2)}, u32[]{:S(2)}) collective-permute-start(bf16[256,512]{1,0:T(8,128)(2,1)S(1)} %get-tuple-element.23), channel_id=1, source_target_pairs={{0,2},{2,0},{1,3},{3,1},{4,6},{6,4},{5,7},{7,5},{8,10},{10,8},{9,1... | collective-permute-start | bytes 786440 | tf_op jit(solution)/shard_map/ppermute | solution.py:26
  63.2 6.8 %collective-permute-done.9 = bf16[256,512]{1,0:T(8,128)(2,1)S(1)} collective-permute-done((bf16[256,512]{1,0:T(8,128)(2,1)S(1)}, bf16[256,512]{1,0:T(8,128)(2,1)S(1)}, u32[]{:S(2)}, u32[]{:S(2)}) %collective-permute-start.9) | collective-permute-done | bytes 262176 | tf_op jit(solution)/shard_map/ppermute | solution.py:26
  70.0 1.9 %convolution_multiply_fusion = f32[1152,512]{1,0:T(8,128)S(1)} fusion(bf16[256,1152]{1,0:T(8,128)(2,1)} %collective-permute-done.4.refs_9_, bf16[256,1152]{1,0:T(8,128)(2,1)S(1)} %get-tuple-element.21, bf16[256,512]{1,0:T(8,128)(2,1)S(1)} %collective-permute-done.9, bf16[256,512]{1,0:T(8,128)(2,1)S(1)} %get-tuple-element.23), kind=kOutput, calls=%fused_computation | convolution fusion | flops 607977472 | bytes 4063232 | tf_op jit(solution)/shard_map/dot_general | solution.py:258
  71.9 0.1 dynamic-slice_convert_fusion
  72.0 0.1 collective-permute-start.10
  72.1 2.1 %collective-permute-done.10 = bf16[576,512]{1,0:T(8,128)(2,1)} collective-permute-done((bf16[576,512]{1,0:T(8,128)(2,1)S(1)}, bf16[576,512]{1,0:T(8,128)(2,1)}, u32[]{:S(2)}, u32[]{:S(2)}) %collective-permute-start.10) | collective-permute-done | bytes 589856 | tf_op jit(solution)/shard_map/ppermute | solution.py:26
  74.2 1.2 %convert_add_fusion = f32[576,512]{1,0:T(8,128)S(1)} fusion(bf16[576,512]{1,0:T(8,128)(2,1)} %collective-permute-done.10, f32[1152,512]{1,0:T(8,128)S(1)} %convolution_multiply_fusion, s32[]{:T(128)S(6)} %select_n.90), kind=kLoop, calls=%fused_computation.5 | loop fusion | flops 589824 | bytes 2949124 | tf_op jit(solution)/shard_map/add | solution.py:271
  75.4 0.1 dynamic-slice_convert_fusion.3
  75.5 5.7 %collective-permute-start.11 = (bf16[144,512]{1,0:T(8,128)(2,1)S(1)}, bf16[144,512]{1,0:T(8,128)(2,1)S(1)}, u32[]{:S(2)}, u32[]{:S(2)}) collective-permute-start(bf16[144,512]{1,0:T(8,128)(2,1)S(1)} %get-tuple-element.18), channel_id=1, source_target_pairs={{0,4},{4,8},{8,12},{12,0},{1,5},{5,9},{9,13},{13,1},{2,6},{6,10},{... | collective-permute-start | bytes 442376 | tf_op jit(solution)/shard_map/ppermute | solution.py:26
  81.2 0.0 collective-permute-start.12
  81.2 2.4 %collective-permute-start.13 = (bf16[144,512]{1,0:T(8,128)(2,1)S(1)}, bf16[144,512]{1,0:T(8,128)(2,1)S(1)}, u32[]{:S(2)}, u32[]{:S(2)}) collective-permute-start(bf16[144,512]{1,0:T(8,128)(2,1)S(1)} %get-tuple-element.19), channel_id=1, source_target_pairs={{0,12},{4,0},{8,4},{12,8},{1,13},{5,1},{9,5},{13,9},{2,14},{6,2},{... | collective-permute-start | bytes 442376 | tf_op jit(solution)/shard_map/ppermute | solution.py:26
  83.6 1.8 %collective-permute-done.11 = bf16[144,512]{1,0:T(8,128)(2,1)S(1)} collective-permute-done((bf16[144,512]{1,0:T(8,128)(2,1)S(1)}, bf16[144,512]{1,0:T(8,128)(2,1)S(1)}, u32[]{:S(2)}, u32[]{:S(2)}) %collective-permute-start.11) | collective-permute-done | bytes 147488 | tf_op jit(solution)/shard_map/ppermute | solution.py:26
  85.4 5.3 %collective-permute-done.12 = bf16[144,512]{1,0:T(8,128)(2,1)S(1)} collective-permute-done((bf16[144,512]{1,0:T(8,128)(2,1)S(1)}, bf16[144,512]{1,0:T(8,128)(2,1)S(1)}, u32[]{:S(2)}, u32[]{:S(2)}) %collective-permute-start.12) | collective-permute-done | bytes 147488 | tf_op jit(solution)/shard_map/ppermute | solution.py:26
  90.7 0.2 collective-permute-done.13
  91.0 0.1 constant_dynamic-update-slice_fusion.3
  91.1 3.5 %collective-permute-start.14 = (bf16[144,512]{1,0:T(8,128)(2,1)S(1)}, bf16[144,512]{1,0:T(8,128)(2,1)S(1)}, u32[]{:S(2)}, u32[]{:S(2)}) collective-permute-start(bf16[144,512]{1,0:T(8,128)(2,1)S(1)} %get-tuple-element.15), channel_id=1, source_target_pairs={{0,4},{4,8},{8,12},{12,0},{1,5},{5,9},{9,13},{13,1},{2,6},{6,10},{... | collective-permute-start | bytes 442376 | tf_op jit(solution)/shard_map/ppermute | solution.py:26
  94.5 3.4 %collective-permute-start.15 = (bf16[144,512]{1,0:T(8,128)(2,1)S(1)}, bf16[144,512]{1,0:T(8,128)(2,1)S(1)}, u32[]{:S(2)}, u32[]{:S(2)}) collective-permute-start(bf16[144,512]{1,0:T(8,128)(2,1)S(1)} %get-tuple-element.15), channel_id=1, source_target_pairs={{0,8},{4,12},{8,0},{12,4},{1,9},{5,13},{9,1},{13,5},{2,10},{6,14},... | collective-permute-start | bytes 442376 | tf_op jit(solution)/shard_map/ppermute | solution.py:26
  97.9 0.0 collective-permute-start.16
  97.9 4.2 %collective-permute-done.14 = bf16[144,512]{1,0:T(8,128)(2,1)S(1)} collective-permute-done((bf16[144,512]{1,0:T(8,128)(2,1)S(1)}, bf16[144,512]{1,0:T(8,128)(2,1)S(1)}, u32[]{:S(2)}, u32[]{:S(2)}) %collective-permute-start.14) | collective-permute-done | bytes 147488 | tf_op jit(solution)/shard_map/ppermute | solution.py:26
  102.2 5.2 %collective-permute-done.15 = bf16[144,512]{1,0:T(8,128)(2,1)S(1)} collective-permute-done((bf16[144,512]{1,0:T(8,128)(2,1)S(1)}, bf16[144,512]{1,0:T(8,128)(2,1)S(1)}, u32[]{:S(2)}, u32[]{:S(2)}) %collective-permute-start.15) | collective-permute-done | bytes 147488 | tf_op jit(solution)/shard_map/ppermute | solution.py:26
  107.4 0.0 collective-permute-done.16
  107.4 0.1 collective-permute-start.17
  107.5 2.0 %collective-permute-done.17 = bf16[576,512]{1,0:T(8,128)(2,1)S(1)} collective-permute-done((bf16[576,512]{1,0:T(8,128)(2,1)S(1)}, bf16[576,512]{1,0:T(8,128)(2,1)S(1)}, u32[]{:S(2)}, u32[]{:S(2)}) %collective-permute-start.17) | collective-permute-done | bytes 589856 | tf_op jit(solution)/shard_map/ppermute | solution.py:26
  109.5 0.1 broadcast_select_fusion.1
  109.6 1.7 %maximum_convert_fusion = f32[1152,512]{1,0:T(8,128)} fusion(bf16[576,512]{1,0:T(8,128)(2,1)S(1)} %get-tuple-element.17, bf16[576,512]{1,0:T(8,128)(2,1)S(1)} %get-tuple-element.16), kind=kLoop, calls=%fused_computation.4 | loop fusion | flops 2359296 | bytes 3538944 | tf_op jit(solution)/shard_map/convert_element_type | solution.py:277
  (5 shorter events, 0.1 us)
Async XLA Ops:
  0.6 18.4 %copy-start.2 = (s32[1,12]{1,0:T(1,128)S(1)}, s32[1,12]{1,0:T(1,128)}, u32[]{:S(2)}) copy-start(s32[1,12]{1,0:T(1,128)} %param.11) | copy-start | bytes 148
  1.7 21.3 %copy-start.1 = (bf16[256,1024]{1,0:T(8,128)(2,1)}, bf16[256,1024]{1,0:T(8,128)(2,1)S(1)}, u32[]{:S(2)}) copy-start(bf16[256,1024]{1,0:T(8,128)(2,1)S(1)} %pad_maximum_fusion.refs_8_) | copy-start | bytes 1572868
  1.7 17.2 %collective-permute-start = (bf16[256,1024]{1,0:T(8,128)(2,1)S(1)}, bf16[256,1024]{1,0:T(8,128)(2,1)S(1)}, u32[]{:S(2)}, u32[]{:S(2)}) collective-permute-start(bf16[256,1024]{1,0:T(8,128)(2,1)S(1)} %pad_maximum_fusion.refs_8_), channel_id=1, source_target_pairs={{0,4},{4,8},{8,12},{1,5},{5,9},{9,13},{2,6},{6,10},{10,14},{3,7},{... | collective-permute-start | bytes 1572872 | tf_op jit(solution)/shard_map/ppermute | solution.py:21
  8.1 15.0 %collective-permute-start.4 = (bf16[256,1152]{1,0:T(8,128)(2,1)S(1)}, bf16[256,1152]{1,0:T(8,128)(2,1)}, u32[]{:S(2)}, u32[]{:S(2)}) collective-permute-start(bf16[256,1152]{1,0:T(8,128)(2,1)S(1)} %get-tuple-element.22), channel_id=1, source_target_pairs={{0,2},{2,0},{1,3},{3,1},{4,6},{6,4},{5,7},{7,5},{8,10},{10,8},{9,1... | collective-permute-start | bytes 1769480 | tf_op jit(solution)/shard_map/ppermute | solution.py:26
  9.6 10.3 %collective-permute-start.1 = (bf16[256,1024]{1,0:T(8,128)(2,1)S(1)}, bf16[256,1024]{1,0:T(8,128)(2,1)S(1)}, u32[]{:S(2)}, u32[]{:S(2)}) collective-permute-start(bf16[256,1024]{1,0:T(8,128)(2,1)S(1)} %pad_maximum_fusion.refs_8_), channel_id=1, source_target_pairs={{0,1},{2,3},{4,5},{6,7},{8,9},{10,11},{12,13},{14,15},{16,17},{18,... | collective-permute-start | bytes 1572872 | tf_op jit(solution)/shard_map/ppermute | solution.py:21
  10.9 9.0 %collective-permute-start.2 = (bf16[256,1024]{1,0:T(8,128)(2,1)S(1)}, bf16[256,1024]{1,0:T(8,128)(2,1)S(1)}, u32[]{:S(2)}, u32[]{:S(2)}) collective-permute-start(bf16[256,1024]{1,0:T(8,128)(2,1)S(1)} %pad_maximum_fusion.refs_8_), channel_id=1, source_target_pairs={{1,8},{5,12},{3,10},{7,14},{17,24},{21,28},{19,26},{23,30}} | collective-permute-start | bytes 1572872 | tf_op jit(solution)/shard_map/ppermute | solution.py:210
  19.0 4.0 %copy-start.3 = (bf16[256,1024]{1,0:T(8,128)(2,1)}, bf16[256,1024]{1,0:T(8,128)(2,1)S(1)}, u32[]{:S(2)}) copy-start(bf16[256,1024]{1,0:T(8,128)(2,1)S(1)} %collective-permute-done.refs_4_) | copy-start | bytes 1572868
  19.0 4.0 %collective-permute-start.3 = (bf16[256,1024]{1,0:T(8,128)(2,1)S(1)}, bf16[256,1024]{1,0:T(8,128)(2,1)}, u32[]{:S(2)}, u32[]{:S(2)}) collective-permute-start(bf16[256,1024]{1,0:T(8,128)(2,1)S(1)} %collective-permute-done.refs_4_), channel_id=1, source_target_pairs={{0,1},{1,0},{2,3},{3,2},{4,5},{5,4},{6,7},{7,6},{8,9},{9,8},{10,11... | collective-permute-start | bytes 1572872 | tf_op jit(solution)/shard_map/ppermute | solution.py:26
  19.9 3.1 %copy-start.4 = (bf16[256,1024]{1,0:T(8,128)(2,1)}, bf16[256,1024]{1,0:T(8,128)(2,1)S(1)}, u32[]{:S(2)}) copy-start(bf16[256,1024]{1,0:T(8,128)(2,1)S(1)} %collective-permute-done.1.refs_5_) | copy-start | bytes 1572868
  19.9 3.1 %copy-start.5 = (bf16[256,1024]{1,0:T(8,128)(2,1)}, bf16[256,1024]{1,0:T(8,128)(2,1)S(1)}, u32[]{:S(2)}) copy-start(bf16[256,1024]{1,0:T(8,128)(2,1)S(1)} %collective-permute-done.2.refs_6_) | copy-start | bytes 1572868
  31.9 28.6 %copy-start = (f32[256,1024]{1,0:T(8,128)S(1)}, f32[256,1024]{1,0:T(8,128)}, u32[]{:S(2)}) copy-start(f32[256,1024]{1,0:T(8,128)} %get-tuple-element.10) | copy-start | bytes 3145732
  31.9 3.4 %collective-permute-start.7 = (bf16[256,1024]{1,0:T(8,128)(2,1)}, bf16[256,1024]{1,0:T(8,128)(2,1)S(1)}, u32[]{:S(2)}, u32[]{:S(2)}) collective-permute-start(bf16[256,1024]{1,0:T(8,128)(2,1)} %get-tuple-element.13), channel_id=1, source_target_pairs={{0,1},{1,0},{2,3},{3,2},{4,5},{5,4},{6,7},{7,6},{8,9},{9,8},{10,11... | collective-permute-start | bytes 1572872 | tf_op jit(solution)/shard_map/ppermute | solution.py:26
  33.3 4.7 %collective-permute-start.5 = (bf16[256,1024]{1,0:T(8,128)(2,1)}, bf16[256,1024]{1,0:T(8,128)(2,1)S(1)}, u32[]{:S(2)}, u32[]{:S(2)}) collective-permute-start(bf16[256,1024]{1,0:T(8,128)(2,1)} %get-tuple-element.11), channel_id=1, source_target_pairs={{1,0},{3,2},{5,4},{7,6},{9,8},{11,10},{13,12},{15,14},{17,16},{19,... | collective-permute-start | bytes 1572872 | tf_op jit(solution)/shard_map/ppermute | solution.py:21
  34.6 3.4 %collective-permute-start.6 = (bf16[256,1024]{1,0:T(8,128)(2,1)}, bf16[256,1024]{1,0:T(8,128)(2,1)S(1)}, u32[]{:S(2)}, u32[]{:S(2)}) collective-permute-start(bf16[256,1024]{1,0:T(8,128)(2,1)} %get-tuple-element.11), channel_id=1, source_target_pairs={{8,1},{12,5},{10,3},{14,7},{24,17},{28,21},{26,19},{30,23}} | collective-permute-start | bytes 1572872 | tf_op jit(solution)/shard_map/ppermute | solution.py:234
  36.7 23.8 %collective-permute-start.8 = (bf16[256,1024]{1,0:T(8,128)(2,1)S(1)}, bf16[256,1024]{1,0:T(8,128)(2,1)S(1)}, u32[]{:S(2)}, u32[]{:S(2)}) collective-permute-start(bf16[256,1024]{1,0:T(8,128)(2,1)S(1)} %add_convert_fusion.1), channel_id=1, source_target_pairs={{4,0},{8,4},{12,8},{5,1},{9,5},{13,9},{6,2},{10,6},{14,10},{7,3},{... | collective-permute-start | bytes 1572872 | tf_op jit(solution)/shard_map/ppermute | solution.py:21
  61.7 8.3 %collective-permute-start.9 = (bf16[256,512]{1,0:T(8,128)(2,1)S(1)}, bf16[256,512]{1,0:T(8,128)(2,1)S(1)}, u32[]{:S(2)}, u32[]{:S(2)}) collective-permute-start(bf16[256,512]{1,0:T(8,128)(2,1)S(1)} %get-tuple-element.23), channel_id=1, source_target_pairs={{0,2},{2,0},{1,3},{3,1},{4,6},{6,4},{5,7},{7,5},{8,10},{10,8},{9,1... | collective-permute-start | bytes 786440 | tf_op jit(solution)/shard_map/ppermute | solution.py:26
  72.0 2.2 %collective-permute-start.10 = (bf16[576,512]{1,0:T(8,128)(2,1)S(1)}, bf16[576,512]{1,0:T(8,128)(2,1)}, u32[]{:S(2)}, u32[]{:S(2)}) collective-permute-start(bf16[576,512]{1,0:T(8,128)(2,1)S(1)} %dynamic-slice_convert_fusion), channel_id=1, source_target_pairs={{0,1},{1,0},{2,3},{3,2},{4,5},{5,4},{6,7},{7,6},{8,9},{9,8},{10,11... | collective-permute-start | bytes 1769480 | tf_op jit(solution)/shard_map/ppermute | solution.py:26
  75.5 9.9 %collective-permute-start.11 = (bf16[144,512]{1,0:T(8,128)(2,1)S(1)}, bf16[144,512]{1,0:T(8,128)(2,1)S(1)}, u32[]{:S(2)}, u32[]{:S(2)}) collective-permute-start(bf16[144,512]{1,0:T(8,128)(2,1)S(1)} %get-tuple-element.18), channel_id=1, source_target_pairs={{0,4},{4,8},{8,12},{12,0},{1,5},{5,9},{9,13},{13,1},{2,6},{6,10},{... | collective-permute-start | bytes 442376 | tf_op jit(solution)/shard_map/ppermute | solution.py:26
  81.2 9.6 %collective-permute-start.12 = (bf16[144,512]{1,0:T(8,128)(2,1)S(1)}, bf16[144,512]{1,0:T(8,128)(2,1)S(1)}, u32[]{:S(2)}, u32[]{:S(2)}) collective-permute-start(bf16[144,512]{1,0:T(8,128)(2,1)S(1)} %get-tuple-element.20), channel_id=1, source_target_pairs={{0,8},{4,12},{8,0},{12,4},{1,9},{5,13},{9,1},{13,5},{2,10},{6,14},... | collective-permute-start | bytes 442376 | tf_op jit(solution)/shard_map/ppermute | solution.py:26
  81.2 9.8 %collective-permute-start.13 = (bf16[144,512]{1,0:T(8,128)(2,1)S(1)}, bf16[144,512]{1,0:T(8,128)(2,1)S(1)}, u32[]{:S(2)}, u32[]{:S(2)}) collective-permute-start(bf16[144,512]{1,0:T(8,128)(2,1)S(1)} %get-tuple-element.19), channel_id=1, source_target_pairs={{0,12},{4,0},{8,4},{12,8},{1,13},{5,1},{9,5},{13,9},{2,14},{6,2},{... | collective-permute-start | bytes 442376 | tf_op jit(solution)/shard_map/ppermute | solution.py:26
  91.1 11.1 %collective-permute-start.14 = (bf16[144,512]{1,0:T(8,128)(2,1)S(1)}, bf16[144,512]{1,0:T(8,128)(2,1)S(1)}, u32[]{:S(2)}, u32[]{:S(2)}) collective-permute-start(bf16[144,512]{1,0:T(8,128)(2,1)S(1)} %get-tuple-element.15), channel_id=1, source_target_pairs={{0,4},{4,8},{8,12},{12,0},{1,5},{5,9},{9,13},{13,1},{2,6},{6,10},{... | collective-permute-start | bytes 442376 | tf_op jit(solution)/shard_map/ppermute | solution.py:26
  94.5 12.9 %collective-permute-start.15 = (bf16[144,512]{1,0:T(8,128)(2,1)S(1)}, bf16[144,512]{1,0:T(8,128)(2,1)S(1)}, u32[]{:S(2)}, u32[]{:S(2)}) collective-permute-start(bf16[144,512]{1,0:T(8,128)(2,1)S(1)} %get-tuple-element.15), channel_id=1, source_target_pairs={{0,8},{4,12},{8,0},{12,4},{1,9},{5,13},{9,1},{13,5},{2,10},{6,14},... | collective-permute-start | bytes 442376 | tf_op jit(solution)/shard_map/ppermute | solution.py:26
  97.9 9.5 %collective-permute-start.16 = (bf16[144,512]{1,0:T(8,128)(2,1)S(1)}, bf16[144,512]{1,0:T(8,128)(2,1)S(1)}, u32[]{:S(2)}, u32[]{:S(2)}) collective-permute-start(bf16[144,512]{1,0:T(8,128)(2,1)S(1)} %get-tuple-element.15), channel_id=1, source_target_pairs={{0,12},{4,0},{8,4},{12,8},{1,13},{5,1},{9,5},{13,9},{2,14},{6,2},{... | collective-permute-start | bytes 442376 | tf_op jit(solution)/shard_map/ppermute | solution.py:26
  107.4 2.1 %collective-permute-start.17 = (bf16[576,512]{1,0:T(8,128)(2,1)S(1)}, bf16[576,512]{1,0:T(8,128)(2,1)S(1)}, u32[]{:S(2)}, u32[]{:S(2)}) collective-permute-start(bf16[576,512]{1,0:T(8,128)(2,1)S(1)} %constant_dynamic-update-slice_fusion), channel_id=1, source_target_pairs={{0,1},{1,0},{2,3},{3,2},{4,5},{5,4},{6,7},{7,6},{8,9},{9,8},{10,11... | collective-permute-start | bytes 1769480 | tf_op jit(solution)/shard_map/ppermute | solution.py:26

commit v18 on v17

--- a/solution.py
+++ b/solution.py
@@ -92,7 +92,8 @@
             q_cols = pl.ds((group * per_group + member) * HEAD_DIM, HEAD_DIM)
             query_h = q_ref[:, q_cols]
             grad_h = do_ref[:, q_cols]
-            scores = lax.dot_general(query_h, key_g, NT, preferred_element_type=jnp.float32) * scale
+            query_scaled = query_h * jnp.asarray(scale, query_h.dtype)
+            scores = lax.dot_general(query_scaled, key_g, NT, preferred_element_type=jnp.float32)
             scores = jnp.where(allowed, scores, -1e30)
             largest = jnp.max(scores, axis=1, keepdims=True)
             raised = jnp.exp(scores - largest)

time: 113 us -> 113 us (level)
  no operation moved by 1% of the time
where the time goes in v18:
time: 113 us; the launch traced here: 111 us
  waiting for transfers between devices  60.6 us (54%)
  starting transfers between devices  29.8 us (26%)
  Pallas kernels  8.85 us (8%)
  other arithmetic  6.7 us (6%)
  local copies, waits for them, and re-layouts  2.59 us (2%)
  matrix products  1.87 us (2%)
    ppermute x12, waiting for transfers between devices, rotated(): lax.ppermute(value, axis, [(source, (source + steps) % count) for source...  30.8 us
    ppermute x4, waiting for transfers between devices, passed_along(): lax.ppermute(value, axis, [(source, source + steps) for source in range(f...  29.8 us
    ppermute x12, starting transfers between devices, rotated(): lax.ppermute(value, axis, [(source, (source + steps) % count) for source...  19.5 us
    pallas_call x1, Pallas kernels, attention(): pl.pallas_call(kernel, out_shape=(jax.ShapeDtypeStruct((rows, width), jnp...  8.85 us
    ppermute x4, starting transfers between devices, passed_along(): lax.ppermute(value, axis, [(source, source + steps) for source in range(f...  8.84 us
  transfers between devices with their start and end apart: 18, of which 11 were waited for; matrix products, arithmetic and copies ran while one was open for 3% of the time, Pallas kernels for 0%

profile of v18, /device:TPU:0, one launch (start us, length us, event | category | flops | bytes accessed | tf_op | source)
XLA Modules:
  0.0 111.3 jit_solution(15960373303651132786)
XLA Ops:
  0.6 0.0 copy-start.2
  0.6 1.1 pad_maximum_fusion.refs_8_
  1.7 0.0 copy-start.1
  1.7 5.0 %collective-permute-start = (bf16[256,1024]{1,0:T(8,128)(2,1)S(1)}, bf16[256,1024]{1,0:T(8,128)(2,1)S(1)}, u32[]{:S(2)}, u32[]{:S(2)}) collective-permute-start(bf16[256,1024]{1,0:T(8,128)(2,1)S(1)} %pad_maximum_fusion.refs_8_), channel_id=1, source_target_pairs={{0,4},{4,8},{8,12},{1,5},{5,9},{9,13},{2,6},{6,10},{10,14},{3,7},{... | collective-permute-start | bytes 1572872 | tf_op jit(solution)/shard_map/ppermute | solution.py:21
  6.7 1.3 %dynamic-slice_bitcast_fusion = (bf16[256,1152]{1,0:T(8,128)(2,1)S(1)}, bf16[256,1152]{1,0:T(8,128)(2,1)S(1)}) fusion(bf16[1,256,2304]{2,1,0:T(8,128)(2,1)} %param.6, s32[]{:T(128)S(6)} %select_n.89, s32[]{:T(128)S(6)} %select_n.87), kind=kLoop, calls=%fused_computation.9 | loop fusion | bytes 2359304 | tf_op jit(solution)/shard_map/dynamic_slice | solution.py:192
  8.1 1.6 %collective-permute-start.4 = (bf16[256,1152]{1,0:T(8,128)(2,1)S(1)}, bf16[256,1152]{1,0:T(8,128)(2,1)}, u32[]{:S(2)}, u32[]{:S(2)}) collective-permute-start(bf16[256,1152]{1,0:T(8,128)(2,1)S(1)} %get-tuple-element.22), channel_id=1, source_target_pairs={{0,2},{2,0},{1,3},{3,1},{4,6},{6,4},{5,7},{7,5},{8,10},{10,8},{9,1... | collective-permute-start | bytes 1769480 | tf_op jit(solution)/shard_map/ppermute | solution.py:26
  9.6 1.3 %collective-permute-start.1 = (bf16[256,1024]{1,0:T(8,128)(2,1)S(1)}, bf16[256,1024]{1,0:T(8,128)(2,1)S(1)}, u32[]{:S(2)}, u32[]{:S(2)}) collective-permute-start(bf16[256,1024]{1,0:T(8,128)(2,1)S(1)} %pad_maximum_fusion.refs_8_), channel_id=1, source_target_pairs={{0,1},{2,3},{4,5},{6,7},{8,9},{10,11},{12,13},{14,15},{16,17},{18,... | collective-permute-start | bytes 1572872 | tf_op jit(solution)/shard_map/ppermute | solution.py:21
  10.9 0.7 collective-permute-start.2
  11.6 7.3 %collective-permute-done.refs_4_ = bf16[256,1024]{1,0:T(8,128)(2,1)S(1)} collective-permute-done((bf16[256,1024]{1,0:T(8,128)(2,1)S(1)}, bf16[256,1024]{1,0:T(8,128)(2,1)S(1)}, u32[]{:S(2)}, u32[]{:S(2)}) %collective-permute-start) | collective-permute-done | bytes 524320 | tf_op jit(solution)/shard_map/ppermute | solution.py:21
  19.0 0.0 copy-start.3
  19.0 0.0 collective-permute-start.3
  19.0 0.0 copy-done.2
  19.0 0.1 select_reduce_fusion
  19.1 0.1 copy.13
  19.2 0.7 subtract_add_fusion.refs_1_
  19.9 0.0 collective-permute-done.1.refs_5_
  19.9 0.0 copy-start.4
  19.9 0.0 collective-permute-done.2.refs_6_
  19.9 0.0 copy-start.5
  20.0 3.1 %collective-permute-done.4.refs_9_ = bf16[256,1152]{1,0:T(8,128)(2,1)} collective-permute-done((bf16[256,1152]{1,0:T(8,128)(2,1)S(1)}, bf16[256,1152]{1,0:T(8,128)(2,1)}, u32[]{:S(2)}, u32[]{:S(2)}) %collective-permute-start.4) | collective-permute-done | bytes 589856 | tf_op jit(solution)/shard_map/ppermute | solution.py:26
  23.0 0.0 collective-permute-done.3.refs_7_
  23.0 0.0 copy-done.1
  23.0 0.0 copy-done.3
  23.0 0.0 copy-done.4
  23.1 0.0 copy-done.5
  23.1 8.8 %shard_map.93 = (bf16[256,1024]{1,0:T(8,128)(2,1)}, bf16[256,1024]{1,0:T(8,128)(2,1)}, bf16[256,1024]{1,0:T(8,128)(2,1)}, f32[256,1024]{1,0:T(8,128)}, f32[256,1024]{1,0:T(8,128)}) custom-call(s32[1]{0:T(128)} %bitcast.refs_0_, s32[256,1]{1,0:T(8,128)} %subtract_add_fusion.refs_1_, bf16[256,1024]{1,0:T(8,128)(2,1)} %bitcast.20, bf16[256,1024]{1,0:T(8,128)(2,1)} %bitcast.21, ...), custom_call_target="tpu_custom_call" | custom-call | flops 2684354560 | bytes 7864320 | tf_op jit(solution)/shard_map/pallas_call | solution.py:161
  31.9 0.0 copy-start
  31.9 1.4 %collective-permute-start.7 = (bf16[256,1024]{1,0:T(8,128)(2,1)}, bf16[256,1024]{1,0:T(8,128)(2,1)S(1)}, u32[]{:S(2)}, u32[]{:S(2)}) collective-permute-start(bf16[256,1024]{1,0:T(8,128)(2,1)} %get-tuple-element.13), channel_id=1, source_target_pairs={{0,1},{1,0},{2,3},{3,2},{4,5},{5,4},{6,7},{7,6},{8,9},{9,8},{10,11... | collective-permute-start | bytes 1572872 | tf_op jit(solution)/shard_map/ppermute | solution.py:26
  33.3 1.3 %collective-permute-start.5 = (bf16[256,1024]{1,0:T(8,128)(2,1)}, bf16[256,1024]{1,0:T(8,128)(2,1)S(1)}, u32[]{:S(2)}, u32[]{:S(2)}) collective-permute-start(bf16[256,1024]{1,0:T(8,128)(2,1)} %get-tuple-element.11), channel_id=1, source_target_pairs={{1,0},{3,2},{5,4},{7,6},{9,8},{11,10},{13,12},{15,14},{17,16},{19,... | collective-permute-start | bytes 1572872 | tf_op jit(solution)/shard_map/ppermute | solution.py:21
  34.6 0.7 collective-permute-start.6
  35.3 0.0 collective-permute-done.7
  35.3 1.4 %add_convert_fusion.1 = bf16[256,1024]{1,0:T(8,128)(2,1)S(1)} fusion(f32[256,1024]{1,0:T(8,128)} %get-tuple-element.12, bf16[256,1024]{1,0:T(8,128)(2,1)S(1)} %collective-permute-done.7), kind=kLoop, calls=%fused_computation.8 | loop fusion | flops 786432 | bytes 2097152 | tf_op jit(solution)/shard_map/convert_element_type | solution.py:230
  36.7 1.3 %collective-permute-start.8 = (bf16[256,1024]{1,0:T(8,128)(2,1)S(1)}, bf16[256,1024]{1,0:T(8,128)(2,1)S(1)}, u32[]{:S(2)}, u32[]{:S(2)}) collective-permute-start(bf16[256,1024]{1,0:T(8,128)(2,1)S(1)} %add_convert_fusion.1), channel_id=1, source_target_pairs={{4,0},{8,4},{12,8},{5,1},{9,5},{13,9},{6,2},{10,6},{14,10},{7,3},{... | collective-permute-start | bytes 1572872 | tf_op jit(solution)/shard_map/ppermute | solution.py:21
  38.0 0.0 collective-permute-done.5
  38.0 0.0 collective-permute-done.6
  38.0 22.5 %collective-permute-done.8 = bf16[256,1024]{1,0:T(8,128)(2,1)S(1)} collective-permute-done((bf16[256,1024]{1,0:T(8,128)(2,1)S(1)}, bf16[256,1024]{1,0:T(8,128)(2,1)S(1)}, u32[]{:S(2)}, u32[]{:S(2)}) %collective-permute-start.8) | collective-permute-done | bytes 524320 | tf_op jit(solution)/shard_map/ppermute | solution.py:21
  60.5 0.0 copy-done
  60.5 0.3 add_convert_fusion
  60.8 0.9 fusion.7
  61.7 1.5 %collective-permute-start.9 = (bf16[256,512]{1,0:T(8,128)(2,1)S(1)}, bf16[256,512]{1,0:T(8,128)(2,1)S(1)}, u32[]{:S(2)}, u32[]{:S(2)}) collective-permute-start(bf16[256,512]{1,0:T(8,128)(2,1)S(1)} %get-tuple-element.23), channel_id=1, source_target_pairs={{0,2},{2,0},{1,3},{3,1},{4,6},{6,4},{5,7},{7,5},{8,10},{10,8},{9,1... | collective-permute-start | bytes 786440 | tf_op jit(solution)/shard_map/ppermute | solution.py:26
  63.1 6.8 %collective-permute-done.9 = bf16[256,512]{1,0:T(8,128)(2,1)S(1)} collective-permute-done((bf16[256,512]{1,0:T(8,128)(2,1)S(1)}, bf16[256,512]{1,0:T(8,128)(2,1)S(1)}, u32[]{:S(2)}, u32[]{:S(2)}) %collective-permute-start.9) | collective-permute-done | bytes 262176 | tf_op jit(solution)/shard_map/ppermute | solution.py:26
  70.0 1.9 %convolution_multiply_fusion = f32[1152,512]{1,0:T(8,128)S(1)} fusion(bf16[256,1152]{1,0:T(8,128)(2,1)} %collective-permute-done.4.refs_9_, bf16[256,1152]{1,0:T(8,128)(2,1)S(1)} %get-tuple-element.21, bf16[256,512]{1,0:T(8,128)(2,1)S(1)} %collective-permute-done.9, bf16[256,512]{1,0:T(8,128)(2,1)S(1)} %get-tuple-element.23), kind=kOutput, calls=%fused_computation | convolution fusion | flops 607977472 | bytes 4063232 | tf_op jit(solution)/shard_map/dot_general | solution.py:259
  71.9 0.1 dynamic-slice_convert_fusion
  72.0 0.1 collective-permute-start.10
  72.1 2.1 %collective-permute-done.10 = bf16[576,512]{1,0:T(8,128)(2,1)} collective-permute-done((bf16[576,512]{1,0:T(8,128)(2,1)S(1)}, bf16[576,512]{1,0:T(8,128)(2,1)}, u32[]{:S(2)}, u32[]{:S(2)}) %collective-permute-start.10) | collective-permute-done | bytes 589856 | tf_op jit(solution)/shard_map/ppermute | solution.py:26
  74.2 1.2 %convert_add_fusion = f32[576,512]{1,0:T(8,128)S(1)} fusion(bf16[576,512]{1,0:T(8,128)(2,1)} %collective-permute-done.10, f32[1152,512]{1,0:T(8,128)S(1)} %convolution_multiply_fusion, s32[]{:T(128)S(6)} %select_n.90), kind=kLoop, calls=%fused_computation.5 | loop fusion | flops 589824 | bytes 2949124 | tf_op jit(solution)/shard_map/add | solution.py:272
  75.4 0.1 dynamic-slice_convert_fusion.3
  75.5 5.7 %collective-permute-start.11 = (bf16[144,512]{1,0:T(8,128)(2,1)S(1)}, bf16[144,512]{1,0:T(8,128)(2,1)S(1)}, u32[]{:S(2)}, u32[]{:S(2)}) collective-permute-start(bf16[144,512]{1,0:T(8,128)(2,1)S(1)} %get-tuple-element.18), channel_id=1, source_target_pairs={{0,4},{4,8},{8,12},{12,0},{1,5},{5,9},{9,13},{13,1},{2,6},{6,10},{... | collective-permute-start | bytes 442376 | tf_op jit(solution)/shard_map/ppermute | solution.py:26
  81.1 0.0 collective-permute-start.12
  81.1 2.4 %collective-permute-start.13 = (bf16[144,512]{1,0:T(8,128)(2,1)S(1)}, bf16[144,512]{1,0:T(8,128)(2,1)S(1)}, u32[]{:S(2)}, u32[]{:S(2)}) collective-permute-start(bf16[144,512]{1,0:T(8,128)(2,1)S(1)} %get-tuple-element.19), channel_id=1, source_target_pairs={{0,12},{4,0},{8,4},{12,8},{1,13},{5,1},{9,5},{13,9},{2,14},{6,2},{... | collective-permute-start | bytes 442376 | tf_op jit(solution)/shard_map/ppermute | solution.py:26
  83.6 1.8 %collective-permute-done.11 = bf16[144,512]{1,0:T(8,128)(2,1)S(1)} collective-permute-done((bf16[144,512]{1,0:T(8,128)(2,1)S(1)}, bf16[144,512]{1,0:T(8,128)(2,1)S(1)}, u32[]{:S(2)}, u32[]{:S(2)}) %collective-permute-start.11) | collective-permute-done | bytes 147488 | tf_op jit(solution)/shard_map/ppermute | solution.py:26
  85.4 5.3 %collective-permute-done.12 = bf16[144,512]{1,0:T(8,128)(2,1)S(1)} collective-permute-done((bf16[144,512]{1,0:T(8,128)(2,1)S(1)}, bf16[144,512]{1,0:T(8,128)(2,1)S(1)}, u32[]{:S(2)}, u32[]{:S(2)}) %collective-permute-start.12) | collective-permute-done | bytes 147488 | tf_op jit(solution)/shard_map/ppermute | solution.py:26
  90.7 0.2 collective-permute-done.13
  91.0 0.1 constant_dynamic-update-slice_fusion.3
  91.0 3.5 %collective-permute-start.14 = (bf16[144,512]{1,0:T(8,128)(2,1)S(1)}, bf16[144,512]{1,0:T(8,128)(2,1)S(1)}, u32[]{:S(2)}, u32[]{:S(2)}) collective-permute-start(bf16[144,512]{1,0:T(8,128)(2,1)S(1)} %get-tuple-element.15), channel_id=1, source_target_pairs={{0,4},{4,8},{8,12},{12,0},{1,5},{5,9},{9,13},{13,1},{2,6},{6,10},{... | collective-permute-start | bytes 442376 | tf_op jit(solution)/shard_map/ppermute | solution.py:26
  94.5 3.4 %collective-permute-start.15 = (bf16[144,512]{1,0:T(8,128)(2,1)S(1)}, bf16[144,512]{1,0:T(8,128)(2,1)S(1)}, u32[]{:S(2)}, u32[]{:S(2)}) collective-permute-start(bf16[144,512]{1,0:T(8,128)(2,1)S(1)} %get-tuple-element.15), channel_id=1, source_target_pairs={{0,8},{4,12},{8,0},{12,4},{1,9},{5,13},{9,1},{13,5},{2,10},{6,14},... | collective-permute-start | bytes 442376 | tf_op jit(solution)/shard_map/ppermute | solution.py:26
  97.9 0.0 collective-permute-start.16
  97.9 4.2 %collective-permute-done.14 = bf16[144,512]{1,0:T(8,128)(2,1)S(1)} collective-permute-done((bf16[144,512]{1,0:T(8,128)(2,1)S(1)}, bf16[144,512]{1,0:T(8,128)(2,1)S(1)}, u32[]{:S(2)}, u32[]{:S(2)}) %collective-permute-start.14) | collective-permute-done | bytes 147488 | tf_op jit(solution)/shard_map/ppermute | solution.py:26
  102.1 5.2 %collective-permute-done.15 = bf16[144,512]{1,0:T(8,128)(2,1)S(1)} collective-permute-done((bf16[144,512]{1,0:T(8,128)(2,1)S(1)}, bf16[144,512]{1,0:T(8,128)(2,1)S(1)}, u32[]{:S(2)}, u32[]{:S(2)}) %collective-permute-start.15) | collective-permute-done | bytes 147488 | tf_op jit(solution)/shard_map/ppermute | solution.py:26
  107.4 0.0 collective-permute-done.16
  107.4 0.1 collective-permute-start.17
  107.5 2.0 %collective-permute-done.17 = bf16[576,512]{1,0:T(8,128)(2,1)S(1)} collective-permute-done((bf16[576,512]{1,0:T(8,128)(2,1)S(1)}, bf16[576,512]{1,0:T(8,128)(2,1)S(1)}, u32[]{:S(2)}, u32[]{:S(2)}) %collective-permute-start.17) | collective-permute-done | bytes 589856 | tf_op jit(solution)/shard_map/ppermute | solution.py:26
  109.5 0.1 broadcast_select_fusion.1
  109.6 1.7 %maximum_convert_fusion = f32[1152,512]{1,0:T(8,128)} fusion(bf16[576,512]{1,0:T(8,128)(2,1)S(1)} %get-tuple-element.17, bf16[576,512]{1,0:T(8,128)(2,1)S(1)} %get-tuple-element.16), kind=kLoop, calls=%fused_computation.4 | loop fusion | flops 2359296 | bytes 3538944 | tf_op jit(solution)/shard_map/convert_element_type | solution.py:278
  (5 shorter events, 0.1 us)
Async XLA Ops:
  0.6 18.4 %copy-start.2 = (s32[1,12]{1,0:T(1,128)S(1)}, s32[1,12]{1,0:T(1,128)}, u32[]{:S(2)}) copy-start(s32[1,12]{1,0:T(1,128)} %param.11) | copy-start | bytes 148
  1.7 21.3 %copy-start.1 = (bf16[256,1024]{1,0:T(8,128)(2,1)}, bf16[256,1024]{1,0:T(8,128)(2,1)S(1)}, u32[]{:S(2)}) copy-start(bf16[256,1024]{1,0:T(8,128)(2,1)S(1)} %pad_maximum_fusion.refs_8_) | copy-start | bytes 1572868
  1.7 17.2 %collective-permute-start = (bf16[256,1024]{1,0:T(8,128)(2,1)S(1)}, bf16[256,1024]{1,0:T(8,128)(2,1)S(1)}, u32[]{:S(2)}, u32[]{:S(2)}) collective-permute-start(bf16[256,1024]{1,0:T(8,128)(2,1)S(1)} %pad_maximum_fusion.refs_8_), channel_id=1, source_target_pairs={{0,4},{4,8},{8,12},{1,5},{5,9},{9,13},{2,6},{6,10},{10,14},{3,7},{... | collective-permute-start | bytes 1572872 | tf_op jit(solution)/shard_map/ppermute | solution.py:21
  8.1 15.0 %collective-permute-start.4 = (bf16[256,1152]{1,0:T(8,128)(2,1)S(1)}, bf16[256,1152]{1,0:T(8,128)(2,1)}, u32[]{:S(2)}, u32[]{:S(2)}) collective-permute-start(bf16[256,1152]{1,0:T(8,128)(2,1)S(1)} %get-tuple-element.22), channel_id=1, source_target_pairs={{0,2},{2,0},{1,3},{3,1},{4,6},{6,4},{5,7},{7,5},{8,10},{10,8},{9,1... | collective-permute-start | bytes 1769480 | tf_op jit(solution)/shard_map/ppermute | solution.py:26
  9.6 10.3 %collective-permute-start.1 = (bf16[256,1024]{1,0:T(8,128)(2,1)S(1)}, bf16[256,1024]{1,0:T(8,128)(2,1)S(1)}, u32[]{:S(2)}, u32[]{:S(2)}) collective-permute-start(bf16[256,1024]{1,0:T(8,128)(2,1)S(1)} %pad_maximum_fusion.refs_8_), channel_id=1, source_target_pairs={{0,1},{2,3},{4,5},{6,7},{8,9},{10,11},{12,13},{14,15},{16,17},{18,... | collective-permute-start | bytes 1572872 | tf_op jit(solution)/shard_map/ppermute | solution.py:21
  10.9 9.0 %collective-permute-start.2 = (bf16[256,1024]{1,0:T(8,128)(2,1)S(1)}, bf16[256,1024]{1,0:T(8,128)(2,1)S(1)}, u32[]{:S(2)}, u32[]{:S(2)}) collective-permute-start(bf16[256,1024]{1,0:T(8,128)(2,1)S(1)} %pad_maximum_fusion.refs_8_), channel_id=1, source_target_pairs={{1,8},{5,12},{3,10},{7,14},{17,24},{21,28},{19,26},{23,30}} | collective-permute-start | bytes 1572872 | tf_op jit(solution)/shard_map/ppermute | solution.py:211
  19.0 4.0 %copy-start.3 = (bf16[256,1024]{1,0:T(8,128)(2,1)}, bf16[256,1024]{1,0:T(8,128)(2,1)S(1)}, u32[]{:S(2)}) copy-start(bf16[256,1024]{1,0:T(8,128)(2,1)S(1)} %collective-permute-done.refs_4_) | copy-start | bytes 1572868
  19.0 4.0 %collective-permute-start.3 = (bf16[256,1024]{1,0:T(8,128)(2,1)S(1)}, bf16[256,1024]{1,0:T(8,128)(2,1)}, u32[]{:S(2)}, u32[]{:S(2)}) collective-permute-start(bf16[256,1024]{1,0:T(8,128)(2,1)S(1)} %collective-permute-done.refs_4_), channel_id=1, source_target_pairs={{0,1},{1,0},{2,3},{3,2},{4,5},{5,4},{6,7},{7,6},{8,9},{9,8},{10,11... | collective-permute-start | bytes 1572872 | tf_op jit(solution)/shard_map/ppermute | solution.py:26
  19.9 3.1 %copy-start.4 = (bf16[256,1024]{1,0:T(8,128)(2,1)}, bf16[256,1024]{1,0:T(8,128)(2,1)S(1)}, u32[]{:S(2)}) copy-start(bf16[256,1024]{1,0:T(8,128)(2,1)S(1)} %collective-permute-done.1.refs_5_) | copy-start | bytes 1572868
  19.9 3.1 %copy-start.5 = (bf16[256,1024]{1,0:T(8,128)(2,1)}, bf16[256,1024]{1,0:T(8,128)(2,1)S(1)}, u32[]{:S(2)}) copy-start(bf16[256,1024]{1,0:T(8,128)(2,1)S(1)} %collective-permute-done.2.refs_6_) | copy-start | bytes 1572868
  31.9 28.6 %copy-start = (f32[256,1024]{1,0:T(8,128)S(1)}, f32[256,1024]{1,0:T(8,128)}, u32[]{:S(2)}) copy-start(f32[256,1024]{1,0:T(8,128)} %get-tuple-element.10) | copy-start | bytes 3145732
  31.9 3.4 %collective-permute-start.7 = (bf16[256,1024]{1,0:T(8,128)(2,1)}, bf16[256,1024]{1,0:T(8,128)(2,1)S(1)}, u32[]{:S(2)}, u32[]{:S(2)}) collective-permute-start(bf16[256,1024]{1,0:T(8,128)(2,1)} %get-tuple-element.13), channel_id=1, source_target_pairs={{0,1},{1,0},{2,3},{3,2},{4,5},{5,4},{6,7},{7,6},{8,9},{9,8},{10,11... | collective-permute-start | bytes 1572872 | tf_op jit(solution)/shard_map/ppermute | solution.py:26
  33.3 4.7 %collective-permute-start.5 = (bf16[256,1024]{1,0:T(8,128)(2,1)}, bf16[256,1024]{1,0:T(8,128)(2,1)S(1)}, u32[]{:S(2)}, u32[]{:S(2)}) collective-permute-start(bf16[256,1024]{1,0:T(8,128)(2,1)} %get-tuple-element.11), channel_id=1, source_target_pairs={{1,0},{3,2},{5,4},{7,6},{9,8},{11,10},{13,12},{15,14},{17,16},{19,... | collective-permute-start | bytes 1572872 | tf_op jit(solution)/shard_map/ppermute | solution.py:21
  34.6 3.4 %collective-permute-start.6 = (bf16[256,1024]{1,0:T(8,128)(2,1)}, bf16[256,1024]{1,0:T(8,128)(2,1)S(1)}, u32[]{:S(2)}, u32[]{:S(2)}) collective-permute-start(bf16[256,1024]{1,0:T(8,128)(2,1)} %get-tuple-element.11), channel_id=1, source_target_pairs={{8,1},{12,5},{10,3},{14,7},{24,17},{28,21},{26,19},{30,23}} | collective-permute-start | bytes 1572872 | tf_op jit(solution)/shard_map/ppermute | solution.py:235
  36.7 23.8 %collective-permute-start.8 = (bf16[256,1024]{1,0:T(8,128)(2,1)S(1)}, bf16[256,1024]{1,0:T(8,128)(2,1)S(1)}, u32[]{:S(2)}, u32[]{:S(2)}) collective-permute-start(bf16[256,1024]{1,0:T(8,128)(2,1)S(1)} %add_convert_fusion.1), channel_id=1, source_target_pairs={{4,0},{8,4},{12,8},{5,1},{9,5},{13,9},{6,2},{10,6},{14,10},{7,3},{... | collective-permute-start | bytes 1572872 | tf_op jit(solution)/shard_map/ppermute | solution.py:21
  61.7 8.3 %collective-permute-start.9 = (bf16[256,512]{1,0:T(8,128)(2,1)S(1)}, bf16[256,512]{1,0:T(8,128)(2,1)S(1)}, u32[]{:S(2)}, u32[]{:S(2)}) collective-permute-start(bf16[256,512]{1,0:T(8,128)(2,1)S(1)} %get-tuple-element.23), channel_id=1, source_target_pairs={{0,2},{2,0},{1,3},{3,1},{4,6},{6,4},{5,7},{7,5},{8,10},{10,8},{9,1... | collective-permute-start | bytes 786440 | tf_op jit(solution)/shard_map/ppermute | solution.py:26
  72.0 2.2 %collective-permute-start.10 = (bf16[576,512]{1,0:T(8,128)(2,1)S(1)}, bf16[576,512]{1,0:T(8,128)(2,1)}, u32[]{:S(2)}, u32[]{:S(2)}) collective-permute-start(bf16[576,512]{1,0:T(8,128)(2,1)S(1)} %dynamic-slice_convert_fusion), channel_id=1, source_target_pairs={{0,1},{1,0},{2,3},{3,2},{4,5},{5,4},{6,7},{7,6},{8,9},{9,8},{10,11... | collective-permute-start | bytes 1769480 | tf_op jit(solution)/shard_map/ppermute | solution.py:26
  75.5 9.9 %collective-permute-start.11 = (bf16[144,512]{1,0:T(8,128)(2,1)S(1)}, bf16[144,512]{1,0:T(8,128)(2,1)S(1)}, u32[]{:S(2)}, u32[]{:S(2)}) collective-permute-start(bf16[144,512]{1,0:T(8,128)(2,1)S(1)} %get-tuple-element.18), channel_id=1, source_target_pairs={{0,4},{4,8},{8,12},{12,0},{1,5},{5,9},{9,13},{13,1},{2,6},{6,10},{... | collective-permute-start | bytes 442376 | tf_op jit(solution)/shard_map/ppermute | solution.py:26
  81.1 9.6 %collective-permute-start.12 = (bf16[144,512]{1,0:T(8,128)(2,1)S(1)}, bf16[144,512]{1,0:T(8,128)(2,1)S(1)}, u32[]{:S(2)}, u32[]{:S(2)}) collective-permute-start(bf16[144,512]{1,0:T(8,128)(2,1)S(1)} %get-tuple-element.20), channel_id=1, source_target_pairs={{0,8},{4,12},{8,0},{12,4},{1,9},{5,13},{9,1},{13,5},{2,10},{6,14},... | collective-permute-start | bytes 442376 | tf_op jit(solution)/shard_map/ppermute | solution.py:26
  81.1 9.8 %collective-permute-start.13 = (bf16[144,512]{1,0:T(8,128)(2,1)S(1)}, bf16[144,512]{1,0:T(8,128)(2,1)S(1)}, u32[]{:S(2)}, u32[]{:S(2)}) collective-permute-start(bf16[144,512]{1,0:T(8,128)(2,1)S(1)} %get-tuple-element.19), channel_id=1, source_target_pairs={{0,12},{4,0},{8,4},{12,8},{1,13},{5,1},{9,5},{13,9},{2,14},{6,2},{... | collective-permute-start | bytes 442376 | tf_op jit(solution)/shard_map/ppermute | solution.py:26
  91.0 11.1 %collective-permute-start.14 = (bf16[144,512]{1,0:T(8,128)(2,1)S(1)}, bf16[144,512]{1,0:T(8,128)(2,1)S(1)}, u32[]{:S(2)}, u32[]{:S(2)}) collective-permute-start(bf16[144,512]{1,0:T(8,128)(2,1)S(1)} %get-tuple-element.15), channel_id=1, source_target_pairs={{0,4},{4,8},{8,12},{12,0},{1,5},{5,9},{9,13},{13,1},{2,6},{6,10},{... | collective-permute-start | bytes 442376 | tf_op jit(solution)/shard_map/ppermute | solution.py:26
  94.5 12.9 %collective-permute-start.15 = (bf16[144,512]{1,0:T(8,128)(2,1)S(1)}, bf16[144,512]{1,0:T(8,128)(2,1)S(1)}, u32[]{:S(2)}, u32[]{:S(2)}) collective-permute-start(bf16[144,512]{1,0:T(8,128)(2,1)S(1)} %get-tuple-element.15), channel_id=1, source_target_pairs={{0,8},{4,12},{8,0},{12,4},{1,9},{5,13},{9,1},{13,5},{2,10},{6,14},... | collective-permute-start | bytes 442376 | tf_op jit(solution)/shard_map/ppermute | solution.py:26
  97.9 9.5 %collective-permute-start.16 = (bf16[144,512]{1,0:T(8,128)(2,1)S(1)}, bf16[144,512]{1,0:T(8,128)(2,1)S(1)}, u32[]{:S(2)}, u32[]{:S(2)}) collective-permute-start(bf16[144,512]{1,0:T(8,128)(2,1)S(1)} %get-tuple-element.15), channel_id=1, source_target_pairs={{0,12},{4,0},{8,4},{12,8},{1,13},{5,1},{9,5},{13,9},{2,14},{6,2},{... | collective-permute-start | bytes 442376 | tf_op jit(solution)/shard_map/ppermute | solution.py:26
  107.4 2.1 %collective-permute-start.17 = (bf16[576,512]{1,0:T(8,128)(2,1)S(1)}, bf16[576,512]{1,0:T(8,128)(2,1)S(1)}, u32[]{:S(2)}, u32[]{:S(2)}) collective-permute-start(bf16[576,512]{1,0:T(8,128)(2,1)S(1)} %constant_dynamic-update-slice_fusion), channel_id=1, source_target_pairs={{0,1},{1,0},{2,3},{3,2},{4,5},{5,4},{6,7},{7,6},{8,9},{9,8},{10,11... | collective-permute-start | bytes 1769480 | tf_op jit(solution)/shard_map/ppermute | solution.py:26

commit v19 on v18

--- a/solution.py
+++ b/solution.py
@@ -98,9 +98,10 @@
             largest = jnp.max(scores, axis=1, keepdims=True)
             raised = jnp.exp(scores - largest)
             probs = raised * (1.0 / jnp.sum(raised, axis=1, keepdims=True))
-            grad_probs = lax.dot_general(grad_h, value_g, NT, preferred_element_type=jnp.float32)
+            grad_scaled = grad_h * jnp.asarray(scale, grad_h.dtype)
+            grad_probs = lax.dot_general(grad_scaled, value_g, NT, preferred_element_type=jnp.float32)
             row_dot = jnp.sum(probs * grad_probs, axis=1, keepdims=True)
-            grad_scores = (probs * (grad_probs - row_dot) * scale).astype(jnp.bfloat16)
+            grad_scores = (probs * (grad_probs - row_dot)).astype(jnp.bfloat16)
             probs_low = probs.astype(jnp.bfloat16)
             dq_ref[:, q_cols] = jnp.dot(
                 grad_scores, key_g, preferred_element_type=jnp.float32

time: 113 us -> 113 us (level)
  no operation moved by 1% of the time
where the time goes in v19:
time: 113 us; the launch traced here: 111 us
  waiting for transfers between devices  60.6 us (54%)
  starting transfers between devices  29.8 us (26%)
  Pallas kernels  8.84 us (8%)
  other arithmetic  6.7 us (6%)
  local copies, waits for them, and re-layouts  2.59 us (2%)
  matrix products  1.87 us (2%)
    ppermute x12, waiting for transfers between devices, rotated(): lax.ppermute(value, axis, [(source, (source + steps) % count) for source...  30.8 us
    ppermute x4, waiting for transfers between devices, passed_along(): lax.ppermute(value, axis, [(source, source + steps) for source in range(f...  29.8 us
    ppermute x12, starting transfers between devices, rotated(): lax.ppermute(value, axis, [(source, (source + steps) % count) for source...  19.5 us
    ppermute x4, starting transfers between devices, passed_along(): lax.ppermute(value, axis, [(source, source + steps) for source in range(f...  8.84 us
    pallas_call x1, Pallas kernels, attention(): pl.pallas_call(kernel, out_shape=(jax.ShapeDtypeStruct((rows, width), jnp...  8.84 us
  transfers between devices with their start and end apart: 18, of which 11 were waited for; matrix products, arithmetic and copies ran while one was open for 3% of the time, Pallas kernels for 0%

profile of v19, /device:TPU:0, one launch (start us, length us, event | category | flops | bytes accessed | tf_op | source)
XLA Modules:
  0.0 111.3 jit_solution(6762208107352928491)
XLA Ops:
  0.6 0.0 copy-start.2
  0.6 1.1 pad_maximum_fusion.refs_8_
  1.7 0.0 copy-start.1
  1.7 5.0 %collective-permute-start = (bf16[256,1024]{1,0:T(8,128)(2,1)S(1)}, bf16[256,1024]{1,0:T(8,128)(2,1)S(1)}, u32[]{:S(2)}, u32[]{:S(2)}) collective-permute-start(bf16[256,1024]{1,0:T(8,128)(2,1)S(1)} %pad_maximum_fusion.refs_8_), channel_id=1, source_target_pairs={{0,4},{4,8},{8,12},{1,5},{5,9},{9,13},{2,6},{6,10},{10,14},{3,7},{... | collective-permute-start | bytes 1572872 | tf_op jit(solution)/shard_map/ppermute | solution.py:21
  6.7 1.3 %dynamic-slice_bitcast_fusion = (bf16[256,1152]{1,0:T(8,128)(2,1)S(1)}, bf16[256,1152]{1,0:T(8,128)(2,1)S(1)}) fusion(bf16[1,256,2304]{2,1,0:T(8,128)(2,1)} %param.6, s32[]{:T(128)S(6)} %select_n.89, s32[]{:T(128)S(6)} %select_n.87), kind=kLoop, calls=%fused_computation.9 | loop fusion | bytes 2359304 | tf_op jit(solution)/shard_map/dynamic_slice | solution.py:193
  8.1 1.6 %collective-permute-start.4 = (bf16[256,1152]{1,0:T(8,128)(2,1)S(1)}, bf16[256,1152]{1,0:T(8,128)(2,1)}, u32[]{:S(2)}, u32[]{:S(2)}) collective-permute-start(bf16[256,1152]{1,0:T(8,128)(2,1)S(1)} %get-tuple-element.22), channel_id=1, source_target_pairs={{0,2},{2,0},{1,3},{3,1},{4,6},{6,4},{5,7},{7,5},{8,10},{10,8},{9,1... | collective-permute-start | bytes 1769480 | tf_op jit(solution)/shard_map/ppermute | solution.py:26
  9.6 1.3 %collective-permute-start.1 = (bf16[256,1024]{1,0:T(8,128)(2,1)S(1)}, bf16[256,1024]{1,0:T(8,128)(2,1)S(1)}, u32[]{:S(2)}, u32[]{:S(2)}) collective-permute-start(bf16[256,1024]{1,0:T(8,128)(2,1)S(1)} %pad_maximum_fusion.refs_8_), channel_id=1, source_target_pairs={{0,1},{2,3},{4,5},{6,7},{8,9},{10,11},{12,13},{14,15},{16,17},{18,... | collective-permute-start | bytes 1572872 | tf_op jit(solution)/shard_map/ppermute | solution.py:21
  10.9 0.7 collective-permute-start.2
  11.6 7.3 %collective-permute-done.refs_4_ = bf16[256,1024]{1,0:T(8,128)(2,1)S(1)} collective-permute-done((bf16[256,1024]{1,0:T(8,128)(2,1)S(1)}, bf16[256,1024]{1,0:T(8,128)(2,1)S(1)}, u32[]{:S(2)}, u32[]{:S(2)}) %collective-permute-start) | collective-permute-done | bytes 524320 | tf_op jit(solution)/shard_map/ppermute | solution.py:21
  19.0 0.0 copy-start.3
  19.0 0.0 collective-permute-start.3
  19.0 0.0 copy-done.2
  19.0 0.1 select_reduce_fusion
  19.1 0.1 copy.13
  19.2 0.7 subtract_add_fusion.refs_1_
  19.9 0.0 collective-permute-done.1.refs_5_
  19.9 0.0 copy-start.4
  19.9 0.0 collective-permute-done.2.refs_6_
  19.9 0.0 copy-start.5
  20.0 3.1 %collective-permute-done.4.refs_9_ = bf16[256,1152]{1,0:T(8,128)(2,1)} collective-permute-done((bf16[256,1152]{1,0:T(8,128)(2,1)S(1)}, bf16[256,1152]{1,0:T(8,128)(2,1)}, u32[]{:S(2)}, u32[]{:S(2)}) %collective-permute-start.4) | collective-permute-done | bytes 589856 | tf_op jit(solution)/shard_map/ppermute | solution.py:26
  23.0 0.0 collective-permute-done.3.refs_7_
  23.0 0.0 copy-done.1
  23.0 0.0 copy-done.3
  23.0 0.0 copy-done.4
  23.1 0.0 copy-done.5
  23.1 8.8 %shard_map.93 = (bf16[256,1024]{1,0:T(8,128)(2,1)}, bf16[256,1024]{1,0:T(8,128)(2,1)}, bf16[256,1024]{1,0:T(8,128)(2,1)}, f32[256,1024]{1,0:T(8,128)}, f32[256,1024]{1,0:T(8,128)}) custom-call(s32[1]{0:T(128)} %bitcast.refs_0_, s32[256,1]{1,0:T(8,128)} %subtract_add_fusion.refs_1_, bf16[256,1024]{1,0:T(8,128)(2,1)} %bitcast.20, bf16[256,1024]{1,0:T(8,128)(2,1)} %bitcast.21, ...), custom_call_target="tpu_custom_call" | custom-call | flops 2684354560 | bytes 7864320 | tf_op jit(solution)/shard_map/pallas_call | solution.py:162
  31.9 0.0 copy-start
  31.9 1.4 %collective-permute-start.7 = (bf16[256,1024]{1,0:T(8,128)(2,1)}, bf16[256,1024]{1,0:T(8,128)(2,1)S(1)}, u32[]{:S(2)}, u32[]{:S(2)}) collective-permute-start(bf16[256,1024]{1,0:T(8,128)(2,1)} %get-tuple-element.13), channel_id=1, source_target_pairs={{0,1},{1,0},{2,3},{3,2},{4,5},{5,4},{6,7},{7,6},{8,9},{9,8},{10,11... | collective-permute-start | bytes 1572872 | tf_op jit(solution)/shard_map/ppermute | solution.py:26
  33.3 1.3 %collective-permute-start.5 = (bf16[256,1024]{1,0:T(8,128)(2,1)}, bf16[256,1024]{1,0:T(8,128)(2,1)S(1)}, u32[]{:S(2)}, u32[]{:S(2)}) collective-permute-start(bf16[256,1024]{1,0:T(8,128)(2,1)} %get-tuple-element.11), channel_id=1, source_target_pairs={{1,0},{3,2},{5,4},{7,6},{9,8},{11,10},{13,12},{15,14},{17,16},{19,... | collective-permute-start | bytes 1572872 | tf_op jit(solution)/shard_map/ppermute | solution.py:21
  34.6 0.7 collective-permute-start.6
  35.3 0.0 collective-permute-done.7
  35.3 1.4 %add_convert_fusion.1 = bf16[256,1024]{1,0:T(8,128)(2,1)S(1)} fusion(f32[256,1024]{1,0:T(8,128)} %get-tuple-element.12, bf16[256,1024]{1,0:T(8,128)(2,1)S(1)} %collective-permute-done.7), kind=kLoop, calls=%fused_computation.8 | loop fusion | flops 786432 | bytes 2097152 | tf_op jit(solution)/shard_map/convert_element_type | solution.py:231
  36.7 1.3 %collective-permute-start.8 = (bf16[256,1024]{1,0:T(8,128)(2,1)S(1)}, bf16[256,1024]{1,0:T(8,128)(2,1)S(1)}, u32[]{:S(2)}, u32[]{:S(2)}) collective-permute-start(bf16[256,1024]{1,0:T(8,128)(2,1)S(1)} %add_convert_fusion.1), channel_id=1, source_target_pairs={{4,0},{8,4},{12,8},{5,1},{9,5},{13,9},{6,2},{10,6},{14,10},{7,3},{... | collective-permute-start | bytes 1572872 | tf_op jit(solution)/shard_map/ppermute | solution.py:21
  38.0 0.0 collective-permute-done.5
  38.0 0.0 collective-permute-done.6
  38.0 22.5 %collective-permute-done.8 = bf16[256,1024]{1,0:T(8,128)(2,1)S(1)} collective-permute-done((bf16[256,1024]{1,0:T(8,128)(2,1)S(1)}, bf16[256,1024]{1,0:T(8,128)(2,1)S(1)}, u32[]{:S(2)}, u32[]{:S(2)}) %collective-permute-start.8) | collective-permute-done | bytes 524320 | tf_op jit(solution)/shard_map/ppermute | solution.py:21
  60.5 0.0 copy-done
  60.5 0.3 add_convert_fusion
  60.8 0.9 fusion.7
  61.6 1.5 %collective-permute-start.9 = (bf16[256,512]{1,0:T(8,128)(2,1)S(1)}, bf16[256,512]{1,0:T(8,128)(2,1)S(1)}, u32[]{:S(2)}, u32[]{:S(2)}) collective-permute-start(bf16[256,512]{1,0:T(8,128)(2,1)S(1)} %get-tuple-element.23), channel_id=1, source_target_pairs={{0,2},{2,0},{1,3},{3,1},{4,6},{6,4},{5,7},{7,5},{8,10},{10,8},{9,1... | collective-permute-start | bytes 786440 | tf_op jit(solution)/shard_map/ppermute | solution.py:26
  63.1 6.8 %collective-permute-done.9 = bf16[256,512]{1,0:T(8,128)(2,1)S(1)} collective-permute-done((bf16[256,512]{1,0:T(8,128)(2,1)S(1)}, bf16[256,512]{1,0:T(8,128)(2,1)S(1)}, u32[]{:S(2)}, u32[]{:S(2)}) %collective-permute-start.9) | collective-permute-done | bytes 262176 | tf_op jit(solution)/shard_map/ppermute | solution.py:26
  70.0 1.9 %convolution_multiply_fusion = f32[1152,512]{1,0:T(8,128)S(1)} fusion(bf16[256,1152]{1,0:T(8,128)(2,1)} %collective-permute-done.4.refs_9_, bf16[256,1152]{1,0:T(8,128)(2,1)S(1)} %get-tuple-element.21, bf16[256,512]{1,0:T(8,128)(2,1)S(1)} %collective-permute-done.9, bf16[256,512]{1,0:T(8,128)(2,1)S(1)} %get-tuple-element.23), kind=kOutput, calls=%fused_computation | convolution fusion | flops 607977472 | bytes 4063232 | tf_op jit(solution)/shard_map/dot_general | solution.py:260
  71.8 0.1 dynamic-slice_convert_fusion
  71.9 0.1 collective-permute-start.10
  72.1 2.1 %collective-permute-done.10 = bf16[576,512]{1,0:T(8,128)(2,1)} collective-permute-done((bf16[576,512]{1,0:T(8,128)(2,1)S(1)}, bf16[576,512]{1,0:T(8,128)(2,1)}, u32[]{:S(2)}, u32[]{:S(2)}) %collective-permute-start.10) | collective-permute-done | bytes 589856 | tf_op jit(solution)/shard_map/ppermute | solution.py:26
  74.1 1.2 %convert_add_fusion = f32[576,512]{1,0:T(8,128)S(1)} fusion(bf16[576,512]{1,0:T(8,128)(2,1)} %collective-permute-done.10, f32[1152,512]{1,0:T(8,128)S(1)} %convolution_multiply_fusion, s32[]{:T(128)S(6)} %select_n.90), kind=kLoop, calls=%fused_computation.5 | loop fusion | flops 589824 | bytes 2949124 | tf_op jit(solution)/shard_map/add | solution.py:273
  75.4 0.1 dynamic-slice_convert_fusion.3
  75.5 5.7 %collective-permute-start.11 = (bf16[144,512]{1,0:T(8,128)(2,1)S(1)}, bf16[144,512]{1,0:T(8,128)(2,1)S(1)}, u32[]{:S(2)}, u32[]{:S(2)}) collective-permute-start(bf16[144,512]{1,0:T(8,128)(2,1)S(1)} %get-tuple-element.18), channel_id=1, source_target_pairs={{0,4},{4,8},{8,12},{12,0},{1,5},{5,9},{9,13},{13,1},{2,6},{6,10},{... | collective-permute-start | bytes 442376 | tf_op jit(solution)/shard_map/ppermute | solution.py:26
  81.1 0.0 collective-permute-start.12
  81.1 2.4 %collective-permute-start.13 = (bf16[144,512]{1,0:T(8,128)(2,1)S(1)}, bf16[144,512]{1,0:T(8,128)(2,1)S(1)}, u32[]{:S(2)}, u32[]{:S(2)}) collective-permute-start(bf16[144,512]{1,0:T(8,128)(2,1)S(1)} %get-tuple-element.19), channel_id=1, source_target_pairs={{0,12},{4,0},{8,4},{12,8},{1,13},{5,1},{9,5},{13,9},{2,14},{6,2},{... | collective-permute-start | bytes 442376 | tf_op jit(solution)/shard_map/ppermute | solution.py:26
  83.6 1.8 %collective-permute-done.11 = bf16[144,512]{1,0:T(8,128)(2,1)S(1)} collective-permute-done((bf16[144,512]{1,0:T(8,128)(2,1)S(1)}, bf16[144,512]{1,0:T(8,128)(2,1)S(1)}, u32[]{:S(2)}, u32[]{:S(2)}) %collective-permute-start.11) | collective-permute-done | bytes 147488 | tf_op jit(solution)/shard_map/ppermute | solution.py:26
  85.3 5.3 %collective-permute-done.12 = bf16[144,512]{1,0:T(8,128)(2,1)S(1)} collective-permute-done((bf16[144,512]{1,0:T(8,128)(2,1)S(1)}, bf16[144,512]{1,0:T(8,128)(2,1)S(1)}, u32[]{:S(2)}, u32[]{:S(2)}) %collective-permute-start.12) | collective-permute-done | bytes 147488 | tf_op jit(solution)/shard_map/ppermute | solution.py:26
  90.7 0.2 collective-permute-done.13
  90.9 0.1 constant_dynamic-update-slice_fusion.3
  91.0 3.5 %collective-permute-start.14 = (bf16[144,512]{1,0:T(8,128)(2,1)S(1)}, bf16[144,512]{1,0:T(8,128)(2,1)S(1)}, u32[]{:S(2)}, u32[]{:S(2)}) collective-permute-start(bf16[144,512]{1,0:T(8,128)(2,1)S(1)} %get-tuple-element.15), channel_id=1, source_target_pairs={{0,4},{4,8},{8,12},{12,0},{1,5},{5,9},{9,13},{13,1},{2,6},{6,10},{... | collective-permute-start | bytes 442376 | tf_op jit(solution)/shard_map/ppermute | solution.py:26
  94.5 3.4 %collective-permute-start.15 = (bf16[144,512]{1,0:T(8,128)(2,1)S(1)}, bf16[144,512]{1,0:T(8,128)(2,1)S(1)}, u32[]{:S(2)}, u32[]{:S(2)}) collective-permute-start(bf16[144,512]{1,0:T(8,128)(2,1)S(1)} %get-tuple-element.15), channel_id=1, source_target_pairs={{0,8},{4,12},{8,0},{12,4},{1,9},{5,13},{9,1},{13,5},{2,10},{6,14},... | collective-permute-start | bytes 442376 | tf_op jit(solution)/shard_map/ppermute | solution.py:26
  97.9 0.0 collective-permute-start.16
  97.9 4.2 %collective-permute-done.14 = bf16[144,512]{1,0:T(8,128)(2,1)S(1)} collective-permute-done((bf16[144,512]{1,0:T(8,128)(2,1)S(1)}, bf16[144,512]{1,0:T(8,128)(2,1)S(1)}, u32[]{:S(2)}, u32[]{:S(2)}) %collective-permute-start.14) | collective-permute-done | bytes 147488 | tf_op jit(solution)/shard_map/ppermute | solution.py:26
  102.1 5.2 %collective-permute-done.15 = bf16[144,512]{1,0:T(8,128)(2,1)S(1)} collective-permute-done((bf16[144,512]{1,0:T(8,128)(2,1)S(1)}, bf16[144,512]{1,0:T(8,128)(2,1)S(1)}, u32[]{:S(2)}, u32[]{:S(2)}) %collective-permute-start.15) | collective-permute-done | bytes 147488 | tf_op jit(solution)/shard_map/ppermute | solution.py:26
  107.4 0.0 collective-permute-done.16
  107.4 0.1 collective-permute-start.17
  107.5 2.0 %collective-permute-done.17 = bf16[576,512]{1,0:T(8,128)(2,1)S(1)} collective-permute-done((bf16[576,512]{1,0:T(8,128)(2,1)S(1)}, bf16[576,512]{1,0:T(8,128)(2,1)S(1)}, u32[]{:S(2)}, u32[]{:S(2)}) %collective-permute-start.17) | collective-permute-done | bytes 589856 | tf_op jit(solution)/shard_map/ppermute | solution.py:26
  109.5 0.1 broadcast_select_fusion.1
  109.6 1.7 %maximum_convert_fusion = f32[1152,512]{1,0:T(8,128)} fusion(bf16[576,512]{1,0:T(8,128)(2,1)S(1)} %get-tuple-element.17, bf16[576,512]{1,0:T(8,128)(2,1)S(1)} %get-tuple-element.16), kind=kLoop, calls=%fused_computation.4 | loop fusion | flops 2359296 | bytes 3538944 | tf_op jit(solution)/shard_map/convert_element_type | solution.py:279
  (5 shorter events, 0.1 us)
Async XLA Ops:
  0.6 18.4 %copy-start.2 = (s32[1,12]{1,0:T(1,128)S(1)}, s32[1,12]{1,0:T(1,128)}, u32[]{:S(2)}) copy-start(s32[1,12]{1,0:T(1,128)} %param.11) | copy-start | bytes 148
  1.7 21.3 %copy-start.1 = (bf16[256,1024]{1,0:T(8,128)(2,1)}, bf16[256,1024]{1,0:T(8,128)(2,1)S(1)}, u32[]{:S(2)}) copy-start(bf16[256,1024]{1,0:T(8,128)(2,1)S(1)} %pad_maximum_fusion.refs_8_) | copy-start | bytes 1572868
  1.7 17.2 %collective-permute-start = (bf16[256,1024]{1,0:T(8,128)(2,1)S(1)}, bf16[256,1024]{1,0:T(8,128)(2,1)S(1)}, u32[]{:S(2)}, u32[]{:S(2)}) collective-permute-start(bf16[256,1024]{1,0:T(8,128)(2,1)S(1)} %pad_maximum_fusion.refs_8_), channel_id=1, source_target_pairs={{0,4},{4,8},{8,12},{1,5},{5,9},{9,13},{2,6},{6,10},{10,14},{3,7},{... | collective-permute-start | bytes 1572872 | tf_op jit(solution)/shard_map/ppermute | solution.py:21
  8.1 15.0 %collective-permute-start.4 = (bf16[256,1152]{1,0:T(8,128)(2,1)S(1)}, bf16[256,1152]{1,0:T(8,128)(2,1)}, u32[]{:S(2)}, u32[]{:S(2)}) collective-permute-start(bf16[256,1152]{1,0:T(8,128)(2,1)S(1)} %get-tuple-element.22), channel_id=1, source_target_pairs={{0,2},{2,0},{1,3},{3,1},{4,6},{6,4},{5,7},{7,5},{8,10},{10,8},{9,1... | collective-permute-start | bytes 1769480 | tf_op jit(solution)/shard_map/ppermute | solution.py:26
  9.6 10.3 %collective-permute-start.1 = (bf16[256,1024]{1,0:T(8,128)(2,1)S(1)}, bf16[256,1024]{1,0:T(8,128)(2,1)S(1)}, u32[]{:S(2)}, u32[]{:S(2)}) collective-permute-start(bf16[256,1024]{1,0:T(8,128)(2,1)S(1)} %pad_maximum_fusion.refs_8_), channel_id=1, source_target_pairs={{0,1},{2,3},{4,5},{6,7},{8,9},{10,11},{12,13},{14,15},{16,17},{18,... | collective-permute-start | bytes 1572872 | tf_op jit(solution)/shard_map/ppermute | solution.py:21
  10.9 9.0 %collective-permute-start.2 = (bf16[256,1024]{1,0:T(8,128)(2,1)S(1)}, bf16[256,1024]{1,0:T(8,128)(2,1)S(1)}, u32[]{:S(2)}, u32[]{:S(2)}) collective-permute-start(bf16[256,1024]{1,0:T(8,128)(2,1)S(1)} %pad_maximum_fusion.refs_8_), channel_id=1, source_target_pairs={{1,8},{5,12},{3,10},{7,14},{17,24},{21,28},{19,26},{23,30}} | collective-permute-start | bytes 1572872 | tf_op jit(solution)/shard_map/ppermute | solution.py:212
  19.0 4.0 %copy-start.3 = (bf16[256,1024]{1,0:T(8,128)(2,1)}, bf16[256,1024]{1,0:T(8,128)(2,1)S(1)}, u32[]{:S(2)}) copy-start(bf16[256,1024]{1,0:T(8,128)(2,1)S(1)} %collective-permute-done.refs_4_) | copy-start | bytes 1572868
  19.0 4.0 %collective-permute-start.3 = (bf16[256,1024]{1,0:T(8,128)(2,1)S(1)}, bf16[256,1024]{1,0:T(8,128)(2,1)}, u32[]{:S(2)}, u32[]{:S(2)}) collective-permute-start(bf16[256,1024]{1,0:T(8,128)(2,1)S(1)} %collective-permute-done.refs_4_), channel_id=1, source_target_pairs={{0,1},{1,0},{2,3},{3,2},{4,5},{5,4},{6,7},{7,6},{8,9},{9,8},{10,11... | collective-permute-start | bytes 1572872 | tf_op jit(solution)/shard_map/ppermute | solution.py:26
  19.9 3.1 %copy-start.4 = (bf16[256,1024]{1,0:T(8,128)(2,1)}, bf16[256,1024]{1,0:T(8,128)(2,1)S(1)}, u32[]{:S(2)}) copy-start(bf16[256,1024]{1,0:T(8,128)(2,1)S(1)} %collective-permute-done.1.refs_5_) | copy-start | bytes 1572868
  19.9 3.1 %copy-start.5 = (bf16[256,1024]{1,0:T(8,128)(2,1)}, bf16[256,1024]{1,0:T(8,128)(2,1)S(1)}, u32[]{:S(2)}) copy-start(bf16[256,1024]{1,0:T(8,128)(2,1)S(1)} %collective-permute-done.2.refs_6_) | copy-start | bytes 1572868
  31.9 28.6 %copy-start = (f32[256,1024]{1,0:T(8,128)S(1)}, f32[256,1024]{1,0:T(8,128)}, u32[]{:S(2)}) copy-start(f32[256,1024]{1,0:T(8,128)} %get-tuple-element.10) | copy-start | bytes 3145732
  31.9 3.4 %collective-permute-start.7 = (bf16[256,1024]{1,0:T(8,128)(2,1)}, bf16[256,1024]{1,0:T(8,128)(2,1)S(1)}, u32[]{:S(2)}, u32[]{:S(2)}) collective-permute-start(bf16[256,1024]{1,0:T(8,128)(2,1)} %get-tuple-element.13), channel_id=1, source_target_pairs={{0,1},{1,0},{2,3},{3,2},{4,5},{5,4},{6,7},{7,6},{8,9},{9,8},{10,11... | collective-permute-start | bytes 1572872 | tf_op jit(solution)/shard_map/ppermute | solution.py:26
  33.3 4.7 %collective-permute-start.5 = (bf16[256,1024]{1,0:T(8,128)(2,1)}, bf16[256,1024]{1,0:T(8,128)(2,1)S(1)}, u32[]{:S(2)}, u32[]{:S(2)}) collective-permute-start(bf16[256,1024]{1,0:T(8,128)(2,1)} %get-tuple-element.11), channel_id=1, source_target_pairs={{1,0},{3,2},{5,4},{7,6},{9,8},{11,10},{13,12},{15,14},{17,16},{19,... | collective-permute-start | bytes 1572872 | tf_op jit(solution)/shard_map/ppermute | solution.py:21
  34.6 3.4 %collective-permute-start.6 = (bf16[256,1024]{1,0:T(8,128)(2,1)}, bf16[256,1024]{1,0:T(8,128)(2,1)S(1)}, u32[]{:S(2)}, u32[]{:S(2)}) collective-permute-start(bf16[256,1024]{1,0:T(8,128)(2,1)} %get-tuple-element.11), channel_id=1, source_target_pairs={{8,1},{12,5},{10,3},{14,7},{24,17},{28,21},{26,19},{30,23}} | collective-permute-start | bytes 1572872 | tf_op jit(solution)/shard_map/ppermute | solution.py:236
  36.7 23.8 %collective-permute-start.8 = (bf16[256,1024]{1,0:T(8,128)(2,1)S(1)}, bf16[256,1024]{1,0:T(8,128)(2,1)S(1)}, u32[]{:S(2)}, u32[]{:S(2)}) collective-permute-start(bf16[256,1024]{1,0:T(8,128)(2,1)S(1)} %add_convert_fusion.1), channel_id=1, source_target_pairs={{4,0},{8,4},{12,8},{5,1},{9,5},{13,9},{6,2},{10,6},{14,10},{7,3},{... | collective-permute-start | bytes 1572872 | tf_op jit(solution)/shard_map/ppermute | solution.py:21
  61.6 8.3 %collective-permute-start.9 = (bf16[256,512]{1,0:T(8,128)(2,1)S(1)}, bf16[256,512]{1,0:T(8,128)(2,1)S(1)}, u32[]{:S(2)}, u32[]{:S(2)}) collective-permute-start(bf16[256,512]{1,0:T(8,128)(2,1)S(1)} %get-tuple-element.23), channel_id=1, source_target_pairs={{0,2},{2,0},{1,3},{3,1},{4,6},{6,4},{5,7},{7,5},{8,10},{10,8},{9,1... | collective-permute-start | bytes 786440 | tf_op jit(solution)/shard_map/ppermute | solution.py:26
  71.9 2.2 %collective-permute-start.10 = (bf16[576,512]{1,0:T(8,128)(2,1)S(1)}, bf16[576,512]{1,0:T(8,128)(2,1)}, u32[]{:S(2)}, u32[]{:S(2)}) collective-permute-start(bf16[576,512]{1,0:T(8,128)(2,1)S(1)} %dynamic-slice_convert_fusion), channel_id=1, source_target_pairs={{0,1},{1,0},{2,3},{3,2},{4,5},{5,4},{6,7},{7,6},{8,9},{9,8},{10,11... | collective-permute-start | bytes 1769480 | tf_op jit(solution)/shard_map/ppermute | solution.py:26
  75.5 9.9 %collective-permute-start.11 = (bf16[144,512]{1,0:T(8,128)(2,1)S(1)}, bf16[144,512]{1,0:T(8,128)(2,1)S(1)}, u32[]{:S(2)}, u32[]{:S(2)}) collective-permute-start(bf16[144,512]{1,0:T(8,128)(2,1)S(1)} %get-tuple-element.18), channel_id=1, source_target_pairs={{0,4},{4,8},{8,12},{12,0},{1,5},{5,9},{9,13},{13,1},{2,6},{6,10},{... | collective-permute-start | bytes 442376 | tf_op jit(solution)/shard_map/ppermute | solution.py:26
  81.1 9.6 %collective-permute-start.12 = (bf16[144,512]{1,0:T(8,128)(2,1)S(1)}, bf16[144,512]{1,0:T(8,128)(2,1)S(1)}, u32[]{:S(2)}, u32[]{:S(2)}) collective-permute-start(bf16[144,512]{1,0:T(8,128)(2,1)S(1)} %get-tuple-element.20), channel_id=1, source_target_pairs={{0,8},{4,12},{8,0},{12,4},{1,9},{5,13},{9,1},{13,5},{2,10},{6,14},... | collective-permute-start | bytes 442376 | tf_op jit(solution)/shard_map/ppermute | solution.py:26
  81.1 9.8 %collective-permute-start.13 = (bf16[144,512]{1,0:T(8,128)(2,1)S(1)}, bf16[144,512]{1,0:T(8,128)(2,1)S(1)}, u32[]{:S(2)}, u32[]{:S(2)}) collective-permute-start(bf16[144,512]{1,0:T(8,128)(2,1)S(1)} %get-tuple-element.19), channel_id=1, source_target_pairs={{0,12},{4,0},{8,4},{12,8},{1,13},{5,1},{9,5},{13,9},{2,14},{6,2},{... | collective-permute-start | bytes 442376 | tf_op jit(solution)/shard_map/ppermute | solution.py:26
  91.0 11.1 %collective-permute-start.14 = (bf16[144,512]{1,0:T(8,128)(2,1)S(1)}, bf16[144,512]{1,0:T(8,128)(2,1)S(1)}, u32[]{:S(2)}, u32[]{:S(2)}) collective-permute-start(bf16[144,512]{1,0:T(8,128)(2,1)S(1)} %get-tuple-element.15), channel_id=1, source_target_pairs={{0,4},{4,8},{8,12},{12,0},{1,5},{5,9},{9,13},{13,1},{2,6},{6,10},{... | collective-permute-start | bytes 442376 | tf_op jit(solution)/shard_map/ppermute | solution.py:26
  94.5 12.9 %collective-permute-start.15 = (bf16[144,512]{1,0:T(8,128)(2,1)S(1)}, bf16[144,512]{1,0:T(8,128)(2,1)S(1)}, u32[]{:S(2)}, u32[]{:S(2)}) collective-permute-start(bf16[144,512]{1,0:T(8,128)(2,1)S(1)} %get-tuple-element.15), channel_id=1, source_target_pairs={{0,8},{4,12},{8,0},{12,4},{1,9},{5,13},{9,1},{13,5},{2,10},{6,14},... | collective-permute-start | bytes 442376 | tf_op jit(solution)/shard_map/ppermute | solution.py:26
  97.9 9.5 %collective-permute-start.16 = (bf16[144,512]{1,0:T(8,128)(2,1)S(1)}, bf16[144,512]{1,0:T(8,128)(2,1)S(1)}, u32[]{:S(2)}, u32[]{:S(2)}) collective-permute-start(bf16[144,512]{1,0:T(8,128)(2,1)S(1)} %get-tuple-element.15), channel_id=1, source_target_pairs={{0,12},{4,0},{8,4},{12,8},{1,13},{5,1},{9,5},{13,9},{2,14},{6,2},{... | collective-permute-start | bytes 442376 | tf_op jit(solution)/shard_map/ppermute | solution.py:26
  107.4 2.1 %collective-permute-start.17 = (bf16[576,512]{1,0:T(8,128)(2,1)S(1)}, bf16[576,512]{1,0:T(8,128)(2,1)S(1)}, u32[]{:S(2)}, u32[]{:S(2)}) collective-permute-start(bf16[576,512]{1,0:T(8,128)(2,1)S(1)} %constant_dynamic-update-slice_fusion), channel_id=1, source_target_pairs={{0,1},{1,0},{2,3},{3,2},{4,5},{5,4},{6,7},{7,6},{8,9},{9,8},{10,11... | collective-permute-start | bytes 1769480 | tf_op jit(solution)/shard_map/ppermute | solution.py:26
